TPU v7x, 32 devices: a whole 2x2x4 slice. The times are simulated.
32 devices in a mesh: dp: 8 (over z, core), shard: 4 (over y, x).
Axes of the slice: x: 2, y: 2, z: 4, core: 2. Of those that a mesh axis runs over, the one named last changes fastest.
Arguments:
- grad_partials: bfloat16 [8, 32, 256, 256], P('dp', 'shard'), may hold values from -8 to 8
- owners: int32 [32, 1], P('shard'), may hold values from 0 to 7; in each aligned block of 8 rows (0 to 7, 8 to 15, ...) at most 2 rows name the same one
- weight_blocks: int32 [9], replicated, may hold values from 1 to 8, 32 in all
- stats_left: float32 [8, 4, 2, 256, 256], P('dp', 'shard'), may hold values from -6 to 6
- stats_right: float32 [8, 4, 2, 256, 256], P('dp', 'shard'), may hold values from -6 to 6
- root_left: bfloat16 [8, 4, 2, 256, 256], P('dp', 'shard'), may hold values from -0.375 to 0.375
- root_right: bfloat16 [8, 4, 2, 256, 256], P('dp', 'shard'), may hold values from -0.375 to 0.375
- second_moment: float32 [8, 4, 2, 256, 256], P('dp', 'shard'), may hold values from 0.0015 to 0.6
- master: float32 [8, 4, 2, 256, 256], P('dp', 'shard'), may hold values from -6 to 6
Outputs:
- new_left: float32 [8, 4, 2, 256, 256], P('dp', 'shard')
- new_right: float32 [8, 4, 2, 256, 256], P('dp', 'shard')
- new_moment: float32 [8, 4, 2, 256, 256], P('dp', 'shard')
- new_master: float32 [8, 4, 2, 256, 256], P('dp', 'shard')
- regathered: bfloat16 [32, 256, 256], P('shard')
Inputs may be any that keep to these rules, and one draw needn't show every extreme that they name: `owners`: in each aligned block of 8 rows (one column) no dp index is named more than 2 times; some column names one exactly 2 times. `weight_blocks`: sums to 32; the largest is 8.
All inputs are finite; a program needn't handle non-finite values.
Results may differ from a plain program's by a relative error of at most 0.0047.
Values may be sent and summed in bfloat16 or wider, within the bound.
No kernel may reach another device: no remote copies, remote signals or barrier semaphores. Data moves between devices by JAX's collectives and lax.ppermute only.
A program may use at most 128 MiB of HBM per device.

v0:
```python
import jax
import jax.numpy as jnp
from jax import lax
from jax.sharding import PartitionSpec as P

BETA = 0.95
RATE = 0.3
ADAM_EPS = 1e-08
NORM_EPS = 1e-06


def local(
    grad_partials,
    owners,
    weight_blocks,
    stats_left,
    stats_right,
    root_left,
    root_right,
    second_moment,
    master,
):
    replica = lax.axis_index("dp")
    column = lax.axis_index("shard")
    replicas = lax.axis_size("dp")
    local_grads = grad_partials[0]
    column_blocks = local_grads.shape[0]
    slot_count = stats_left.shape[2]
    owner_of = owners[:, 0]
    onehot = (owner_of[:, None] == jnp.arange(replicas, dtype=jnp.int32)[None, :]).astype(jnp.int32)
    slot_rank = jnp.sum((jnp.cumsum(onehot, axis=0) - onehot) * onehot, axis=1)
    matches = (owner_of[None, None, :] == jnp.arange(replicas, dtype=jnp.int32)[:, None, None]) & (
        slot_rank[None, None, :] == jnp.arange(slot_count, dtype=jnp.int32)[None, :, None]
    )
    slot_table = jnp.sum(
        matches.astype(jnp.int32) * jnp.arange(column_blocks, dtype=jnp.int32)[None, None, :],
        axis=2,
    )
    slot_live = jnp.any(matches, axis=2)
    my_table = lax.dynamic_index_in_dim(slot_table, replica, 0, keepdims=False)
    my_live = lax.dynamic_index_in_dim(slot_live, replica, 0, keepdims=False)
    live_float = my_live.astype(jnp.float32)[:, None, None]
    summed = lax.psum(local_grads.astype(jnp.float32), "dp")
    owned_grad = jnp.take(summed, my_table, axis=0) * live_float
    left = stats_left[0, 0]
    right = stats_right[0, 0]
    moment = second_moment[0, 0]
    weights = master[0, 0]
    global_block = column * column_blocks + my_table
    ends = jnp.cumsum(weight_blocks)
    weight_id = jnp.sum((global_block[:, None] >= ends[None, :]).astype(jnp.int32), axis=1)
    member = (
        weight_id[:, None] == jnp.arange(weight_blocks.shape[0], dtype=jnp.int32)[None, :]
    ).astype(jnp.float32) * my_live.astype(jnp.float32)[:, None]
    vnew = BETA * moment + (1.0 - BETA) * owned_grad * owned_grad
    adam = owned_grad / (jnp.sqrt(vnew) + ADAM_EPS)
    adam_terms = jnp.sum(member * jnp.sum(adam * adam, axis=(1, 2))[:, None], axis=0)
    norm_adam = lax.psum(adam_terms, ("dp", "shard"))
    highest = lax.Precision.HIGHEST
    lnew = BETA * left + (1.0 - BETA) * jnp.einsum(
        "sij,skj->sik", owned_grad, owned_grad, precision=highest
    )
    rnew = BETA * right + (1.0 - BETA) * jnp.einsum(
        "sji,sjk->sik", owned_grad, owned_grad, precision=highest
    )
    grad_half = owned_grad.astype(jnp.bfloat16)
    inner = jnp.einsum(
        "sij,sjk->sik", root_left[0, 0], grad_half, preferred_element_type=jnp.float32
    ).astype(jnp.bfloat16)
    precond = jnp.einsum(
        "sij,sjk->sik", inner, root_right[0, 0], preferred_element_type=jnp.float32
    )
    prec_terms = jnp.sum(member * jnp.sum(precond * precond, axis=(1, 2))[:, None], axis=0)
    norm_prec = lax.psum(prec_terms, ("dp", "shard"))
    scales = jnp.sqrt(norm_adam / (norm_prec + NORM_EPS))
    slot_scale = jnp.sum(member * scales[None, :], axis=1)
    wnew = weights - RATE * slot_scale[:, None, None] * precond
    live_mask = my_live[:, None, None]
    out_left = jnp.where(live_mask, lnew, left)
    out_right = jnp.where(live_mask, rnew, right)
    out_moment = jnp.where(live_mask, vnew, moment)
    out_master = jnp.where(live_mask, wnew, weights)
    gathered = lax.all_gather(out_master.astype(jnp.bfloat16), "dp", axis=0, tiled=True)
    regathered = jnp.take(gathered, owner_of * slot_count + slot_rank, axis=0)
    return (
        out_left[None, None],
        out_right[None, None],
        out_moment[None, None],
        out_master[None, None],
        regathered,
    )


def solution(mesh):
    in_specs = (
        P("dp", "shard", None, None),
        P("shard", None),
        P(),
        P("dp", "shard", None, None, None),
        P("dp", "shard", None, None, None),
        P("dp", "shard", None, None, None),
        P("dp", "shard", None, None, None),
        P("dp", "shard", None, None, None),
        P("dp", "shard", None, None, None),
    )
    out_specs = (
        P("dp", "shard", None, None, None),
        P("dp", "shard", None, None, None),
        P("dp", "shard", None, None, None),
        P("dp", "shard", None, None, None),
        P("shard", None, None),
    )
    return jax.shard_map(local, mesh=mesh, in_specs=in_specs, out_specs=out_specs, check_vma=False)
```

profile of v0, /device:TPU:1, one launch (start us, length us, event | category | flops | bytes accessed | tf_op | source)
XLA Modules:
  0.0 160.8 jit_solution(1101177767100305149)
XLA Ops:
  7.2 2.7 %bitcast_convert_fusion = f32[8,256,256]{2,1,0:T(8,128)} fusion(bf16[1,8,256,256]{3,2,1,0:T(8,128)(2,1)} %param.9), kind=kLoop, calls=%fused_computation.12 | loop fusion | flops 524288 | bytes 3145728 | tf_op jit(solution)/shard_map/convert_element_type | solution.py:43
  10.0 0.0 all-gather.2.cloned.1.call-start
  10.1 0.1 iota_compare_fusion.1
  10.2 0.2 select_reduce_fusion
  10.4 0.1 and_reduce_fusion
  10.5 0.2 dynamic-slice_reduce_fusion
  10.7 0.1 fusion.34
  10.9 0.2 dynamic-slice_reduce_fusion.1
  11.1 0.2 reduce-window.8
  11.3 0.2 fusion.36
  11.5 64.5 %all-reduce.3.cloned.1.call-done = f32[8,256,256]{2,1,0:T(8,128)} async-done(((f32[8,256,256]{2,1,0:T(8,128)}), f32[8,256,256]{2,1,0:T(8,128)}) %all-reduce.3.cloned.1.call-update) | async-done | bytes 2097168 | tf_op jit(solution)/shard_map/psum | solution.py:43
  76.0 2.2 %gather_fusion = f32[2,256,256]{2,1,0:T(8,128)S(1)} fusion(f32[8,256,256]{2,1,0:T(8,128)} %all-reduce.3.cloned.1.call-done, s32[1024]{0:T(1024)S(1)} %pad_clamp_fusion.1), kind=kCustom, calls=%fused_computation | custom fusion | bytes 1048584 | tf_op jit(solution)/shard_map/jit(_take)/gather | solution.py:44
  78.2 0.5 fusion.15
  78.7 0.7 multiply_reduce_fusion
  79.4 0.1 multiply_reduce_fusion.2
  79.5 40.4 %all-reduce = (f32[9]{0:T(128)S(1)}, f32[9]{0:T(128)S(1)}) all-reduce(f32[9]{0:T(128)S(1)} %get-tuple-element.6, f32[9]{0:T(128)S(1)} %get-tuple-element.5), channel_id=1, replica_groups=mesh['dp'=8,'shard'=4] {'dp','shard'}, use_global_device_ids=true, to_apply=%region_9.10 | all-reduce | flops 18 | bytes 144 | tf_op jit(solution)/shard_map/psum | solution.py:58
  119.9 0.2 multiply_reduce_fusion.1
  120.1 1.0 fusion.43
  121.2 2.0 %fusion.2 = f32[1,1,2,256,256]{4,3,2,1,0:T(8,128)} fusion(f32[1,1,2,256,256]{4,3,2,1,0:T(8,128)S(1)} %copy-done.3, f32[2,256,256]{2,1,0:T(8,128)S(1)} %gather_fusion, f32[2]{0:T(128)S(1)} %convert_element_type.39, pred[2]{0:T(512)(128)(4,1)S(1)} %compare_and_fusion, pred[2]{0:T(512)(128)(4,1)S(1)} %dynamic-slice_reduce_fusion), kind=kOutput, calls=%fused_computation.5 | convolution fusion | flops 403439616 | bytes 1572876 | tf_op jit(solution)/shard_map/sji,sjk->sik/dot_general | solution.py:63
  123.1 1.7 %fusion.5 = f32[1,1,2,256,256]{4,3,2,1,0:T(8,128)} fusion(f32[1,1,2,256,256]{4,3,2,1,0:T(8,128)S(1)} %copy-done.4, f32[2,256,256]{2,1,0:T(8,128)S(1)} %gather_fusion, f32[2]{0:T(128)S(1)} %convert_element_type.39, pred[2]{0:T(512)(128)(4,1)S(1)} %compare_and_fusion, pred[2]{0:T(512)(128)(4,1)S(1)} %dynamic-slice_reduce_fusion), kind=kOutput, calls=%fused_computation.9 | convolution fusion | flops 403439616 | bytes 1572876 | tf_op jit(solution)/shard_map/sij,skj->sik/dot_general | solution.py:60
  124.8 1.0 fusion.8
  125.8 24.9 %all-gather.2.cloned.1.call-done = bf16[16,256,256]{2,1,0:T(8,128)(2,1)} async-done(((bf16[2,256,256]{2,1,0:T(8,128)(2,1)}), bf16[16,256,256]{2,1,0:T(8,128)(2,1)}) %all-gather.2.cloned.1.call-update) | async-done | bytes 2097168 | tf_op jit(solution)/shard_map/all_gather | solution.py:83
  150.6 2.2 %gather_fusion.1 = bf16[8,256,256]{2,1,0:T(8,128)(2,1)S(1)} fusion(bf16[16,256,256]{2,1,0:T(8,128)(2,1)} %all-gather.2.cloned.1.call-done, s32[1024]{0:T(1024)S(1)} %pad_clamp_fusion), kind=kCustom, calls=%fused_computation.1 | custom fusion | bytes 2097184 | tf_op jit(solution)/shard_map/jit(_take)/gather | solution.py:84
  152.8 1.1 broadcast_select_fusion
  (30 shorter events, 0.2 us)
Async XLA Ops:
  7.2 71.5 %copy-start = (bf16[1,1,2,256,256]{4,3,2,1,0:T(8,128)(2,1)S(1)}, bf16[1,1,2,256,256]{4,3,2,1,0:T(8,128)(2,1)}, u32[]{:S(2)}) copy-start(bf16[1,1,2,256,256]{4,3,2,1,0:T(8,128)(2,1)} %param.15) | copy-start | bytes 786436
  7.2 2.9 %copy-start.6 = (s32[8,1]{0,1:T(1,128)S(1)}, s32[8,1]{0,1:T(1,128)}, u32[]{:S(2)}) copy-start(s32[8,1]{0,1:T(1,128)} %param.10) | copy-start | bytes 100
  7.2 3.9 %copy-start.7 = (s32[9]{0:T(128)S(1)}, s32[9]{0:T(128)}, u32[]{:S(2)}) copy-start(s32[9]{0:T(128)} %param.11) | copy-start | bytes 112
  7.2 68.8 %all-reduce.3.cloned.1.call-start = ((), (), s32[]{:S(2)}) async-start(), calls=%async_computation | async-start | bytes 4194304 | tf_op jit(solution)/shard_map/psum | solution.py:43
  10.0 68.2 %copy-start.1 = (f32[1,1,2,256,256]{4,3,2,1,0:T(8,128)S(1)}, f32[1,1,2,256,256]{4,3,2,1,0:T(8,128)}, u32[]{:S(2)}) copy-start(f32[1,1,2,256,256]{4,3,2,1,0:T(8,128)} %param.16) | copy-start | bytes 1572868
  10.0 68.7 %copy-start.5 = (bf16[1,1,2,256,256]{4,3,2,1,0:T(8,128)(2,1)S(1)}, bf16[1,1,2,256,256]{4,3,2,1,0:T(8,128)(2,1)}, u32[]{:S(2)}) copy-start(bf16[1,1,2,256,256]{4,3,2,1,0:T(8,128)(2,1)} %param.14) | copy-start | bytes 786436
  10.0 110.1 %copy-start.2 = (f32[1,1,2,256,256]{4,3,2,1,0:T(8,128)S(1)}, f32[1,1,2,256,256]{4,3,2,1,0:T(8,128)}, u32[]{:S(2)}) copy-start(f32[1,1,2,256,256]{4,3,2,1,0:T(8,128)} %param.17) | copy-start | bytes 1572868
  10.0 140.6 %all-gather.2.cloned.1.call-start = ((), (), s32[]{:S(2)}) async-start(), calls=%async_computation.1 | async-start | bytes 2359296 | tf_op jit(solution)/shard_map/all_gather | solution.py:83
  78.7 42.5 %copy-start.3 = (f32[1,1,2,256,256]{4,3,2,1,0:T(8,128)S(1)}, f32[1,1,2,256,256]{4,3,2,1,0:T(8,128)}, u32[]{:S(2)}) copy-start(f32[1,1,2,256,256]{4,3,2,1,0:T(8,128)} %param.13) | copy-start | bytes 1572868
  79.4 43.8 %copy-start.4 = (f32[1,1,2,256,256]{4,3,2,1,0:T(8,128)S(1)}, f32[1,1,2,256,256]{4,3,2,1,0:T(8,128)}, u32[]{:S(2)}) copy-start(f32[1,1,2,256,256]{4,3,2,1,0:T(8,128)} %param.12) | copy-start | bytes 1572868
Sparse Core Ops, SparseCore 0:
  10.4 65.5 all-reduce.2
  121.3 29.3 all-gather.1
where the time goes:
time: 161 us
  waiting for transfers between devices  89.4 us (56%)
  blocking collectives  40.4 us (25%)
  between operations  14.2 us (9%)
  other arithmetic  7.65 us (5%)
  local copies, waits for them, and re-layouts  4.78 us (3%)
  matrix products  4.3 us (3%)
    psum x1, waiting for transfers between devices, local(): summed = lax.psum(local_grads.astype(jnp.float32), 'dp')  64.5 us
    psum x1, blocking collectives, local(): norm_adam = lax.psum(adam_terms, ('dp', 'shard'))  40.4 us
    all_gather x1, waiting for transfers between devices, local(): lax.all_gather(out_master.astype(jnp.bfloat16), 'dp', axis=0, tiled=True)  24.9 us
  transfers between devices with their start and end apart: 2, of which 2 were waited for; matrix products, arithmetic and copies ran while one was open for 4% of the time, Pallas kernels for 0%

commit v1 on v0

--- a/solution.py
+++ b/solution.py
@@ -7,6 +7,17 @@
 RATE = 0.3
 ADAM_EPS = 1e-08
 NORM_EPS = 1e-06
+
+
+def butterfly_sum(x, axis):
+    size = lax.axis_size(axis)
+    if size & (size - 1):
+        return lax.psum(x, axis)
+    step = 1
+    while step < size:
+        x = x + lax.ppermute(x, axis, [(i, i ^ step) for i in range(size)])
+        step *= 2
+    return x
 
 
 def local(
@@ -55,7 +66,6 @@
     vnew = BETA * moment + (1.0 - BETA) * owned_grad * owned_grad
     adam = owned_grad / (jnp.sqrt(vnew) + ADAM_EPS)
     adam_terms = jnp.sum(member * jnp.sum(adam * adam, axis=(1, 2))[:, None], axis=0)
-    norm_adam = lax.psum(adam_terms, ("dp", "shard"))
     highest = lax.Precision.HIGHEST
     lnew = BETA * left + (1.0 - BETA) * jnp.einsum(
         "sij,skj->sik", owned_grad, owned_grad, precision=highest
@@ -71,7 +81,9 @@
         "sij,sjk->sik", inner, root_right[0, 0], preferred_element_type=jnp.float32
     )
     prec_terms = jnp.sum(member * jnp.sum(precond * precond, axis=(1, 2))[:, None], axis=0)
-    norm_prec = lax.psum(prec_terms, ("dp", "shard"))
+    norms = butterfly_sum(butterfly_sum(jnp.stack([adam_terms, prec_terms]), "dp"), "shard")
+    norm_adam = norms[0]
+    norm_prec = norms[1]
     scales = jnp.sqrt(norm_adam / (norm_prec + NORM_EPS))
     slot_scale = jnp.sum(member * scales[None, :], axis=1)
     wnew = weights - RATE * slot_scale[:, None, None] * precond

time: 161 us -> 139 us (0.86)
  blocking collectives: 40.4 us -> 0 us
  waiting for transfers between devices: 89.4 us -> 101 us
  starting transfers between devices: 0.08 us -> 6.45 us
    psum x1 -> x0, blocking collectives: 40.4 us -> none  [local(): norm_adam = lax.psum(adam_terms, ('dp', 'shard'))]
    ppermute x0 -> x5, waiting for transfers between devices: none -> 7.32 us  [butterfly_sum(): x = x + lax.ppermute(x, axis, [(i, i ^ step) for i in range(size)])]
    ppermute x0 -> x5, starting transfers between devices: none -> 6.37 us  [butterfly_sum(): x = x + lax.ppermute(x, axis, [(i, i ^ step) for i in range(size)])]
    all_gather x1, waiting for transfers between devices: 24.9 us -> 28.9 us  [local(): lax.all_gather(out_master.astype(jnp.bfloat16), 'dp', axis=0, tiled=True)]
  transfers between devices with their start and end apart: 2 -> 7, of which waited for: 2 -> 7; matrix products, arithmetic and copies ran while one was open for 4% -> 4% of each run, Pallas kernels for 0% -> 0%
where the time goes in v1:
time: 139 us; the launch traced here: 138 us
  waiting for transfers between devices  101 us (73%)
  between operations  14.2 us (10%)
  other arithmetic  7.7 us (6%)
  starting transfers between devices  6.45 us (5%)
  local copies, waits for them, and re-layouts  4.78 us (3%)
  matrix products  4.3 us (3%)
    psum x1, waiting for transfers between devices, local(): summed = lax.psum(local_grads.astype(jnp.float32), 'dp')  64.5 us
    all_gather x1, waiting for transfers between devices, local(): lax.all_gather(out_master.astype(jnp.bfloat16), 'dp', axis=0, tiled=True)  28.9 us
    ppermute x5, waiting for transfers between devices, butterfly_sum(): x = x + lax.ppermute(x, axis, [(i, i ^ step) for i in range(size)])  7.32 us
    ppermute x5, starting transfers between devices, butterfly_sum(): x = x + lax.ppermute(x, axis, [(i, i ^ step) for i in range(size)])  6.37 us
  transfers between devices with their start and end apart: 7, of which 7 were waited for; matrix products, arithmetic and copies ran while one was open for 4% of the time, Pallas kernels for 0%

profile of v1, /device:TPU:1, one launch (start us, length us, event | category | flops | bytes accessed | tf_op | source)
XLA Modules:
  0.0 138.2 jit_solution(13024483994053994536)
XLA Ops:
  7.2 2.7 %bitcast_convert_fusion = f32[8,256,256]{2,1,0:T(8,128)} fusion(bf16[1,8,256,256]{3,2,1,0:T(8,128)(2,1)} %param.9), kind=kLoop, calls=%fused_computation.12 | loop fusion | flops 524288 | bytes 3145728 | tf_op jit(solution)/shard_map/convert_element_type | solution.py:54
  10.5 0.2 dynamic-slice_reduce_fusion
  10.9 0.2 dynamic-slice_reduce_fusion.1
  11.5 64.5 %all-reduce.2.cloned.1.call-done = f32[8,256,256]{2,1,0:T(8,128)} async-done(((f32[8,256,256]{2,1,0:T(8,128)}), f32[8,256,256]{2,1,0:T(8,128)}) %all-reduce.2.cloned.1.call-update) | async-done | bytes 2097168 | tf_op jit(solution)/shard_map/psum | solution.py:54
  76.0 2.2 %gather_fusion = f32[2,256,256]{2,1,0:T(8,128)S(1)} fusion(f32[8,256,256]{2,1,0:T(8,128)} %all-reduce.2.cloned.1.call-done, s32[1024]{0:T(1024)S(1)} %pad_clamp_fusion.1), kind=kCustom, calls=%fused_computation | custom fusion | bytes 1048584 | tf_op jit(solution)/shard_map/jit(_take)/gather | solution.py:55
  78.2 0.5 fusion.15
  78.7 0.7 multiply_reduce_fusion
  79.5 2.2 %collective-permute-start = (f32[2,9]{1,0:T(2,128)S(1)}, f32[2,9]{1,0:T(2,128)S(1)}, u32[]{:S(2)}, u32[]{:S(2)}) collective-permute-start(f32[2,9]{1,0:T(2,128)S(1)} %pad_maximum_fusion), channel_id=1, source_target_pairs={{0,4},{4,0},{8,12},{12,8},{16,20},{20,16},{24,28},{28,24},{1,5},{5... | collective-permute-start | bytes 224 | tf_op jit(solution)/shard_map/ppermute | solution.py:18
  81.6 0.8 collective-permute-done
  82.5 0.9 collective-permute-start.1
  83.4 1.5 %collective-permute-done.1 = f32[2,9]{1,0:T(2,128)S(1)} collective-permute-done((f32[2,9]{1,0:T(2,128)S(1)}, f32[2,9]{1,0:T(2,128)S(1)}, u32[]{:S(2)}, u32[]{:S(2)}) %collective-permute-start.1) | collective-permute-done | bytes 104 | tf_op jit(solution)/shard_map/ppermute | solution.py:18
  85.0 0.9 collective-permute-start.2
  85.8 2.5 %collective-permute-done.2 = f32[2,9]{1,0:T(2,128)S(1)} collective-permute-done((f32[2,9]{1,0:T(2,128)S(1)}, f32[2,9]{1,0:T(2,128)S(1)}, u32[]{:S(2)}, u32[]{:S(2)}) %collective-permute-start.2) | collective-permute-done | bytes 104 | tf_op jit(solution)/shard_map/ppermute | solution.py:18
  88.4 1.2 collective-permute-start.3
  89.5 1.2 collective-permute-done.3
  90.8 1.2 collective-permute-start.4
  92.0 1.2 collective-permute-done.4
  93.4 1.0 fusion.43
  94.5 2.0 %fusion.2 = f32[1,1,2,256,256]{4,3,2,1,0:T(8,128)} fusion(f32[1,1,2,256,256]{4,3,2,1,0:T(8,128)S(1)} %copy-done.3, f32[2,256,256]{2,1,0:T(8,128)S(1)} %gather_fusion, f32[2]{0:T(128)S(1)} %convert_element_type.39, pred[2]{0:T(512)(128)(4,1)S(1)} %compare_and_fusion, pred[2]{0:T(512)(128)(4,1)S(1)} %dynamic-slice_reduce_fusion), kind=kOutput, calls=%fused_computation.5 | convolution fusion | flops 403439616 | bytes 1572876 | tf_op jit(solution)/shard_map/sji,sjk->sik/dot_general | solution.py:73
  96.5 1.7 %fusion.5 = f32[1,1,2,256,256]{4,3,2,1,0:T(8,128)} fusion(f32[1,1,2,256,256]{4,3,2,1,0:T(8,128)S(1)} %copy-done.4, f32[2,256,256]{2,1,0:T(8,128)S(1)} %gather_fusion, f32[2]{0:T(128)S(1)} %convert_element_type.39, pred[2]{0:T(512)(128)(4,1)S(1)} %compare_and_fusion, pred[2]{0:T(512)(128)(4,1)S(1)} %dynamic-slice_reduce_fusion), kind=kOutput, calls=%fused_computation.9 | convolution fusion | flops 403439616 | bytes 1572876 | tf_op jit(solution)/shard_map/sij,skj->sik/dot_general | solution.py:70
  98.1 1.0 fusion.8
  99.1 28.9 %all-gather.2.cloned.1.call-done = bf16[16,256,256]{2,1,0:T(8,128)(2,1)} async-done(((bf16[2,256,256]{2,1,0:T(8,128)(2,1)}), bf16[16,256,256]{2,1,0:T(8,128)(2,1)}) %all-gather.2.cloned.1.call-update) | async-done | bytes 2097168 | tf_op jit(solution)/shard_map/all_gather | solution.py:95
  128.0 2.2 %gather_fusion.1 = bf16[8,256,256]{2,1,0:T(8,128)(2,1)S(1)} fusion(bf16[16,256,256]{2,1,0:T(8,128)(2,1)} %all-gather.2.cloned.1.call-done, s32[1024]{0:T(1024)S(1)} %pad_clamp_fusion), kind=kCustom, calls=%fused_computation.1 | custom fusion | bytes 2097184 | tf_op jit(solution)/shard_map/jit(_take)/gather | solution.py:96
  130.2 1.1 broadcast_select_fusion
  (45 shorter events, 1.5 us)
Async XLA Ops:
  7.2 71.5 %copy-start = (bf16[1,1,2,256,256]{4,3,2,1,0:T(8,128)(2,1)S(1)}, bf16[1,1,2,256,256]{4,3,2,1,0:T(8,128)(2,1)}, u32[]{:S(2)}) copy-start(bf16[1,1,2,256,256]{4,3,2,1,0:T(8,128)(2,1)} %param.15) | copy-start | bytes 786436
  7.2 2.9 %copy-start.6 = (s32[8,1]{0,1:T(1,128)S(1)}, s32[8,1]{0,1:T(1,128)}, u32[]{:S(2)}) copy-start(s32[8,1]{0,1:T(1,128)} %param.10) | copy-start | bytes 100
  7.2 3.9 %copy-start.7 = (s32[9]{0:T(128)S(1)}, s32[9]{0:T(128)}, u32[]{:S(2)}) copy-start(s32[9]{0:T(128)} %param.11) | copy-start | bytes 112
  7.2 68.8 %all-reduce.2.cloned.1.call-start = ((), (), s32[]{:S(2)}) async-start(), calls=%async_computation | async-start | bytes 4194304 | tf_op jit(solution)/shard_map/psum | solution.py:54
  10.0 68.2 %copy-start.1 = (f32[1,1,2,256,256]{4,3,2,1,0:T(8,128)S(1)}, f32[1,1,2,256,256]{4,3,2,1,0:T(8,128)}, u32[]{:S(2)}) copy-start(f32[1,1,2,256,256]{4,3,2,1,0:T(8,128)} %param.16) | copy-start | bytes 1572868
  10.0 68.7 %copy-start.5 = (bf16[1,1,2,256,256]{4,3,2,1,0:T(8,128)(2,1)S(1)}, bf16[1,1,2,256,256]{4,3,2,1,0:T(8,128)(2,1)}, u32[]{:S(2)}) copy-start(bf16[1,1,2,256,256]{4,3,2,1,0:T(8,128)(2,1)} %param.14) | copy-start | bytes 786436
  10.0 83.4 %copy-start.2 = (f32[1,1,2,256,256]{4,3,2,1,0:T(8,128)S(1)}, f32[1,1,2,256,256]{4,3,2,1,0:T(8,128)}, u32[]{:S(2)}) copy-start(f32[1,1,2,256,256]{4,3,2,1,0:T(8,128)} %param.17) | copy-start | bytes 1572868
  10.0 118.0 %all-gather.2.cloned.1.call-start = ((), (), s32[]{:S(2)}) async-start(), calls=%async_computation.1 | async-start | bytes 2359296 | tf_op jit(solution)/shard_map/all_gather | solution.py:95
  78.7 15.8 %copy-start.3 = (f32[1,1,2,256,256]{4,3,2,1,0:T(8,128)S(1)}, f32[1,1,2,256,256]{4,3,2,1,0:T(8,128)}, u32[]{:S(2)}) copy-start(f32[1,1,2,256,256]{4,3,2,1,0:T(8,128)} %param.13) | copy-start | bytes 1572868
  79.4 17.1 %copy-start.4 = (f32[1,1,2,256,256]{4,3,2,1,0:T(8,128)S(1)}, f32[1,1,2,256,256]{4,3,2,1,0:T(8,128)}, u32[]{:S(2)}) copy-start(f32[1,1,2,256,256]{4,3,2,1,0:T(8,128)} %param.12) | copy-start | bytes 1572868
  79.5 3.0 %collective-permute-start = (f32[2,9]{1,0:T(2,128)S(1)}, f32[2,9]{1,0:T(2,128)S(1)}, u32[]{:S(2)}, u32[]{:S(2)}) collective-permute-start(f32[2,9]{1,0:T(2,128)S(1)} %pad_maximum_fusion), channel_id=1, source_target_pairs={{0,4},{4,0},{8,12},{12,8},{16,20},{20,16},{24,28},{28,24},{1,5},{5... | collective-permute-start | bytes 224 | tf_op jit(solution)/shard_map/ppermute | solution.py:18
  82.5 2.5 %collective-permute-start.1 = (f32[2,9]{1,0:T(2,128)S(1)}, f32[2,9]{1,0:T(2,128)S(1)}, u32[]{:S(2)}, u32[]{:S(2)}) collective-permute-start(f32[2,9]{1,0:T(2,128)S(1)} %fusion.42), channel_id=1, source_target_pairs={{0,8},{4,12},{8,0},{12,4},{16,24},{20,28},{24,16},{28,20},{1,9},{5... | collective-permute-start | bytes 224 | tf_op jit(solution)/shard_map/ppermute | solution.py:18
  85.0 3.4 %collective-permute-start.2 = (f32[2,9]{1,0:T(2,128)S(1)}, f32[2,9]{1,0:T(2,128)S(1)}, u32[]{:S(2)}, u32[]{:S(2)}) collective-permute-start(f32[2,9]{1,0:T(2,128)S(1)} %fusion.49), channel_id=1, source_target_pairs={{0,16},{4,20},{8,24},{12,28},{16,0},{20,4},{24,8},{28,12},{1,17},{... | collective-permute-start | bytes 224 | tf_op jit(solution)/shard_map/ppermute | solution.py:18
  88.4 2.4 %collective-permute-start.3 = (f32[2,9]{1,0:T(2,128)S(1)}, f32[2,9]{1,0:T(2,128)S(1)}, u32[]{:S(2)}, u32[]{:S(2)}) collective-permute-start(f32[2,9]{1,0:T(2,128)S(1)} %add.94), channel_id=1, source_target_pairs={{0,1},{1,0},{2,3},{3,2},{4,5},{5,4},{6,7},{7,6},{8,9},{9,8},{10,11... | collective-permute-start | bytes 224 | tf_op jit(solution)/shard_map/ppermute | solution.py:18
  90.8 2.4 %collective-permute-start.4 = (f32[2,9]{1,0:T(2,128)S(1)}, f32[2,9]{1,0:T(2,128)S(1)}, u32[]{:S(2)}, u32[]{:S(2)}) collective-permute-start(f32[2,9]{1,0:T(2,128)S(1)} %add.95), channel_id=1, source_target_pairs={{0,2},{1,3},{2,0},{3,1},{4,6},{5,7},{6,4},{7,5},{8,10},{9,11},{10,... | collective-permute-start | bytes 224 | tf_op jit(solution)/shard_map/ppermute | solution.py:18
Sparse Core Ops, SparseCore 0:
  10.4 65.5 all-reduce.1
  94.6 33.3 all-gather.1

commit v2 on v1

--- a/solution.py
+++ b/solution.py
@@ -51,8 +51,11 @@
     my_table = lax.dynamic_index_in_dim(slot_table, replica, 0, keepdims=False)
     my_live = lax.dynamic_index_in_dim(slot_live, replica, 0, keepdims=False)
     live_float = my_live.astype(jnp.float32)[:, None, None]
-    summed = lax.psum(local_grads.astype(jnp.float32), "dp")
-    owned_grad = jnp.take(summed, my_table, axis=0) * live_float
+    by_owner = jnp.take(local_grads, slot_table.reshape(-1), axis=0).reshape(
+        (replicas, slot_count) + local_grads.shape[1:]
+    )
+    received = lax.all_to_all(by_owner, "dp", 0, 0, tiled=True)
+    owned_grad = jnp.sum(received.astype(jnp.float32), axis=0) * live_float
     left = stats_left[0, 0]
     right = stats_right[0, 0]
     moment = second_moment[0, 0]

time: 139 us -> 128 us (0.921)
  waiting for transfers between devices: 101 us -> 83.4 us
  starting transfers between devices: 6.45 us -> 10.1 us
  other arithmetic: 7.7 us -> 9.99 us
  matrix products: 4.3 us -> 6.3 us
  local copies, waits for them, and re-layouts: 4.78 us -> 3.37 us
    psum x1 -> x0, waiting for transfers between devices: 64.5 us -> none  [local(): summed = lax.psum(local_grads.astype(jnp.float32), 'dp')]
    all_to_all x0 -> x1, waiting for transfers between devices: none -> 47.3 us  [local(): received = lax.all_to_all(by_owner, 'dp', 0, 0, tiled=True)]
    all_to_all x0 -> x1, starting transfers between devices: none -> 6.51 us  [local(): received = lax.all_to_all(by_owner, 'dp', 0, 0, tiled=True)]
    ppermute x5, starting transfers between devices: 6.37 us -> 3.52 us  [butterfly_sum(): x = x + lax.ppermute(x, axis, [(i, i ^ step) for i in range(size)])]
    convert_element_type x1 -> x0, other arithmetic: 2.74 us -> none  [local(): summed = lax.psum(local_grads.astype(jnp.float32), 'dp')]
    reduce_sum x0 -> x1, other arithmetic: none -> 1.92 us  [local(): owned_grad = jnp.sum(received.astype(jnp.float32), axis=0) * live_float]
    all_gather x1, waiting for transfers between devices: 28.9 us -> 27.2 us  [local(): lax.all_gather(out_master.astype(jnp.bfloat16), 'dp', axis=0, tiled=True)]
    ppermute x5, waiting for transfers between devices: 7.32 us -> 8.92 us  [butterfly_sum(): x = x + lax.ppermute(x, axis, [(i, i ^ step) for i in range(size)])]
  transfers between devices with their start and end apart: 7 -> 7, of which waited for: 7 -> 7; matrix products, arithmetic and copies ran while one was open for 4% -> 5% of each run, Pallas kernels for 0% -> 0%
where the time goes in v2:
time: 128 us; the launch traced here: 127 us
  waiting for transfers between devices  83.4 us (65%)
  between operations  14.2 us (11%)
  starting transfers between devices  10.1 us (8%)
  other arithmetic  9.99 us (8%)
  matrix products  6.3 us (5%)
  local copies, waits for them, and re-layouts  3.37 us (3%)
    all_to_all x1, waiting for transfers between devices, local(): received = lax.all_to_all(by_owner, 'dp', 0, 0, tiled=True)  47.3 us
    all_gather x1, waiting for transfers between devices, local(): lax.all_gather(out_master.astype(jnp.bfloat16), 'dp', axis=0, tiled=True)  27.2 us
    ppermute x5, waiting for transfers between devices, butterfly_sum(): x = x + lax.ppermute(x, axis, [(i, i ^ step) for i in range(size)])  8.92 us
    all_to_all x1, starting transfers between devices, local(): received = lax.all_to_all(by_owner, 'dp', 0, 0, tiled=True)  6.51 us
    ppermute x5, starting transfers between devices, butterfly_sum(): x = x + lax.ppermute(x, axis, [(i, i ^ step) for i in range(size)])  3.52 us
    dot_general x1, matrix products, local(): jnp.einsum('sji,sjk->sik', owned_grad, owned_grad, precision=highest)  3.03 us
  transfers between devices with their start and end apart: 7, of which 7 were waited for; matrix products, arithmetic and copies ran while one was open for 5% of the time, Pallas kernels for 0%

profile of v2, /device:TPU:1, one launch (start us, length us, event | category | flops | bytes accessed | tf_op | source)
XLA Modules:
  0.0 127.3 jit_solution(15245772660108911283)
XLA Ops:
  7.2 0.8 iota_compare_fusion.1
  8.0 0.8 select_reduce_fusion
  9.3 0.7 gather_fusion
  10.0 1.6 %broadcast_select_fusion = bf16[8,2,256,256]{3,2,1,0:T(8,128)(2,1)} fusion(bf16[8,2,256,256]{3,2,1,0:T(8,128)(2,1)S(1)} %bitcast.61, pred[8,2]{1,0:T(8,128)(4,1)S(1)} %copy.24), kind=kLoop, calls=%fused_computation.3 | loop fusion | flops 1048576 | bytes 4194320 | tf_op jit(solution)/shard_map/jit(_take)/select_n | solution.py:54
  11.6 6.5 %all-to-all-start = ((bf16[8,2,256,256]{3,2,1,0:T(8,128)(2,1)}), bf16[8,2,256,256]{3,2,1,0:T(8,128)(2,1)}, u32[]{:S(2)}, u32[]{:S(2)}) async-start(bf16[8,2,256,256]{3,2,1,0:T(8,128)(2,1)} %broadcast_select_fusion), calls=%async_computation | async-start | bytes 4194304 | tf_op jit(solution)/shard_map/all_to_all | solution.py:57
  19.1 47.3 %all-to-all-done = bf16[8,2,256,256]{3,2,1,0:T(8,128)(2,1)} async-done(((bf16[8,2,256,256]{3,2,1,0:T(8,128)(2,1)}), bf16[8,2,256,256]{3,2,1,0:T(8,128)(2,1)}, u32[]{:S(2)}, u32[]{:S(2)}) %all-to-all-start) | async-done | bytes 2097184 | tf_op jit(solution)/shard_map/all_to_all | solution.py:57
  66.4 1.9 %convert_reduce_fusion = f32[2,256,256]{2,1,0:T(8,128)S(1)} fusion(bf16[8,2,256,256]{3,2,1,0:T(8,128)(2,1)} %all-to-all-done), kind=kLoop, calls=%fused_computation.2 | loop fusion | flops 1966080 | bytes 2621440 | tf_op jit(solution)/shard_map/reduce_sum | solution.py:58
  68.3 0.5 fusion.14
  68.8 1.6 %multiply_reduce_fusion = (f32[2]{0:T(128)S(1)}, f32[2,256,256]{2,1,0:T(8,128)S(1)}) fusion(bf16[1,1,2,256,256]{4,3,2,1,0:T(8,128)(2,1)S(1)} %copy-done.4, f32[2,256,256]{2,1,0:T(8,128)S(1)} %convert_reduce_fusion, bf16[1,1,2,256,256]{4,3,2,1,0:T(8,128)(2,1)} %param.14, f32[2]{0:T(128)S(1)} %convert_element_type.35), kind=kOutput, calls=%fused_computation.28 | convolution fusion | flops 134873088 | bytes 1572880 | tf_op jit(solution)/shard_map/sij,sjk->sik/dot_general | solution.py:83
  70.5 0.9 collective-permute-start
  71.5 0.8 collective-permute-done
  72.4 2.4 %collective-permute-done.1 = f32[2,9]{1,0:T(2,128)S(1)} collective-permute-done((f32[2,9]{1,0:T(2,128)S(1)}, f32[2,9]{1,0:T(2,128)S(1)}, u32[]{:S(2)}, u32[]{:S(2)}) %collective-permute-start.1) | collective-permute-done | bytes 104 | tf_op jit(solution)/shard_map/ppermute | solution.py:18
  74.9 3.3 %collective-permute-done.2 = f32[2,9]{1,0:T(2,128)S(1)} collective-permute-done((f32[2,9]{1,0:T(2,128)S(1)}, f32[2,9]{1,0:T(2,128)S(1)}, u32[]{:S(2)}, u32[]{:S(2)}) %collective-permute-start.2) | collective-permute-done | bytes 104 | tf_op jit(solution)/shard_map/ppermute | solution.py:18
  78.2 1.2 collective-permute-start.3
  79.4 1.2 collective-permute-done.3
  80.6 1.2 collective-permute-start.4
  81.9 1.2 collective-permute-done.4
  83.3 1.0 fusion.29
  84.4 3.0 %fusion.2 = f32[1,1,2,256,256]{4,3,2,1,0:T(8,128)} fusion(f32[1,1,2,256,256]{4,3,2,1,0:T(8,128)} %param.13, f32[2,256,256]{2,1,0:T(8,128)S(1)} %convert_reduce_fusion, f32[2]{0:T(128)S(1)} %convert_element_type.35, pred[2]{0:T(512)(128)(4,1)S(1)} %dynamic-slice_reduce_fusion), kind=kOutput, calls=%fused_computation.7 | convolution fusion | flops 403308544 | bytes 1572874 | tf_op jit(solution)/shard_map/sji,sjk->sik/dot_general | solution.py:76
  87.4 1.6 %fusion.5 = f32[1,1,2,256,256]{4,3,2,1,0:T(8,128)} fusion(f32[1,1,2,256,256]{4,3,2,1,0:T(8,128)S(1)} %copy-done.3, f32[2,256,256]{2,1,0:T(8,128)S(1)} %convert_reduce_fusion, f32[2]{0:T(128)S(1)} %convert_element_type.35, pred[2]{0:T(512)(128)(4,1)S(1)} %dynamic-slice_reduce_fusion), kind=kOutput, calls=%fused_computation.11 | convolution fusion | flops 403308544 | bytes 1572874 | tf_op jit(solution)/shard_map/sij,skj->sik/dot_general | solution.py:73
  89.0 1.0 fusion.8
  90.0 27.2 %all-gather.2.cloned.1.call-done = bf16[16,256,256]{2,1,0:T(8,128)(2,1)} async-done(((bf16[2,256,256]{2,1,0:T(8,128)(2,1)}), bf16[16,256,256]{2,1,0:T(8,128)(2,1)}) %all-gather.2.cloned.1.call-update) | async-done | bytes 2097168 | tf_op jit(solution)/shard_map/all_gather | solution.py:98
  117.1 2.2 %gather_fusion.1 = bf16[8,256,256]{2,1,0:T(8,128)(2,1)S(1)} fusion(bf16[16,256,256]{2,1,0:T(8,128)(2,1)} %all-gather.2.cloned.1.call-done, s32[1024]{0:T(1024)S(1)} %pad_clamp_fusion), kind=kCustom, calls=%fused_computation.1 | custom fusion | bytes 2097184 | tf_op jit(solution)/shard_map/jit(_take)/gather | solution.py:99
  119.3 1.1 broadcast_select_fusion.1
  (45 shorter events, 1.9 us)
Async XLA Ops:
  7.2 2.2 %copy-start = (bf16[1,8,256,256]{3,2,1,0:T(8,128)(2,1)S(1)}, bf16[1,8,256,256]{3,2,1,0:T(8,128)(2,1)}, u32[]{:S(2)}) copy-start(bf16[1,8,256,256]{3,2,1,0:T(8,128)(2,1)} %param.9) | copy-start | bytes 3145732
  11.6 6.9 %copy-start.6 = (s32[9]{0:T(128)S(1)}, s32[9]{0:T(128)}, u32[]{:S(2)}) copy-start(s32[9]{0:T(128)} %param.11) | copy-start | bytes 112
  11.6 54.8 %all-to-all-start = ((bf16[8,2,256,256]{3,2,1,0:T(8,128)(2,1)}), bf16[8,2,256,256]{3,2,1,0:T(8,128)(2,1)}, u32[]{:S(2)}, u32[]{:S(2)}) async-start(bf16[8,2,256,256]{3,2,1,0:T(8,128)(2,1)} %broadcast_select_fusion), calls=%async_computation | async-start | bytes 4194304 | tf_op jit(solution)/shard_map/all_to_all | solution.py:57
  18.1 50.2 %copy-start.1 = (f32[1,1,2,256,256]{4,3,2,1,0:T(8,128)S(1)}, f32[1,1,2,256,256]{4,3,2,1,0:T(8,128)}, u32[]{:S(2)}) copy-start(f32[1,1,2,256,256]{4,3,2,1,0:T(8,128)} %param.16) | copy-start | bytes 1572868
  18.1 50.7 %copy-start.4 = (bf16[1,1,2,256,256]{4,3,2,1,0:T(8,128)(2,1)S(1)}, bf16[1,1,2,256,256]{4,3,2,1,0:T(8,128)(2,1)}, u32[]{:S(2)}) copy-start(bf16[1,1,2,256,256]{4,3,2,1,0:T(8,128)(2,1)} %param.15) | copy-start | bytes 786436
  18.1 99.0 %all-gather.2.cloned.1.call-start = ((), (), s32[]{:S(2)}) async-start(), calls=%async_computation.1 | async-start | bytes 2359296 | tf_op jit(solution)/shard_map/all_gather | solution.py:98
  19.1 64.2 %copy-start.2 = (f32[1,1,2,256,256]{4,3,2,1,0:T(8,128)S(1)}, f32[1,1,2,256,256]{4,3,2,1,0:T(8,128)}, u32[]{:S(2)}) copy-start(f32[1,1,2,256,256]{4,3,2,1,0:T(8,128)} %param.17) | copy-start | bytes 1572868
  68.8 15.5 %copy-start.5 = (s32[8,1]{0,1:T(1,128)S(1)}, s32[8,1]{0,1:T(1,128)}, u32[]{:S(2)}) copy-start(s32[8,1]{0,1:T(1,128)} %param.10) | copy-start | bytes 100
  70.5 1.8 %collective-permute-start = (f32[2,9]{1,0:T(2,128)S(1)}, f32[2,9]{1,0:T(2,128)S(1)}, u32[]{:S(2)}, u32[]{:S(2)}) collective-permute-start(f32[2,9]{1,0:T(2,128)S(1)} %pad_maximum_fusion), channel_id=1, source_target_pairs={{0,4},{4,0},{8,12},{12,8},{16,20},{20,16},{24,28},{28,24},{1,5},{5... | collective-permute-start | bytes 224 | tf_op jit(solution)/shard_map/ppermute | solution.py:18
  72.3 2.5 %collective-permute-start.1 = (f32[2,9]{1,0:T(2,128)S(1)}, f32[2,9]{1,0:T(2,128)S(1)}, u32[]{:S(2)}, u32[]{:S(2)}) collective-permute-start(f32[2,9]{1,0:T(2,128)S(1)} %fusion.28), channel_id=1, source_target_pairs={{0,8},{4,12},{8,0},{12,4},{16,24},{20,28},{24,16},{28,20},{1,9},{5... | collective-permute-start | bytes 224 | tf_op jit(solution)/shard_map/ppermute | solution.py:18
  74.8 3.4 %collective-permute-start.2 = (f32[2,9]{1,0:T(2,128)S(1)}, f32[2,9]{1,0:T(2,128)S(1)}, u32[]{:S(2)}, u32[]{:S(2)}) collective-permute-start(f32[2,9]{1,0:T(2,128)S(1)} %fusion.33), channel_id=1, source_target_pairs={{0,16},{4,20},{8,24},{12,28},{16,0},{20,4},{24,8},{28,12},{1,17},{... | collective-permute-start | bytes 224 | tf_op jit(solution)/shard_map/ppermute | solution.py:18
  78.2 2.4 %collective-permute-start.3 = (f32[2,9]{1,0:T(2,128)S(1)}, f32[2,9]{1,0:T(2,128)S(1)}, u32[]{:S(2)}, u32[]{:S(2)}) collective-permute-start(f32[2,9]{1,0:T(2,128)S(1)} %add.97), channel_id=1, source_target_pairs={{0,1},{1,0},{2,3},{3,2},{4,5},{5,4},{6,7},{7,6},{8,9},{9,8},{10,11... | collective-permute-start | bytes 224 | tf_op jit(solution)/shard_map/ppermute | solution.py:18
  80.6 2.4 %collective-permute-start.4 = (f32[2,9]{1,0:T(2,128)S(1)}, f32[2,9]{1,0:T(2,128)S(1)}, u32[]{:S(2)}, u32[]{:S(2)}) collective-permute-start(f32[2,9]{1,0:T(2,128)S(1)} %add.98), channel_id=1, source_target_pairs={{0,2},{1,3},{2,0},{3,1},{4,6},{5,7},{6,4},{7,5},{8,10},{9,11},{10,... | collective-permute-start | bytes 224 | tf_op jit(solution)/shard_map/ppermute | solution.py:18
  84.3 3.1 %copy-start.3 = (f32[1,1,2,256,256]{4,3,2,1,0:T(8,128)S(1)}, f32[1,1,2,256,256]{4,3,2,1,0:T(8,128)}, u32[]{:S(2)}) copy-start(f32[1,1,2,256,256]{4,3,2,1,0:T(8,128)} %param.12) | copy-start | bytes 1572868
Sparse Core Ops, SparseCore 0:
  84.4 32.6 all-gather.1

commit v3 on v2

--- a/solution.py
+++ b/solution.py
@@ -18,6 +18,40 @@
         x = x + lax.ppermute(x, axis, [(i, i ^ step) for i in range(size)])
         step *= 2
     return x
+
+
+def gather_blocks(mine, owner_of, slot_rank, replica):
+    size = lax.axis_size("dp")
+    slot_count = mine.shape[0]
+    if size % 2 or size < 4:
+        gathered = lax.all_gather(mine, "dp", axis=0, tiled=True)
+        return jnp.take(gathered, owner_of * slot_count + slot_rank, axis=0)
+    chips = size // 2
+    rightward = [(i, i + 2) for i in range(size - 2)]
+    leftward = [(i + 2, i) for i in range(size - 2)]
+    partner = [(i, i ^ 1) for i in range(size)]
+    from_left = [None] * chips
+    from_right = [None] * chips
+    from_left[0] = mine
+    from_right[0] = mine
+    near_left = [None] * chips
+    near_right = [None] * chips
+    near_left[0] = lax.ppermute(mine, "dp", partner)
+    near_right[0] = near_left[0]
+    for step in range(1, chips):
+        from_left[step] = lax.ppermute(from_left[step - 1], "dp", rightward)
+        from_right[step] = lax.ppermute(from_right[step - 1], "dp", leftward)
+        near_left[step] = lax.ppermute(from_left[step], "dp", partner)
+        near_right[step] = lax.ppermute(from_right[step], "dp", partner)
+    same_core = from_left[::-1] + from_right[1:]
+    other_core = near_left[::-1] + near_right[1:]
+    pieces = jnp.stack(same_core + other_core)
+    chip, core = replica // 2, replica % 2
+    owner_chip, owner_core = owner_of // 2, owner_of % 2
+    offset = owner_chip - chip + chips - 1
+    which = jnp.where(owner_core == core, 0, 1)
+    index = (which * (2 * chips - 1) + offset) * slot_count + slot_rank
+    return jnp.take(pieces.reshape((-1,) + mine.shape[1:]), index, axis=0)
 
 
 def local(
@@ -95,8 +129,7 @@
     out_right = jnp.where(live_mask, rnew, right)
     out_moment = jnp.where(live_mask, vnew, moment)
     out_master = jnp.where(live_mask, wnew, weights)
-    gathered = lax.all_gather(out_master.astype(jnp.bfloat16), "dp", axis=0, tiled=True)
-    regathered = jnp.take(gathered, owner_of * slot_count + slot_rank, axis=0)
+    regathered = gather_blocks(out_master.astype(jnp.bfloat16), owner_of, slot_rank, replica)
     return (
         out_left[None, None],
         out_right[None, None],

time: 128 us -> 127 us (level)
  starting transfers between devices: 10.1 us -> 34.9 us
  waiting for transfers between devices: 83.4 us -> 60.3 us
  between operations: 14.2 us -> 0.87 us
  local copies, waits for them, and re-layouts: 3.37 us -> 14 us
    all_gather x1 -> x0, waiting for transfers between devices: 27.2 us -> none  [local(): lax.all_gather(out_master.astype(jnp.bfloat16), 'dp', axis=0, tiled=True)]
    ppermute x0 -> x13, starting transfers between devices: none -> 24.9 us  [the longest x3 9.73 us: gather_blocks(): from_left[step] = lax.ppermute(from_left[step - 1], 'dp', rightward)]
    unnamed x14 -> x27, local copies, waits for them, and re-layouts: 0.03 us -> 9.48 us
    ppermute x0 -> x13, waiting for transfers between devices: none -> 4.04 us  [the longest x3 2.08 us: gather_blocks(): from_right[step] = lax.ppermute(from_right[step - 1], 'dp', leftward)]
  transfers between devices with their start and end apart: 7 -> 19, of which waited for: 7 -> 8; matrix products, arithmetic and copies ran while one was open for 5% -> 13% of each run, Pallas kernels for 0% -> 0%
where the time goes in v3:
time: 127 us; the launch traced here: 126 us
  waiting for transfers between devices  60.3 us (47%)
  starting transfers between devices  34.9 us (27%)
  local copies, waits for them, and re-layouts  14 us (11%)
  other arithmetic  9.92 us (8%)
  matrix products  6.24 us (5%)
    all_to_all x1, waiting for transfers between devices, local(): received = lax.all_to_all(by_owner, 'dp', 0, 0, tiled=True)  47.4 us
    ppermute x3, starting transfers between devices, gather_blocks(): from_left[step] = lax.ppermute(from_left[step - 1], 'dp', rightward)  9.73 us
    unnamed x27, local copies, waits for them, and re-layouts  9.48 us
    ppermute x5, waiting for transfers between devices, butterfly_sum(): x = x + lax.ppermute(x, axis, [(i, i ^ step) for i in range(size)])  8.91 us
    ppermute x1, starting transfers between devices, gather_blocks(): near_left[0] = lax.ppermute(mine, 'dp', partner)  7.37 us
    all_to_all x1, starting transfers between devices, local(): received = lax.all_to_all(by_owner, 'dp', 0, 0, tiled=True)  6.51 us
    ppermute x3, starting transfers between devices, gather_blocks(): from_right[step] = lax.ppermute(from_right[step - 1], 'dp', leftward)  3.85 us
    ppermute x5, starting transfers between devices, butterfly_sum(): x = x + lax.ppermute(x, axis, [(i, i ^ step) for i in range(size)])  3.52 us
  transfers between devices with their start and end apart: 19, of which 8 were waited for; matrix products, arithmetic and copies ran while one was open for 13% of the time, Pallas kernels for 0%

profile of v3, /device:TPU:1, one launch (start us, length us, event | category | flops | bytes accessed | tf_op | source)
XLA Modules:
  0.0 126.2 jit_solution(2662102170576772354)
XLA Ops:
  3.5 1.6 %broadcast_select_fusion = bf16[8,2,256,256]{3,2,1,0:T(8,128)(2,1)} fusion(bf16[8,2,256,256]{3,2,1,0:T(8,128)(2,1)S(1)} %bitcast.90, pred[8,2]{1,0:T(8,128)(4,1)S(1)} %copy.21), kind=kLoop, calls=%fused_computation.3 | loop fusion | flops 1048576 | bytes 4194320 | tf_op jit(solution)/shard_map/jit(_take)/select_n | solution.py:88
  5.1 6.5 %all-to-all-start = ((bf16[8,2,256,256]{3,2,1,0:T(8,128)(2,1)}), bf16[8,2,256,256]{3,2,1,0:T(8,128)(2,1)}, u32[]{:S(2)}, u32[]{:S(2)}) async-start(bf16[8,2,256,256]{3,2,1,0:T(8,128)(2,1)} %broadcast_select_fusion), calls=%async_computation | async-start | bytes 4194304 | tf_op jit(solution)/shard_map/all_to_all | solution.py:91
  12.5 47.4 %all-to-all-done = bf16[8,2,256,256]{3,2,1,0:T(8,128)(2,1)} async-done(((bf16[8,2,256,256]{3,2,1,0:T(8,128)(2,1)}), bf16[8,2,256,256]{3,2,1,0:T(8,128)(2,1)}, u32[]{:S(2)}, u32[]{:S(2)}) %all-to-all-start) | async-done | bytes 2097184 | tf_op jit(solution)/shard_map/all_to_all | solution.py:91
  59.9 1.9 %convert_reduce_fusion = f32[2,256,256]{2,1,0:T(8,128)S(1)} fusion(bf16[8,2,256,256]{3,2,1,0:T(8,128)(2,1)} %all-to-all-done), kind=kLoop, calls=%fused_computation.2 | loop fusion | flops 1966080 | bytes 2621440 | tf_op jit(solution)/shard_map/reduce_sum | solution.py:92
  62.3 1.6 %multiply_reduce_fusion = (f32[2]{0:T(128)S(1)}, f32[2,256,256]{2,1,0:T(8,128)S(1)}) fusion(bf16[1,1,2,256,256]{4,3,2,1,0:T(8,128)(2,1)S(1)} %copy-done.4, f32[2,256,256]{2,1,0:T(8,128)S(1)} %convert_reduce_fusion, bf16[1,1,2,256,256]{4,3,2,1,0:T(8,128)(2,1)} %param.14, f32[2]{0:T(128)S(1)} %convert_element_type.35), kind=kOutput, calls=%fused_computation.28 | convolution fusion | flops 134873088 | bytes 1572880 | tf_op jit(solution)/shard_map/sij,sjk->sik/dot_general | solution.py:117
  65.9 2.4 %collective-permute-done.1 = f32[2,9]{1,0:T(2,128)S(1)} collective-permute-done((f32[2,9]{1,0:T(2,128)S(1)}, f32[2,9]{1,0:T(2,128)S(1)}, u32[]{:S(2)}, u32[]{:S(2)}) %collective-permute-start.1) | collective-permute-done | bytes 104 | tf_op jit(solution)/shard_map/ppermute | solution.py:18
  68.4 3.3 %collective-permute-done.2 = f32[2,9]{1,0:T(2,128)S(1)} collective-permute-done((f32[2,9]{1,0:T(2,128)S(1)}, f32[2,9]{1,0:T(2,128)S(1)}, u32[]{:S(2)}, u32[]{:S(2)}) %collective-permute-start.2) | collective-permute-done | bytes 104 | tf_op jit(solution)/shard_map/ppermute | solution.py:18
  71.7 1.2 collective-permute-start.3
  72.9 1.2 collective-permute-done.3
  74.1 1.2 collective-permute-start.4
  75.3 1.2 collective-permute-done.4
  77.7 1.9 %collective-permute-start.5 = (bf16[2,256,256]{2,1,0:T(8,128)(2,1)S(1)}, bf16[2,256,256]{2,1,0:T(8,128)(2,1)S(1)}, u32[]{:S(2)}, u32[]{:S(2)}) collective-permute-start(bf16[2,256,256]{2,1,0:T(8,128)(2,1)S(1)} %get-tuple-element.9), channel_id=1, source_target_pairs={{0,8},{4,12},{8,16},{12,20},{16,24},{20,28},{1,9},{5,13},{9,17},{1... | collective-permute-start | bytes 786440 | tf_op jit(solution)/shard_map/ppermute | solution.py:42
  79.6 1.3 %collective-permute-start.8 = (bf16[2,256,256]{2,1,0:T(8,128)(2,1)S(1)}, bf16[2,256,256]{2,1,0:T(8,128)(2,1)S(1)}, u32[]{:S(2)}, u32[]{:S(2)}) collective-permute-start(bf16[2,256,256]{2,1,0:T(8,128)(2,1)S(1)} %get-tuple-element.9), channel_id=1, source_target_pairs={{8,0},{12,4},{16,8},{20,12},{24,16},{28,20},{9,1},{13,5},{17,9},{2... | collective-permute-start | bytes 786440 | tf_op jit(solution)/shard_map/ppermute | solution.py:43
  80.9 1.9 %collective-permute-done.5 = bf16[2,256,256]{2,1,0:T(8,128)(2,1)S(1)} collective-permute-done((bf16[2,256,256]{2,1,0:T(8,128)(2,1)S(1)}, bf16[2,256,256]{2,1,0:T(8,128)(2,1)S(1)}, u32[]{:S(2)}, u32[]{:S(2)}) %collective-permute-start.5) | collective-permute-done | bytes 262176 | tf_op jit(solution)/shard_map/ppermute | solution.py:42
  82.9 3.8 %collective-permute-start.6 = (bf16[2,256,256]{2,1,0:T(8,128)(2,1)S(1)}, bf16[2,256,256]{2,1,0:T(8,128)(2,1)S(1)}, u32[]{:S(2)}, u32[]{:S(2)}) collective-permute-start(bf16[2,256,256]{2,1,0:T(8,128)(2,1)S(1)} %collective-permute-done.5), channel_id=1, source_target_pairs={{0,8},{4,12},{8,16},{12,20},{16,24},{20,28},{1,9},{5,13},{9,17},{1... | collective-permute-start | bytes 786440 | tf_op jit(solution)/shard_map/ppermute | solution.py:42
  86.7 3.0 %fusion.2 = f32[1,1,2,256,256]{4,3,2,1,0:T(8,128)} fusion(f32[1,1,2,256,256]{4,3,2,1,0:T(8,128)} %param.13, f32[2,256,256]{2,1,0:T(8,128)S(1)} %convert_reduce_fusion, f32[2]{0:T(128)S(1)} %convert_element_type.35, pred[2]{0:T(512)(128)(4,1)S(1)} %dynamic-slice_reduce_fusion), kind=kOutput, calls=%fused_computation.7 | convolution fusion | flops 403308544 | bytes 1572874 | tf_op jit(solution)/shard_map/sji,sjk->sik/dot_general | solution.py:110
  89.7 1.6 %fusion.5 = f32[1,1,2,256,256]{4,3,2,1,0:T(8,128)} fusion(f32[1,1,2,256,256]{4,3,2,1,0:T(8,128)S(1)} %copy-done.3, f32[2,256,256]{2,1,0:T(8,128)S(1)} %convert_reduce_fusion, f32[2]{0:T(128)S(1)} %convert_element_type.35, pred[2]{0:T(512)(128)(4,1)S(1)} %dynamic-slice_reduce_fusion), kind=kOutput, calls=%fused_computation.11 | convolution fusion | flops 403308544 | bytes 1572874 | tf_op jit(solution)/shard_map/sij,skj->sik/dot_general | solution.py:107
  91.3 1.3 %collective-permute-start.9 = (bf16[2,256,256]{2,1,0:T(8,128)(2,1)S(1)}, bf16[2,256,256]{2,1,0:T(8,128)(2,1)S(1)}, u32[]{:S(2)}, u32[]{:S(2)}) collective-permute-start(bf16[2,256,256]{2,1,0:T(8,128)(2,1)S(1)} %collective-permute-done.8), channel_id=1, source_target_pairs={{8,0},{12,4},{16,8},{20,12},{24,16},{28,20},{9,1},{13,5},{17,9},{2... | collective-permute-start | bytes 786440 | tf_op jit(solution)/shard_map/ppermute | solution.py:43
  92.6 4.0 %collective-permute-start.7 = (bf16[2,256,256]{2,1,0:T(8,128)(2,1)S(1)}, bf16[2,256,256]{2,1,0:T(8,128)(2,1)S(1)}, u32[]{:S(2)}, u32[]{:S(2)}) collective-permute-start(bf16[2,256,256]{2,1,0:T(8,128)(2,1)S(1)} %collective-permute-done.6), channel_id=1, source_target_pairs={{0,8},{4,12},{8,16},{12,20},{16,24},{20,28},{1,9},{5,13},{9,17},{1... | collective-permute-start | bytes 786440 | tf_op jit(solution)/shard_map/ppermute | solution.py:42
  97.6 7.4 %collective-permute-start.14 = (bf16[2,256,256]{2,1,0:T(8,128)(2,1)S(1)}, bf16[2,256,256]{2,1,0:T(8,128)(2,1)S(1)}, u32[]{:S(2)}, u32[]{:S(2)}) collective-permute-start(bf16[2,256,256]{2,1,0:T(8,128)(2,1)S(1)} %get-tuple-element.9), channel_id=1, source_target_pairs={{0,4},{4,0},{8,12},{12,8},{16,20},{20,16},{24,28},{28,24},{1,5},{5... | collective-permute-start | bytes 786440 | tf_op jit(solution)/shard_map/ppermute | solution.py:39
  105.5 1.3 %collective-permute-start.10 = (bf16[2,256,256]{2,1,0:T(8,128)(2,1)S(1)}, bf16[2,256,256]{2,1,0:T(8,128)(2,1)S(1)}, u32[]{:S(2)}, u32[]{:S(2)}) collective-permute-start(bf16[2,256,256]{2,1,0:T(8,128)(2,1)S(1)} %collective-permute-done.9), channel_id=1, source_target_pairs={{8,0},{12,4},{16,8},{20,12},{24,16},{28,20},{9,1},{13,5},{17,9},{2... | collective-permute-start | bytes 786440 | tf_op jit(solution)/shard_map/ppermute | solution.py:43
  112.2 2.1 %collective-permute-done.10 = bf16[2,256,256]{2,1,0:T(8,128)(2,1)S(1)} collective-permute-done((bf16[2,256,256]{2,1,0:T(8,128)(2,1)S(1)}, bf16[2,256,256]{2,1,0:T(8,128)(2,1)S(1)}, u32[]{:S(2)}, u32[]{:S(2)}) %collective-permute-start.10) | collective-permute-done | bytes 262176 | tf_op jit(solution)/shard_map/ppermute | solution.py:43
  114.3 1.8 %collective-permute-start.12 = (bf16[2,256,256]{2,1,0:T(8,128)(2,1)S(1)}, bf16[2,256,256]{2,1,0:T(8,128)(2,1)S(1)}, u32[]{:S(2)}, u32[]{:S(2)}) collective-permute-start(bf16[2,256,256]{2,1,0:T(8,128)(2,1)S(1)} %collective-permute-done.6), channel_id=1, source_target_pairs={{0,4},{4,0},{8,12},{12,8},{16,20},{20,16},{24,28},{28,24},{1,5},{5... | collective-permute-start | bytes 786440 | tf_op jit(solution)/shard_map/ppermute | solution.py:44
  122.4 2.6 %gather_fusion.1 = bf16[8,256,256]{2,1,0:T(8,128)(2,1)S(1)} fusion(bf16[28,256,256]{2,1,0:T(8,128)(2,1)} %bitcast.35, s32[1024]{0:T(1024)S(1)} %pad_clamp_fusion), kind=kCustom, calls=%fused_computation.1 | custom fusion | bytes 2097184 | tf_op jit(solution)/shard_map/jit(_take)/gather | solution.py:54
  (82 shorter events, 21.8 us)
Async XLA Ops:
  5.1 56.7 %copy-start.1 = (f32[1,1,2,256,256]{4,3,2,1,0:T(8,128)S(1)}, f32[1,1,2,256,256]{4,3,2,1,0:T(8,128)}, u32[]{:S(2)}) copy-start(f32[1,1,2,256,256]{4,3,2,1,0:T(8,128)} %param.16) | copy-start | bytes 1572868
  5.1 57.2 %copy-start.4 = (bf16[1,1,2,256,256]{4,3,2,1,0:T(8,128)(2,1)S(1)}, bf16[1,1,2,256,256]{4,3,2,1,0:T(8,128)(2,1)}, u32[]{:S(2)}) copy-start(bf16[1,1,2,256,256]{4,3,2,1,0:T(8,128)(2,1)} %param.15) | copy-start | bytes 786436
  5.1 54.8 %all-to-all-start = ((bf16[8,2,256,256]{3,2,1,0:T(8,128)(2,1)}), bf16[8,2,256,256]{3,2,1,0:T(8,128)(2,1)}, u32[]{:S(2)}, u32[]{:S(2)}) async-start(bf16[8,2,256,256]{3,2,1,0:T(8,128)(2,1)} %broadcast_select_fusion), calls=%async_computation | async-start | bytes 4194304 | tf_op jit(solution)/shard_map/all_to_all | solution.py:91
  11.6 65.1 %copy-start.2 = (f32[1,1,2,256,256]{4,3,2,1,0:T(8,128)S(1)}, f32[1,1,2,256,256]{4,3,2,1,0:T(8,128)}, u32[]{:S(2)}) copy-start(f32[1,1,2,256,256]{4,3,2,1,0:T(8,128)} %param.17) | copy-start | bytes 1572868
  11.6 68.0 %copy-start.5 = (s32[8,1]{0,1:T(1,128)S(1)}, s32[8,1]{0,1:T(1,128)}, u32[]{:S(2)}) copy-start(s32[8,1]{0,1:T(1,128)} %param.10) | copy-start | bytes 100
  64.0 1.8 %collective-permute-start = (f32[2,9]{1,0:T(2,128)S(1)}, f32[2,9]{1,0:T(2,128)S(1)}, u32[]{:S(2)}, u32[]{:S(2)}) collective-permute-start(f32[2,9]{1,0:T(2,128)S(1)} %pad_maximum_fusion), channel_id=1, source_target_pairs={{0,4},{4,0},{8,12},{12,8},{16,20},{20,16},{24,28},{28,24},{1,5},{5... | collective-permute-start | bytes 224 | tf_op jit(solution)/shard_map/ppermute | solution.py:18
  65.8 2.5 %collective-permute-start.1 = (f32[2,9]{1,0:T(2,128)S(1)}, f32[2,9]{1,0:T(2,128)S(1)}, u32[]{:S(2)}, u32[]{:S(2)}) collective-permute-start(f32[2,9]{1,0:T(2,128)S(1)} %fusion.30), channel_id=1, source_target_pairs={{0,8},{4,12},{8,0},{12,4},{16,24},{20,28},{24,16},{28,20},{1,9},{5... | collective-permute-start | bytes 224 | tf_op jit(solution)/shard_map/ppermute | solution.py:18
  68.3 3.4 %collective-permute-start.2 = (f32[2,9]{1,0:T(2,128)S(1)}, f32[2,9]{1,0:T(2,128)S(1)}, u32[]{:S(2)}, u32[]{:S(2)}) collective-permute-start(f32[2,9]{1,0:T(2,128)S(1)} %fusion.35), channel_id=1, source_target_pairs={{0,16},{4,20},{8,24},{12,28},{16,0},{20,4},{24,8},{28,12},{1,17},{... | collective-permute-start | bytes 224 | tf_op jit(solution)/shard_map/ppermute | solution.py:18
  71.7 2.4 %collective-permute-start.3 = (f32[2,9]{1,0:T(2,128)S(1)}, f32[2,9]{1,0:T(2,128)S(1)}, u32[]{:S(2)}, u32[]{:S(2)}) collective-permute-start(f32[2,9]{1,0:T(2,128)S(1)} %add.126), channel_id=1, source_target_pairs={{0,1},{1,0},{2,3},{3,2},{4,5},{5,4},{6,7},{7,6},{8,9},{9,8},{10,11... | collective-permute-start | bytes 224 | tf_op jit(solution)/shard_map/ppermute | solution.py:18
  74.1 2.4 %collective-permute-start.4 = (f32[2,9]{1,0:T(2,128)S(1)}, f32[2,9]{1,0:T(2,128)S(1)}, u32[]{:S(2)}, u32[]{:S(2)}) collective-permute-start(f32[2,9]{1,0:T(2,128)S(1)} %add.127), channel_id=1, source_target_pairs={{0,2},{1,3},{2,0},{3,1},{4,6},{5,7},{6,4},{7,5},{8,10},{9,11},{10,... | collective-permute-start | bytes 224 | tf_op jit(solution)/shard_map/ppermute | solution.py:18
  75.3 14.4 %copy-start.3 = (f32[1,1,2,256,256]{4,3,2,1,0:T(8,128)S(1)}, f32[1,1,2,256,256]{4,3,2,1,0:T(8,128)}, u32[]{:S(2)}) copy-start(f32[1,1,2,256,256]{4,3,2,1,0:T(8,128)} %param.12) | copy-start | bytes 1572868
  77.7 5.2 %collective-permute-start.5 = (bf16[2,256,256]{2,1,0:T(8,128)(2,1)S(1)}, bf16[2,256,256]{2,1,0:T(8,128)(2,1)S(1)}, u32[]{:S(2)}, u32[]{:S(2)}) collective-permute-start(bf16[2,256,256]{2,1,0:T(8,128)(2,1)S(1)} %get-tuple-element.9), channel_id=1, source_target_pairs={{0,8},{4,12},{8,16},{12,20},{16,24},{20,28},{1,9},{5,13},{9,17},{1... | collective-permute-start | bytes 786440 | tf_op jit(solution)/shard_map/ppermute | solution.py:42
  79.6 11.7 %collective-permute-start.8 = (bf16[2,256,256]{2,1,0:T(8,128)(2,1)S(1)}, bf16[2,256,256]{2,1,0:T(8,128)(2,1)S(1)}, u32[]{:S(2)}, u32[]{:S(2)}) collective-permute-start(bf16[2,256,256]{2,1,0:T(8,128)(2,1)S(1)} %get-tuple-element.9), channel_id=1, source_target_pairs={{8,0},{12,4},{16,8},{20,12},{24,16},{28,20},{9,1},{13,5},{17,9},{2... | collective-permute-start | bytes 786440 | tf_op jit(solution)/shard_map/ppermute | solution.py:43
  82.9 9.7 %collective-permute-start.6 = (bf16[2,256,256]{2,1,0:T(8,128)(2,1)S(1)}, bf16[2,256,256]{2,1,0:T(8,128)(2,1)S(1)}, u32[]{:S(2)}, u32[]{:S(2)}) collective-permute-start(bf16[2,256,256]{2,1,0:T(8,128)(2,1)S(1)} %collective-permute-done.5), channel_id=1, source_target_pairs={{0,8},{4,12},{8,16},{12,20},{16,24},{20,28},{1,9},{5,13},{9,17},{1... | collective-permute-start | bytes 786440 | tf_op jit(solution)/shard_map/ppermute | solution.py:42
  91.3 14.2 %collective-permute-start.9 = (bf16[2,256,256]{2,1,0:T(8,128)(2,1)S(1)}, bf16[2,256,256]{2,1,0:T(8,128)(2,1)S(1)}, u32[]{:S(2)}, u32[]{:S(2)}) collective-permute-start(bf16[2,256,256]{2,1,0:T(8,128)(2,1)S(1)} %collective-permute-done.8), channel_id=1, source_target_pairs={{8,0},{12,4},{16,8},{20,12},{24,16},{28,20},{9,1},{13,5},{17,9},{2... | collective-permute-start | bytes 786440 | tf_op jit(solution)/shard_map/ppermute | solution.py:43
  92.6 14.2 %collective-permute-start.7 = (bf16[2,256,256]{2,1,0:T(8,128)(2,1)S(1)}, bf16[2,256,256]{2,1,0:T(8,128)(2,1)S(1)}, u32[]{:S(2)}, u32[]{:S(2)}) collective-permute-start(bf16[2,256,256]{2,1,0:T(8,128)(2,1)S(1)} %collective-permute-done.6), channel_id=1, source_target_pairs={{0,8},{4,12},{8,16},{12,20},{16,24},{20,28},{1,9},{5,13},{9,17},{1... | collective-permute-start | bytes 786440 | tf_op jit(solution)/shard_map/ppermute | solution.py:42
  97.6 21.9 %collective-permute-start.14 = (bf16[2,256,256]{2,1,0:T(8,128)(2,1)S(1)}, bf16[2,256,256]{2,1,0:T(8,128)(2,1)S(1)}, u32[]{:S(2)}, u32[]{:S(2)}) collective-permute-start(bf16[2,256,256]{2,1,0:T(8,128)(2,1)S(1)} %get-tuple-element.9), channel_id=1, source_target_pairs={{0,4},{4,0},{8,12},{12,8},{16,20},{20,16},{24,28},{28,24},{1,5},{5... | collective-permute-start | bytes 786440 | tf_op jit(solution)/shard_map/ppermute | solution.py:39
  105.0 13.8 %collective-permute-start.13 = (bf16[2,256,256]{2,1,0:T(8,128)(2,1)S(1)}, bf16[2,256,256]{2,1,0:T(8,128)(2,1)S(1)}, u32[]{:S(2)}, u32[]{:S(2)}) collective-permute-start(bf16[2,256,256]{2,1,0:T(8,128)(2,1)S(1)} %collective-permute-done.5), channel_id=1, source_target_pairs={{0,4},{4,0},{8,12},{12,8},{16,20},{20,16},{24,28},{28,24},{1,5},{5... | collective-permute-start | bytes 786440 | tf_op jit(solution)/shard_map/ppermute | solution.py:44
  105.0 15.3 %collective-permute-start.15 = (bf16[2,256,256]{2,1,0:T(8,128)(2,1)S(1)}, bf16[2,256,256]{2,1,0:T(8,128)(2,1)S(1)}, u32[]{:S(2)}, u32[]{:S(2)}) collective-permute-start(bf16[2,256,256]{2,1,0:T(8,128)(2,1)S(1)} %collective-permute-done.8), channel_id=1, source_target_pairs={{0,4},{4,0},{8,12},{12,8},{16,20},{20,16},{24,28},{28,24},{1,5},{5... | collective-permute-start | bytes 786440 | tf_op jit(solution)/shard_map/ppermute | solution.py:45
  105.5 8.8 %collective-permute-start.10 = (bf16[2,256,256]{2,1,0:T(8,128)(2,1)S(1)}, bf16[2,256,256]{2,1,0:T(8,128)(2,1)S(1)}, u32[]{:S(2)}, u32[]{:S(2)}) collective-permute-start(bf16[2,256,256]{2,1,0:T(8,128)(2,1)S(1)} %collective-permute-done.9), channel_id=1, source_target_pairs={{8,0},{12,4},{16,8},{20,12},{24,16},{28,20},{9,1},{13,5},{17,9},{2... | collective-permute-start | bytes 786440 | tf_op jit(solution)/shard_map/ppermute | solution.py:43
  109.7 7.2 %collective-permute-start.11 = (bf16[2,256,256]{2,1,0:T(8,128)(2,1)S(1)}, bf16[2,256,256]{2,1,0:T(8,128)(2,1)S(1)}, u32[]{:S(2)}, u32[]{:S(2)}) collective-permute-start(bf16[2,256,256]{2,1,0:T(8,128)(2,1)S(1)} %collective-permute-done.7), channel_id=1, source_target_pairs={{0,4},{4,0},{8,12},{12,8},{16,20},{20,16},{24,28},{28,24},{1,5},{5... | collective-permute-start | bytes 786440 | tf_op jit(solution)/shard_map/ppermute | solution.py:44
  114.3 3.3 %collective-permute-start.12 = (bf16[2,256,256]{2,1,0:T(8,128)(2,1)S(1)}, bf16[2,256,256]{2,1,0:T(8,128)(2,1)S(1)}, u32[]{:S(2)}, u32[]{:S(2)}) collective-permute-start(bf16[2,256,256]{2,1,0:T(8,128)(2,1)S(1)} %collective-permute-done.6), channel_id=1, source_target_pairs={{0,4},{4,0},{8,12},{12,8},{16,20},{20,16},{24,28},{28,24},{1,5},{5... | collective-permute-start | bytes 786440 | tf_op jit(solution)/shard_map/ppermute | solution.py:44
  116.8 4.2 %collective-permute-start.16 = (bf16[2,256,256]{2,1,0:T(8,128)(2,1)S(1)}, bf16[2,256,256]{2,1,0:T(8,128)(2,1)S(1)}, u32[]{:S(2)}, u32[]{:S(2)}) collective-permute-start(bf16[2,256,256]{2,1,0:T(8,128)(2,1)S(1)} %collective-permute-done.9), channel_id=1, source_target_pairs={{0,4},{4,0},{8,12},{12,8},{16,20},{20,16},{24,28},{28,24},{1,5},{5... | collective-permute-start | bytes 786440 | tf_op jit(solution)/shard_map/ppermute | solution.py:45
  117.5 4.2 %collective-permute-start.17 = (bf16[2,256,256]{2,1,0:T(8,128)(2,1)S(1)}, bf16[2,256,256]{2,1,0:T(8,128)(2,1)S(1)}, u32[]{:S(2)}, u32[]{:S(2)}) collective-permute-start(bf16[2,256,256]{2,1,0:T(8,128)(2,1)S(1)} %collective-permute-done.10), channel_id=1, source_target_pairs={{0,4},{4,0},{8,12},{12,8},{16,20},{20,16},{24,28},{28,24},{1,5},{5... | collective-permute-start | bytes 786440 | tf_op jit(solution)/shard_map/ppermute | solution.py:45
  (2 other events, 10.6 us)

commit v4 on v3

--- a/solution.py
+++ b/solution.py
@@ -1,6 +1,8 @@
 import jax
 import jax.numpy as jnp
 from jax import lax
+from jax.experimental import pallas as pl
+from jax.experimental.pallas import tpu as pltpu
 from jax.sharding import PartitionSpec as P
 
 BETA = 0.95
@@ -43,15 +45,44 @@
         from_right[step] = lax.ppermute(from_right[step - 1], "dp", leftward)
         near_left[step] = lax.ppermute(from_left[step], "dp", partner)
         near_right[step] = lax.ppermute(from_right[step], "dp", partner)
-    same_core = from_left[::-1] + from_right[1:]
-    other_core = near_left[::-1] + near_right[1:]
-    pieces = jnp.stack(same_core + other_core)
+    pieces = from_left[::-1] + from_right[1:] + near_left[::-1] + near_right[1:]
     chip, core = replica // 2, replica % 2
     owner_chip, owner_core = owner_of // 2, owner_of % 2
     offset = owner_chip - chip + chips - 1
     which = jnp.where(owner_core == core, 0, 1)
-    index = (which * (2 * chips - 1) + offset) * slot_count + slot_rank
-    return jnp.take(pieces.reshape((-1,) + mine.shape[1:]), index, axis=0)
+    source = jnp.clip(which * (2 * chips - 1) + offset, 0, len(pieces) - 1)
+    table = jnp.stack([source, jnp.clip(slot_rank, 0, slot_count - 1)], axis=1).astype(jnp.int32)
+    return pick_blocks(table, pieces)
+
+
+def pick_kernel(table_ref, *refs):
+    pieces, out_ref, sems = refs[:-2], refs[-2], refs[-1]
+
+    def start(block, carry):
+        for index, piece in enumerate(pieces):
+            @pl.when(table_ref[block, 0] == index)
+            def _():
+                pltpu.make_async_copy(piece.at[table_ref[block, 1]], out_ref.at[block], sems.at[block]).start()
+
+        return carry
+
+    def finish(block, carry):
+        pltpu.make_async_copy(pieces[0].at[0], out_ref.at[block], sems.at[block]).wait()
+        return carry
+
+    lax.fori_loop(0, out_ref.shape[0], start, 0)
+    lax.fori_loop(0, out_ref.shape[0], finish, 0)
+
+
+def pick_blocks(table, pieces):
+    blocks = table.shape[0]
+    return pl.pallas_call(
+        pick_kernel,
+        out_shape=jax.ShapeDtypeStruct((blocks,) + pieces[0].shape[1:], pieces[0].dtype),
+        in_specs=[pl.BlockSpec(memory_space=pltpu.SMEM)] + [pl.BlockSpec(memory_space=pl.ANY)] * len(pieces),
+        out_specs=pl.BlockSpec(memory_space=pl.ANY),
+        scratch_shapes=[pltpu.SemaphoreType.DMA((blocks,))],
+    )(table, *pieces)
 
 
 def local(

time: 127 us -> 148 us (1.17)
  Pallas kernels: 0 us -> 33.8 us
  local copies, waits for them, and re-layouts: 14 us -> 3.37 us
  waiting for transfers between devices: 60.3 us -> 58.3 us
    pallas_call x0 -> x1, Pallas kernels: none -> 33.8 us  [pick_blocks(): pl.pallas_call(pick_kernel, out_shape=jax.ShapeDtypeStruct((blocks,) + pi...]
    unnamed x27 -> x38, local copies, waits for them, and re-layouts: 9.48 us -> 1.56 us
    ppermute x3, starting transfers between devices: 2.89 us -> 0.16 us  [gather_blocks(): near_left[step] = lax.ppermute(from_left[step], 'dp', partner)]
    gather x1 -> x0, local copies, waits for them, and re-layouts: 2.65 us -> none  [gather_blocks(): return jnp.take(pieces.reshape((-1,) + mine.shape[1:]), index, axis=0)]
    ppermute x3, starting transfers between devices: 1.02 us -> 3.49 us  [gather_blocks(): near_right[step] = lax.ppermute(from_right[step], 'dp', partner)]
    ppermute x3, waiting for transfers between devices: 2.08 us -> 0.01 us  [gather_blocks(): from_right[step] = lax.ppermute(from_right[step - 1], 'dp', leftward)]
  transfers between devices with their start and end apart: 19 -> 19, of which waited for: 8 -> 7; matrix products, arithmetic and copies ran while one was open for 13% -> 6% of each run, Pallas kernels for 0% -> 0%
where the time goes in v4:
time: 148 us; the launch traced here: 147 us
  waiting for transfers between devices  58.3 us (39%)
  starting transfers between devices  34.6 us (23%)
  Pallas kernels  33.8 us (23%)
  other arithmetic  8.79 us (6%)
  matrix products  7.28 us (5%)
  local copies, waits for them, and re-layouts  3.37 us (2%)
    all_to_all x1, waiting for transfers between devices, local(): received = lax.all_to_all(by_owner, 'dp', 0, 0, tiled=True)  47.4 us
    pallas_call x1, Pallas kernels, pick_blocks(): pl.pallas_call(pick_kernel, out_shape=jax.ShapeDtypeStruct((blocks,) + pi...  33.8 us
    ppermute x3, starting transfers between devices, gather_blocks(): from_left[step] = lax.ppermute(from_left[step - 1], 'dp', rightward)  10 us
    ppermute x5, waiting for transfers between devices, butterfly_sum(): x = x + lax.ppermute(x, axis, [(i, i ^ step) for i in range(size)])  8.92 us
    ppermute x1, starting transfers between devices, gather_blocks(): near_left[0] = lax.ppermute(mine, 'dp', partner)  7.05 us
    all_to_all x1, starting transfers between devices, local(): received = lax.all_to_all(by_owner, 'dp', 0, 0, tiled=True)  6.51 us
    ppermute x3, starting transfers between devices, gather_blocks(): from_right[step] = lax.ppermute(from_right[step - 1], 'dp', leftward)  3.88 us
    ppermute x5, starting transfers between devices, butterfly_sum(): x = x + lax.ppermute(x, axis, [(i, i ^ step) for i in range(size)])  3.52 us
  transfers between devices with their start and end apart: 19, of which 7 were waited for; matrix products, arithmetic and copies ran while one was open for 6% of the time, Pallas kernels for 0%

profile of v4, /device:TPU:1, one launch (start us, length us, event | category | flops | bytes accessed | tf_op | source)
XLA Modules:
  0.0 147.1 jit_solution(16857622311814940466)
XLA Ops:
  3.5 1.6 %broadcast_select_fusion = bf16[8,2,256,256]{3,2,1,0:T(8,128)(2,1)} fusion(bf16[8,2,256,256]{3,2,1,0:T(8,128)(2,1)S(1)} %bitcast.55, pred[8,2]{1,0:T(8,128)(4,1)S(1)} %copy.36), kind=kLoop, calls=%fused_computation.2 | loop fusion | flops 1048576 | bytes 4194320 | tf_op jit(solution)/shard_map/jit(_take)/select_n | solution.py:119
  5.1 6.5 %all-to-all-start = ((bf16[8,2,256,256]{3,2,1,0:T(8,128)(2,1)}), bf16[8,2,256,256]{3,2,1,0:T(8,128)(2,1)}, u32[]{:S(2)}, u32[]{:S(2)}) async-start(bf16[8,2,256,256]{3,2,1,0:T(8,128)(2,1)} %broadcast_select_fusion), calls=%async_computation | async-start | bytes 4194304 | tf_op jit(solution)/shard_map/all_to_all | solution.py:122
  12.5 47.4 %all-to-all-done = bf16[8,2,256,256]{3,2,1,0:T(8,128)(2,1)} async-done(((bf16[8,2,256,256]{3,2,1,0:T(8,128)(2,1)}), bf16[8,2,256,256]{3,2,1,0:T(8,128)(2,1)}, u32[]{:S(2)}, u32[]{:S(2)}) %all-to-all-start) | async-done | bytes 2097184 | tf_op jit(solution)/shard_map/all_to_all | solution.py:122
  59.9 1.9 %convert_reduce_fusion = f32[2,256,256]{2,1,0:T(8,128)S(1)} fusion(bf16[8,2,256,256]{3,2,1,0:T(8,128)(2,1)} %all-to-all-done), kind=kLoop, calls=%fused_computation.1 | loop fusion | flops 1966080 | bytes 2621440 | tf_op jit(solution)/shard_map/reduce_sum | solution.py:123
  62.3 1.6 %multiply_reduce_fusion = (f32[2]{0:T(128)S(1)}, f32[2,256,256]{2,1,0:T(8,128)S(1)}) fusion(bf16[1,1,2,256,256]{4,3,2,1,0:T(8,128)(2,1)S(1)} %copy-done.4, f32[2,256,256]{2,1,0:T(8,128)S(1)} %convert_reduce_fusion, bf16[1,1,2,256,256]{4,3,2,1,0:T(8,128)(2,1)} %param.14, f32[2]{0:T(128)S(1)} %convert_element_type.35), kind=kOutput, calls=%fused_computation.26 | convolution fusion | flops 134873088 | bytes 1572880 | tf_op jit(solution)/shard_map/sij,sjk->sik/dot_general | solution.py:148
  65.9 2.4 %collective-permute-done.1 = f32[2,9]{1,0:T(2,128)S(1)} collective-permute-done((f32[2,9]{1,0:T(2,128)S(1)}, f32[2,9]{1,0:T(2,128)S(1)}, u32[]{:S(2)}, u32[]{:S(2)}) %collective-permute-start.1) | collective-permute-done | bytes 104 | tf_op jit(solution)/shard_map/ppermute | solution.py:20
  68.4 3.3 %collective-permute-done.2 = f32[2,9]{1,0:T(2,128)S(1)} collective-permute-done((f32[2,9]{1,0:T(2,128)S(1)}, f32[2,9]{1,0:T(2,128)S(1)}, u32[]{:S(2)}, u32[]{:S(2)}) %collective-permute-start.2) | collective-permute-done | bytes 104 | tf_op jit(solution)/shard_map/ppermute | solution.py:20
  71.7 1.2 collective-permute-start.3
  72.9 1.2 collective-permute-done.3
  74.1 1.2 collective-permute-start.4
  75.3 1.2 collective-permute-done.4
  77.7 1.9 %collective-permute-start.5 = (bf16[2,256,256]{2,1,0:T(8,128)(2,1)S(1)}, bf16[2,256,256]{2,1,0:T(8,128)(2,1)S(1)}, u32[]{:S(2)}, u32[]{:S(2)}) collective-permute-start(bf16[2,256,256]{2,1,0:T(8,128)(2,1)S(1)} %get-tuple-element.7.refs_3_), channel_id=1, source_target_pairs={{0,8},{4,12},{8,16},{12,20},{16,24},{20,28},{1,9},{5,13},{9,17},{1... | collective-permute-start | bytes 786440 | tf_op jit(solution)/shard_map/ppermute | solution.py:44
  79.6 1.3 collective-permute-start.8
  80.9 2.0 %collective-permute-done.5.refs_2_ = bf16[2,256,256]{2,1,0:T(8,128)(2,1)S(1)} collective-permute-done((bf16[2,256,256]{2,1,0:T(8,128)(2,1)S(1)}, bf16[2,256,256]{2,1,0:T(8,128)(2,1)S(1)}, u32[]{:S(2)}, u32[]{:S(2)}) %collective-permute-start.5) | collective-permute-done | bytes 262176 | tf_op jit(solution)/shard_map/ppermute | solution.py:44
  82.9 3.8 %collective-permute-start.6 = (bf16[2,256,256]{2,1,0:T(8,128)(2,1)S(1)}, bf16[2,256,256]{2,1,0:T(8,128)(2,1)S(1)}, u32[]{:S(2)}, u32[]{:S(2)}) collective-permute-start(bf16[2,256,256]{2,1,0:T(8,128)(2,1)S(1)} %collective-permute-done.5.refs_2_), channel_id=1, source_target_pairs={{0,8},{4,12},{8,16},{12,20},{16,24},{20,28},{1,9},{5,13},{9,17},{1... | collective-permute-start | bytes 786440 | tf_op jit(solution)/shard_map/ppermute | solution.py:44
  86.7 1.3 collective-permute-start.9
  88.7 7.1 %collective-permute-start.14 = (bf16[2,256,256]{2,1,0:T(8,128)(2,1)S(1)}, bf16[2,256,256]{2,1,0:T(8,128)(2,1)S(1)}, u32[]{:S(2)}, u32[]{:S(2)}) collective-permute-start(bf16[2,256,256]{2,1,0:T(8,128)(2,1)S(1)} %get-tuple-element.7.refs_3_), channel_id=1, source_target_pairs={{0,4},{4,0},{8,12},{12,8},{16,20},{20,16},{24,28},{28,24},{1,5},{5... | collective-permute-start | bytes 786440 | tf_op jit(solution)/shard_map/ppermute | solution.py:41
  95.8 4.3 %collective-permute-start.7 = (bf16[2,256,256]{2,1,0:T(8,128)(2,1)S(1)}, bf16[2,256,256]{2,1,0:T(8,128)(2,1)S(1)}, u32[]{:S(2)}, u32[]{:S(2)}) collective-permute-start(bf16[2,256,256]{2,1,0:T(8,128)(2,1)S(1)} %collective-permute-done.6.refs_1_), channel_id=1, source_target_pairs={{0,8},{4,12},{8,16},{12,20},{16,24},{20,28},{1,9},{5,13},{9,17},{1... | collective-permute-start | bytes 786440 | tf_op jit(solution)/shard_map/ppermute | solution.py:44
  100.1 1.3 collective-permute-start.10
  101.4 3.0 %fusion.2 = f32[1,1,2,256,256]{4,3,2,1,0:T(8,128)} fusion(f32[1,1,2,256,256]{4,3,2,1,0:T(8,128)} %param.13, f32[2,256,256]{2,1,0:T(8,128)S(1)} %convert_reduce_fusion, f32[2]{0:T(128)S(1)} %convert_element_type.35, pred[2]{0:T(512)(128)(4,1)S(1)} %dynamic-slice_reduce_fusion), kind=kOutput, calls=%fused_computation.6 | convolution fusion | flops 403308544 | bytes 1572874 | tf_op jit(solution)/shard_map/sji,sjk->sik/dot_general | solution.py:141
  104.4 2.7 %fusion.5 = f32[1,1,2,256,256]{4,3,2,1,0:T(8,128)} fusion(f32[1,1,2,256,256]{4,3,2,1,0:T(8,128)} %param.12, f32[2,256,256]{2,1,0:T(8,128)S(1)} %convert_reduce_fusion, f32[2]{0:T(128)S(1)} %convert_element_type.35, pred[2]{0:T(512)(128)(4,1)S(1)} %dynamic-slice_reduce_fusion), kind=kOutput, calls=%fused_computation.10 | convolution fusion | flops 403308544 | bytes 1572874 | tf_op jit(solution)/shard_map/sij,skj->sik/dot_general | solution.py:138
  107.1 1.9 %collective-permute-start.15 = (bf16[2,256,256]{2,1,0:T(8,128)(2,1)S(1)}, bf16[2,256,256]{2,1,0:T(8,128)(2,1)S(1)}, u32[]{:S(2)}, u32[]{:S(2)}) collective-permute-start(bf16[2,256,256]{2,1,0:T(8,128)(2,1)S(1)} %collective-permute-done.8.refs_4_), channel_id=1, source_target_pairs={{0,4},{4,0},{8,12},{12,8},{16,20},{20,16},{24,28},{28,24},{1,5},{5... | collective-permute-start | bytes 786440 | tf_op jit(solution)/shard_map/ppermute | solution.py:47
  109.6 1.1 collective-permute-start.17
  113.3 33.8 %shard_map.128 = bf16[8,256,256]{2,1,0:T(8,128)(2,1)} custom-call(s32[8,2]{1,0:T(8,128)} %copy.41.table_ref, bf16[2,256,256]{2,1,0:T(8,128)(2,1)} %copy-done.11, bf16[2,256,256]{2,1,0:T(8,128)(2,1)} %copy-done.7, bf16[2,256,256]{2,1,0:T(8,128)(2,1)} %copy-done.5, bf16[2,256,256]{2,1,0:T(8,128)(2,1)} %copy-done.2, bf16[2,256,256]{2,1,0:T(8,128)(2,1)} %copy-done.6, ...), custom_call_target="tpu_custom_call" | custom-call | tf_op jit(solution)/shard_map/pallas_call | solution.py:79
  (93 shorter events, 11.2 us)
Async XLA Ops:
  5.1 54.8 %all-to-all-start = ((bf16[8,2,256,256]{3,2,1,0:T(8,128)(2,1)}), bf16[8,2,256,256]{3,2,1,0:T(8,128)(2,1)}, u32[]{:S(2)}, u32[]{:S(2)}) async-start(bf16[8,2,256,256]{3,2,1,0:T(8,128)(2,1)} %broadcast_select_fusion), calls=%async_computation | async-start | bytes 4194304 | tf_op jit(solution)/shard_map/all_to_all | solution.py:122
  11.6 50.2 %copy-start.1 = (f32[1,1,2,256,256]{4,3,2,1,0:T(8,128)S(1)}, f32[1,1,2,256,256]{4,3,2,1,0:T(8,128)}, u32[]{:S(2)}) copy-start(f32[1,1,2,256,256]{4,3,2,1,0:T(8,128)} %param.16) | copy-start | bytes 1572868
  11.6 50.7 %copy-start.4 = (bf16[1,1,2,256,256]{4,3,2,1,0:T(8,128)(2,1)S(1)}, bf16[1,1,2,256,256]{4,3,2,1,0:T(8,128)(2,1)}, u32[]{:S(2)}) copy-start(bf16[1,1,2,256,256]{4,3,2,1,0:T(8,128)(2,1)} %param.15) | copy-start | bytes 786436
  12.5 64.2 %copy-start.3 = (f32[1,1,2,256,256]{4,3,2,1,0:T(8,128)S(1)}, f32[1,1,2,256,256]{4,3,2,1,0:T(8,128)}, u32[]{:S(2)}) copy-start(f32[1,1,2,256,256]{4,3,2,1,0:T(8,128)} %param.17) | copy-start | bytes 1572868
  64.0 1.8 %collective-permute-start = (f32[2,9]{1,0:T(2,128)S(1)}, f32[2,9]{1,0:T(2,128)S(1)}, u32[]{:S(2)}, u32[]{:S(2)}) collective-permute-start(f32[2,9]{1,0:T(2,128)S(1)} %pad_maximum_fusion), channel_id=1, source_target_pairs={{0,4},{4,0},{8,12},{12,8},{16,20},{20,16},{24,28},{28,24},{1,5},{5... | collective-permute-start | bytes 224 | tf_op jit(solution)/shard_map/ppermute | solution.py:20
  65.8 2.5 %collective-permute-start.1 = (f32[2,9]{1,0:T(2,128)S(1)}, f32[2,9]{1,0:T(2,128)S(1)}, u32[]{:S(2)}, u32[]{:S(2)}) collective-permute-start(f32[2,9]{1,0:T(2,128)S(1)} %fusion.31), channel_id=1, source_target_pairs={{0,8},{4,12},{8,0},{12,4},{16,24},{20,28},{24,16},{28,20},{1,9},{5... | collective-permute-start | bytes 224 | tf_op jit(solution)/shard_map/ppermute | solution.py:20
  68.3 3.4 %collective-permute-start.2 = (f32[2,9]{1,0:T(2,128)S(1)}, f32[2,9]{1,0:T(2,128)S(1)}, u32[]{:S(2)}, u32[]{:S(2)}) collective-permute-start(f32[2,9]{1,0:T(2,128)S(1)} %fusion.36), channel_id=1, source_target_pairs={{0,16},{4,20},{8,24},{12,28},{16,0},{20,4},{24,8},{28,12},{1,17},{... | collective-permute-start | bytes 224 | tf_op jit(solution)/shard_map/ppermute | solution.py:20
  71.7 2.4 %collective-permute-start.3 = (f32[2,9]{1,0:T(2,128)S(1)}, f32[2,9]{1,0:T(2,128)S(1)}, u32[]{:S(2)}, u32[]{:S(2)}) collective-permute-start(f32[2,9]{1,0:T(2,128)S(1)} %add.110), channel_id=1, source_target_pairs={{0,1},{1,0},{2,3},{3,2},{4,5},{5,4},{6,7},{7,6},{8,9},{9,8},{10,11... | collective-permute-start | bytes 224 | tf_op jit(solution)/shard_map/ppermute | solution.py:20
  74.1 2.4 %collective-permute-start.4 = (f32[2,9]{1,0:T(2,128)S(1)}, f32[2,9]{1,0:T(2,128)S(1)}, u32[]{:S(2)}, u32[]{:S(2)}) collective-permute-start(f32[2,9]{1,0:T(2,128)S(1)} %add.111), channel_id=1, source_target_pairs={{0,2},{1,3},{2,0},{3,1},{4,6},{5,7},{6,4},{7,5},{8,10},{9,11},{10,... | collective-permute-start | bytes 224 | tf_op jit(solution)/shard_map/ppermute | solution.py:20
  77.7 34.0 %copy-start.2 = (bf16[2,256,256]{2,1,0:T(8,128)(2,1)}, bf16[2,256,256]{2,1,0:T(8,128)(2,1)S(1)}, u32[]{:S(2)}) copy-start(bf16[2,256,256]{2,1,0:T(8,128)(2,1)S(1)} %get-tuple-element.7.refs_3_) | copy-start | bytes 786436
  77.7 5.2 %collective-permute-start.5 = (bf16[2,256,256]{2,1,0:T(8,128)(2,1)S(1)}, bf16[2,256,256]{2,1,0:T(8,128)(2,1)S(1)}, u32[]{:S(2)}, u32[]{:S(2)}) collective-permute-start(bf16[2,256,256]{2,1,0:T(8,128)(2,1)S(1)} %get-tuple-element.7.refs_3_), channel_id=1, source_target_pairs={{0,8},{4,12},{8,16},{12,20},{16,24},{20,28},{1,9},{5,13},{9,17},{1... | collective-permute-start | bytes 786440 | tf_op jit(solution)/shard_map/ppermute | solution.py:44
  79.6 7.1 %collective-permute-start.8 = (bf16[2,256,256]{2,1,0:T(8,128)(2,1)S(1)}, bf16[2,256,256]{2,1,0:T(8,128)(2,1)S(1)}, u32[]{:S(2)}, u32[]{:S(2)}) collective-permute-start(bf16[2,256,256]{2,1,0:T(8,128)(2,1)S(1)} %get-tuple-element.7.refs_3_), channel_id=1, source_target_pairs={{8,0},{12,4},{16,8},{20,12},{24,16},{28,20},{9,1},{13,5},{17,9},{2... | collective-permute-start | bytes 786440 | tf_op jit(solution)/shard_map/ppermute | solution.py:45
  82.9 28.8 %copy-start.5 = (bf16[2,256,256]{2,1,0:T(8,128)(2,1)}, bf16[2,256,256]{2,1,0:T(8,128)(2,1)S(1)}, u32[]{:S(2)}) copy-start(bf16[2,256,256]{2,1,0:T(8,128)(2,1)S(1)} %collective-permute-done.5.refs_2_) | copy-start | bytes 786436
  82.9 12.9 %collective-permute-start.6 = (bf16[2,256,256]{2,1,0:T(8,128)(2,1)S(1)}, bf16[2,256,256]{2,1,0:T(8,128)(2,1)S(1)}, u32[]{:S(2)}, u32[]{:S(2)}) collective-permute-start(bf16[2,256,256]{2,1,0:T(8,128)(2,1)S(1)} %collective-permute-done.5.refs_2_), channel_id=1, source_target_pairs={{0,8},{4,12},{8,16},{12,20},{16,24},{20,28},{1,9},{5,13},{9,17},{1... | collective-permute-start | bytes 786440 | tf_op jit(solution)/shard_map/ppermute | solution.py:44
  86.7 13.4 %collective-permute-start.9 = (bf16[2,256,256]{2,1,0:T(8,128)(2,1)S(1)}, bf16[2,256,256]{2,1,0:T(8,128)(2,1)S(1)}, u32[]{:S(2)}, u32[]{:S(2)}) collective-permute-start(bf16[2,256,256]{2,1,0:T(8,128)(2,1)S(1)} %collective-permute-done.8.refs_4_), channel_id=1, source_target_pairs={{8,0},{12,4},{16,8},{20,12},{24,16},{28,20},{9,1},{13,5},{17,9},{2... | collective-permute-start | bytes 786440 | tf_op jit(solution)/shard_map/ppermute | solution.py:45
  88.7 20.2 %collective-permute-start.14 = (bf16[2,256,256]{2,1,0:T(8,128)(2,1)S(1)}, bf16[2,256,256]{2,1,0:T(8,128)(2,1)S(1)}, u32[]{:S(2)}, u32[]{:S(2)}) collective-permute-start(bf16[2,256,256]{2,1,0:T(8,128)(2,1)S(1)} %get-tuple-element.7.refs_3_), channel_id=1, source_target_pairs={{0,4},{4,0},{8,12},{12,8},{16,20},{20,16},{24,28},{28,24},{1,5},{5... | collective-permute-start | bytes 786440 | tf_op jit(solution)/shard_map/ppermute | solution.py:41
  95.8 13.3 %collective-permute-start.13 = (bf16[2,256,256]{2,1,0:T(8,128)(2,1)S(1)}, bf16[2,256,256]{2,1,0:T(8,128)(2,1)S(1)}, u32[]{:S(2)}, u32[]{:S(2)}) collective-permute-start(bf16[2,256,256]{2,1,0:T(8,128)(2,1)S(1)} %collective-permute-done.5.refs_2_), channel_id=1, source_target_pairs={{0,4},{4,0},{8,12},{12,8},{16,20},{20,16},{24,28},{28,24},{1,5},{5... | collective-permute-start | bytes 786440 | tf_op jit(solution)/shard_map/ppermute | solution.py:46
  95.8 13.7 %collective-permute-start.7 = (bf16[2,256,256]{2,1,0:T(8,128)(2,1)S(1)}, bf16[2,256,256]{2,1,0:T(8,128)(2,1)S(1)}, u32[]{:S(2)}, u32[]{:S(2)}) collective-permute-start(bf16[2,256,256]{2,1,0:T(8,128)(2,1)S(1)} %collective-permute-done.6.refs_1_), channel_id=1, source_target_pairs={{0,8},{4,12},{8,16},{12,20},{16,24},{20,28},{1,9},{5,13},{9,17},{1... | collective-permute-start | bytes 786440 | tf_op jit(solution)/shard_map/ppermute | solution.py:44
  100.1 9.5 %collective-permute-start.10 = (bf16[2,256,256]{2,1,0:T(8,128)(2,1)S(1)}, bf16[2,256,256]{2,1,0:T(8,128)(2,1)S(1)}, u32[]{:S(2)}, u32[]{:S(2)}) collective-permute-start(bf16[2,256,256]{2,1,0:T(8,128)(2,1)S(1)} %collective-permute-done.9.refs_5_), channel_id=1, source_target_pairs={{8,0},{12,4},{16,8},{20,12},{24,16},{28,20},{9,1},{13,5},{17,9},{2... | collective-permute-start | bytes 786440 | tf_op jit(solution)/shard_map/ppermute | solution.py:45
  107.1 4.7 %collective-permute-start.15 = (bf16[2,256,256]{2,1,0:T(8,128)(2,1)S(1)}, bf16[2,256,256]{2,1,0:T(8,128)(2,1)S(1)}, u32[]{:S(2)}, u32[]{:S(2)}) collective-permute-start(bf16[2,256,256]{2,1,0:T(8,128)(2,1)S(1)} %collective-permute-done.8.refs_4_), channel_id=1, source_target_pairs={{0,4},{4,0},{8,12},{12,8},{16,20},{20,16},{24,28},{28,24},{1,5},{5... | collective-permute-start | bytes 786440 | tf_op jit(solution)/shard_map/ppermute | solution.py:47
  109.0 2.8 %collective-permute-start.12 = (bf16[2,256,256]{2,1,0:T(8,128)(2,1)S(1)}, bf16[2,256,256]{2,1,0:T(8,128)(2,1)S(1)}, u32[]{:S(2)}, u32[]{:S(2)}) collective-permute-start(bf16[2,256,256]{2,1,0:T(8,128)(2,1)S(1)} %collective-permute-done.6.refs_1_), channel_id=1, source_target_pairs={{0,4},{4,0},{8,12},{12,8},{16,20},{20,16},{24,28},{28,24},{1,5},{5... | collective-permute-start | bytes 786440 | tf_op jit(solution)/shard_map/ppermute | solution.py:46
  109.1 2.7 %collective-permute-start.16 = (bf16[2,256,256]{2,1,0:T(8,128)(2,1)S(1)}, bf16[2,256,256]{2,1,0:T(8,128)(2,1)S(1)}, u32[]{:S(2)}, u32[]{:S(2)}) collective-permute-start(bf16[2,256,256]{2,1,0:T(8,128)(2,1)S(1)} %collective-permute-done.9.refs_5_), channel_id=1, source_target_pairs={{0,4},{4,0},{8,12},{12,8},{16,20},{20,16},{24,28},{28,24},{1,5},{5... | collective-permute-start | bytes 786440 | tf_op jit(solution)/shard_map/ppermute | solution.py:47
  109.5 2.3 %collective-permute-start.11 = (bf16[2,256,256]{2,1,0:T(8,128)(2,1)S(1)}, bf16[2,256,256]{2,1,0:T(8,128)(2,1)S(1)}, u32[]{:S(2)}, u32[]{:S(2)}) collective-permute-start(bf16[2,256,256]{2,1,0:T(8,128)(2,1)S(1)} %collective-permute-done.7.refs_0_), channel_id=1, source_target_pairs={{0,4},{4,0},{8,12},{12,8},{16,20},{20,16},{24,28},{28,24},{1,5},{5... | collective-permute-start | bytes 786440 | tf_op jit(solution)/shard_map/ppermute | solution.py:46
  109.6 3.7 %collective-permute-start.17 = (bf16[2,256,256]{2,1,0:T(8,128)(2,1)S(1)}, bf16[2,256,256]{2,1,0:T(8,128)(2,1)}, u32[]{:S(2)}, u32[]{:S(2)}) collective-permute-start(bf16[2,256,256]{2,1,0:T(8,128)(2,1)S(1)} %collective-permute-done.10.refs_6_), channel_id=1, source_target_pairs={{0,4},{4,0},{8,12},{12,8},{16,20},{20,16},{24,28},{28,24},{1,5},{5... | collective-permute-start | bytes 786440 | tf_op jit(solution)/shard_map/ppermute | solution.py:47
  (14 other events, 100.9 us)

commit v5 on v4

--- a/solution.py
+++ b/solution.py
@@ -80,7 +80,7 @@
         pick_kernel,
         out_shape=jax.ShapeDtypeStruct((blocks,) + pieces[0].shape[1:], pieces[0].dtype),
         in_specs=[pl.BlockSpec(memory_space=pltpu.SMEM)] + [pl.BlockSpec(memory_space=pl.ANY)] * len(pieces),
-        out_specs=pl.BlockSpec(memory_space=pl.ANY),
+        out_specs=pl.BlockSpec(memory_space=pltpu.VMEM),
         scratch_shapes=[pltpu.SemaphoreType.DMA((blocks,))],
     )(table, *pieces)
 

time: 148 us -> 117 us (0.79)
  Pallas kernels: 33.8 us -> 3.12 us
    pallas_call x1, Pallas kernels: 33.8 us -> 3.12 us  [pick_blocks(): pl.pallas_call(pick_kernel, out_shape=jax.ShapeDtypeStruct((blocks,) + pi...]
  transfers between devices with their start and end apart: 19 -> 19, of which waited for: 7 -> 7; matrix products, arithmetic and copies ran while one was open for 6% -> 7% of each run, Pallas kernels for 0% -> 0%
where the time goes in v5:
time: 117 us; the launch traced here: 116 us
  waiting for transfers between devices  58.3 us (50%)
  starting transfers between devices  34.6 us (30%)
  other arithmetic  8.79 us (8%)
  matrix products  7.28 us (6%)
  local copies, waits for them, and re-layouts  3.37 us (3%)
  Pallas kernels  3.12 us (3%)
    all_to_all x1, waiting for transfers between devices, local(): received = lax.all_to_all(by_owner, 'dp', 0, 0, tiled=True)  47.4 us
    ppermute x3, starting transfers between devices, gather_blocks(): from_left[step] = lax.ppermute(from_left[step - 1], 'dp', rightward)  10 us
    ppermute x5, waiting for transfers between devices, butterfly_sum(): x = x + lax.ppermute(x, axis, [(i, i ^ step) for i in range(size)])  8.92 us
    ppermute x1, starting transfers between devices, gather_blocks(): near_left[0] = lax.ppermute(mine, 'dp', partner)  7.05 us
    all_to_all x1, starting transfers between devices, local(): received = lax.all_to_all(by_owner, 'dp', 0, 0, tiled=True)  6.51 us
    ppermute x3, starting transfers between devices, gather_blocks(): from_right[step] = lax.ppermute(from_right[step - 1], 'dp', leftward)  3.88 us
    ppermute x5, starting transfers between devices, butterfly_sum(): x = x + lax.ppermute(x, axis, [(i, i ^ step) for i in range(size)])  3.52 us
    ppermute x3, starting transfers between devices, gather_blocks(): near_right[step] = lax.ppermute(from_right[step], 'dp', partner)  3.49 us
  transfers between devices with their start and end apart: 19, of which 7 were waited for; matrix products, arithmetic and copies ran while one was open for 7% of the time, Pallas kernels for 0%

profile of v5, /device:TPU:1, one launch (start us, length us, event | category | flops | bytes accessed | tf_op | source)
XLA Modules:
  0.0 116.5 jit_solution(6578414710872847812)
XLA Ops:
  3.5 1.6 %broadcast_select_fusion = bf16[8,2,256,256]{3,2,1,0:T(8,128)(2,1)} fusion(bf16[8,2,256,256]{3,2,1,0:T(8,128)(2,1)S(1)} %bitcast.55, pred[8,2]{1,0:T(8,128)(4,1)S(1)} %copy.36), kind=kLoop, calls=%fused_computation.2 | loop fusion | flops 1048576 | bytes 4194320 | tf_op jit(solution)/shard_map/jit(_take)/select_n | solution.py:119
  5.1 6.5 %all-to-all-start = ((bf16[8,2,256,256]{3,2,1,0:T(8,128)(2,1)}), bf16[8,2,256,256]{3,2,1,0:T(8,128)(2,1)}, u32[]{:S(2)}, u32[]{:S(2)}) async-start(bf16[8,2,256,256]{3,2,1,0:T(8,128)(2,1)} %broadcast_select_fusion), calls=%async_computation | async-start | bytes 4194304 | tf_op jit(solution)/shard_map/all_to_all | solution.py:122
  12.5 47.4 %all-to-all-done = bf16[8,2,256,256]{3,2,1,0:T(8,128)(2,1)} async-done(((bf16[8,2,256,256]{3,2,1,0:T(8,128)(2,1)}), bf16[8,2,256,256]{3,2,1,0:T(8,128)(2,1)}, u32[]{:S(2)}, u32[]{:S(2)}) %all-to-all-start) | async-done | bytes 2097184 | tf_op jit(solution)/shard_map/all_to_all | solution.py:122
  59.9 1.9 %convert_reduce_fusion = f32[2,256,256]{2,1,0:T(8,128)S(1)} fusion(bf16[8,2,256,256]{3,2,1,0:T(8,128)(2,1)} %all-to-all-done), kind=kLoop, calls=%fused_computation.1 | loop fusion | flops 1966080 | bytes 2621440 | tf_op jit(solution)/shard_map/reduce_sum | solution.py:123
  62.3 1.6 %multiply_reduce_fusion = (f32[2]{0:T(128)S(1)}, f32[2,256,256]{2,1,0:T(8,128)S(1)}) fusion(bf16[1,1,2,256,256]{4,3,2,1,0:T(8,128)(2,1)S(1)} %copy-done.4, f32[2,256,256]{2,1,0:T(8,128)S(1)} %convert_reduce_fusion, bf16[1,1,2,256,256]{4,3,2,1,0:T(8,128)(2,1)} %param.14, f32[2]{0:T(128)S(1)} %convert_element_type.35), kind=kOutput, calls=%fused_computation.26 | convolution fusion | flops 134873088 | bytes 1572880 | tf_op jit(solution)/shard_map/sij,sjk->sik/dot_general | solution.py:148
  65.9 2.4 %collective-permute-done.1 = f32[2,9]{1,0:T(2,128)S(1)} collective-permute-done((f32[2,9]{1,0:T(2,128)S(1)}, f32[2,9]{1,0:T(2,128)S(1)}, u32[]{:S(2)}, u32[]{:S(2)}) %collective-permute-start.1) | collective-permute-done | bytes 104 | tf_op jit(solution)/shard_map/ppermute | solution.py:20
  68.4 3.3 %collective-permute-done.2 = f32[2,9]{1,0:T(2,128)S(1)} collective-permute-done((f32[2,9]{1,0:T(2,128)S(1)}, f32[2,9]{1,0:T(2,128)S(1)}, u32[]{:S(2)}, u32[]{:S(2)}) %collective-permute-start.2) | collective-permute-done | bytes 104 | tf_op jit(solution)/shard_map/ppermute | solution.py:20
  71.7 1.2 %collective-permute-start.3 = (f32[2,9]{1,0:T(2,128)S(1)}, f32[2,9]{1,0:T(2,128)S(1)}, u32[]{:S(2)}, u32[]{:S(2)}) collective-permute-start(f32[2,9]{1,0:T(2,128)S(1)} %add.110), channel_id=1, source_target_pairs={{0,1},{1,0},{2,3},{3,2},{4,5},{5,4},{6,7},{7,6},{8,9},{9,8},{10,11... | collective-permute-start | bytes 224 | tf_op jit(solution)/shard_map/ppermute | solution.py:20
  72.9 1.2 %collective-permute-done.3 = f32[2,9]{1,0:T(2,128)S(1)} collective-permute-done((f32[2,9]{1,0:T(2,128)S(1)}, f32[2,9]{1,0:T(2,128)S(1)}, u32[]{:S(2)}, u32[]{:S(2)}) %collective-permute-start.3) | collective-permute-done | bytes 104 | tf_op jit(solution)/shard_map/ppermute | solution.py:20
  74.1 1.2 %collective-permute-start.4 = (f32[2,9]{1,0:T(2,128)S(1)}, f32[2,9]{1,0:T(2,128)S(1)}, u32[]{:S(2)}, u32[]{:S(2)}) collective-permute-start(f32[2,9]{1,0:T(2,128)S(1)} %add.111), channel_id=1, source_target_pairs={{0,2},{1,3},{2,0},{3,1},{4,6},{5,7},{6,4},{7,5},{8,10},{9,11},{10,... | collective-permute-start | bytes 224 | tf_op jit(solution)/shard_map/ppermute | solution.py:20
  75.3 1.2 %collective-permute-done.4 = f32[2,9]{1,0:T(2,128)S(1)} collective-permute-done((f32[2,9]{1,0:T(2,128)S(1)}, f32[2,9]{1,0:T(2,128)S(1)}, u32[]{:S(2)}, u32[]{:S(2)}) %collective-permute-start.4) | collective-permute-done | bytes 104 | tf_op jit(solution)/shard_map/ppermute | solution.py:20
  77.7 1.9 %collective-permute-start.5 = (bf16[2,256,256]{2,1,0:T(8,128)(2,1)S(1)}, bf16[2,256,256]{2,1,0:T(8,128)(2,1)S(1)}, u32[]{:S(2)}, u32[]{:S(2)}) collective-permute-start(bf16[2,256,256]{2,1,0:T(8,128)(2,1)S(1)} %get-tuple-element.7.refs_3_), channel_id=1, source_target_pairs={{0,8},{4,12},{8,16},{12,20},{16,24},{20,28},{1,9},{5,13},{9,17},{1... | collective-permute-start | bytes 786440 | tf_op jit(solution)/shard_map/ppermute | solution.py:44
  79.6 1.3 %collective-permute-start.8 = (bf16[2,256,256]{2,1,0:T(8,128)(2,1)S(1)}, bf16[2,256,256]{2,1,0:T(8,128)(2,1)S(1)}, u32[]{:S(2)}, u32[]{:S(2)}) collective-permute-start(bf16[2,256,256]{2,1,0:T(8,128)(2,1)S(1)} %get-tuple-element.7.refs_3_), channel_id=1, source_target_pairs={{8,0},{12,4},{16,8},{20,12},{24,16},{28,20},{9,1},{13,5},{17,9},{2... | collective-permute-start | bytes 786440 | tf_op jit(solution)/shard_map/ppermute | solution.py:45
  80.9 2.0 %collective-permute-done.5.refs_2_ = bf16[2,256,256]{2,1,0:T(8,128)(2,1)S(1)} collective-permute-done((bf16[2,256,256]{2,1,0:T(8,128)(2,1)S(1)}, bf16[2,256,256]{2,1,0:T(8,128)(2,1)S(1)}, u32[]{:S(2)}, u32[]{:S(2)}) %collective-permute-start.5) | collective-permute-done | bytes 262176 | tf_op jit(solution)/shard_map/ppermute | solution.py:44
  82.9 3.8 %collective-permute-start.6 = (bf16[2,256,256]{2,1,0:T(8,128)(2,1)S(1)}, bf16[2,256,256]{2,1,0:T(8,128)(2,1)S(1)}, u32[]{:S(2)}, u32[]{:S(2)}) collective-permute-start(bf16[2,256,256]{2,1,0:T(8,128)(2,1)S(1)} %collective-permute-done.5.refs_2_), channel_id=1, source_target_pairs={{0,8},{4,12},{8,16},{12,20},{16,24},{20,28},{1,9},{5,13},{9,17},{1... | collective-permute-start | bytes 786440 | tf_op jit(solution)/shard_map/ppermute | solution.py:44
  86.7 1.3 %collective-permute-start.9 = (bf16[2,256,256]{2,1,0:T(8,128)(2,1)S(1)}, bf16[2,256,256]{2,1,0:T(8,128)(2,1)S(1)}, u32[]{:S(2)}, u32[]{:S(2)}) collective-permute-start(bf16[2,256,256]{2,1,0:T(8,128)(2,1)S(1)} %collective-permute-done.8.refs_4_), channel_id=1, source_target_pairs={{8,0},{12,4},{16,8},{20,12},{24,16},{28,20},{9,1},{13,5},{17,9},{2... | collective-permute-start | bytes 786440 | tf_op jit(solution)/shard_map/ppermute | solution.py:45
  88.7 7.1 %collective-permute-start.14 = (bf16[2,256,256]{2,1,0:T(8,128)(2,1)S(1)}, bf16[2,256,256]{2,1,0:T(8,128)(2,1)S(1)}, u32[]{:S(2)}, u32[]{:S(2)}) collective-permute-start(bf16[2,256,256]{2,1,0:T(8,128)(2,1)S(1)} %get-tuple-element.7.refs_3_), channel_id=1, source_target_pairs={{0,4},{4,0},{8,12},{12,8},{16,20},{20,16},{24,28},{28,24},{1,5},{5... | collective-permute-start | bytes 786440 | tf_op jit(solution)/shard_map/ppermute | solution.py:41
  95.8 4.3 %collective-permute-start.7 = (bf16[2,256,256]{2,1,0:T(8,128)(2,1)S(1)}, bf16[2,256,256]{2,1,0:T(8,128)(2,1)S(1)}, u32[]{:S(2)}, u32[]{:S(2)}) collective-permute-start(bf16[2,256,256]{2,1,0:T(8,128)(2,1)S(1)} %collective-permute-done.6.refs_1_), channel_id=1, source_target_pairs={{0,8},{4,12},{8,16},{12,20},{16,24},{20,28},{1,9},{5,13},{9,17},{1... | collective-permute-start | bytes 786440 | tf_op jit(solution)/shard_map/ppermute | solution.py:44
  100.1 1.3 %collective-permute-start.10 = (bf16[2,256,256]{2,1,0:T(8,128)(2,1)S(1)}, bf16[2,256,256]{2,1,0:T(8,128)(2,1)S(1)}, u32[]{:S(2)}, u32[]{:S(2)}) collective-permute-start(bf16[2,256,256]{2,1,0:T(8,128)(2,1)S(1)} %collective-permute-done.9.refs_5_), channel_id=1, source_target_pairs={{8,0},{12,4},{16,8},{20,12},{24,16},{28,20},{9,1},{13,5},{17,9},{2... | collective-permute-start | bytes 786440 | tf_op jit(solution)/shard_map/ppermute | solution.py:45
  101.4 3.0 %fusion.2 = f32[1,1,2,256,256]{4,3,2,1,0:T(8,128)} fusion(f32[1,1,2,256,256]{4,3,2,1,0:T(8,128)} %param.13, f32[2,256,256]{2,1,0:T(8,128)S(1)} %convert_reduce_fusion, f32[2]{0:T(128)S(1)} %convert_element_type.35, pred[2]{0:T(512)(128)(4,1)S(1)} %dynamic-slice_reduce_fusion), kind=kOutput, calls=%fused_computation.6 | convolution fusion | flops 403308544 | bytes 1572874 | tf_op jit(solution)/shard_map/sji,sjk->sik/dot_general | solution.py:141
  104.4 2.7 %fusion.5 = f32[1,1,2,256,256]{4,3,2,1,0:T(8,128)} fusion(f32[1,1,2,256,256]{4,3,2,1,0:T(8,128)} %param.12, f32[2,256,256]{2,1,0:T(8,128)S(1)} %convert_reduce_fusion, f32[2]{0:T(128)S(1)} %convert_element_type.35, pred[2]{0:T(512)(128)(4,1)S(1)} %dynamic-slice_reduce_fusion), kind=kOutput, calls=%fused_computation.10 | convolution fusion | flops 403308544 | bytes 1572874 | tf_op jit(solution)/shard_map/sij,skj->sik/dot_general | solution.py:138
  107.1 1.9 %collective-permute-start.15 = (bf16[2,256,256]{2,1,0:T(8,128)(2,1)S(1)}, bf16[2,256,256]{2,1,0:T(8,128)(2,1)S(1)}, u32[]{:S(2)}, u32[]{:S(2)}) collective-permute-start(bf16[2,256,256]{2,1,0:T(8,128)(2,1)S(1)} %collective-permute-done.8.refs_4_), channel_id=1, source_target_pairs={{0,4},{4,0},{8,12},{12,8},{16,20},{20,16},{24,28},{28,24},{1,5},{5... | collective-permute-start | bytes 786440 | tf_op jit(solution)/shard_map/ppermute | solution.py:47
  109.6 1.1 collective-permute-start.17
  113.3 3.1 %shard_map.128 = bf16[8,256,256]{2,1,0:T(8,128)(2,1)} custom-call(s32[8,2]{1,0:T(8,128)} %copy.41.table_ref, bf16[2,256,256]{2,1,0:T(8,128)(2,1)} %copy-done.11, bf16[2,256,256]{2,1,0:T(8,128)(2,1)} %copy-done.7, bf16[2,256,256]{2,1,0:T(8,128)(2,1)} %copy-done.5, bf16[2,256,256]{2,1,0:T(8,128)(2,1)} %copy-done.2, bf16[2,256,256]{2,1,0:T(8,128)(2,1)} %copy-done.6, ...), custom_call_target="tpu_custom_call" | custom-call | tf_op jit(solution)/shard_map/pallas_call | solution.py:79
  (93 shorter events, 11.2 us)
Async XLA Ops:
  5.1 54.8 %all-to-all-start = ((bf16[8,2,256,256]{3,2,1,0:T(8,128)(2,1)}), bf16[8,2,256,256]{3,2,1,0:T(8,128)(2,1)}, u32[]{:S(2)}, u32[]{:S(2)}) async-start(bf16[8,2,256,256]{3,2,1,0:T(8,128)(2,1)} %broadcast_select_fusion), calls=%async_computation | async-start | bytes 4194304 | tf_op jit(solution)/shard_map/all_to_all | solution.py:122
  11.6 50.2 %copy-start.1 = (f32[1,1,2,256,256]{4,3,2,1,0:T(8,128)S(1)}, f32[1,1,2,256,256]{4,3,2,1,0:T(8,128)}, u32[]{:S(2)}) copy-start(f32[1,1,2,256,256]{4,3,2,1,0:T(8,128)} %param.16) | copy-start | bytes 1572868
  11.6 50.7 %copy-start.4 = (bf16[1,1,2,256,256]{4,3,2,1,0:T(8,128)(2,1)S(1)}, bf16[1,1,2,256,256]{4,3,2,1,0:T(8,128)(2,1)}, u32[]{:S(2)}) copy-start(bf16[1,1,2,256,256]{4,3,2,1,0:T(8,128)(2,1)} %param.15) | copy-start | bytes 786436
  12.5 64.2 %copy-start.3 = (f32[1,1,2,256,256]{4,3,2,1,0:T(8,128)S(1)}, f32[1,1,2,256,256]{4,3,2,1,0:T(8,128)}, u32[]{:S(2)}) copy-start(f32[1,1,2,256,256]{4,3,2,1,0:T(8,128)} %param.17) | copy-start | bytes 1572868
  64.0 1.8 %collective-permute-start = (f32[2,9]{1,0:T(2,128)S(1)}, f32[2,9]{1,0:T(2,128)S(1)}, u32[]{:S(2)}, u32[]{:S(2)}) collective-permute-start(f32[2,9]{1,0:T(2,128)S(1)} %pad_maximum_fusion), channel_id=1, source_target_pairs={{0,4},{4,0},{8,12},{12,8},{16,20},{20,16},{24,28},{28,24},{1,5},{5... | collective-permute-start | bytes 224 | tf_op jit(solution)/shard_map/ppermute | solution.py:20
  65.8 2.5 %collective-permute-start.1 = (f32[2,9]{1,0:T(2,128)S(1)}, f32[2,9]{1,0:T(2,128)S(1)}, u32[]{:S(2)}, u32[]{:S(2)}) collective-permute-start(f32[2,9]{1,0:T(2,128)S(1)} %fusion.31), channel_id=1, source_target_pairs={{0,8},{4,12},{8,0},{12,4},{16,24},{20,28},{24,16},{28,20},{1,9},{5... | collective-permute-start | bytes 224 | tf_op jit(solution)/shard_map/ppermute | solution.py:20
  68.3 3.4 %collective-permute-start.2 = (f32[2,9]{1,0:T(2,128)S(1)}, f32[2,9]{1,0:T(2,128)S(1)}, u32[]{:S(2)}, u32[]{:S(2)}) collective-permute-start(f32[2,9]{1,0:T(2,128)S(1)} %fusion.36), channel_id=1, source_target_pairs={{0,16},{4,20},{8,24},{12,28},{16,0},{20,4},{24,8},{28,12},{1,17},{... | collective-permute-start | bytes 224 | tf_op jit(solution)/shard_map/ppermute | solution.py:20
  71.7 2.4 %collective-permute-start.3 = (f32[2,9]{1,0:T(2,128)S(1)}, f32[2,9]{1,0:T(2,128)S(1)}, u32[]{:S(2)}, u32[]{:S(2)}) collective-permute-start(f32[2,9]{1,0:T(2,128)S(1)} %add.110), channel_id=1, source_target_pairs={{0,1},{1,0},{2,3},{3,2},{4,5},{5,4},{6,7},{7,6},{8,9},{9,8},{10,11... | collective-permute-start | bytes 224 | tf_op jit(solution)/shard_map/ppermute | solution.py:20
  74.1 2.4 %collective-permute-start.4 = (f32[2,9]{1,0:T(2,128)S(1)}, f32[2,9]{1,0:T(2,128)S(1)}, u32[]{:S(2)}, u32[]{:S(2)}) collective-permute-start(f32[2,9]{1,0:T(2,128)S(1)} %add.111), channel_id=1, source_target_pairs={{0,2},{1,3},{2,0},{3,1},{4,6},{5,7},{6,4},{7,5},{8,10},{9,11},{10,... | collective-permute-start | bytes 224 | tf_op jit(solution)/shard_map/ppermute | solution.py:20
  77.7 34.0 %copy-start.2 = (bf16[2,256,256]{2,1,0:T(8,128)(2,1)}, bf16[2,256,256]{2,1,0:T(8,128)(2,1)S(1)}, u32[]{:S(2)}) copy-start(bf16[2,256,256]{2,1,0:T(8,128)(2,1)S(1)} %get-tuple-element.7.refs_3_) | copy-start | bytes 786436
  77.7 5.2 %collective-permute-start.5 = (bf16[2,256,256]{2,1,0:T(8,128)(2,1)S(1)}, bf16[2,256,256]{2,1,0:T(8,128)(2,1)S(1)}, u32[]{:S(2)}, u32[]{:S(2)}) collective-permute-start(bf16[2,256,256]{2,1,0:T(8,128)(2,1)S(1)} %get-tuple-element.7.refs_3_), channel_id=1, source_target_pairs={{0,8},{4,12},{8,16},{12,20},{16,24},{20,28},{1,9},{5,13},{9,17},{1... | collective-permute-start | bytes 786440 | tf_op jit(solution)/shard_map/ppermute | solution.py:44
  79.6 7.1 %collective-permute-start.8 = (bf16[2,256,256]{2,1,0:T(8,128)(2,1)S(1)}, bf16[2,256,256]{2,1,0:T(8,128)(2,1)S(1)}, u32[]{:S(2)}, u32[]{:S(2)}) collective-permute-start(bf16[2,256,256]{2,1,0:T(8,128)(2,1)S(1)} %get-tuple-element.7.refs_3_), channel_id=1, source_target_pairs={{8,0},{12,4},{16,8},{20,12},{24,16},{28,20},{9,1},{13,5},{17,9},{2... | collective-permute-start | bytes 786440 | tf_op jit(solution)/shard_map/ppermute | solution.py:45
  82.9 28.8 %copy-start.5 = (bf16[2,256,256]{2,1,0:T(8,128)(2,1)}, bf16[2,256,256]{2,1,0:T(8,128)(2,1)S(1)}, u32[]{:S(2)}) copy-start(bf16[2,256,256]{2,1,0:T(8,128)(2,1)S(1)} %collective-permute-done.5.refs_2_) | copy-start | bytes 786436
  82.9 12.9 %collective-permute-start.6 = (bf16[2,256,256]{2,1,0:T(8,128)(2,1)S(1)}, bf16[2,256,256]{2,1,0:T(8,128)(2,1)S(1)}, u32[]{:S(2)}, u32[]{:S(2)}) collective-permute-start(bf16[2,256,256]{2,1,0:T(8,128)(2,1)S(1)} %collective-permute-done.5.refs_2_), channel_id=1, source_target_pairs={{0,8},{4,12},{8,16},{12,20},{16,24},{20,28},{1,9},{5,13},{9,17},{1... | collective-permute-start | bytes 786440 | tf_op jit(solution)/shard_map/ppermute | solution.py:44
  86.7 13.4 %collective-permute-start.9 = (bf16[2,256,256]{2,1,0:T(8,128)(2,1)S(1)}, bf16[2,256,256]{2,1,0:T(8,128)(2,1)S(1)}, u32[]{:S(2)}, u32[]{:S(2)}) collective-permute-start(bf16[2,256,256]{2,1,0:T(8,128)(2,1)S(1)} %collective-permute-done.8.refs_4_), channel_id=1, source_target_pairs={{8,0},{12,4},{16,8},{20,12},{24,16},{28,20},{9,1},{13,5},{17,9},{2... | collective-permute-start | bytes 786440 | tf_op jit(solution)/shard_map/ppermute | solution.py:45
  88.7 20.2 %collective-permute-start.14 = (bf16[2,256,256]{2,1,0:T(8,128)(2,1)S(1)}, bf16[2,256,256]{2,1,0:T(8,128)(2,1)S(1)}, u32[]{:S(2)}, u32[]{:S(2)}) collective-permute-start(bf16[2,256,256]{2,1,0:T(8,128)(2,1)S(1)} %get-tuple-element.7.refs_3_), channel_id=1, source_target_pairs={{0,4},{4,0},{8,12},{12,8},{16,20},{20,16},{24,28},{28,24},{1,5},{5... | collective-permute-start | bytes 786440 | tf_op jit(solution)/shard_map/ppermute | solution.py:41
  95.8 13.3 %collective-permute-start.13 = (bf16[2,256,256]{2,1,0:T(8,128)(2,1)S(1)}, bf16[2,256,256]{2,1,0:T(8,128)(2,1)S(1)}, u32[]{:S(2)}, u32[]{:S(2)}) collective-permute-start(bf16[2,256,256]{2,1,0:T(8,128)(2,1)S(1)} %collective-permute-done.5.refs_2_), channel_id=1, source_target_pairs={{0,4},{4,0},{8,12},{12,8},{16,20},{20,16},{24,28},{28,24},{1,5},{5... | collective-permute-start | bytes 786440 | tf_op jit(solution)/shard_map/ppermute | solution.py:46
  95.8 13.7 %collective-permute-start.7 = (bf16[2,256,256]{2,1,0:T(8,128)(2,1)S(1)}, bf16[2,256,256]{2,1,0:T(8,128)(2,1)S(1)}, u32[]{:S(2)}, u32[]{:S(2)}) collective-permute-start(bf16[2,256,256]{2,1,0:T(8,128)(2,1)S(1)} %collective-permute-done.6.refs_1_), channel_id=1, source_target_pairs={{0,8},{4,12},{8,16},{12,20},{16,24},{20,28},{1,9},{5,13},{9,17},{1... | collective-permute-start | bytes 786440 | tf_op jit(solution)/shard_map/ppermute | solution.py:44
  100.1 9.5 %collective-permute-start.10 = (bf16[2,256,256]{2,1,0:T(8,128)(2,1)S(1)}, bf16[2,256,256]{2,1,0:T(8,128)(2,1)S(1)}, u32[]{:S(2)}, u32[]{:S(2)}) collective-permute-start(bf16[2,256,256]{2,1,0:T(8,128)(2,1)S(1)} %collective-permute-done.9.refs_5_), channel_id=1, source_target_pairs={{8,0},{12,4},{16,8},{20,12},{24,16},{28,20},{9,1},{13,5},{17,9},{2... | collective-permute-start | bytes 786440 | tf_op jit(solution)/shard_map/ppermute | solution.py:45
  107.1 4.7 %collective-permute-start.15 = (bf16[2,256,256]{2,1,0:T(8,128)(2,1)S(1)}, bf16[2,256,256]{2,1,0:T(8,128)(2,1)S(1)}, u32[]{:S(2)}, u32[]{:S(2)}) collective-permute-start(bf16[2,256,256]{2,1,0:T(8,128)(2,1)S(1)} %collective-permute-done.8.refs_4_), channel_id=1, source_target_pairs={{0,4},{4,0},{8,12},{12,8},{16,20},{20,16},{24,28},{28,24},{1,5},{5... | collective-permute-start | bytes 786440 | tf_op jit(solution)/shard_map/ppermute | solution.py:47
  109.0 2.8 %collective-permute-start.12 = (bf16[2,256,256]{2,1,0:T(8,128)(2,1)S(1)}, bf16[2,256,256]{2,1,0:T(8,128)(2,1)S(1)}, u32[]{:S(2)}, u32[]{:S(2)}) collective-permute-start(bf16[2,256,256]{2,1,0:T(8,128)(2,1)S(1)} %collective-permute-done.6.refs_1_), channel_id=1, source_target_pairs={{0,4},{4,0},{8,12},{12,8},{16,20},{20,16},{24,28},{28,24},{1,5},{5... | collective-permute-start | bytes 786440 | tf_op jit(solution)/shard_map/ppermute | solution.py:46
  109.1 2.7 %collective-permute-start.16 = (bf16[2,256,256]{2,1,0:T(8,128)(2,1)S(1)}, bf16[2,256,256]{2,1,0:T(8,128)(2,1)S(1)}, u32[]{:S(2)}, u32[]{:S(2)}) collective-permute-start(bf16[2,256,256]{2,1,0:T(8,128)(2,1)S(1)} %collective-permute-done.9.refs_5_), channel_id=1, source_target_pairs={{0,4},{4,0},{8,12},{12,8},{16,20},{20,16},{24,28},{28,24},{1,5},{5... | collective-permute-start | bytes 786440 | tf_op jit(solution)/shard_map/ppermute | solution.py:47
  109.5 2.3 %collective-permute-start.11 = (bf16[2,256,256]{2,1,0:T(8,128)(2,1)S(1)}, bf16[2,256,256]{2,1,0:T(8,128)(2,1)S(1)}, u32[]{:S(2)}, u32[]{:S(2)}) collective-permute-start(bf16[2,256,256]{2,1,0:T(8,128)(2,1)S(1)} %collective-permute-done.7.refs_0_), channel_id=1, source_target_pairs={{0,4},{4,0},{8,12},{12,8},{16,20},{20,16},{24,28},{28,24},{1,5},{5... | collective-permute-start | bytes 786440 | tf_op jit(solution)/shard_map/ppermute | solution.py:46
  109.6 3.7 %collective-permute-start.17 = (bf16[2,256,256]{2,1,0:T(8,128)(2,1)S(1)}, bf16[2,256,256]{2,1,0:T(8,128)(2,1)}, u32[]{:S(2)}, u32[]{:S(2)}) collective-permute-start(bf16[2,256,256]{2,1,0:T(8,128)(2,1)S(1)} %collective-permute-done.10.refs_6_), channel_id=1, source_target_pairs={{0,4},{4,0},{8,12},{12,8},{16,20},{20,16},{24,28},{28,24},{1,5},{5... | collective-permute-start | bytes 786440 | tf_op jit(solution)/shard_map/ppermute | solution.py:47
  (14 other events, 100.9 us)

commit v6 on v5

--- a/solution.py
+++ b/solution.py
@@ -11,15 +11,14 @@
 NORM_EPS = 1e-06
 
 
-def butterfly_sum(x, axis):
+def spread_sum(x, axis):
     size = lax.axis_size(axis)
-    if size & (size - 1):
-        return lax.psum(x, axis)
-    step = 1
-    while step < size:
-        x = x + lax.ppermute(x, axis, [(i, i ^ step) for i in range(size)])
-        step *= 2
-    return x
+    here = lax.axis_index(axis)
+    received = [x] + [
+        lax.ppermute(x, axis, [(i, (i + shift) % size) for i in range(size)]) for shift in range(1, size)
+    ]
+    by_source = jnp.take(jnp.stack(received), (here - jnp.arange(size)) % size, axis=0)
+    return jnp.sum(by_source, axis=0)
 
 
 def gather_blocks(mine, owner_of, slot_rank, replica):
@@ -149,7 +148,8 @@
         "sij,sjk->sik", inner, root_right[0, 0], preferred_element_type=jnp.float32
     )
     prec_terms = jnp.sum(member * jnp.sum(precond * precond, axis=(1, 2))[:, None], axis=0)
-    norms = butterfly_sum(butterfly_sum(jnp.stack([adam_terms, prec_terms]), "dp"), "shard")
+    norms = spread_sum(spread_sum(jnp.stack([adam_terms, prec_terms]), "dp"), "shard")
+    norms, lnew, rnew = lax.optimization_barrier((norms, lnew, rnew))
     norm_adam = norms[0]
     norm_prec = norms[1]
     scales = jnp.sqrt(norm_adam / (norm_prec + NORM_EPS))

time: 117 us -> 127 us (1.085)
  starting transfers between devices: 34.6 us -> 43.3 us
  other arithmetic: 8.79 us -> 10.9 us
  local copies, waits for them, and re-layouts: 3.37 us -> 5.16 us
  matrix products: 7.28 us -> 5.87 us
    ppermute x5 -> x10, starting transfers between devices: 3.52 us -> 11.2 us  [spread_sum(): lax.ppermute(x, axis, [(i, (i + shift) % size) for i in range(size)])]
    ppermute x1, starting transfers between devices: 7.05 us -> 1.85 us  [gather_blocks(): near_left[0] = lax.ppermute(mine, 'dp', partner)]
    ppermute x3, starting transfers between devices: 10 us -> 14.6 us  [gather_blocks(): from_left[step] = lax.ppermute(from_left[step - 1], 'dp', rightward)]
    ppermute x3, starting transfers between devices: 0.16 us -> 4.39 us  [gather_blocks(): near_left[step] = lax.ppermute(from_left[step], 'dp', partner)]
    ppermute x3, waiting for transfers between devices: 0.01 us -> 3.38 us  [gather_blocks(): from_right[step] = lax.ppermute(from_right[step - 1], 'dp', leftward)]
    ppermute x3, starting transfers between devices: 3.49 us -> 0.86 us  [gather_blocks(): near_right[step] = lax.ppermute(from_right[step], 'dp', partner)]
    ppermute x5 -> x10, waiting for transfers between devices: 8.92 us -> 6.39 us  [spread_sum(): lax.ppermute(x, axis, [(i, (i + shift) % size) for i in range(size)])]
    ppermute x3, waiting for transfers between devices: 1.96 us -> 0.01 us  [gather_blocks(): from_left[step] = lax.ppermute(from_left[step - 1], 'dp', rightward)]
  transfers between devices with their start and end apart: 19 -> 24, of which waited for: 7 -> 8; matrix products, arithmetic and copies ran while one was open for 7% -> 5% of each run, Pallas kernels for 0% -> 0%
where the time goes in v6:
time: 127 us; the launch traced here: 126 us
  waiting for transfers between devices  57.1 us (45%)
  starting transfers between devices  43.3 us (34%)
  other arithmetic  10.9 us (9%)
  matrix products  5.87 us (5%)
  local copies, waits for them, and re-layouts  5.16 us (4%)
  Pallas kernels  3.16 us (2%)
    all_to_all x1, waiting for transfers between devices, local(): received = lax.all_to_all(by_owner, 'dp', 0, 0, tiled=True)  47.3 us
    ppermute x3, starting transfers between devices, gather_blocks(): from_left[step] = lax.ppermute(from_left[step - 1], 'dp', rightward)  14.6 us
    ppermute x10, starting transfers between devices, spread_sum(): lax.ppermute(x, axis, [(i, (i + shift) % size) for i in range(size)])  11.2 us
    all_to_all x1, starting transfers between devices, local(): received = lax.all_to_all(by_owner, 'dp', 0, 0, tiled=True)  6.51 us
    ppermute x10, waiting for transfers between devices, spread_sum(): lax.ppermute(x, axis, [(i, (i + shift) % size) for i in range(size)])  6.39 us
    ppermute x3, starting transfers between devices, gather_blocks(): near_left[step] = lax.ppermute(from_left[step], 'dp', partner)  4.39 us
    ppermute x3, starting transfers between devices, gather_blocks(): from_right[step] = lax.ppermute(from_right[step - 1], 'dp', leftward)  3.84 us
    ppermute x3, waiting for transfers between devices, gather_blocks(): from_right[step] = lax.ppermute(from_right[step - 1], 'dp', leftward)  3.38 us
  transfers between devices with their start and end apart: 24, of which 8 were waited for; matrix products, arithmetic and copies ran while one was open for 5% of the time, Pallas kernels for 0%

profile of v6, /device:TPU:1, one launch (start us, length us, event | category | flops | bytes accessed | tf_op | source)
XLA Modules:
  0.0 126.4 jit_solution(5690740921074400359)
XLA Ops:
  3.5 1.6 %broadcast_select_fusion = bf16[8,2,256,256]{3,2,1,0:T(8,128)(2,1)} fusion(bf16[8,2,256,256]{3,2,1,0:T(8,128)(2,1)S(1)} %bitcast.83, pred[8,2]{1,0:T(8,128)(4,1)S(1)} %copy.36), kind=kLoop, calls=%fused_computation.4 | loop fusion | flops 1048576 | bytes 4194320 | tf_op jit(solution)/shard_map/jit(_take)/select_n | solution.py:118
  5.1 6.5 %all-to-all-start = ((bf16[8,2,256,256]{3,2,1,0:T(8,128)(2,1)}), bf16[8,2,256,256]{3,2,1,0:T(8,128)(2,1)}, u32[]{:S(2)}, u32[]{:S(2)}) async-start(bf16[8,2,256,256]{3,2,1,0:T(8,128)(2,1)} %broadcast_select_fusion), calls=%async_computation | async-start | bytes 4194304 | tf_op jit(solution)/shard_map/all_to_all | solution.py:121
  12.6 47.3 %all-to-all-done = bf16[8,2,256,256]{3,2,1,0:T(8,128)(2,1)} async-done(((bf16[8,2,256,256]{3,2,1,0:T(8,128)(2,1)}), bf16[8,2,256,256]{3,2,1,0:T(8,128)(2,1)}, u32[]{:S(2)}, u32[]{:S(2)}) %all-to-all-start) | async-done | bytes 2097184 | tf_op jit(solution)/shard_map/all_to_all | solution.py:121
  59.9 1.9 %convert_reduce_fusion = f32[2,256,256]{2,1,0:T(8,128)S(1)} fusion(bf16[8,2,256,256]{3,2,1,0:T(8,128)(2,1)} %all-to-all-done), kind=kLoop, calls=%fused_computation.3 | loop fusion | flops 1966080 | bytes 2621440 | tf_op jit(solution)/shard_map/reduce_sum | solution.py:122
  62.3 2.3 %multiply_reduce_fusion = (f32[2]{0:T(128)S(1)}, f32[2,256,256]{2,1,0:T(8,128)}) fusion(bf16[1,1,2,256,256]{4,3,2,1,0:T(8,128)(2,1)S(1)} %copy-done.5, f32[2,256,256]{2,1,0:T(8,128)S(1)} %convert_reduce_fusion, bf16[1,1,2,256,256]{4,3,2,1,0:T(8,128)(2,1)} %param.14, f32[2]{0:T(128)S(1)} %convert_element_type.35), kind=kOutput, calls=%fused_computation.28 | convolution fusion | flops 134873088 | bytes 1572880 | tf_op jit(solution)/shard_map/sij,sjk->sik/dot_general | solution.py:147
  64.7 1.5 %collective-permute-start.5 = (f32[2,9]{1,0:T(2,128)S(1)}, f32[2,9]{1,0:T(2,128)S(1)}, u32[]{:S(2)}, u32[]{:S(2)}) collective-permute-start(f32[2,9]{1,0:T(2,128)S(1)} %pad_maximum_fusion.1), channel_id=1, source_target_pairs={{0,24},{4,28},{8,0},{12,4},{16,8},{20,12},{24,16},{28,20},{1,25},{... | collective-permute-start | bytes 224 | tf_op jit(solution)/shard_map/ppermute | solution.py:18
  66.6 1.9 %collective-permute-start.3 = (f32[2,9]{1,0:T(2,128)S(1)}, f32[2,9]{1,0:T(2,128)S(1)}, u32[]{:S(2)}, u32[]{:S(2)}) collective-permute-start(f32[2,9]{1,0:T(2,128)S(1)} %pad_maximum_fusion.1), channel_id=1, source_target_pairs={{0,16},{4,20},{8,24},{12,28},{16,0},{20,4},{24,8},{28,12},{1,17},{... | collective-permute-start | bytes 224 | tf_op jit(solution)/shard_map/ppermute | solution.py:18
  69.2 1.6 %fusion.1 = f32[2,256,256]{2,1,0:T(8,128)} fusion(f32[1,1,2,256,256]{4,3,2,1,0:T(8,128)S(1)} %copy-done.3, f32[2,256,256]{2,1,0:T(8,128)S(1)} %convert_reduce_fusion, f32[2]{0:T(128)S(1)} %convert_element_type.35), kind=kOutput, calls=%fused_computation.8 | convolution fusion | flops 403177472 | bytes 1572872 | tf_op jit(solution)/shard_map/sij,skj->sik/dot_general | solution.py:137
  70.8 1.9 %fusion = f32[2,256,256]{2,1,0:T(8,128)} fusion(f32[1,1,2,256,256]{4,3,2,1,0:T(8,128)S(1)} %copy-done.2, f32[2,256,256]{2,1,0:T(8,128)S(1)} %convert_reduce_fusion, f32[2]{0:T(128)S(1)} %convert_element_type.35), kind=kOutput, calls=%fused_computation.6 | convolution fusion | flops 403177472 | bytes 1572872 | tf_op jit(solution)/shard_map/sji,sjk->sik/dot_general | solution.py:140
  73.0 1.6 %collective-permute-start.1 = (f32[2,9]{1,0:T(2,128)S(1)}, f32[2,9]{1,0:T(2,128)S(1)}, u32[]{:S(2)}, u32[]{:S(2)}) collective-permute-start(f32[2,9]{1,0:T(2,128)S(1)} %pad_maximum_fusion.1), channel_id=1, source_target_pairs={{0,8},{4,12},{8,16},{12,20},{16,24},{20,28},{24,0},{28,4},{1,9},{5... | collective-permute-start | bytes 224 | tf_op jit(solution)/shard_map/ppermute | solution.py:18
  74.6 2.6 %collective-permute-done.1 = f32[2,9]{1,0:T(2,128)S(1)} collective-permute-done((f32[2,9]{1,0:T(2,128)S(1)}, f32[2,9]{1,0:T(2,128)S(1)}, u32[]{:S(2)}, u32[]{:S(2)}) %collective-permute-start.1) | collective-permute-done | bytes 104 | tf_op jit(solution)/shard_map/ppermute | solution.py:18
  77.2 2.2 %collective-permute-start.6 = (f32[2,9]{1,0:T(2,128)S(1)}, f32[2,9]{1,0:T(2,128)S(1)}, u32[]{:S(2)}, u32[]{:S(2)}) collective-permute-start(f32[2,9]{1,0:T(2,128)S(1)} %pad_maximum_fusion.1), channel_id=1, source_target_pairs={{0,28},{4,0},{8,4},{12,8},{16,12},{20,16},{24,20},{28,24},{1,29},{... | collective-permute-start | bytes 224 | tf_op jit(solution)/shard_map/ppermute | solution.py:18
  80.9 2.2 %collective-permute-start.9 = (f32[2,9]{1,0:T(2,128)S(1)}, f32[2,9]{1,0:T(2,128)S(1)}, u32[]{:S(2)}, u32[]{:S(2)}) collective-permute-start(f32[2,9]{1,0:T(2,128)S(1)} %select_reduce_fusion), channel_id=1, source_target_pairs={{0,3},{1,0},{2,1},{3,2},{4,7},{5,4},{6,5},{7,6},{8,11},{9,8},{10,9... | collective-permute-start | bytes 224 | tf_op jit(solution)/shard_map/ppermute | solution.py:18
  83.8 1.7 %collective-permute-done.8 = f32[2,9]{1,0:T(2,128)S(1)} collective-permute-done((f32[2,9]{1,0:T(2,128)S(1)}, f32[2,9]{1,0:T(2,128)S(1)}, u32[]{:S(2)}, u32[]{:S(2)}) %collective-permute-start.8) | collective-permute-done | bytes 104 | tf_op jit(solution)/shard_map/ppermute | solution.py:18
  87.5 2.8 %fusion.35 = (bf16[2,256,256]{2,1,0:T(8,128)(2,1)S(1)}, f32[1,1,2,256,256]{4,3,2,1,0:T(8,128)}, f32[1,1,2,256,256]{4,3,2,1,0:T(8,128)}, f32[1,1,2,256,256]{4,3,2,1,0:T(8,128)}) fusion(f32[2,256,256]{2,1,0:T(8,128)} %get-tuple-element.20, f32[2]{0:T(128)S(1)} %broadcast_multiply_fusion, f32[1,1,2,256,256]{4,3,2,1,0:T(8,128)} %param.17, ...), kind=kLoop, calls=%fused_computation.111 | loop fusion | flops 786432 | bytes 4980746 | tf_op jit(solution)/shard_map/convert_element_type | solution.py:163
  90.3 1.3 %collective-permute-start.13 = (bf16[2,256,256]{2,1,0:T(8,128)(2,1)S(1)}, bf16[2,256,256]{2,1,0:T(8,128)(2,1)S(1)}, u32[]{:S(2)}, u32[]{:S(2)}) collective-permute-start(bf16[2,256,256]{2,1,0:T(8,128)(2,1)S(1)} %get-tuple-element.13.refs_3_), channel_id=1, source_target_pairs={{8,0},{12,4},{16,8},{20,12},{24,16},{28,20},{9,1},{13,5},{17,9},{2... | collective-permute-start | bytes 786440 | tf_op jit(solution)/shard_map/ppermute | solution.py:44
  91.6 4.0 %collective-permute-start.10 = (bf16[2,256,256]{2,1,0:T(8,128)(2,1)S(1)}, bf16[2,256,256]{2,1,0:T(8,128)(2,1)S(1)}, u32[]{:S(2)}, u32[]{:S(2)}) collective-permute-start(bf16[2,256,256]{2,1,0:T(8,128)(2,1)S(1)} %get-tuple-element.13.refs_3_), channel_id=1, source_target_pairs={{0,8},{4,12},{8,16},{12,20},{16,24},{20,28},{1,9},{5,13},{9,17},{1... | collective-permute-start | bytes 786440 | tf_op jit(solution)/shard_map/ppermute | solution.py:43
  95.6 2.2 %collective-permute-done.13.refs_4_ = bf16[2,256,256]{2,1,0:T(8,128)(2,1)S(1)} collective-permute-done((bf16[2,256,256]{2,1,0:T(8,128)(2,1)S(1)}, bf16[2,256,256]{2,1,0:T(8,128)(2,1)S(1)}, u32[]{:S(2)}, u32[]{:S(2)}) %collective-permute-start.13) | collective-permute-done | bytes 262176 | tf_op jit(solution)/shard_map/ppermute | solution.py:44
  97.9 1.3 %collective-permute-start.14 = (bf16[2,256,256]{2,1,0:T(8,128)(2,1)S(1)}, bf16[2,256,256]{2,1,0:T(8,128)(2,1)S(1)}, u32[]{:S(2)}, u32[]{:S(2)}) collective-permute-start(bf16[2,256,256]{2,1,0:T(8,128)(2,1)S(1)} %collective-permute-done.13.refs_4_), channel_id=1, source_target_pairs={{8,0},{12,4},{16,8},{20,12},{24,16},{28,20},{9,1},{13,5},{17,9},{2... | collective-permute-start | bytes 786440 | tf_op jit(solution)/shard_map/ppermute | solution.py:44
  99.2 5.9 %collective-permute-start.11 = (bf16[2,256,256]{2,1,0:T(8,128)(2,1)S(1)}, bf16[2,256,256]{2,1,0:T(8,128)(2,1)S(1)}, u32[]{:S(2)}, u32[]{:S(2)}) collective-permute-start(bf16[2,256,256]{2,1,0:T(8,128)(2,1)S(1)} %collective-permute-done.10.refs_2_), channel_id=1, source_target_pairs={{0,8},{4,12},{8,16},{12,20},{16,24},{20,28},{1,9},{5,13},{9,17},{1... | collective-permute-start | bytes 786440 | tf_op jit(solution)/shard_map/ppermute | solution.py:43
  105.1 1.9 %collective-permute-start.19 = (bf16[2,256,256]{2,1,0:T(8,128)(2,1)S(1)}, bf16[2,256,256]{2,1,0:T(8,128)(2,1)}, u32[]{:S(2)}, u32[]{:S(2)}) collective-permute-start(bf16[2,256,256]{2,1,0:T(8,128)(2,1)S(1)} %get-tuple-element.13.refs_3_), channel_id=1, source_target_pairs={{0,4},{4,0},{8,12},{12,8},{16,20},{20,16},{24,28},{28,24},{1,5},{5... | collective-permute-start | bytes 786440 | tf_op jit(solution)/shard_map/ppermute | solution.py:40
  109.5 4.7 %collective-permute-start.12 = (bf16[2,256,256]{2,1,0:T(8,128)(2,1)S(1)}, bf16[2,256,256]{2,1,0:T(8,128)(2,1)}, u32[]{:S(2)}, u32[]{:S(2)}) collective-permute-start(bf16[2,256,256]{2,1,0:T(8,128)(2,1)S(1)} %collective-permute-done.11.refs_1_), channel_id=1, source_target_pairs={{0,8},{4,12},{8,16},{12,20},{16,24},{20,28},{1,9},{5,13},{9,17},{1... | collective-permute-start | bytes 786440 | tf_op jit(solution)/shard_map/ppermute | solution.py:43
  114.9 2.7 %collective-permute-start.18 = (bf16[2,256,256]{2,1,0:T(8,128)(2,1)S(1)}, bf16[2,256,256]{2,1,0:T(8,128)(2,1)S(1)}, u32[]{:S(2)}, u32[]{:S(2)}) collective-permute-start(bf16[2,256,256]{2,1,0:T(8,128)(2,1)S(1)} %collective-permute-done.10.refs_2_), channel_id=1, source_target_pairs={{0,4},{4,0},{8,12},{12,8},{16,20},{20,16},{24,28},{28,24},{1,5},{5... | collective-permute-start | bytes 786440 | tf_op jit(solution)/shard_map/ppermute | solution.py:45
  123.2 3.2 %shard_map.128 = bf16[8,256,256]{2,1,0:T(8,128)(2,1)} custom-call(s32[8,2]{1,0:T(8,128)} %copy.41.table_ref, bf16[2,256,256]{2,1,0:T(8,128)(2,1)} %collective-permute-done.12.refs_0_, bf16[2,256,256]{2,1,0:T(8,128)(2,1)} %copy-done.9, bf16[2,256,256]{2,1,0:T(8,128)(2,1)} %copy-done.7, bf16[2,256,256]{2,1,0:T(8,128)(2,1)} %copy-done.4, ...), custom_call_target="tpu_custom_call" | custom-call | tf_op jit(solution)/shard_map/pallas_call | solution.py:78
  (111 shorter events, 18.7 us)
Async XLA Ops:
  5.1 54.8 %all-to-all-start = ((bf16[8,2,256,256]{3,2,1,0:T(8,128)(2,1)}), bf16[8,2,256,256]{3,2,1,0:T(8,128)(2,1)}, u32[]{:S(2)}, u32[]{:S(2)}) async-start(bf16[8,2,256,256]{3,2,1,0:T(8,128)(2,1)} %broadcast_select_fusion), calls=%async_computation | async-start | bytes 4194304 | tf_op jit(solution)/shard_map/all_to_all | solution.py:121
  64.7 14.7 %collective-permute-start.5 = (f32[2,9]{1,0:T(2,128)S(1)}, f32[2,9]{1,0:T(2,128)S(1)}, u32[]{:S(2)}, u32[]{:S(2)}) collective-permute-start(f32[2,9]{1,0:T(2,128)S(1)} %pad_maximum_fusion.1), channel_id=1, source_target_pairs={{0,24},{4,28},{8,0},{12,4},{16,8},{20,12},{24,16},{28,20},{1,25},{... | collective-permute-start | bytes 224 | tf_op jit(solution)/shard_map/ppermute | solution.py:18
  66.2 13.2 %collective-permute-start.4 = (f32[2,9]{1,0:T(2,128)S(1)}, f32[2,9]{1,0:T(2,128)S(1)}, u32[]{:S(2)}, u32[]{:S(2)}) collective-permute-start(f32[2,9]{1,0:T(2,128)S(1)} %pad_maximum_fusion.1), channel_id=1, source_target_pairs={{0,20},{4,24},{8,28},{12,0},{16,4},{20,8},{24,12},{28,16},{1,21},{... | collective-permute-start | bytes 224 | tf_op jit(solution)/shard_map/ppermute | solution.py:18
  66.6 12.8 %collective-permute-start.3 = (f32[2,9]{1,0:T(2,128)S(1)}, f32[2,9]{1,0:T(2,128)S(1)}, u32[]{:S(2)}, u32[]{:S(2)}) collective-permute-start(f32[2,9]{1,0:T(2,128)S(1)} %pad_maximum_fusion.1), channel_id=1, source_target_pairs={{0,16},{4,20},{8,24},{12,28},{16,0},{20,4},{24,8},{28,12},{1,17},{... | collective-permute-start | bytes 224 | tf_op jit(solution)/shard_map/ppermute | solution.py:18
  68.5 4.5 %collective-permute-start = (f32[2,9]{1,0:T(2,128)S(1)}, f32[2,9]{1,0:T(2,128)S(1)}, u32[]{:S(2)}, u32[]{:S(2)}) collective-permute-start(f32[2,9]{1,0:T(2,128)S(1)} %pad_maximum_fusion.1), channel_id=1, source_target_pairs={{0,4},{4,8},{8,12},{12,16},{16,20},{20,24},{24,28},{28,0},{1,5},{5... | collective-permute-start | bytes 224 | tf_op jit(solution)/shard_map/ppermute | solution.py:18
  72.7 6.7 %collective-permute-start.2 = (f32[2,9]{1,0:T(2,128)S(1)}, f32[2,9]{1,0:T(2,128)S(1)}, u32[]{:S(2)}, u32[]{:S(2)}) collective-permute-start(f32[2,9]{1,0:T(2,128)S(1)} %pad_maximum_fusion.1), channel_id=1, source_target_pairs={{0,12},{4,16},{8,20},{12,24},{16,28},{20,0},{24,4},{28,8},{1,13},{... | collective-permute-start | bytes 224 | tf_op jit(solution)/shard_map/ppermute | solution.py:18
  73.0 4.2 %collective-permute-start.1 = (f32[2,9]{1,0:T(2,128)S(1)}, f32[2,9]{1,0:T(2,128)S(1)}, u32[]{:S(2)}, u32[]{:S(2)}) collective-permute-start(f32[2,9]{1,0:T(2,128)S(1)} %pad_maximum_fusion.1), channel_id=1, source_target_pairs={{0,8},{4,12},{8,16},{12,20},{16,24},{20,28},{24,0},{28,4},{1,9},{5... | collective-permute-start | bytes 224 | tf_op jit(solution)/shard_map/ppermute | solution.py:18
  77.2 3.0 %collective-permute-start.6 = (f32[2,9]{1,0:T(2,128)S(1)}, f32[2,9]{1,0:T(2,128)S(1)}, u32[]{:S(2)}, u32[]{:S(2)}) collective-permute-start(f32[2,9]{1,0:T(2,128)S(1)} %pad_maximum_fusion.1), channel_id=1, source_target_pairs={{0,28},{4,0},{8,4},{12,8},{16,12},{20,16},{24,20},{28,24},{1,29},{... | collective-permute-start | bytes 224 | tf_op jit(solution)/shard_map/ppermute | solution.py:18
  80.9 2.9 %collective-permute-start.9 = (f32[2,9]{1,0:T(2,128)S(1)}, f32[2,9]{1,0:T(2,128)S(1)}, u32[]{:S(2)}, u32[]{:S(2)}) collective-permute-start(f32[2,9]{1,0:T(2,128)S(1)} %select_reduce_fusion), channel_id=1, source_target_pairs={{0,3},{1,0},{2,1},{3,2},{4,7},{5,4},{6,5},{7,6},{8,11},{9,8},{10,9... | collective-permute-start | bytes 224 | tf_op jit(solution)/shard_map/ppermute | solution.py:18
  83.1 2.4 %collective-permute-start.8 = (f32[2,9]{1,0:T(2,128)S(1)}, f32[2,9]{1,0:T(2,128)S(1)}, u32[]{:S(2)}, u32[]{:S(2)}) collective-permute-start(f32[2,9]{1,0:T(2,128)S(1)} %select_reduce_fusion), channel_id=1, source_target_pairs={{0,2},{1,3},{2,0},{3,1},{4,6},{5,7},{6,4},{7,5},{8,10},{9,11},{10,... | collective-permute-start | bytes 224 | tf_op jit(solution)/shard_map/ppermute | solution.py:18
  83.3 3.3 %collective-permute-start.7 = (f32[2,9]{1,0:T(2,128)S(1)}, f32[2,9]{1,0:T(2,128)S(1)}, u32[]{:S(2)}, u32[]{:S(2)}) collective-permute-start(f32[2,9]{1,0:T(2,128)S(1)} %select_reduce_fusion), channel_id=1, source_target_pairs={{0,1},{1,2},{2,3},{3,0},{4,5},{5,6},{6,7},{7,4},{8,9},{9,10},{10,1... | collective-permute-start | bytes 224 | tf_op jit(solution)/shard_map/ppermute | solution.py:18
  90.3 7.5 %collective-permute-start.13 = (bf16[2,256,256]{2,1,0:T(8,128)(2,1)S(1)}, bf16[2,256,256]{2,1,0:T(8,128)(2,1)S(1)}, u32[]{:S(2)}, u32[]{:S(2)}) collective-permute-start(bf16[2,256,256]{2,1,0:T(8,128)(2,1)S(1)} %get-tuple-element.13.refs_3_), channel_id=1, source_target_pairs={{8,0},{12,4},{16,8},{20,12},{24,16},{28,20},{9,1},{13,5},{17,9},{2... | collective-permute-start | bytes 786440 | tf_op jit(solution)/shard_map/ppermute | solution.py:44
  91.6 7.5 %collective-permute-start.10 = (bf16[2,256,256]{2,1,0:T(8,128)(2,1)S(1)}, bf16[2,256,256]{2,1,0:T(8,128)(2,1)S(1)}, u32[]{:S(2)}, u32[]{:S(2)}) collective-permute-start(bf16[2,256,256]{2,1,0:T(8,128)(2,1)S(1)} %get-tuple-element.13.refs_3_), channel_id=1, source_target_pairs={{0,8},{4,12},{8,16},{12,20},{16,24},{20,28},{1,9},{5,13},{9,17},{1... | collective-permute-start | bytes 786440 | tf_op jit(solution)/shard_map/ppermute | solution.py:43
  97.9 10.3 %collective-permute-start.14 = (bf16[2,256,256]{2,1,0:T(8,128)(2,1)S(1)}, bf16[2,256,256]{2,1,0:T(8,128)(2,1)S(1)}, u32[]{:S(2)}, u32[]{:S(2)}) collective-permute-start(bf16[2,256,256]{2,1,0:T(8,128)(2,1)S(1)} %collective-permute-done.13.refs_4_), channel_id=1, source_target_pairs={{8,0},{12,4},{16,8},{20,12},{24,16},{28,20},{9,1},{13,5},{17,9},{2... | collective-permute-start | bytes 786440 | tf_op jit(solution)/shard_map/ppermute | solution.py:44
  99.2 10.3 %collective-permute-start.11 = (bf16[2,256,256]{2,1,0:T(8,128)(2,1)S(1)}, bf16[2,256,256]{2,1,0:T(8,128)(2,1)S(1)}, u32[]{:S(2)}, u32[]{:S(2)}) collective-permute-start(bf16[2,256,256]{2,1,0:T(8,128)(2,1)S(1)} %collective-permute-done.10.refs_2_), channel_id=1, source_target_pairs={{0,8},{4,12},{8,16},{12,20},{16,24},{20,28},{1,9},{5,13},{9,17},{1... | collective-permute-start | bytes 786440 | tf_op jit(solution)/shard_map/ppermute | solution.py:43
  105.1 12.5 %collective-permute-start.19 = (bf16[2,256,256]{2,1,0:T(8,128)(2,1)S(1)}, bf16[2,256,256]{2,1,0:T(8,128)(2,1)}, u32[]{:S(2)}, u32[]{:S(2)}) collective-permute-start(bf16[2,256,256]{2,1,0:T(8,128)(2,1)S(1)} %get-tuple-element.13.refs_3_), channel_id=1, source_target_pairs={{0,4},{4,0},{8,12},{12,8},{16,20},{20,16},{24,28},{28,24},{1,5},{5... | collective-permute-start | bytes 786440 | tf_op jit(solution)/shard_map/ppermute | solution.py:40
  106.9 10.7 %collective-permute-start.20 = (bf16[2,256,256]{2,1,0:T(8,128)(2,1)S(1)}, bf16[2,256,256]{2,1,0:T(8,128)(2,1)}, u32[]{:S(2)}, u32[]{:S(2)}) collective-permute-start(bf16[2,256,256]{2,1,0:T(8,128)(2,1)S(1)} %collective-permute-done.13.refs_4_), channel_id=1, source_target_pairs={{0,4},{4,0},{8,12},{12,8},{16,20},{20,16},{24,28},{28,24},{1,5},{5... | collective-permute-start | bytes 786440 | tf_op jit(solution)/shard_map/ppermute | solution.py:46
  108.2 9.9 %collective-permute-start.15 = (bf16[2,256,256]{2,1,0:T(8,128)(2,1)S(1)}, bf16[2,256,256]{2,1,0:T(8,128)(2,1)}, u32[]{:S(2)}, u32[]{:S(2)}) collective-permute-start(bf16[2,256,256]{2,1,0:T(8,128)(2,1)S(1)} %collective-permute-done.14.refs_5_), channel_id=1, source_target_pairs={{8,0},{12,4},{16,8},{20,12},{24,16},{28,20},{9,1},{13,5},{17,9},{2... | collective-permute-start | bytes 786440 | tf_op jit(solution)/shard_map/ppermute | solution.py:44
  109.5 9.4 %collective-permute-start.12 = (bf16[2,256,256]{2,1,0:T(8,128)(2,1)S(1)}, bf16[2,256,256]{2,1,0:T(8,128)(2,1)}, u32[]{:S(2)}, u32[]{:S(2)}) collective-permute-start(bf16[2,256,256]{2,1,0:T(8,128)(2,1)S(1)} %collective-permute-done.11.refs_1_), channel_id=1, source_target_pairs={{0,8},{4,12},{8,16},{12,20},{16,24},{20,28},{1,9},{5,13},{9,17},{1... | collective-permute-start | bytes 786440 | tf_op jit(solution)/shard_map/ppermute | solution.py:43
  114.9 6.2 %collective-permute-start.18 = (bf16[2,256,256]{2,1,0:T(8,128)(2,1)S(1)}, bf16[2,256,256]{2,1,0:T(8,128)(2,1)S(1)}, u32[]{:S(2)}, u32[]{:S(2)}) collective-permute-start(bf16[2,256,256]{2,1,0:T(8,128)(2,1)S(1)} %collective-permute-done.10.refs_2_), channel_id=1, source_target_pairs={{0,4},{4,0},{8,12},{12,8},{16,20},{20,16},{24,28},{28,24},{1,5},{5... | collective-permute-start | bytes 786440 | tf_op jit(solution)/shard_map/ppermute | solution.py:45
  117.6 3.4 %collective-permute-start.21 = (bf16[2,256,256]{2,1,0:T(8,128)(2,1)S(1)}, bf16[2,256,256]{2,1,0:T(8,128)(2,1)S(1)}, u32[]{:S(2)}, u32[]{:S(2)}) collective-permute-start(bf16[2,256,256]{2,1,0:T(8,128)(2,1)S(1)} %collective-permute-done.14.refs_5_), channel_id=1, source_target_pairs={{0,4},{4,0},{8,12},{12,8},{16,20},{20,16},{24,28},{28,24},{1,5},{5... | collective-permute-start | bytes 786440 | tf_op jit(solution)/shard_map/ppermute | solution.py:46
  117.6 3.5 %collective-permute-start.17 = (bf16[2,256,256]{2,1,0:T(8,128)(2,1)S(1)}, bf16[2,256,256]{2,1,0:T(8,128)(2,1)S(1)}, u32[]{:S(2)}, u32[]{:S(2)}) collective-permute-start(bf16[2,256,256]{2,1,0:T(8,128)(2,1)S(1)} %collective-permute-done.11.refs_1_), channel_id=1, source_target_pairs={{0,4},{4,0},{8,12},{12,8},{16,20},{20,16},{24,28},{28,24},{1,5},{5... | collective-permute-start | bytes 786440 | tf_op jit(solution)/shard_map/ppermute | solution.py:45
  118.1 3.6 %collective-permute-start.22 = (bf16[2,256,256]{2,1,0:T(8,128)(2,1)}, bf16[2,256,256]{2,1,0:T(8,128)(2,1)S(1)}, u32[]{:S(2)}, u32[]{:S(2)}) collective-permute-start(bf16[2,256,256]{2,1,0:T(8,128)(2,1)} %collective-permute-done.15.refs_6_), channel_id=1, source_target_pairs={{0,4},{4,0},{8,12},{12,8},{16,20},{20,16},{24,28},{28,24},{1,5},{5... | collective-permute-start | bytes 786440 | tf_op jit(solution)/shard_map/ppermute | solution.py:46
  118.9 4.3 %collective-permute-start.16 = (bf16[2,256,256]{2,1,0:T(8,128)(2,1)}, bf16[2,256,256]{2,1,0:T(8,128)(2,1)}, u32[]{:S(2)}, u32[]{:S(2)}) collective-permute-start(bf16[2,256,256]{2,1,0:T(8,128)(2,1)} %collective-permute-done.12.refs_0_), channel_id=1, source_target_pairs={{0,4},{4,0},{8,12},{12,8},{16,20},{20,16},{24,28},{28,24},{1,5},{5... | collective-permute-start | bytes 786440 | tf_op jit(solution)/shard_map/ppermute | solution.py:45
  (16 other events, 315.8 us)

commit v7 on v5

--- a/solution.py
+++ b/solution.py
@@ -150,6 +150,7 @@
     )
     prec_terms = jnp.sum(member * jnp.sum(precond * precond, axis=(1, 2))[:, None], axis=0)
     norms = butterfly_sum(butterfly_sum(jnp.stack([adam_terms, prec_terms]), "dp"), "shard")
+    norms, lnew, rnew = lax.optimization_barrier((norms, lnew, rnew))
     norm_adam = norms[0]
     norm_prec = norms[1]
     scales = jnp.sqrt(norm_adam / (norm_prec + NORM_EPS))

time: 117 us -> 118 us (level)
  starting transfers between devices: 34.6 us -> 39.4 us
  matrix products: 7.28 us -> 4.29 us
  waiting for transfers between devices: 58.3 us -> 56.3 us
    ppermute x3, starting transfers between devices: 0.16 us -> 4.48 us  [gather_blocks(): near_left[step] = lax.ppermute(from_left[step], 'dp', partner)]
    ppermute x3, starting transfers between devices: 10 us -> 12.8 us  [gather_blocks(): from_left[step] = lax.ppermute(from_left[step - 1], 'dp', rightward)]
    ppermute x3, starting transfers between devices: 3.49 us -> 0.81 us  [gather_blocks(): near_right[step] = lax.ppermute(from_right[step], 'dp', partner)]
    ppermute x5, waiting for transfers between devices: 8.92 us -> 6.94 us  [butterfly_sum(): x = x + lax.ppermute(x, axis, [(i, i ^ step) for i in range(size)])]
    dot_general x1, matrix products: 2.66 us -> 0.79 us  [local(): jnp.einsum('sij,skj->sik', owned_grad, owned_grad, precision=highest)]
    dot_general x1, matrix products: 2.99 us -> 1.17 us  [local(): jnp.einsum('sji,sjk->sik', owned_grad, owned_grad, precision=highest)]
    ppermute x3, waiting for transfers between devices: 0.01 us -> 1.81 us  [gather_blocks(): from_right[step] = lax.ppermute(from_right[step - 1], 'dp', leftward)]
    ppermute x3, waiting for transfers between devices: 1.96 us -> 0.19 us  [gather_blocks(): from_left[step] = lax.ppermute(from_left[step - 1], 'dp', rightward)]
  transfers between devices with their start and end apart: 19 -> 19, of which waited for: 7 -> 7; matrix products, arithmetic and copies ran while one was open for 7% -> 4% of each run, Pallas kernels for 0% -> 0%
where the time goes in v7:
time: 118 us; the launch traced here: 117 us
  waiting for transfers between devices  56.3 us (48%)
  starting transfers between devices  39.4 us (33%)
  other arithmetic  9.15 us (8%)
  matrix products  4.29 us (4%)
  local copies, waits for them, and re-layouts  3.99 us (3%)
  Pallas kernels  3.16 us (3%)
    all_to_all x1, waiting for transfers between devices, local(): received = lax.all_to_all(by_owner, 'dp', 0, 0, tiled=True)  47.4 us
    ppermute x3, starting transfers between devices, gather_blocks(): from_left[step] = lax.ppermute(from_left[step - 1], 'dp', rightward)  12.8 us
    ppermute x1, starting transfers between devices, gather_blocks(): near_left[0] = lax.ppermute(mine, 'dp', partner)  7.41 us
    ppermute x5, waiting for transfers between devices, butterfly_sum(): x = x + lax.ppermute(x, axis, [(i, i ^ step) for i in range(size)])  6.94 us
    all_to_all x1, starting transfers between devices, local(): received = lax.all_to_all(by_owner, 'dp', 0, 0, tiled=True)  6.51 us
    ppermute x3, starting transfers between devices, gather_blocks(): near_left[step] = lax.ppermute(from_left[step], 'dp', partner)  4.48 us
    ppermute x3, starting transfers between devices, gather_blocks(): from_right[step] = lax.ppermute(from_right[step - 1], 'dp', leftward)  3.84 us
    ppermute x5, starting transfers between devices, butterfly_sum(): x = x + lax.ppermute(x, axis, [(i, i ^ step) for i in range(size)])  3.52 us
  transfers between devices with their start and end apart: 19, of which 7 were waited for; matrix products, arithmetic and copies ran while one was open for 4% of the time, Pallas kernels for 0%

profile of v7, /device:TPU:1, one launch (start us, length us, event | category | flops | bytes accessed | tf_op | source)
XLA Modules:
  0.0 117.3 jit_solution(15573337805229433608)
XLA Ops:
  3.5 1.6 %broadcast_select_fusion = bf16[8,2,256,256]{3,2,1,0:T(8,128)(2,1)} fusion(bf16[8,2,256,256]{3,2,1,0:T(8,128)(2,1)S(1)} %bitcast.59, pred[8,2]{1,0:T(8,128)(4,1)S(1)} %copy.36), kind=kLoop, calls=%fused_computation.2 | loop fusion | flops 1048576 | bytes 4194320 | tf_op jit(solution)/shard_map/jit(_take)/select_n | solution.py:119
  5.1 6.5 %all-to-all-start = ((bf16[8,2,256,256]{3,2,1,0:T(8,128)(2,1)}), bf16[8,2,256,256]{3,2,1,0:T(8,128)(2,1)}, u32[]{:S(2)}, u32[]{:S(2)}) async-start(bf16[8,2,256,256]{3,2,1,0:T(8,128)(2,1)} %broadcast_select_fusion), calls=%async_computation | async-start | bytes 4194304 | tf_op jit(solution)/shard_map/all_to_all | solution.py:122
  12.5 47.4 %all-to-all-done = bf16[8,2,256,256]{3,2,1,0:T(8,128)(2,1)} async-done(((bf16[8,2,256,256]{3,2,1,0:T(8,128)(2,1)}), bf16[8,2,256,256]{3,2,1,0:T(8,128)(2,1)}, u32[]{:S(2)}, u32[]{:S(2)}) %all-to-all-start) | async-done | bytes 2097184 | tf_op jit(solution)/shard_map/all_to_all | solution.py:122
  59.9 1.9 %convert_reduce_fusion = f32[2,256,256]{2,1,0:T(8,128)S(1)} fusion(bf16[8,2,256,256]{3,2,1,0:T(8,128)(2,1)} %all-to-all-done), kind=kLoop, calls=%fused_computation.1 | loop fusion | flops 1966080 | bytes 2621440 | tf_op jit(solution)/shard_map/reduce_sum | solution.py:123
  62.3 2.3 %multiply_reduce_fusion = (f32[2]{0:T(128)S(1)}, f32[2,256,256]{2,1,0:T(8,128)}) fusion(bf16[1,1,2,256,256]{4,3,2,1,0:T(8,128)(2,1)S(1)} %copy-done.7, f32[2,256,256]{2,1,0:T(8,128)S(1)} %convert_reduce_fusion, bf16[1,1,2,256,256]{4,3,2,1,0:T(8,128)(2,1)} %param.14, f32[2]{0:T(128)S(1)} %convert_element_type.35), kind=kOutput, calls=%fused_computation.26 | convolution fusion | flops 134873088 | bytes 1572880 | tf_op jit(solution)/shard_map/sij,sjk->sik/dot_general | solution.py:148
  64.7 0.9 collective-permute-start
  66.6 2.4 %collective-permute-done.1 = f32[2,9]{1,0:T(2,128)S(1)} collective-permute-done((f32[2,9]{1,0:T(2,128)S(1)}, f32[2,9]{1,0:T(2,128)S(1)}, u32[]{:S(2)}, u32[]{:S(2)}) %collective-permute-start.1) | collective-permute-done | bytes 104 | tf_op jit(solution)/shard_map/ppermute | solution.py:20
  69.1 3.3 %collective-permute-done.2 = f32[2,9]{1,0:T(2,128)S(1)} collective-permute-done((f32[2,9]{1,0:T(2,128)S(1)}, f32[2,9]{1,0:T(2,128)S(1)}, u32[]{:S(2)}, u32[]{:S(2)}) %collective-permute-start.2) | collective-permute-done | bytes 104 | tf_op jit(solution)/shard_map/ppermute | solution.py:20
  72.4 1.2 %collective-permute-start.3 = (f32[2,9]{1,0:T(2,128)S(1)}, f32[2,9]{1,0:T(2,128)S(1)}, u32[]{:S(2)}, u32[]{:S(2)}) collective-permute-start(f32[2,9]{1,0:T(2,128)S(1)} %add.107), channel_id=1, source_target_pairs={{0,1},{1,0},{2,3},{3,2},{4,5},{5,4},{6,7},{7,6},{8,9},{9,8},{10,11... | collective-permute-start | bytes 224 | tf_op jit(solution)/shard_map/ppermute | solution.py:20
  74.8 1.2 %collective-permute-start.4 = (f32[2,9]{1,0:T(2,128)S(1)}, f32[2,9]{1,0:T(2,128)S(1)}, u32[]{:S(2)}, u32[]{:S(2)}) collective-permute-start(f32[2,9]{1,0:T(2,128)S(1)} %add.108), channel_id=1, source_target_pairs={{0,2},{1,3},{2,0},{3,1},{4,6},{5,7},{6,4},{7,5},{8,10},{9,11},{10,... | collective-permute-start | bytes 224 | tf_op jit(solution)/shard_map/ppermute | solution.py:20
  76.0 1.2 fusion
  77.5 1.3 %fusion.30 = (bf16[2,256,256]{2,1,0:T(8,128)(2,1)S(1)}, f32[1,1,2,256,256]{4,3,2,1,0:T(8,128)}, f32[1,1,2,256,256]{4,3,2,1,0:T(8,128)}, f32[1,1,2,256,256]{4,3,2,1,0:T(8,128)}) fusion(f32[2,256,256]{2,1,0:T(8,128)S(1)} %copy-done.4, f32[2]{0:T(128)S(1)} %broadcast_multiply_fusion, f32[1,1,2,256,256]{4,3,2,1,0:T(8,128)S(1)} %copy-done.6, ...), kind=kLoop, calls=%fused_computation.73 | loop fusion | flops 786432 | bytes 4980746 | tf_op jit(solution)/shard_map/convert_element_type | solution.py:164
  78.8 1.3 %collective-permute-start.8 = (bf16[2,256,256]{2,1,0:T(8,128)(2,1)S(1)}, bf16[2,256,256]{2,1,0:T(8,128)(2,1)S(1)}, u32[]{:S(2)}, u32[]{:S(2)}) collective-permute-start(bf16[2,256,256]{2,1,0:T(8,128)(2,1)S(1)} %get-tuple-element.13.refs_3_), channel_id=1, source_target_pairs={{8,0},{12,4},{16,8},{20,12},{24,16},{28,20},{9,1},{13,5},{17,9},{2... | collective-permute-start | bytes 786440 | tf_op jit(solution)/shard_map/ppermute | solution.py:45
  80.1 4.0 %collective-permute-start.5 = (bf16[2,256,256]{2,1,0:T(8,128)(2,1)S(1)}, bf16[2,256,256]{2,1,0:T(8,128)(2,1)S(1)}, u32[]{:S(2)}, u32[]{:S(2)}) collective-permute-start(bf16[2,256,256]{2,1,0:T(8,128)(2,1)S(1)} %get-tuple-element.13.refs_3_), channel_id=1, source_target_pairs={{0,8},{4,12},{8,16},{12,20},{16,24},{20,28},{1,9},{5,13},{9,17},{1... | collective-permute-start | bytes 786440 | tf_op jit(solution)/shard_map/ppermute | solution.py:44
  84.1 1.8 %collective-permute-done.8.refs_4_ = bf16[2,256,256]{2,1,0:T(8,128)(2,1)S(1)} collective-permute-done((bf16[2,256,256]{2,1,0:T(8,128)(2,1)S(1)}, bf16[2,256,256]{2,1,0:T(8,128)(2,1)S(1)}, u32[]{:S(2)}, u32[]{:S(2)}) %collective-permute-start.8) | collective-permute-done | bytes 262176 | tf_op jit(solution)/shard_map/ppermute | solution.py:45
  85.9 1.3 %collective-permute-start.9 = (bf16[2,256,256]{2,1,0:T(8,128)(2,1)S(1)}, bf16[2,256,256]{2,1,0:T(8,128)(2,1)S(1)}, u32[]{:S(2)}, u32[]{:S(2)}) collective-permute-start(bf16[2,256,256]{2,1,0:T(8,128)(2,1)S(1)} %collective-permute-done.8.refs_4_), channel_id=1, source_target_pairs={{8,0},{12,4},{16,8},{20,12},{24,16},{28,20},{9,1},{13,5},{17,9},{2... | collective-permute-start | bytes 786440 | tf_op jit(solution)/shard_map/ppermute | solution.py:45
  87.3 4.1 %collective-permute-start.6 = (bf16[2,256,256]{2,1,0:T(8,128)(2,1)S(1)}, bf16[2,256,256]{2,1,0:T(8,128)(2,1)S(1)}, u32[]{:S(2)}, u32[]{:S(2)}) collective-permute-start(bf16[2,256,256]{2,1,0:T(8,128)(2,1)S(1)} %collective-permute-done.5.refs_2_), channel_id=1, source_target_pairs={{0,8},{4,12},{8,16},{12,20},{16,24},{20,28},{1,9},{5,13},{9,17},{1... | collective-permute-start | bytes 786440 | tf_op jit(solution)/shard_map/ppermute | solution.py:44
  91.5 7.4 %collective-permute-start.14 = (bf16[2,256,256]{2,1,0:T(8,128)(2,1)S(1)}, bf16[2,256,256]{2,1,0:T(8,128)(2,1)}, u32[]{:S(2)}, u32[]{:S(2)}) collective-permute-start(bf16[2,256,256]{2,1,0:T(8,128)(2,1)S(1)} %get-tuple-element.13.refs_3_), channel_id=1, source_target_pairs={{0,4},{4,0},{8,12},{12,8},{16,20},{20,16},{24,28},{28,24},{1,5},{5... | collective-permute-start | bytes 786440 | tf_op jit(solution)/shard_map/ppermute | solution.py:41
  99.0 1.3 %collective-permute-start.10 = (bf16[2,256,256]{2,1,0:T(8,128)(2,1)S(1)}, bf16[2,256,256]{2,1,0:T(8,128)(2,1)}, u32[]{:S(2)}, u32[]{:S(2)}) collective-permute-start(bf16[2,256,256]{2,1,0:T(8,128)(2,1)S(1)} %collective-permute-done.9.refs_5_), channel_id=1, source_target_pairs={{8,0},{12,4},{16,8},{20,12},{24,16},{28,20},{9,1},{13,5},{17,9},{2... | collective-permute-start | bytes 786440 | tf_op jit(solution)/shard_map/ppermute | solution.py:45
  100.3 4.7 %collective-permute-start.7 = (bf16[2,256,256]{2,1,0:T(8,128)(2,1)S(1)}, bf16[2,256,256]{2,1,0:T(8,128)(2,1)}, u32[]{:S(2)}, u32[]{:S(2)}) collective-permute-start(bf16[2,256,256]{2,1,0:T(8,128)(2,1)S(1)} %collective-permute-done.6.refs_1_), channel_id=1, source_target_pairs={{0,8},{4,12},{8,16},{12,20},{16,24},{20,28},{1,9},{5,13},{9,17},{1... | collective-permute-start | bytes 786440 | tf_op jit(solution)/shard_map/ppermute | solution.py:44
  105.7 2.8 %collective-permute-start.13 = (bf16[2,256,256]{2,1,0:T(8,128)(2,1)S(1)}, bf16[2,256,256]{2,1,0:T(8,128)(2,1)S(1)}, u32[]{:S(2)}, u32[]{:S(2)}) collective-permute-start(bf16[2,256,256]{2,1,0:T(8,128)(2,1)S(1)} %collective-permute-done.5.refs_2_), channel_id=1, source_target_pairs={{0,4},{4,0},{8,12},{12,8},{16,20},{20,16},{24,28},{28,24},{1,5},{5... | collective-permute-start | bytes 786440 | tf_op jit(solution)/shard_map/ppermute | solution.py:46
  109.7 1.2 %collective-permute-start.11 = (bf16[2,256,256]{2,1,0:T(8,128)(2,1)}, bf16[2,256,256]{2,1,0:T(8,128)(2,1)}, u32[]{:S(2)}, u32[]{:S(2)}) collective-permute-start(bf16[2,256,256]{2,1,0:T(8,128)(2,1)} %collective-permute-done.7.refs_0_), channel_id=1, source_target_pairs={{0,4},{4,0},{8,12},{12,8},{16,20},{20,16},{24,28},{28,24},{1,5},{5... | collective-permute-start | bytes 786440 | tf_op jit(solution)/shard_map/ppermute | solution.py:46
  110.9 1.0 fusion.9
  114.1 3.2 %shard_map.128 = bf16[8,256,256]{2,1,0:T(8,128)(2,1)} custom-call(s32[8,2]{1,0:T(8,128)} %copy.41.table_ref, bf16[2,256,256]{2,1,0:T(8,128)(2,1)} %collective-permute-done.7.refs_0_, bf16[2,256,256]{2,1,0:T(8,128)(2,1)} %copy-done.11, bf16[2,256,256]{2,1,0:T(8,128)(2,1)} %copy-done.9, bf16[2,256,256]{2,1,0:T(8,128)(2,1)} %copy-done.5, ...), custom_call_target="tpu_custom_call" | custom-call | tf_op jit(solution)/shard_map/pallas_call | solution.py:79
  (91 shorter events, 11.1 us)
Async XLA Ops:
  5.1 54.8 %all-to-all-start = ((bf16[8,2,256,256]{3,2,1,0:T(8,128)(2,1)}), bf16[8,2,256,256]{3,2,1,0:T(8,128)(2,1)}, u32[]{:S(2)}, u32[]{:S(2)}) async-start(bf16[8,2,256,256]{3,2,1,0:T(8,128)(2,1)} %broadcast_select_fusion), calls=%async_computation | async-start | bytes 4194304 | tf_op jit(solution)/shard_map/all_to_all | solution.py:122
  11.6 50.2 %copy-start.1 = (f32[1,1,2,256,256]{4,3,2,1,0:T(8,128)S(1)}, f32[1,1,2,256,256]{4,3,2,1,0:T(8,128)}, u32[]{:S(2)}) copy-start(f32[1,1,2,256,256]{4,3,2,1,0:T(8,128)} %param.16) | copy-start | bytes 1572868
  11.6 50.7 %copy-start.7 = (bf16[1,1,2,256,256]{4,3,2,1,0:T(8,128)(2,1)S(1)}, bf16[1,1,2,256,256]{4,3,2,1,0:T(8,128)(2,1)}, u32[]{:S(2)}) copy-start(bf16[1,1,2,256,256]{4,3,2,1,0:T(8,128)(2,1)} %param.15) | copy-start | bytes 786436
  12.5 61.1 %copy-start.3 = (f32[1,1,2,256,256]{4,3,2,1,0:T(8,128)S(1)}, f32[1,1,2,256,256]{4,3,2,1,0:T(8,128)}, u32[]{:S(2)}) copy-start(f32[1,1,2,256,256]{4,3,2,1,0:T(8,128)} %param.12) | copy-start | bytes 1572868
  64.7 1.7 %collective-permute-start = (f32[2,9]{1,0:T(2,128)S(1)}, f32[2,9]{1,0:T(2,128)S(1)}, u32[]{:S(2)}, u32[]{:S(2)}) collective-permute-start(f32[2,9]{1,0:T(2,128)S(1)} %pad_maximum_fusion), channel_id=1, source_target_pairs={{0,4},{4,0},{8,12},{12,8},{16,20},{20,16},{24,28},{28,24},{1,5},{5... | collective-permute-start | bytes 224 | tf_op jit(solution)/shard_map/ppermute | solution.py:20
  66.5 2.5 %collective-permute-start.1 = (f32[2,9]{1,0:T(2,128)S(1)}, f32[2,9]{1,0:T(2,128)S(1)}, u32[]{:S(2)}, u32[]{:S(2)}) collective-permute-start(f32[2,9]{1,0:T(2,128)S(1)} %fusion.29), channel_id=1, source_target_pairs={{0,8},{4,12},{8,0},{12,4},{16,24},{20,28},{24,16},{28,20},{1,9},{5... | collective-permute-start | bytes 224 | tf_op jit(solution)/shard_map/ppermute | solution.py:20
  69.0 3.4 %collective-permute-start.2 = (f32[2,9]{1,0:T(2,128)S(1)}, f32[2,9]{1,0:T(2,128)S(1)}, u32[]{:S(2)}, u32[]{:S(2)}) collective-permute-start(f32[2,9]{1,0:T(2,128)S(1)} %fusion.34), channel_id=1, source_target_pairs={{0,16},{4,20},{8,24},{12,28},{16,0},{20,4},{24,8},{28,12},{1,17},{... | collective-permute-start | bytes 224 | tf_op jit(solution)/shard_map/ppermute | solution.py:20
  72.4 2.4 %collective-permute-start.3 = (f32[2,9]{1,0:T(2,128)S(1)}, f32[2,9]{1,0:T(2,128)S(1)}, u32[]{:S(2)}, u32[]{:S(2)}) collective-permute-start(f32[2,9]{1,0:T(2,128)S(1)} %add.107), channel_id=1, source_target_pairs={{0,1},{1,0},{2,3},{3,2},{4,5},{5,4},{6,7},{7,6},{8,9},{9,8},{10,11... | collective-permute-start | bytes 224 | tf_op jit(solution)/shard_map/ppermute | solution.py:20
  74.8 2.4 %collective-permute-start.4 = (f32[2,9]{1,0:T(2,128)S(1)}, f32[2,9]{1,0:T(2,128)S(1)}, u32[]{:S(2)}, u32[]{:S(2)}) collective-permute-start(f32[2,9]{1,0:T(2,128)S(1)} %add.108), channel_id=1, source_target_pairs={{0,2},{1,3},{2,0},{3,1},{4,6},{5,7},{6,4},{7,5},{8,10},{9,11},{10,... | collective-permute-start | bytes 224 | tf_op jit(solution)/shard_map/ppermute | solution.py:20
  78.8 35.3 %copy-start.5 = (bf16[2,256,256]{2,1,0:T(8,128)(2,1)}, bf16[2,256,256]{2,1,0:T(8,128)(2,1)S(1)}, u32[]{:S(2)}) copy-start(bf16[2,256,256]{2,1,0:T(8,128)(2,1)S(1)} %get-tuple-element.13.refs_3_) | copy-start | bytes 786436
  78.8 7.1 %collective-permute-start.8 = (bf16[2,256,256]{2,1,0:T(8,128)(2,1)S(1)}, bf16[2,256,256]{2,1,0:T(8,128)(2,1)S(1)}, u32[]{:S(2)}, u32[]{:S(2)}) collective-permute-start(bf16[2,256,256]{2,1,0:T(8,128)(2,1)S(1)} %get-tuple-element.13.refs_3_), channel_id=1, source_target_pairs={{8,0},{12,4},{16,8},{20,12},{24,16},{28,20},{9,1},{13,5},{17,9},{2... | collective-permute-start | bytes 786440 | tf_op jit(solution)/shard_map/ppermute | solution.py:45
  80.1 7.3 %collective-permute-start.5 = (bf16[2,256,256]{2,1,0:T(8,128)(2,1)S(1)}, bf16[2,256,256]{2,1,0:T(8,128)(2,1)S(1)}, u32[]{:S(2)}, u32[]{:S(2)}) collective-permute-start(bf16[2,256,256]{2,1,0:T(8,128)(2,1)S(1)} %get-tuple-element.13.refs_3_), channel_id=1, source_target_pairs={{0,8},{4,12},{8,16},{12,20},{16,24},{20,28},{1,9},{5,13},{9,17},{1... | collective-permute-start | bytes 786440 | tf_op jit(solution)/shard_map/ppermute | solution.py:44
  85.9 28.2 %copy-start.8 = (bf16[2,256,256]{2,1,0:T(8,128)(2,1)}, bf16[2,256,256]{2,1,0:T(8,128)(2,1)S(1)}, u32[]{:S(2)}) copy-start(bf16[2,256,256]{2,1,0:T(8,128)(2,1)S(1)} %collective-permute-done.8.refs_4_) | copy-start | bytes 786436
  85.9 13.1 %collective-permute-start.9 = (bf16[2,256,256]{2,1,0:T(8,128)(2,1)S(1)}, bf16[2,256,256]{2,1,0:T(8,128)(2,1)S(1)}, u32[]{:S(2)}, u32[]{:S(2)}) collective-permute-start(bf16[2,256,256]{2,1,0:T(8,128)(2,1)S(1)} %collective-permute-done.8.refs_4_), channel_id=1, source_target_pairs={{8,0},{12,4},{16,8},{20,12},{24,16},{28,20},{9,1},{13,5},{17,9},{2... | collective-permute-start | bytes 786440 | tf_op jit(solution)/shard_map/ppermute | solution.py:45
  87.3 12.9 %collective-permute-start.6 = (bf16[2,256,256]{2,1,0:T(8,128)(2,1)S(1)}, bf16[2,256,256]{2,1,0:T(8,128)(2,1)S(1)}, u32[]{:S(2)}, u32[]{:S(2)}) collective-permute-start(bf16[2,256,256]{2,1,0:T(8,128)(2,1)S(1)} %collective-permute-done.5.refs_2_), channel_id=1, source_target_pairs={{0,8},{4,12},{8,16},{12,20},{16,24},{20,28},{1,9},{5,13},{9,17},{1... | collective-permute-start | bytes 786440 | tf_op jit(solution)/shard_map/ppermute | solution.py:44
  91.5 17.0 %collective-permute-start.14 = (bf16[2,256,256]{2,1,0:T(8,128)(2,1)S(1)}, bf16[2,256,256]{2,1,0:T(8,128)(2,1)}, u32[]{:S(2)}, u32[]{:S(2)}) collective-permute-start(bf16[2,256,256]{2,1,0:T(8,128)(2,1)S(1)} %get-tuple-element.13.refs_3_), channel_id=1, source_target_pairs={{0,4},{4,0},{8,12},{12,8},{16,20},{20,16},{24,28},{28,24},{1,5},{5... | collective-permute-start | bytes 786440 | tf_op jit(solution)/shard_map/ppermute | solution.py:41
  98.9 9.6 %collective-permute-start.15 = (bf16[2,256,256]{2,1,0:T(8,128)(2,1)S(1)}, bf16[2,256,256]{2,1,0:T(8,128)(2,1)}, u32[]{:S(2)}, u32[]{:S(2)}) collective-permute-start(bf16[2,256,256]{2,1,0:T(8,128)(2,1)S(1)} %collective-permute-done.8.refs_4_), channel_id=1, source_target_pairs={{0,4},{4,0},{8,12},{12,8},{16,20},{20,16},{24,28},{28,24},{1,5},{5... | collective-permute-start | bytes 786440 | tf_op jit(solution)/shard_map/ppermute | solution.py:47
  99.0 10.0 %collective-permute-start.10 = (bf16[2,256,256]{2,1,0:T(8,128)(2,1)S(1)}, bf16[2,256,256]{2,1,0:T(8,128)(2,1)}, u32[]{:S(2)}, u32[]{:S(2)}) collective-permute-start(bf16[2,256,256]{2,1,0:T(8,128)(2,1)S(1)} %collective-permute-done.9.refs_5_), channel_id=1, source_target_pairs={{8,0},{12,4},{16,8},{20,12},{24,16},{28,20},{9,1},{13,5},{17,9},{2... | collective-permute-start | bytes 786440 | tf_op jit(solution)/shard_map/ppermute | solution.py:45
  100.3 9.4 %collective-permute-start.7 = (bf16[2,256,256]{2,1,0:T(8,128)(2,1)S(1)}, bf16[2,256,256]{2,1,0:T(8,128)(2,1)}, u32[]{:S(2)}, u32[]{:S(2)}) collective-permute-start(bf16[2,256,256]{2,1,0:T(8,128)(2,1)S(1)} %collective-permute-done.6.refs_1_), channel_id=1, source_target_pairs={{0,8},{4,12},{8,16},{12,20},{16,24},{20,28},{1,9},{5,13},{9,17},{1... | collective-permute-start | bytes 786440 | tf_op jit(solution)/shard_map/ppermute | solution.py:44
  105.7 6.2 %collective-permute-start.13 = (bf16[2,256,256]{2,1,0:T(8,128)(2,1)S(1)}, bf16[2,256,256]{2,1,0:T(8,128)(2,1)S(1)}, u32[]{:S(2)}, u32[]{:S(2)}) collective-permute-start(bf16[2,256,256]{2,1,0:T(8,128)(2,1)S(1)} %collective-permute-done.5.refs_2_), channel_id=1, source_target_pairs={{0,4},{4,0},{8,12},{12,8},{16,20},{20,16},{24,28},{28,24},{1,5},{5... | collective-permute-start | bytes 786440 | tf_op jit(solution)/shard_map/ppermute | solution.py:46
  108.5 3.4 %collective-permute-start.16 = (bf16[2,256,256]{2,1,0:T(8,128)(2,1)S(1)}, bf16[2,256,256]{2,1,0:T(8,128)(2,1)S(1)}, u32[]{:S(2)}, u32[]{:S(2)}) collective-permute-start(bf16[2,256,256]{2,1,0:T(8,128)(2,1)S(1)} %collective-permute-done.9.refs_5_), channel_id=1, source_target_pairs={{0,4},{4,0},{8,12},{12,8},{16,20},{20,16},{24,28},{28,24},{1,5},{5... | collective-permute-start | bytes 786440 | tf_op jit(solution)/shard_map/ppermute | solution.py:47
  108.5 3.4 %collective-permute-start.12 = (bf16[2,256,256]{2,1,0:T(8,128)(2,1)S(1)}, bf16[2,256,256]{2,1,0:T(8,128)(2,1)S(1)}, u32[]{:S(2)}, u32[]{:S(2)}) collective-permute-start(bf16[2,256,256]{2,1,0:T(8,128)(2,1)S(1)} %collective-permute-done.6.refs_1_), channel_id=1, source_target_pairs={{0,4},{4,0},{8,12},{12,8},{16,20},{20,16},{24,28},{28,24},{1,5},{5... | collective-permute-start | bytes 786440 | tf_op jit(solution)/shard_map/ppermute | solution.py:46
  109.0 3.6 %collective-permute-start.17 = (bf16[2,256,256]{2,1,0:T(8,128)(2,1)}, bf16[2,256,256]{2,1,0:T(8,128)(2,1)S(1)}, u32[]{:S(2)}, u32[]{:S(2)}) collective-permute-start(bf16[2,256,256]{2,1,0:T(8,128)(2,1)} %collective-permute-done.10.refs_6_), channel_id=1, source_target_pairs={{0,4},{4,0},{8,12},{12,8},{16,20},{20,16},{24,28},{28,24},{1,5},{5... | collective-permute-start | bytes 786440 | tf_op jit(solution)/shard_map/ppermute | solution.py:47
  109.7 4.4 %collective-permute-start.11 = (bf16[2,256,256]{2,1,0:T(8,128)(2,1)}, bf16[2,256,256]{2,1,0:T(8,128)(2,1)}, u32[]{:S(2)}, u32[]{:S(2)}) collective-permute-start(bf16[2,256,256]{2,1,0:T(8,128)(2,1)} %collective-permute-done.7.refs_0_), channel_id=1, source_target_pairs={{0,4},{4,0},{8,12},{12,8},{16,20},{20,16},{24,28},{28,24},{1,5},{5... | collective-permute-start | bytes 786440 | tf_op jit(solution)/shard_map/ppermute | solution.py:46
  (13 other events, 134.7 us)

commit v8 on v5

--- a/solution.py
+++ b/solution.py
@@ -103,8 +103,9 @@
     column_blocks = local_grads.shape[0]
     slot_count = stats_left.shape[2]
     owner_of = owners[:, 0]
-    onehot = (owner_of[:, None] == jnp.arange(replicas, dtype=jnp.int32)[None, :]).astype(jnp.int32)
-    slot_rank = jnp.sum((jnp.cumsum(onehot, axis=0) - onehot) * onehot, axis=1)
+    block_ids = jnp.arange(column_blocks, dtype=jnp.int32)
+    earlier = (owner_of[None, :] == owner_of[:, None]) & (block_ids[None, :] < block_ids[:, None])
+    slot_rank = jnp.sum(earlier.astype(jnp.int32), axis=1)
     matches = (owner_of[None, None, :] == jnp.arange(replicas, dtype=jnp.int32)[:, None, None]) & (
         slot_rank[None, None, :] == jnp.arange(slot_count, dtype=jnp.int32)[None, :, None]
     )
@@ -116,7 +117,7 @@
     my_table = lax.dynamic_index_in_dim(slot_table, replica, 0, keepdims=False)
     my_live = lax.dynamic_index_in_dim(slot_live, replica, 0, keepdims=False)
     live_float = my_live.astype(jnp.float32)[:, None, None]
-    by_owner = jnp.take(local_grads, slot_table.reshape(-1), axis=0).reshape(
+    by_owner = jnp.take(local_grads, slot_table.reshape(-1), axis=0, mode="clip").reshape(
         (replicas, slot_count) + local_grads.shape[1:]
     )
     received = lax.all_to_all(by_owner, "dp", 0, 0, tiled=True)

time: 117 us -> 117 us (level)
  other arithmetic: 8.79 us -> 7.11 us
  local copies, waits for them, and re-layouts: 3.37 us -> 4.58 us
    select_n x2 -> x0, other arithmetic: 1.58 us -> none  [local(): jnp.take(local_grads, slot_table.reshape(-1), axis=0)]
    gather x1, local copies, waits for them, and re-layouts: 0.68 us -> 1.99 us  [local(): jnp.take(local_grads, slot_table.reshape(-1), axis=0, mode='clip')]
where the time goes in v8:
time: 117 us; the launch traced here: 116 us
  waiting for transfers between devices  58.3 us (50%)
  starting transfers between devices  34.6 us (30%)
  matrix products  7.28 us (6%)
  other arithmetic  7.11 us (6%)
  local copies, waits for them, and re-layouts  4.58 us (4%)
  Pallas kernels  3.15 us (3%)
    all_to_all x1, waiting for transfers between devices, local(): received = lax.all_to_all(by_owner, 'dp', 0, 0, tiled=True)  47.4 us
    ppermute x3, starting transfers between devices, gather_blocks(): from_left[step] = lax.ppermute(from_left[step - 1], 'dp', rightward)  10 us
    ppermute x5, waiting for transfers between devices, butterfly_sum(): x = x + lax.ppermute(x, axis, [(i, i ^ step) for i in range(size)])  8.91 us
    ppermute x1, starting transfers between devices, gather_blocks(): near_left[0] = lax.ppermute(mine, 'dp', partner)  7.05 us
    all_to_all x1, starting transfers between devices, local(): received = lax.all_to_all(by_owner, 'dp', 0, 0, tiled=True)  6.51 us
    ppermute x3, starting transfers between devices, gather_blocks(): from_right[step] = lax.ppermute(from_right[step - 1], 'dp', leftward)  3.88 us
    ppermute x5, starting transfers between devices, butterfly_sum(): x = x + lax.ppermute(x, axis, [(i, i ^ step) for i in range(size)])  3.53 us
    ppermute x3, starting transfers between devices, gather_blocks(): near_right[step] = lax.ppermute(from_right[step], 'dp', partner)  3.49 us
  transfers between devices with their start and end apart: 19, of which 7 were waited for; matrix products, arithmetic and copies ran while one was open for 7% of the time, Pallas kernels for 0%

profile of v8, /device:TPU:1, one launch (start us, length us, event | category | flops | bytes accessed | tf_op | source)
XLA Modules:
  0.0 116.0 jit_solution(17553907242375873711)
XLA Ops:
  2.6 2.0 %gather_fusion = bf16[16,256,256]{2,1,0:T(8,128)(2,1)} fusion(bf16[8,256,256]{2,1,0:T(8,128)(2,1)S(1)} %bitcast.52, s32[1024]{0:T(1024)S(1)} %pad_clamp_fusion), kind=kCustom, calls=%fused_computation | custom fusion | bytes 4194368 | tf_op jit(solution)/shard_map/jit(_take)/gather | solution.py:120
  4.6 6.5 %all-to-all-start = ((bf16[8,2,256,256]{3,2,1,0:T(8,128)(2,1)}), bf16[8,2,256,256]{3,2,1,0:T(8,128)(2,1)}, u32[]{:S(2)}, u32[]{:S(2)}) async-start(bf16[8,2,256,256]{3,2,1,0:T(8,128)(2,1)} %bitcast.3), calls=%async_computation | async-start | bytes 4194304 | tf_op jit(solution)/shard_map/all_to_all | solution.py:123
  12.0 47.4 %all-to-all-done = bf16[8,2,256,256]{3,2,1,0:T(8,128)(2,1)} async-done(((bf16[8,2,256,256]{3,2,1,0:T(8,128)(2,1)}), bf16[8,2,256,256]{3,2,1,0:T(8,128)(2,1)}, u32[]{:S(2)}, u32[]{:S(2)}) %all-to-all-start) | async-done | bytes 2097184 | tf_op jit(solution)/shard_map/all_to_all | solution.py:123
  59.4 1.9 %convert_reduce_fusion = f32[2,256,256]{2,1,0:T(8,128)S(1)} fusion(bf16[8,2,256,256]{3,2,1,0:T(8,128)(2,1)} %all-to-all-done), kind=kLoop, calls=%fused_computation.1 | loop fusion | flops 1966080 | bytes 2621440 | tf_op jit(solution)/shard_map/reduce_sum | solution.py:124
  61.8 1.6 %multiply_reduce_fusion = (f32[2]{0:T(128)S(1)}, f32[2,256,256]{2,1,0:T(8,128)S(1)}) fusion(bf16[1,1,2,256,256]{4,3,2,1,0:T(8,128)(2,1)S(1)} %copy-done.4, f32[2,256,256]{2,1,0:T(8,128)S(1)} %convert_reduce_fusion, bf16[1,1,2,256,256]{4,3,2,1,0:T(8,128)(2,1)} %param.14, f32[2]{0:T(128)S(1)} %convert_element_type.35), kind=kOutput, calls=%fused_computation.25 | convolution fusion | flops 134873088 | bytes 1572880 | tf_op jit(solution)/shard_map/sij,sjk->sik/dot_general | solution.py:149
  65.4 2.4 %collective-permute-done.1 = f32[2,9]{1,0:T(2,128)S(1)} collective-permute-done((f32[2,9]{1,0:T(2,128)S(1)}, f32[2,9]{1,0:T(2,128)S(1)}, u32[]{:S(2)}, u32[]{:S(2)}) %collective-permute-start.1) | collective-permute-done | bytes 104 | tf_op jit(solution)/shard_map/ppermute | solution.py:20
  67.9 3.3 %collective-permute-done.2 = f32[2,9]{1,0:T(2,128)S(1)} collective-permute-done((f32[2,9]{1,0:T(2,128)S(1)}, f32[2,9]{1,0:T(2,128)S(1)}, u32[]{:S(2)}, u32[]{:S(2)}) %collective-permute-start.2) | collective-permute-done | bytes 104 | tf_op jit(solution)/shard_map/ppermute | solution.py:20
  71.2 1.2 %collective-permute-start.3 = (f32[2,9]{1,0:T(2,128)S(1)}, f32[2,9]{1,0:T(2,128)S(1)}, u32[]{:S(2)}, u32[]{:S(2)}) collective-permute-start(f32[2,9]{1,0:T(2,128)S(1)} %add.92), channel_id=1, source_target_pairs={{0,1},{1,0},{2,3},{3,2},{4,5},{5,4},{6,7},{7,6},{8,9},{9,8},{10,11... | collective-permute-start | bytes 224 | tf_op jit(solution)/shard_map/ppermute | solution.py:20
  72.4 1.2 %collective-permute-done.3 = f32[2,9]{1,0:T(2,128)S(1)} collective-permute-done((f32[2,9]{1,0:T(2,128)S(1)}, f32[2,9]{1,0:T(2,128)S(1)}, u32[]{:S(2)}, u32[]{:S(2)}) %collective-permute-start.3) | collective-permute-done | bytes 104 | tf_op jit(solution)/shard_map/ppermute | solution.py:20
  73.6 1.2 %collective-permute-start.4 = (f32[2,9]{1,0:T(2,128)S(1)}, f32[2,9]{1,0:T(2,128)S(1)}, u32[]{:S(2)}, u32[]{:S(2)}) collective-permute-start(f32[2,9]{1,0:T(2,128)S(1)} %add.93), channel_id=1, source_target_pairs={{0,2},{1,3},{2,0},{3,1},{4,6},{5,7},{6,4},{7,5},{8,10},{9,11},{10,... | collective-permute-start | bytes 224 | tf_op jit(solution)/shard_map/ppermute | solution.py:20
  74.9 1.2 %collective-permute-done.4 = f32[2,9]{1,0:T(2,128)S(1)} collective-permute-done((f32[2,9]{1,0:T(2,128)S(1)}, f32[2,9]{1,0:T(2,128)S(1)}, u32[]{:S(2)}, u32[]{:S(2)}) %collective-permute-start.4) | collective-permute-done | bytes 104 | tf_op jit(solution)/shard_map/ppermute | solution.py:20
  77.2 1.9 %collective-permute-start.5 = (bf16[2,256,256]{2,1,0:T(8,128)(2,1)S(1)}, bf16[2,256,256]{2,1,0:T(8,128)(2,1)S(1)}, u32[]{:S(2)}, u32[]{:S(2)}) collective-permute-start(bf16[2,256,256]{2,1,0:T(8,128)(2,1)S(1)} %get-tuple-element.7.refs_3_), channel_id=1, source_target_pairs={{0,8},{4,12},{8,16},{12,20},{16,24},{20,28},{1,9},{5,13},{9,17},{1... | collective-permute-start | bytes 786440 | tf_op jit(solution)/shard_map/ppermute | solution.py:44
  79.1 1.3 %collective-permute-start.8 = (bf16[2,256,256]{2,1,0:T(8,128)(2,1)S(1)}, bf16[2,256,256]{2,1,0:T(8,128)(2,1)S(1)}, u32[]{:S(2)}, u32[]{:S(2)}) collective-permute-start(bf16[2,256,256]{2,1,0:T(8,128)(2,1)S(1)} %get-tuple-element.7.refs_3_), channel_id=1, source_target_pairs={{8,0},{12,4},{16,8},{20,12},{24,16},{28,20},{9,1},{13,5},{17,9},{2... | collective-permute-start | bytes 786440 | tf_op jit(solution)/shard_map/ppermute | solution.py:45
  80.5 2.0 %collective-permute-done.5.refs_2_ = bf16[2,256,256]{2,1,0:T(8,128)(2,1)S(1)} collective-permute-done((bf16[2,256,256]{2,1,0:T(8,128)(2,1)S(1)}, bf16[2,256,256]{2,1,0:T(8,128)(2,1)S(1)}, u32[]{:S(2)}, u32[]{:S(2)}) %collective-permute-start.5) | collective-permute-done | bytes 262176 | tf_op jit(solution)/shard_map/ppermute | solution.py:44
  82.4 3.8 %collective-permute-start.6 = (bf16[2,256,256]{2,1,0:T(8,128)(2,1)S(1)}, bf16[2,256,256]{2,1,0:T(8,128)(2,1)S(1)}, u32[]{:S(2)}, u32[]{:S(2)}) collective-permute-start(bf16[2,256,256]{2,1,0:T(8,128)(2,1)S(1)} %collective-permute-done.5.refs_2_), channel_id=1, source_target_pairs={{0,8},{4,12},{8,16},{12,20},{16,24},{20,28},{1,9},{5,13},{9,17},{1... | collective-permute-start | bytes 786440 | tf_op jit(solution)/shard_map/ppermute | solution.py:44
  86.3 1.3 %collective-permute-start.9 = (bf16[2,256,256]{2,1,0:T(8,128)(2,1)S(1)}, bf16[2,256,256]{2,1,0:T(8,128)(2,1)S(1)}, u32[]{:S(2)}, u32[]{:S(2)}) collective-permute-start(bf16[2,256,256]{2,1,0:T(8,128)(2,1)S(1)} %collective-permute-done.8.refs_4_), channel_id=1, source_target_pairs={{8,0},{12,4},{16,8},{20,12},{24,16},{28,20},{9,1},{13,5},{17,9},{2... | collective-permute-start | bytes 786440 | tf_op jit(solution)/shard_map/ppermute | solution.py:45
  88.3 7.1 %collective-permute-start.14 = (bf16[2,256,256]{2,1,0:T(8,128)(2,1)S(1)}, bf16[2,256,256]{2,1,0:T(8,128)(2,1)S(1)}, u32[]{:S(2)}, u32[]{:S(2)}) collective-permute-start(bf16[2,256,256]{2,1,0:T(8,128)(2,1)S(1)} %get-tuple-element.7.refs_3_), channel_id=1, source_target_pairs={{0,4},{4,0},{8,12},{12,8},{16,20},{20,16},{24,28},{28,24},{1,5},{5... | collective-permute-start | bytes 786440 | tf_op jit(solution)/shard_map/ppermute | solution.py:41
  95.3 4.3 %collective-permute-start.7 = (bf16[2,256,256]{2,1,0:T(8,128)(2,1)S(1)}, bf16[2,256,256]{2,1,0:T(8,128)(2,1)S(1)}, u32[]{:S(2)}, u32[]{:S(2)}) collective-permute-start(bf16[2,256,256]{2,1,0:T(8,128)(2,1)S(1)} %collective-permute-done.6.refs_1_), channel_id=1, source_target_pairs={{0,8},{4,12},{8,16},{12,20},{16,24},{20,28},{1,9},{5,13},{9,17},{1... | collective-permute-start | bytes 786440 | tf_op jit(solution)/shard_map/ppermute | solution.py:44
  99.6 1.3 %collective-permute-start.10 = (bf16[2,256,256]{2,1,0:T(8,128)(2,1)S(1)}, bf16[2,256,256]{2,1,0:T(8,128)(2,1)S(1)}, u32[]{:S(2)}, u32[]{:S(2)}) collective-permute-start(bf16[2,256,256]{2,1,0:T(8,128)(2,1)S(1)} %collective-permute-done.9.refs_5_), channel_id=1, source_target_pairs={{8,0},{12,4},{16,8},{20,12},{24,16},{28,20},{9,1},{13,5},{17,9},{2... | collective-permute-start | bytes 786440 | tf_op jit(solution)/shard_map/ppermute | solution.py:45
  100.9 3.0 %fusion.2 = f32[1,1,2,256,256]{4,3,2,1,0:T(8,128)} fusion(f32[1,1,2,256,256]{4,3,2,1,0:T(8,128)} %param.13, f32[2,256,256]{2,1,0:T(8,128)S(1)} %convert_reduce_fusion, f32[2]{0:T(128)S(1)} %convert_element_type.35, pred[2]{0:T(512)(128)(4,1)S(1)} %dynamic-slice_reduce_fusion), kind=kOutput, calls=%fused_computation.5 | convolution fusion | flops 403308544 | bytes 1572874 | tf_op jit(solution)/shard_map/sji,sjk->sik/dot_general | solution.py:142
  103.9 2.7 %fusion.5 = f32[1,1,2,256,256]{4,3,2,1,0:T(8,128)} fusion(f32[1,1,2,256,256]{4,3,2,1,0:T(8,128)} %param.12, f32[2,256,256]{2,1,0:T(8,128)S(1)} %convert_reduce_fusion, f32[2]{0:T(128)S(1)} %convert_element_type.35, pred[2]{0:T(512)(128)(4,1)S(1)} %dynamic-slice_reduce_fusion), kind=kOutput, calls=%fused_computation.9 | convolution fusion | flops 403308544 | bytes 1572874 | tf_op jit(solution)/shard_map/sij,skj->sik/dot_general | solution.py:139
  106.6 1.9 %collective-permute-start.15 = (bf16[2,256,256]{2,1,0:T(8,128)(2,1)S(1)}, bf16[2,256,256]{2,1,0:T(8,128)(2,1)S(1)}, u32[]{:S(2)}, u32[]{:S(2)}) collective-permute-start(bf16[2,256,256]{2,1,0:T(8,128)(2,1)S(1)} %collective-permute-done.8.refs_4_), channel_id=1, source_target_pairs={{0,4},{4,0},{8,12},{12,8},{16,20},{20,16},{24,28},{28,24},{1,5},{5... | collective-permute-start | bytes 786440 | tf_op jit(solution)/shard_map/ppermute | solution.py:47
  109.1 1.1 collective-permute-start.17
  112.9 3.1 %shard_map.128 = bf16[8,256,256]{2,1,0:T(8,128)(2,1)} custom-call(s32[8,2]{1,0:T(8,128)} %copy.39.table_ref, bf16[2,256,256]{2,1,0:T(8,128)(2,1)} %copy-done.11, bf16[2,256,256]{2,1,0:T(8,128)(2,1)} %copy-done.7, bf16[2,256,256]{2,1,0:T(8,128)(2,1)} %copy-done.5, bf16[2,256,256]{2,1,0:T(8,128)(2,1)} %copy-done.2, bf16[2,256,256]{2,1,0:T(8,128)(2,1)} %copy-done.6, ...), custom_call_target="tpu_custom_call" | custom-call | tf_op jit(solution)/shard_map/pallas_call | solution.py:79
  (88 shorter events, 10.3 us)
Async XLA Ops:
  4.6 54.8 %all-to-all-start = ((bf16[8,2,256,256]{3,2,1,0:T(8,128)(2,1)}), bf16[8,2,256,256]{3,2,1,0:T(8,128)(2,1)}, u32[]{:S(2)}, u32[]{:S(2)}) async-start(bf16[8,2,256,256]{3,2,1,0:T(8,128)(2,1)} %bitcast.3), calls=%async_computation | async-start | bytes 4194304 | tf_op jit(solution)/shard_map/all_to_all | solution.py:123
  11.1 50.2 %copy-start.1 = (f32[1,1,2,256,256]{4,3,2,1,0:T(8,128)S(1)}, f32[1,1,2,256,256]{4,3,2,1,0:T(8,128)}, u32[]{:S(2)}) copy-start(f32[1,1,2,256,256]{4,3,2,1,0:T(8,128)} %param.16) | copy-start | bytes 1572868
  11.1 50.7 %copy-start.4 = (bf16[1,1,2,256,256]{4,3,2,1,0:T(8,128)(2,1)S(1)}, bf16[1,1,2,256,256]{4,3,2,1,0:T(8,128)(2,1)}, u32[]{:S(2)}) copy-start(bf16[1,1,2,256,256]{4,3,2,1,0:T(8,128)(2,1)} %param.15) | copy-start | bytes 786436
  12.0 64.2 %copy-start.3 = (f32[1,1,2,256,256]{4,3,2,1,0:T(8,128)S(1)}, f32[1,1,2,256,256]{4,3,2,1,0:T(8,128)}, u32[]{:S(2)}) copy-start(f32[1,1,2,256,256]{4,3,2,1,0:T(8,128)} %param.17) | copy-start | bytes 1572868
  63.5 1.8 %collective-permute-start = (f32[2,9]{1,0:T(2,128)S(1)}, f32[2,9]{1,0:T(2,128)S(1)}, u32[]{:S(2)}, u32[]{:S(2)}) collective-permute-start(f32[2,9]{1,0:T(2,128)S(1)} %pad_maximum_fusion), channel_id=1, source_target_pairs={{0,4},{4,0},{8,12},{12,8},{16,20},{20,16},{24,28},{28,24},{1,5},{5... | collective-permute-start | bytes 224 | tf_op jit(solution)/shard_map/ppermute | solution.py:20
  65.3 2.5 %collective-permute-start.1 = (f32[2,9]{1,0:T(2,128)S(1)}, f32[2,9]{1,0:T(2,128)S(1)}, u32[]{:S(2)}, u32[]{:S(2)}) collective-permute-start(f32[2,9]{1,0:T(2,128)S(1)} %fusion.30), channel_id=1, source_target_pairs={{0,8},{4,12},{8,0},{12,4},{16,24},{20,28},{24,16},{28,20},{1,9},{5... | collective-permute-start | bytes 224 | tf_op jit(solution)/shard_map/ppermute | solution.py:20
  67.8 3.4 %collective-permute-start.2 = (f32[2,9]{1,0:T(2,128)S(1)}, f32[2,9]{1,0:T(2,128)S(1)}, u32[]{:S(2)}, u32[]{:S(2)}) collective-permute-start(f32[2,9]{1,0:T(2,128)S(1)} %fusion.35), channel_id=1, source_target_pairs={{0,16},{4,20},{8,24},{12,28},{16,0},{20,4},{24,8},{28,12},{1,17},{... | collective-permute-start | bytes 224 | tf_op jit(solution)/shard_map/ppermute | solution.py:20
  71.2 2.4 %collective-permute-start.3 = (f32[2,9]{1,0:T(2,128)S(1)}, f32[2,9]{1,0:T(2,128)S(1)}, u32[]{:S(2)}, u32[]{:S(2)}) collective-permute-start(f32[2,9]{1,0:T(2,128)S(1)} %add.92), channel_id=1, source_target_pairs={{0,1},{1,0},{2,3},{3,2},{4,5},{5,4},{6,7},{7,6},{8,9},{9,8},{10,11... | collective-permute-start | bytes 224 | tf_op jit(solution)/shard_map/ppermute | solution.py:20
  73.6 2.4 %collective-permute-start.4 = (f32[2,9]{1,0:T(2,128)S(1)}, f32[2,9]{1,0:T(2,128)S(1)}, u32[]{:S(2)}, u32[]{:S(2)}) collective-permute-start(f32[2,9]{1,0:T(2,128)S(1)} %add.93), channel_id=1, source_target_pairs={{0,2},{1,3},{2,0},{3,1},{4,6},{5,7},{6,4},{7,5},{8,10},{9,11},{10,... | collective-permute-start | bytes 224 | tf_op jit(solution)/shard_map/ppermute | solution.py:20
  77.2 34.0 %copy-start.2 = (bf16[2,256,256]{2,1,0:T(8,128)(2,1)}, bf16[2,256,256]{2,1,0:T(8,128)(2,1)S(1)}, u32[]{:S(2)}) copy-start(bf16[2,256,256]{2,1,0:T(8,128)(2,1)S(1)} %get-tuple-element.7.refs_3_) | copy-start | bytes 786436
  77.2 5.2 %collective-permute-start.5 = (bf16[2,256,256]{2,1,0:T(8,128)(2,1)S(1)}, bf16[2,256,256]{2,1,0:T(8,128)(2,1)S(1)}, u32[]{:S(2)}, u32[]{:S(2)}) collective-permute-start(bf16[2,256,256]{2,1,0:T(8,128)(2,1)S(1)} %get-tuple-element.7.refs_3_), channel_id=1, source_target_pairs={{0,8},{4,12},{8,16},{12,20},{16,24},{20,28},{1,9},{5,13},{9,17},{1... | collective-permute-start | bytes 786440 | tf_op jit(solution)/shard_map/ppermute | solution.py:44
  79.1 7.1 %collective-permute-start.8 = (bf16[2,256,256]{2,1,0:T(8,128)(2,1)S(1)}, bf16[2,256,256]{2,1,0:T(8,128)(2,1)S(1)}, u32[]{:S(2)}, u32[]{:S(2)}) collective-permute-start(bf16[2,256,256]{2,1,0:T(8,128)(2,1)S(1)} %get-tuple-element.7.refs_3_), channel_id=1, source_target_pairs={{8,0},{12,4},{16,8},{20,12},{24,16},{28,20},{9,1},{13,5},{17,9},{2... | collective-permute-start | bytes 786440 | tf_op jit(solution)/shard_map/ppermute | solution.py:45
  82.4 28.8 %copy-start.5 = (bf16[2,256,256]{2,1,0:T(8,128)(2,1)}, bf16[2,256,256]{2,1,0:T(8,128)(2,1)S(1)}, u32[]{:S(2)}) copy-start(bf16[2,256,256]{2,1,0:T(8,128)(2,1)S(1)} %collective-permute-done.5.refs_2_) | copy-start | bytes 786436
  82.4 12.9 %collective-permute-start.6 = (bf16[2,256,256]{2,1,0:T(8,128)(2,1)S(1)}, bf16[2,256,256]{2,1,0:T(8,128)(2,1)S(1)}, u32[]{:S(2)}, u32[]{:S(2)}) collective-permute-start(bf16[2,256,256]{2,1,0:T(8,128)(2,1)S(1)} %collective-permute-done.5.refs_2_), channel_id=1, source_target_pairs={{0,8},{4,12},{8,16},{12,20},{16,24},{20,28},{1,9},{5,13},{9,17},{1... | collective-permute-start | bytes 786440 | tf_op jit(solution)/shard_map/ppermute | solution.py:44
  86.3 13.4 %collective-permute-start.9 = (bf16[2,256,256]{2,1,0:T(8,128)(2,1)S(1)}, bf16[2,256,256]{2,1,0:T(8,128)(2,1)S(1)}, u32[]{:S(2)}, u32[]{:S(2)}) collective-permute-start(bf16[2,256,256]{2,1,0:T(8,128)(2,1)S(1)} %collective-permute-done.8.refs_4_), channel_id=1, source_target_pairs={{8,0},{12,4},{16,8},{20,12},{24,16},{28,20},{9,1},{13,5},{17,9},{2... | collective-permute-start | bytes 786440 | tf_op jit(solution)/shard_map/ppermute | solution.py:45
  88.3 20.2 %collective-permute-start.14 = (bf16[2,256,256]{2,1,0:T(8,128)(2,1)S(1)}, bf16[2,256,256]{2,1,0:T(8,128)(2,1)S(1)}, u32[]{:S(2)}, u32[]{:S(2)}) collective-permute-start(bf16[2,256,256]{2,1,0:T(8,128)(2,1)S(1)} %get-tuple-element.7.refs_3_), channel_id=1, source_target_pairs={{0,4},{4,0},{8,12},{12,8},{16,20},{20,16},{24,28},{28,24},{1,5},{5... | collective-permute-start | bytes 786440 | tf_op jit(solution)/shard_map/ppermute | solution.py:41
  95.3 13.3 %collective-permute-start.13 = (bf16[2,256,256]{2,1,0:T(8,128)(2,1)S(1)}, bf16[2,256,256]{2,1,0:T(8,128)(2,1)S(1)}, u32[]{:S(2)}, u32[]{:S(2)}) collective-permute-start(bf16[2,256,256]{2,1,0:T(8,128)(2,1)S(1)} %collective-permute-done.5.refs_2_), channel_id=1, source_target_pairs={{0,4},{4,0},{8,12},{12,8},{16,20},{20,16},{24,28},{28,24},{1,5},{5... | collective-permute-start | bytes 786440 | tf_op jit(solution)/shard_map/ppermute | solution.py:46
  95.3 13.7 %collective-permute-start.7 = (bf16[2,256,256]{2,1,0:T(8,128)(2,1)S(1)}, bf16[2,256,256]{2,1,0:T(8,128)(2,1)S(1)}, u32[]{:S(2)}, u32[]{:S(2)}) collective-permute-start(bf16[2,256,256]{2,1,0:T(8,128)(2,1)S(1)} %collective-permute-done.6.refs_1_), channel_id=1, source_target_pairs={{0,8},{4,12},{8,16},{12,20},{16,24},{20,28},{1,9},{5,13},{9,17},{1... | collective-permute-start | bytes 786440 | tf_op jit(solution)/shard_map/ppermute | solution.py:44
  99.6 9.5 %collective-permute-start.10 = (bf16[2,256,256]{2,1,0:T(8,128)(2,1)S(1)}, bf16[2,256,256]{2,1,0:T(8,128)(2,1)S(1)}, u32[]{:S(2)}, u32[]{:S(2)}) collective-permute-start(bf16[2,256,256]{2,1,0:T(8,128)(2,1)S(1)} %collective-permute-done.9.refs_5_), channel_id=1, source_target_pairs={{8,0},{12,4},{16,8},{20,12},{24,16},{28,20},{9,1},{13,5},{17,9},{2... | collective-permute-start | bytes 786440 | tf_op jit(solution)/shard_map/ppermute | solution.py:45
  106.6 4.7 %collective-permute-start.15 = (bf16[2,256,256]{2,1,0:T(8,128)(2,1)S(1)}, bf16[2,256,256]{2,1,0:T(8,128)(2,1)S(1)}, u32[]{:S(2)}, u32[]{:S(2)}) collective-permute-start(bf16[2,256,256]{2,1,0:T(8,128)(2,1)S(1)} %collective-permute-done.8.refs_4_), channel_id=1, source_target_pairs={{0,4},{4,0},{8,12},{12,8},{16,20},{20,16},{24,28},{28,24},{1,5},{5... | collective-permute-start | bytes 786440 | tf_op jit(solution)/shard_map/ppermute | solution.py:47
  108.5 2.8 %collective-permute-start.12 = (bf16[2,256,256]{2,1,0:T(8,128)(2,1)S(1)}, bf16[2,256,256]{2,1,0:T(8,128)(2,1)S(1)}, u32[]{:S(2)}, u32[]{:S(2)}) collective-permute-start(bf16[2,256,256]{2,1,0:T(8,128)(2,1)S(1)} %collective-permute-done.6.refs_1_), channel_id=1, source_target_pairs={{0,4},{4,0},{8,12},{12,8},{16,20},{20,16},{24,28},{28,24},{1,5},{5... | collective-permute-start | bytes 786440 | tf_op jit(solution)/shard_map/ppermute | solution.py:46
  108.6 2.7 %collective-permute-start.16 = (bf16[2,256,256]{2,1,0:T(8,128)(2,1)S(1)}, bf16[2,256,256]{2,1,0:T(8,128)(2,1)S(1)}, u32[]{:S(2)}, u32[]{:S(2)}) collective-permute-start(bf16[2,256,256]{2,1,0:T(8,128)(2,1)S(1)} %collective-permute-done.9.refs_5_), channel_id=1, source_target_pairs={{0,4},{4,0},{8,12},{12,8},{16,20},{20,16},{24,28},{28,24},{1,5},{5... | collective-permute-start | bytes 786440 | tf_op jit(solution)/shard_map/ppermute | solution.py:47
  109.0 2.3 %collective-permute-start.11 = (bf16[2,256,256]{2,1,0:T(8,128)(2,1)S(1)}, bf16[2,256,256]{2,1,0:T(8,128)(2,1)S(1)}, u32[]{:S(2)}, u32[]{:S(2)}) collective-permute-start(bf16[2,256,256]{2,1,0:T(8,128)(2,1)S(1)} %collective-permute-done.7.refs_0_), channel_id=1, source_target_pairs={{0,4},{4,0},{8,12},{12,8},{16,20},{20,16},{24,28},{28,24},{1,5},{5... | collective-permute-start | bytes 786440 | tf_op jit(solution)/shard_map/ppermute | solution.py:46
  109.1 3.7 %collective-permute-start.17 = (bf16[2,256,256]{2,1,0:T(8,128)(2,1)S(1)}, bf16[2,256,256]{2,1,0:T(8,128)(2,1)}, u32[]{:S(2)}, u32[]{:S(2)}) collective-permute-start(bf16[2,256,256]{2,1,0:T(8,128)(2,1)S(1)} %collective-permute-done.10.refs_6_), channel_id=1, source_target_pairs={{0,4},{4,0},{8,12},{12,8},{16,20},{20,16},{24,28},{28,24},{1,5},{5... | collective-permute-start | bytes 786440 | tf_op jit(solution)/shard_map/ppermute | solution.py:47
  (14 other events, 100.7 us)

commit v9 on v8

--- a/solution.py
+++ b/solution.py
@@ -29,23 +29,16 @@
         gathered = lax.all_gather(mine, "dp", axis=0, tiled=True)
         return jnp.take(gathered, owner_of * slot_count + slot_rank, axis=0)
     chips = size // 2
-    rightward = [(i, i + 2) for i in range(size - 2)]
-    leftward = [(i + 2, i) for i in range(size - 2)]
     partner = [(i, i ^ 1) for i in range(size)]
-    from_left = [None] * chips
-    from_right = [None] * chips
-    from_left[0] = mine
-    from_right[0] = mine
-    near_left = [None] * chips
-    near_right = [None] * chips
-    near_left[0] = lax.ppermute(mine, "dp", partner)
-    near_right[0] = near_left[0]
-    for step in range(1, chips):
-        from_left[step] = lax.ppermute(from_left[step - 1], "dp", rightward)
-        from_right[step] = lax.ppermute(from_right[step - 1], "dp", leftward)
-        near_left[step] = lax.ppermute(from_left[step], "dp", partner)
-        near_right[step] = lax.ppermute(from_right[step], "dp", partner)
-    pieces = from_left[::-1] + from_right[1:] + near_left[::-1] + near_right[1:]
+    same_core = []
+    for offset in range(1 - chips, chips):
+        if offset == 0:
+            same_core.append(mine)
+            continue
+        pairs = [(i, i - 2 * offset) for i in range(size) if 0 <= i - 2 * offset < size]
+        same_core.append(lax.ppermute(mine, "dp", pairs))
+    other_core = [lax.ppermute(piece, "dp", partner) for piece in same_core]
+    pieces = same_core + other_core
     chip, core = replica // 2, replica % 2
     owner_chip, owner_core = owner_of // 2, owner_of % 2
     offset = owner_chip - chip + chips - 1

time: 117 us -> 119 us (1.017)
  starting transfers between devices: 34.6 us -> 38.5 us
  waiting for transfers between devices: 58.3 us -> 56.9 us
    ppermute x13, starting transfers between devices: 24.6 us -> 28.5 us  [the longest x7 18.2 us: gather_blocks(): other_core = [lax.ppermute(piece, 'dp', partner) for piece in same_core]]
    ppermute x13, waiting for transfers between devices: 1.99 us -> 0.65 us  [the longest x7 0.64 us: gather_blocks(): other_core = [lax.ppermute(piece, 'dp', partner) for piece in same_core]]
where the time goes in v9:
time: 119 us; the launch traced here: 118 us
  waiting for transfers between devices  56.9 us (48%)
  starting transfers between devices  38.5 us (32%)
  matrix products  7.28 us (6%)
  other arithmetic  7.11 us (6%)
  local copies, waits for them, and re-layouts  4.01 us (3%)
  Pallas kernels  3.13 us (3%)
    all_to_all x1, waiting for transfers between devices, local(): received = lax.all_to_all(by_owner, 'dp', 0, 0, tiled=True)  47.4 us
    ppermute x7, starting transfers between devices, gather_blocks(): other_core = [lax.ppermute(piece, 'dp', partner) for piece in same_core]  18.2 us
    ppermute x6, starting transfers between devices, gather_blocks(): same_core.append(lax.ppermute(mine, 'dp', pairs))  10.3 us
    ppermute x5, waiting for transfers between devices, butterfly_sum(): x = x + lax.ppermute(x, axis, [(i, i ^ step) for i in range(size)])  8.9 us
    all_to_all x1, starting transfers between devices, local(): received = lax.all_to_all(by_owner, 'dp', 0, 0, tiled=True)  6.51 us
    ppermute x5, starting transfers between devices, butterfly_sum(): x = x + lax.ppermute(x, axis, [(i, i ^ step) for i in range(size)])  3.53 us
    pallas_call x1, Pallas kernels, pick_blocks(): pl.pallas_call(pick_kernel, out_shape=jax.ShapeDtypeStruct((blocks,) + pi...  3.13 us
    dot_general x1, matrix products, local(): jnp.einsum('sji,sjk->sik', owned_grad, owned_grad, precision=highest)  2.98 us
  transfers between devices with their start and end apart: 19, of which 7 were waited for; matrix products, arithmetic and copies ran while one was open for 7% of the time, Pallas kernels for 0%

profile of v9, /device:TPU:1, one launch (start us, length us, event | category | flops | bytes accessed | tf_op | source)
XLA Modules:
  0.0 117.9 jit_solution(16176576188916755767)
XLA Ops:
  2.6 2.0 %gather_fusion = bf16[16,256,256]{2,1,0:T(8,128)(2,1)} fusion(bf16[8,256,256]{2,1,0:T(8,128)(2,1)S(1)} %bitcast.52, s32[1024]{0:T(1024)S(1)} %pad_clamp_fusion), kind=kCustom, calls=%fused_computation | custom fusion | bytes 4194368 | tf_op jit(solution)/shard_map/jit(_take)/gather | solution.py:113
  4.6 6.5 %all-to-all-start = ((bf16[8,2,256,256]{3,2,1,0:T(8,128)(2,1)}), bf16[8,2,256,256]{3,2,1,0:T(8,128)(2,1)}, u32[]{:S(2)}, u32[]{:S(2)}) async-start(bf16[8,2,256,256]{3,2,1,0:T(8,128)(2,1)} %bitcast.3), calls=%async_computation | async-start | bytes 4194304 | tf_op jit(solution)/shard_map/all_to_all | solution.py:116
  12.0 47.4 %all-to-all-done = bf16[8,2,256,256]{3,2,1,0:T(8,128)(2,1)} async-done(((bf16[8,2,256,256]{3,2,1,0:T(8,128)(2,1)}), bf16[8,2,256,256]{3,2,1,0:T(8,128)(2,1)}, u32[]{:S(2)}, u32[]{:S(2)}) %all-to-all-start) | async-done | bytes 2097184 | tf_op jit(solution)/shard_map/all_to_all | solution.py:116
  59.4 1.9 %convert_reduce_fusion = f32[2,256,256]{2,1,0:T(8,128)S(1)} fusion(bf16[8,2,256,256]{3,2,1,0:T(8,128)(2,1)} %all-to-all-done), kind=kLoop, calls=%fused_computation.1 | loop fusion | flops 1966080 | bytes 2621440 | tf_op jit(solution)/shard_map/reduce_sum | solution.py:117
  61.8 1.6 %multiply_reduce_fusion = (f32[2]{0:T(128)S(1)}, f32[2,256,256]{2,1,0:T(8,128)S(1)}) fusion(bf16[1,1,2,256,256]{4,3,2,1,0:T(8,128)(2,1)S(1)} %copy-done.4, f32[2,256,256]{2,1,0:T(8,128)S(1)} %convert_reduce_fusion, bf16[1,1,2,256,256]{4,3,2,1,0:T(8,128)(2,1)} %param.14, f32[2]{0:T(128)S(1)} %convert_element_type.35), kind=kOutput, calls=%fused_computation.25 | convolution fusion | flops 134873088 | bytes 1572880 | tf_op jit(solution)/shard_map/sij,sjk->sik/dot_general | solution.py:142
  65.4 2.4 %collective-permute-done.1 = f32[2,9]{1,0:T(2,128)S(1)} collective-permute-done((f32[2,9]{1,0:T(2,128)S(1)}, f32[2,9]{1,0:T(2,128)S(1)}, u32[]{:S(2)}, u32[]{:S(2)}) %collective-permute-start.1) | collective-permute-done | bytes 104 | tf_op jit(solution)/shard_map/ppermute | solution.py:20
  67.9 3.3 %collective-permute-done.2 = f32[2,9]{1,0:T(2,128)S(1)} collective-permute-done((f32[2,9]{1,0:T(2,128)S(1)}, f32[2,9]{1,0:T(2,128)S(1)}, u32[]{:S(2)}, u32[]{:S(2)}) %collective-permute-start.2) | collective-permute-done | bytes 104 | tf_op jit(solution)/shard_map/ppermute | solution.py:20
  71.2 1.2 %collective-permute-start.3 = (f32[2,9]{1,0:T(2,128)S(1)}, f32[2,9]{1,0:T(2,128)S(1)}, u32[]{:S(2)}, u32[]{:S(2)}) collective-permute-start(f32[2,9]{1,0:T(2,128)S(1)} %add.92), channel_id=1, source_target_pairs={{0,1},{1,0},{2,3},{3,2},{4,5},{5,4},{6,7},{7,6},{8,9},{9,8},{10,11... | collective-permute-start | bytes 224 | tf_op jit(solution)/shard_map/ppermute | solution.py:20
  72.4 1.2 %collective-permute-done.3 = f32[2,9]{1,0:T(2,128)S(1)} collective-permute-done((f32[2,9]{1,0:T(2,128)S(1)}, f32[2,9]{1,0:T(2,128)S(1)}, u32[]{:S(2)}, u32[]{:S(2)}) %collective-permute-start.3) | collective-permute-done | bytes 104 | tf_op jit(solution)/shard_map/ppermute | solution.py:20
  73.6 1.2 %collective-permute-start.4 = (f32[2,9]{1,0:T(2,128)S(1)}, f32[2,9]{1,0:T(2,128)S(1)}, u32[]{:S(2)}, u32[]{:S(2)}) collective-permute-start(f32[2,9]{1,0:T(2,128)S(1)} %add.93), channel_id=1, source_target_pairs={{0,2},{1,3},{2,0},{3,1},{4,6},{5,7},{6,4},{7,5},{8,10},{9,11},{10,... | collective-permute-start | bytes 224 | tf_op jit(solution)/shard_map/ppermute | solution.py:20
  74.9 1.2 collective-permute-done.4
  77.2 2.9 %collective-permute-start.5 = (bf16[2,256,256]{2,1,0:T(8,128)(2,1)S(1)}, bf16[2,256,256]{2,1,0:T(8,128)(2,1)S(1)}, u32[]{:S(2)}, u32[]{:S(2)}) collective-permute-start(bf16[2,256,256]{2,1,0:T(8,128)(2,1)S(1)} %get-tuple-element.7.refs_3_), channel_id=1, source_target_pairs={{0,24},{4,28},{1,25},{5,29},{2,26},{6,30},{3,27},{7,31}} | collective-permute-start | bytes 786440 | tf_op jit(solution)/shard_map/ppermute | solution.py:39
  80.1 1.3 %collective-permute-start.6 = (bf16[2,256,256]{2,1,0:T(8,128)(2,1)S(1)}, bf16[2,256,256]{2,1,0:T(8,128)(2,1)S(1)}, u32[]{:S(2)}, u32[]{:S(2)}) collective-permute-start(bf16[2,256,256]{2,1,0:T(8,128)(2,1)S(1)} %get-tuple-element.7.refs_3_), channel_id=1, source_target_pairs={{0,16},{4,20},{8,24},{12,28},{1,17},{5,21},{9,25},{13,29},{2,18},{... | collective-permute-start | bytes 786440 | tf_op jit(solution)/shard_map/ppermute | solution.py:39
  81.4 2.2 %collective-permute-start.7 = (bf16[2,256,256]{2,1,0:T(8,128)(2,1)S(1)}, bf16[2,256,256]{2,1,0:T(8,128)(2,1)S(1)}, u32[]{:S(2)}, u32[]{:S(2)}) collective-permute-start(bf16[2,256,256]{2,1,0:T(8,128)(2,1)S(1)} %get-tuple-element.7.refs_3_), channel_id=1, source_target_pairs={{0,8},{4,12},{8,16},{12,20},{16,24},{20,28},{1,9},{5,13},{9,17},{1... | collective-permute-start | bytes 786440 | tf_op jit(solution)/shard_map/ppermute | solution.py:39
  84.3 1.3 %collective-permute-start.8 = (bf16[2,256,256]{2,1,0:T(8,128)(2,1)S(1)}, bf16[2,256,256]{2,1,0:T(8,128)(2,1)S(1)}, u32[]{:S(2)}, u32[]{:S(2)}) collective-permute-start(bf16[2,256,256]{2,1,0:T(8,128)(2,1)S(1)} %get-tuple-element.7.refs_3_), channel_id=1, source_target_pairs={{8,0},{12,4},{16,8},{20,12},{24,16},{28,20},{9,1},{13,5},{17,9},{2... | collective-permute-start | bytes 786440 | tf_op jit(solution)/shard_map/ppermute | solution.py:39
  85.6 1.3 %collective-permute-start.9 = (bf16[2,256,256]{2,1,0:T(8,128)(2,1)S(1)}, bf16[2,256,256]{2,1,0:T(8,128)(2,1)S(1)}, u32[]{:S(2)}, u32[]{:S(2)}) collective-permute-start(bf16[2,256,256]{2,1,0:T(8,128)(2,1)S(1)} %get-tuple-element.7.refs_3_), channel_id=1, source_target_pairs={{16,0},{20,4},{24,8},{28,12},{17,1},{21,5},{25,9},{29,13},{18,2},{... | collective-permute-start | bytes 786440 | tf_op jit(solution)/shard_map/ppermute | solution.py:39
  86.9 1.3 %collective-permute-start.10 = (bf16[2,256,256]{2,1,0:T(8,128)(2,1)S(1)}, bf16[2,256,256]{2,1,0:T(8,128)(2,1)S(1)}, u32[]{:S(2)}, u32[]{:S(2)}) collective-permute-start(bf16[2,256,256]{2,1,0:T(8,128)(2,1)S(1)} %get-tuple-element.7.refs_3_), channel_id=1, source_target_pairs={{24,0},{28,4},{25,1},{29,5},{26,2},{30,6},{27,3},{31,7}} | collective-permute-start | bytes 786440 | tf_op jit(solution)/shard_map/ppermute | solution.py:39
  88.3 6.8 %collective-permute-start.14 = (bf16[2,256,256]{2,1,0:T(8,128)(2,1)S(1)}, bf16[2,256,256]{2,1,0:T(8,128)(2,1)S(1)}, u32[]{:S(2)}, u32[]{:S(2)}) collective-permute-start(bf16[2,256,256]{2,1,0:T(8,128)(2,1)S(1)} %get-tuple-element.7.refs_3_), channel_id=1, source_target_pairs={{0,4},{4,0},{8,12},{12,8},{16,20},{20,16},{24,28},{28,24},{1,5},{5... | collective-permute-start | bytes 786440 | tf_op jit(solution)/shard_map/ppermute | solution.py:40
  95.1 2.8 %collective-permute-start.11 = (bf16[2,256,256]{2,1,0:T(8,128)(2,1)S(1)}, bf16[2,256,256]{2,1,0:T(8,128)(2,1)S(1)}, u32[]{:S(2)}, u32[]{:S(2)}) collective-permute-start(bf16[2,256,256]{2,1,0:T(8,128)(2,1)S(1)} %collective-permute-done.5.refs_0_), channel_id=1, source_target_pairs={{0,4},{4,0},{8,12},{12,8},{16,20},{20,16},{24,28},{28,24},{1,5},{5... | collective-permute-start | bytes 786440 | tf_op jit(solution)/shard_map/ppermute | solution.py:40
  97.9 3.0 %fusion.2 = f32[1,1,2,256,256]{4,3,2,1,0:T(8,128)} fusion(f32[1,1,2,256,256]{4,3,2,1,0:T(8,128)} %param.13, f32[2,256,256]{2,1,0:T(8,128)S(1)} %convert_reduce_fusion, f32[2]{0:T(128)S(1)} %convert_element_type.35, pred[2]{0:T(512)(128)(4,1)S(1)} %dynamic-slice_reduce_fusion), kind=kOutput, calls=%fused_computation.5 | convolution fusion | flops 403308544 | bytes 1572874 | tf_op jit(solution)/shard_map/sji,sjk->sik/dot_general | solution.py:135
  100.9 2.7 %fusion.5 = f32[1,1,2,256,256]{4,3,2,1,0:T(8,128)} fusion(f32[1,1,2,256,256]{4,3,2,1,0:T(8,128)} %param.12, f32[2,256,256]{2,1,0:T(8,128)S(1)} %convert_reduce_fusion, f32[2]{0:T(128)S(1)} %convert_element_type.35, pred[2]{0:T(512)(128)(4,1)S(1)} %dynamic-slice_reduce_fusion), kind=kOutput, calls=%fused_computation.9 | convolution fusion | flops 403308544 | bytes 1572874 | tf_op jit(solution)/shard_map/sij,skj->sik/dot_general | solution.py:132
  103.7 7.9 %collective-permute-start.13 = (bf16[2,256,256]{2,1,0:T(8,128)(2,1)S(1)}, bf16[2,256,256]{2,1,0:T(8,128)(2,1)S(1)}, u32[]{:S(2)}, u32[]{:S(2)}) collective-permute-start(bf16[2,256,256]{2,1,0:T(8,128)(2,1)S(1)} %collective-permute-done.7.refs_2_), channel_id=1, source_target_pairs={{0,4},{4,0},{8,12},{12,8},{16,20},{20,16},{24,28},{28,24},{1,5},{5... | collective-permute-start | bytes 786440 | tf_op jit(solution)/shard_map/ppermute | solution.py:40
  112.2 1.0 fusion.8
  114.8 3.1 %shard_map.128 = bf16[8,256,256]{2,1,0:T(8,128)(2,1)} custom-call(s32[8,2]{1,0:T(8,128)} %copy.39.table_ref, bf16[2,256,256]{2,1,0:T(8,128)(2,1)} %copy-done.5, bf16[2,256,256]{2,1,0:T(8,128)(2,1)} %copy-done.6, bf16[2,256,256]{2,1,0:T(8,128)(2,1)} %copy-done.7, bf16[2,256,256]{2,1,0:T(8,128)(2,1)} %copy-done.2, bf16[2,256,256]{2,1,0:T(8,128)(2,1)} %copy-done.8, ...), custom_call_target="tpu_custom_call" | custom-call | tf_op jit(solution)/shard_map/pallas_call | solution.py:72
  (88 shorter events, 9.5 us)
Async XLA Ops:
  4.6 54.8 %all-to-all-start = ((bf16[8,2,256,256]{3,2,1,0:T(8,128)(2,1)}), bf16[8,2,256,256]{3,2,1,0:T(8,128)(2,1)}, u32[]{:S(2)}, u32[]{:S(2)}) async-start(bf16[8,2,256,256]{3,2,1,0:T(8,128)(2,1)} %bitcast.3), calls=%async_computation | async-start | bytes 4194304 | tf_op jit(solution)/shard_map/all_to_all | solution.py:116
  11.1 50.2 %copy-start.1 = (f32[1,1,2,256,256]{4,3,2,1,0:T(8,128)S(1)}, f32[1,1,2,256,256]{4,3,2,1,0:T(8,128)}, u32[]{:S(2)}) copy-start(f32[1,1,2,256,256]{4,3,2,1,0:T(8,128)} %param.16) | copy-start | bytes 1572868
  11.1 50.7 %copy-start.4 = (bf16[1,1,2,256,256]{4,3,2,1,0:T(8,128)(2,1)S(1)}, bf16[1,1,2,256,256]{4,3,2,1,0:T(8,128)(2,1)}, u32[]{:S(2)}) copy-start(bf16[1,1,2,256,256]{4,3,2,1,0:T(8,128)(2,1)} %param.15) | copy-start | bytes 786436
  12.0 64.2 %copy-start.3 = (f32[1,1,2,256,256]{4,3,2,1,0:T(8,128)S(1)}, f32[1,1,2,256,256]{4,3,2,1,0:T(8,128)}, u32[]{:S(2)}) copy-start(f32[1,1,2,256,256]{4,3,2,1,0:T(8,128)} %param.17) | copy-start | bytes 1572868
  63.5 1.8 %collective-permute-start = (f32[2,9]{1,0:T(2,128)S(1)}, f32[2,9]{1,0:T(2,128)S(1)}, u32[]{:S(2)}, u32[]{:S(2)}) collective-permute-start(f32[2,9]{1,0:T(2,128)S(1)} %pad_maximum_fusion), channel_id=1, source_target_pairs={{0,4},{4,0},{8,12},{12,8},{16,20},{20,16},{24,28},{28,24},{1,5},{5... | collective-permute-start | bytes 224 | tf_op jit(solution)/shard_map/ppermute | solution.py:20
  65.3 2.5 %collective-permute-start.1 = (f32[2,9]{1,0:T(2,128)S(1)}, f32[2,9]{1,0:T(2,128)S(1)}, u32[]{:S(2)}, u32[]{:S(2)}) collective-permute-start(f32[2,9]{1,0:T(2,128)S(1)} %fusion.30), channel_id=1, source_target_pairs={{0,8},{4,12},{8,0},{12,4},{16,24},{20,28},{24,16},{28,20},{1,9},{5... | collective-permute-start | bytes 224 | tf_op jit(solution)/shard_map/ppermute | solution.py:20
  67.8 3.4 %collective-permute-start.2 = (f32[2,9]{1,0:T(2,128)S(1)}, f32[2,9]{1,0:T(2,128)S(1)}, u32[]{:S(2)}, u32[]{:S(2)}) collective-permute-start(f32[2,9]{1,0:T(2,128)S(1)} %fusion.35), channel_id=1, source_target_pairs={{0,16},{4,20},{8,24},{12,28},{16,0},{20,4},{24,8},{28,12},{1,17},{... | collective-permute-start | bytes 224 | tf_op jit(solution)/shard_map/ppermute | solution.py:20
  71.2 2.4 %collective-permute-start.3 = (f32[2,9]{1,0:T(2,128)S(1)}, f32[2,9]{1,0:T(2,128)S(1)}, u32[]{:S(2)}, u32[]{:S(2)}) collective-permute-start(f32[2,9]{1,0:T(2,128)S(1)} %add.92), channel_id=1, source_target_pairs={{0,1},{1,0},{2,3},{3,2},{4,5},{5,4},{6,7},{7,6},{8,9},{9,8},{10,11... | collective-permute-start | bytes 224 | tf_op jit(solution)/shard_map/ppermute | solution.py:20
  73.6 2.4 %collective-permute-start.4 = (f32[2,9]{1,0:T(2,128)S(1)}, f32[2,9]{1,0:T(2,128)S(1)}, u32[]{:S(2)}, u32[]{:S(2)}) collective-permute-start(f32[2,9]{1,0:T(2,128)S(1)} %add.93), channel_id=1, source_target_pairs={{0,2},{1,3},{2,0},{3,1},{4,6},{5,7},{6,4},{7,5},{8,10},{9,11},{10,... | collective-permute-start | bytes 224 | tf_op jit(solution)/shard_map/ppermute | solution.py:20
  77.2 35.9 %copy-start.2 = (bf16[2,256,256]{2,1,0:T(8,128)(2,1)}, bf16[2,256,256]{2,1,0:T(8,128)(2,1)S(1)}, u32[]{:S(2)}) copy-start(bf16[2,256,256]{2,1,0:T(8,128)(2,1)S(1)} %get-tuple-element.7.refs_3_) | copy-start | bytes 786436
  77.2 9.7 %collective-permute-start.5 = (bf16[2,256,256]{2,1,0:T(8,128)(2,1)S(1)}, bf16[2,256,256]{2,1,0:T(8,128)(2,1)S(1)}, u32[]{:S(2)}, u32[]{:S(2)}) collective-permute-start(bf16[2,256,256]{2,1,0:T(8,128)(2,1)S(1)} %get-tuple-element.7.refs_3_), channel_id=1, source_target_pairs={{0,24},{4,28},{1,25},{5,29},{2,26},{6,30},{3,27},{7,31}} | collective-permute-start | bytes 786440 | tf_op jit(solution)/shard_map/ppermute | solution.py:39
  80.1 8.1 %collective-permute-start.6 = (bf16[2,256,256]{2,1,0:T(8,128)(2,1)S(1)}, bf16[2,256,256]{2,1,0:T(8,128)(2,1)S(1)}, u32[]{:S(2)}, u32[]{:S(2)}) collective-permute-start(bf16[2,256,256]{2,1,0:T(8,128)(2,1)S(1)} %get-tuple-element.7.refs_3_), channel_id=1, source_target_pairs={{0,16},{4,20},{8,24},{12,28},{1,17},{5,21},{9,25},{13,29},{2,18},{... | collective-permute-start | bytes 786440 | tf_op jit(solution)/shard_map/ppermute | solution.py:39
  81.4 13.7 %collective-permute-start.7 = (bf16[2,256,256]{2,1,0:T(8,128)(2,1)S(1)}, bf16[2,256,256]{2,1,0:T(8,128)(2,1)S(1)}, u32[]{:S(2)}, u32[]{:S(2)}) collective-permute-start(bf16[2,256,256]{2,1,0:T(8,128)(2,1)S(1)} %get-tuple-element.7.refs_3_), channel_id=1, source_target_pairs={{0,8},{4,12},{8,16},{12,20},{16,24},{20,28},{1,9},{5,13},{9,17},{1... | collective-permute-start | bytes 786440 | tf_op jit(solution)/shard_map/ppermute | solution.py:39
  84.3 19.2 %collective-permute-start.8 = (bf16[2,256,256]{2,1,0:T(8,128)(2,1)S(1)}, bf16[2,256,256]{2,1,0:T(8,128)(2,1)S(1)}, u32[]{:S(2)}, u32[]{:S(2)}) collective-permute-start(bf16[2,256,256]{2,1,0:T(8,128)(2,1)S(1)} %get-tuple-element.7.refs_3_), channel_id=1, source_target_pairs={{8,0},{12,4},{16,8},{20,12},{24,16},{28,20},{9,1},{13,5},{17,9},{2... | collective-permute-start | bytes 786440 | tf_op jit(solution)/shard_map/ppermute | solution.py:39
  85.6 18.0 %collective-permute-start.9 = (bf16[2,256,256]{2,1,0:T(8,128)(2,1)S(1)}, bf16[2,256,256]{2,1,0:T(8,128)(2,1)S(1)}, u32[]{:S(2)}, u32[]{:S(2)}) collective-permute-start(bf16[2,256,256]{2,1,0:T(8,128)(2,1)S(1)} %get-tuple-element.7.refs_3_), channel_id=1, source_target_pairs={{16,0},{20,4},{24,8},{28,12},{17,1},{21,5},{25,9},{29,13},{18,2},{... | collective-permute-start | bytes 786440 | tf_op jit(solution)/shard_map/ppermute | solution.py:39
  86.9 26.2 %copy-start.5 = (bf16[2,256,256]{2,1,0:T(8,128)(2,1)}, bf16[2,256,256]{2,1,0:T(8,128)(2,1)S(1)}, u32[]{:S(2)}) copy-start(bf16[2,256,256]{2,1,0:T(8,128)(2,1)S(1)} %collective-permute-done.5.refs_0_) | copy-start | bytes 786436
  86.9 24.6 %collective-permute-start.10 = (bf16[2,256,256]{2,1,0:T(8,128)(2,1)S(1)}, bf16[2,256,256]{2,1,0:T(8,128)(2,1)S(1)}, u32[]{:S(2)}, u32[]{:S(2)}) collective-permute-start(bf16[2,256,256]{2,1,0:T(8,128)(2,1)S(1)} %get-tuple-element.7.refs_3_), channel_id=1, source_target_pairs={{24,0},{28,4},{25,1},{29,5},{26,2},{30,6},{27,3},{31,7}} | collective-permute-start | bytes 786440 | tf_op jit(solution)/shard_map/ppermute | solution.py:39
  88.3 23.4 %collective-permute-start.14 = (bf16[2,256,256]{2,1,0:T(8,128)(2,1)S(1)}, bf16[2,256,256]{2,1,0:T(8,128)(2,1)S(1)}, u32[]{:S(2)}, u32[]{:S(2)}) collective-permute-start(bf16[2,256,256]{2,1,0:T(8,128)(2,1)S(1)} %get-tuple-element.7.refs_3_), channel_id=1, source_target_pairs={{0,4},{4,0},{8,12},{12,8},{16,20},{20,16},{24,28},{28,24},{1,5},{5... | collective-permute-start | bytes 786440 | tf_op jit(solution)/shard_map/ppermute | solution.py:40
  95.1 17.0 %collective-permute-start.11 = (bf16[2,256,256]{2,1,0:T(8,128)(2,1)S(1)}, bf16[2,256,256]{2,1,0:T(8,128)(2,1)S(1)}, u32[]{:S(2)}, u32[]{:S(2)}) collective-permute-start(bf16[2,256,256]{2,1,0:T(8,128)(2,1)S(1)} %collective-permute-done.5.refs_0_), channel_id=1, source_target_pairs={{0,4},{4,0},{8,12},{12,8},{16,20},{20,16},{24,28},{28,24},{1,5},{5... | collective-permute-start | bytes 786440 | tf_op jit(solution)/shard_map/ppermute | solution.py:40
  103.6 9.6 %collective-permute-start.12 = (bf16[2,256,256]{2,1,0:T(8,128)(2,1)S(1)}, bf16[2,256,256]{2,1,0:T(8,128)(2,1)S(1)}, u32[]{:S(2)}, u32[]{:S(2)}) collective-permute-start(bf16[2,256,256]{2,1,0:T(8,128)(2,1)S(1)} %collective-permute-done.6.refs_1_), channel_id=1, source_target_pairs={{0,4},{4,0},{8,12},{12,8},{16,20},{20,16},{24,28},{28,24},{1,5},{5... | collective-permute-start | bytes 786440 | tf_op jit(solution)/shard_map/ppermute | solution.py:40
  103.7 9.5 %collective-permute-start.13 = (bf16[2,256,256]{2,1,0:T(8,128)(2,1)S(1)}, bf16[2,256,256]{2,1,0:T(8,128)(2,1)S(1)}, u32[]{:S(2)}, u32[]{:S(2)}) collective-permute-start(bf16[2,256,256]{2,1,0:T(8,128)(2,1)S(1)} %collective-permute-done.7.refs_2_), channel_id=1, source_target_pairs={{0,4},{4,0},{8,12},{12,8},{16,20},{20,16},{24,28},{28,24},{1,5},{5... | collective-permute-start | bytes 786440 | tf_op jit(solution)/shard_map/ppermute | solution.py:40
  111.6 1.6 %collective-permute-start.15 = (bf16[2,256,256]{2,1,0:T(8,128)(2,1)S(1)}, bf16[2,256,256]{2,1,0:T(8,128)(2,1)S(1)}, u32[]{:S(2)}, u32[]{:S(2)}) collective-permute-start(bf16[2,256,256]{2,1,0:T(8,128)(2,1)S(1)} %collective-permute-done.8.refs_4_), channel_id=1, source_target_pairs={{0,4},{4,0},{8,12},{12,8},{16,20},{20,16},{24,28},{28,24},{1,5},{5... | collective-permute-start | bytes 786440 | tf_op jit(solution)/shard_map/ppermute | solution.py:40
  111.6 2.2 %collective-permute-start.16 = (bf16[2,256,256]{2,1,0:T(8,128)(2,1)S(1)}, bf16[2,256,256]{2,1,0:T(8,128)(2,1)S(1)}, u32[]{:S(2)}, u32[]{:S(2)}) collective-permute-start(bf16[2,256,256]{2,1,0:T(8,128)(2,1)S(1)} %collective-permute-done.9.refs_5_), channel_id=1, source_target_pairs={{0,4},{4,0},{8,12},{12,8},{16,20},{20,16},{24,28},{28,24},{1,5},{5... | collective-permute-start | bytes 786440 | tf_op jit(solution)/shard_map/ppermute | solution.py:40
  112.1 2.7 %collective-permute-start.17 = (bf16[2,256,256]{2,1,0:T(8,128)(2,1)S(1)}, bf16[2,256,256]{2,1,0:T(8,128)(2,1)}, u32[]{:S(2)}, u32[]{:S(2)}) collective-permute-start(bf16[2,256,256]{2,1,0:T(8,128)(2,1)S(1)} %collective-permute-done.10.refs_6_), channel_id=1, source_target_pairs={{0,4},{4,0},{8,12},{12,8},{16,20},{20,16},{24,28},{28,24},{1,5},{5... | collective-permute-start | bytes 786440 | tf_op jit(solution)/shard_map/ppermute | solution.py:40
  (14 other events, 104.1 us)

commit v10 on v9

--- a/solution.py
+++ b/solution.py
@@ -29,23 +29,21 @@
         gathered = lax.all_gather(mine, "dp", axis=0, tiled=True)
         return jnp.take(gathered, owner_of * slot_count + slot_rank, axis=0)
     chips = size // 2
-    partner = [(i, i ^ 1) for i in range(size)]
-    same_core = []
-    for offset in range(1 - chips, chips):
-        if offset == 0:
-            same_core.append(mine)
-            continue
-        pairs = [(i, i - 2 * offset) for i in range(size) if 0 <= i - 2 * offset < size]
-        same_core.append(lax.ppermute(mine, "dp", pairs))
-    other_core = [lax.ppermute(piece, "dp", partner) for piece in same_core]
-    pieces = same_core + other_core
+    rightward = [(i, i + 2) for i in range(size - 2)]
+    leftward = [(i + 2, i) for i in range(size - 2)]
+    from_left = [mine]
+    from_right = [mine]
+    for step in range(1, chips):
+        from_left.append(lax.ppermute(from_left[-1], "dp", rightward))
+        from_right.append(lax.ppermute(from_right[-1], "dp", leftward))
+    pieces = from_left[::-1] + from_right[1:]
     chip, core = replica // 2, replica % 2
     owner_chip, owner_core = owner_of // 2, owner_of % 2
-    offset = owner_chip - chip + chips - 1
-    which = jnp.where(owner_core == core, 0, 1)
-    source = jnp.clip(which * (2 * chips - 1) + offset, 0, len(pieces) - 1)
+    source = jnp.clip(owner_chip - chip + chips - 1, 0, len(pieces) - 1)
     table = jnp.stack([source, jnp.clip(slot_rank, 0, slot_count - 1)], axis=1).astype(jnp.int32)
-    return pick_blocks(table, pieces)
+    line_blocks = pick_blocks(table, pieces)
+    other_blocks = lax.ppermute(line_blocks, "dp", [(i, i ^ 1) for i in range(size)])
+    return jnp.where((owner_core == core)[:, None, None], line_blocks, other_blocks)
 
 
 def pick_kernel(table_ref, *refs):

time: 119 us -> 123 us (1.034)
  waiting for transfers between devices: 56.9 us -> 65.1 us
  starting transfers between devices: 38.5 us -> 34.9 us
    ppermute x13 -> x7, waiting for transfers between devices: 0.65 us -> 8.83 us  [the longest x3 6.5 us: gather_blocks(): from_right.append(lax.ppermute(from_right[-1], 'dp', leftward))]
    ppermute x13 -> x7, starting transfers between devices: 28.5 us -> 24.9 us  [the longest x3 12.9 us: gather_blocks(): from_left.append(lax.ppermute(from_left[-1], 'dp', rightward))]
  transfers between devices with their start and end apart: 19 -> 13, of which waited for: 7 -> 12; matrix products, arithmetic and copies ran while one was open for 7% -> 7% of each run, Pallas kernels for 0% -> 0%
where the time goes in v10:
time: 123 us
  waiting for transfers between devices  65.1 us (53%)
  starting transfers between devices  34.9 us (28%)
  other arithmetic  8.3 us (7%)
  matrix products  7.37 us (6%)
  Pallas kernels  3.11 us (3%)
  local copies, waits for them, and re-layouts  3.05 us (2%)
    all_to_all x1, waiting for transfers between devices, local(): received = lax.all_to_all(by_owner, 'dp', 0, 0, tiled=True)  47.4 us
    ppermute x3, starting transfers between devices, gather_blocks(): from_left.append(lax.ppermute(from_left[-1], 'dp', rightward))  12.9 us
    ppermute x5, waiting for transfers between devices, butterfly_sum(): x = x + lax.ppermute(x, axis, [(i, i ^ step) for i in range(size)])  8.92 us
    ppermute x1, starting transfers between devices, gather_blocks(): lax.ppermute(line_blocks, 'dp', [(i, i ^ 1) for i in range(size)])  8.12 us
    all_to_all x1, starting transfers between devices, local(): received = lax.all_to_all(by_owner, 'dp', 0, 0, tiled=True)  6.51 us
    ppermute x3, waiting for transfers between devices, gather_blocks(): from_right.append(lax.ppermute(from_right[-1], 'dp', leftward))  6.5 us
    ppermute x3, starting transfers between devices, gather_blocks(): from_right.append(lax.ppermute(from_right[-1], 'dp', leftward))  3.84 us
    ppermute x5, starting transfers between devices, butterfly_sum(): x = x + lax.ppermute(x, axis, [(i, i ^ step) for i in range(size)])  3.52 us
  transfers between devices with their start and end apart: 13, of which 12 were waited for; matrix products, arithmetic and copies ran while one was open for 7% of the time, Pallas kernels for 0%

profile of v10, /device:TPU:1, one launch (start us, length us, event | category | flops | bytes accessed | tf_op | source)
XLA Modules:
  0.0 122.7 jit_solution(2307407734473629946)
XLA Ops:
  2.6 2.0 %gather_fusion = bf16[16,256,256]{2,1,0:T(8,128)(2,1)} fusion(bf16[8,256,256]{2,1,0:T(8,128)(2,1)S(1)} %bitcast.53, s32[1024]{0:T(1024)S(1)} %pad_clamp_fusion), kind=kCustom, calls=%fused_computation | custom fusion | bytes 4194368 | tf_op jit(solution)/shard_map/jit(_take)/gather | solution.py:111
  4.6 6.5 %all-to-all-start = ((bf16[8,2,256,256]{3,2,1,0:T(8,128)(2,1)}), bf16[8,2,256,256]{3,2,1,0:T(8,128)(2,1)}, u32[]{:S(2)}, u32[]{:S(2)}) async-start(bf16[8,2,256,256]{3,2,1,0:T(8,128)(2,1)} %bitcast.3), calls=%async_computation | async-start | bytes 4194304 | tf_op jit(solution)/shard_map/all_to_all | solution.py:114
  12.0 47.4 %all-to-all-done = bf16[8,2,256,256]{3,2,1,0:T(8,128)(2,1)} async-done(((bf16[8,2,256,256]{3,2,1,0:T(8,128)(2,1)}), bf16[8,2,256,256]{3,2,1,0:T(8,128)(2,1)}, u32[]{:S(2)}, u32[]{:S(2)}) %all-to-all-start) | async-done | bytes 2097184 | tf_op jit(solution)/shard_map/all_to_all | solution.py:114
  59.4 1.9 %convert_reduce_fusion = f32[2,256,256]{2,1,0:T(8,128)S(1)} fusion(bf16[8,2,256,256]{3,2,1,0:T(8,128)(2,1)} %all-to-all-done), kind=kLoop, calls=%fused_computation.1 | loop fusion | flops 1966080 | bytes 2621440 | tf_op jit(solution)/shard_map/reduce_sum | solution.py:115
  61.8 1.6 %multiply_reduce_fusion = (f32[2]{0:T(128)S(1)}, f32[2,256,256]{2,1,0:T(8,128)S(1)}) fusion(bf16[1,1,2,256,256]{4,3,2,1,0:T(8,128)(2,1)S(1)} %copy-done.5, f32[2,256,256]{2,1,0:T(8,128)S(1)} %convert_reduce_fusion, bf16[1,1,2,256,256]{4,3,2,1,0:T(8,128)(2,1)} %param.14, f32[2]{0:T(128)S(1)} %convert_element_type.35), kind=kOutput, calls=%fused_computation.26 | convolution fusion | flops 134873088 | bytes 1572880 | tf_op jit(solution)/shard_map/sij,sjk->sik/dot_general | solution.py:140
  65.4 2.4 %collective-permute-done.1 = f32[2,9]{1,0:T(2,128)S(1)} collective-permute-done((f32[2,9]{1,0:T(2,128)S(1)}, f32[2,9]{1,0:T(2,128)S(1)}, u32[]{:S(2)}, u32[]{:S(2)}) %collective-permute-start.1) | collective-permute-done | bytes 104 | tf_op jit(solution)/shard_map/ppermute | solution.py:20
  67.9 3.3 %collective-permute-done.2 = f32[2,9]{1,0:T(2,128)S(1)} collective-permute-done((f32[2,9]{1,0:T(2,128)S(1)}, f32[2,9]{1,0:T(2,128)S(1)}, u32[]{:S(2)}, u32[]{:S(2)}) %collective-permute-start.2) | collective-permute-done | bytes 104 | tf_op jit(solution)/shard_map/ppermute | solution.py:20
  71.2 1.2 collective-permute-start.3
  72.4 1.2 collective-permute-done.3
  73.6 1.2 %collective-permute-start.4 = (f32[2,9]{1,0:T(2,128)S(1)}, f32[2,9]{1,0:T(2,128)S(1)}, u32[]{:S(2)}, u32[]{:S(2)}) collective-permute-start(f32[2,9]{1,0:T(2,128)S(1)} %add.92), channel_id=1, source_target_pairs={{0,2},{1,3},{2,0},{3,1},{4,6},{5,7},{6,4},{7,5},{8,10},{9,11},{10,... | collective-permute-start | bytes 224 | tf_op jit(solution)/shard_map/ppermute | solution.py:20
  77.2 1.3 %collective-permute-start.8 = (bf16[2,256,256]{2,1,0:T(8,128)(2,1)S(1)}, bf16[2,256,256]{2,1,0:T(8,128)(2,1)S(1)}, u32[]{:S(2)}, u32[]{:S(2)}) collective-permute-start(bf16[2,256,256]{2,1,0:T(8,128)(2,1)S(1)} %get-tuple-element.7.refs_3_), channel_id=1, source_target_pairs={{8,0},{12,4},{16,8},{20,12},{24,16},{28,20},{9,1},{13,5},{17,9},{2... | collective-permute-start | bytes 786440 | tf_op jit(solution)/shard_map/ppermute | solution.py:38
  78.5 4.0 %collective-permute-start.5 = (bf16[2,256,256]{2,1,0:T(8,128)(2,1)S(1)}, bf16[2,256,256]{2,1,0:T(8,128)(2,1)S(1)}, u32[]{:S(2)}, u32[]{:S(2)}) collective-permute-start(bf16[2,256,256]{2,1,0:T(8,128)(2,1)S(1)} %get-tuple-element.7.refs_3_), channel_id=1, source_target_pairs={{0,8},{4,12},{8,16},{12,20},{16,24},{20,28},{1,9},{5,13},{9,17},{1... | collective-permute-start | bytes 786440 | tf_op jit(solution)/shard_map/ppermute | solution.py:37
  82.5 1.8 %collective-permute-done.8.refs_4_ = bf16[2,256,256]{2,1,0:T(8,128)(2,1)S(1)} collective-permute-done((bf16[2,256,256]{2,1,0:T(8,128)(2,1)S(1)}, bf16[2,256,256]{2,1,0:T(8,128)(2,1)S(1)}, u32[]{:S(2)}, u32[]{:S(2)}) %collective-permute-start.8) | collective-permute-done | bytes 262176 | tf_op jit(solution)/shard_map/ppermute | solution.py:38
  84.3 1.3 %collective-permute-start.9 = (bf16[2,256,256]{2,1,0:T(8,128)(2,1)S(1)}, bf16[2,256,256]{2,1,0:T(8,128)(2,1)S(1)}, u32[]{:S(2)}, u32[]{:S(2)}) collective-permute-start(bf16[2,256,256]{2,1,0:T(8,128)(2,1)S(1)} %collective-permute-done.8.refs_4_), channel_id=1, source_target_pairs={{8,0},{12,4},{16,8},{20,12},{24,16},{28,20},{9,1},{13,5},{17,9},{2... | collective-permute-start | bytes 786440 | tf_op jit(solution)/shard_map/ppermute | solution.py:38
  85.8 4.1 %collective-permute-start.6 = (bf16[2,256,256]{2,1,0:T(8,128)(2,1)S(1)}, bf16[2,256,256]{2,1,0:T(8,128)(2,1)S(1)}, u32[]{:S(2)}, u32[]{:S(2)}) collective-permute-start(bf16[2,256,256]{2,1,0:T(8,128)(2,1)S(1)} %collective-permute-done.5.refs_2_), channel_id=1, source_target_pairs={{0,8},{4,12},{8,16},{12,20},{16,24},{20,28},{1,9},{5,13},{9,17},{1... | collective-permute-start | bytes 786440 | tf_op jit(solution)/shard_map/ppermute | solution.py:37
  89.9 2.6 %collective-permute-done.9.refs_5_ = bf16[2,256,256]{2,1,0:T(8,128)(2,1)S(1)} collective-permute-done((bf16[2,256,256]{2,1,0:T(8,128)(2,1)S(1)}, bf16[2,256,256]{2,1,0:T(8,128)(2,1)S(1)}, u32[]{:S(2)}, u32[]{:S(2)}) %collective-permute-start.9) | collective-permute-done | bytes 262176 | tf_op jit(solution)/shard_map/ppermute | solution.py:38
  92.5 1.3 %collective-permute-start.10 = (bf16[2,256,256]{2,1,0:T(8,128)(2,1)S(1)}, bf16[2,256,256]{2,1,0:T(8,128)(2,1)}, u32[]{:S(2)}, u32[]{:S(2)}) collective-permute-start(bf16[2,256,256]{2,1,0:T(8,128)(2,1)S(1)} %collective-permute-done.9.refs_5_), channel_id=1, source_target_pairs={{8,0},{12,4},{16,8},{20,12},{24,16},{28,20},{9,1},{13,5},{17,9},{2... | collective-permute-start | bytes 786440 | tf_op jit(solution)/shard_map/ppermute | solution.py:38
  94.2 4.8 %collective-permute-start.7 = (bf16[2,256,256]{2,1,0:T(8,128)(2,1)S(1)}, bf16[2,256,256]{2,1,0:T(8,128)(2,1)}, u32[]{:S(2)}, u32[]{:S(2)}) collective-permute-start(bf16[2,256,256]{2,1,0:T(8,128)(2,1)S(1)} %collective-permute-done.6.refs_1_), channel_id=1, source_target_pairs={{0,8},{4,12},{8,16},{12,20},{16,24},{20,28},{1,9},{5,13},{9,17},{1... | collective-permute-start | bytes 786440 | tf_op jit(solution)/shard_map/ppermute | solution.py:37
  99.7 2.1 %collective-permute-done.10.refs_6_ = bf16[2,256,256]{2,1,0:T(8,128)(2,1)} collective-permute-done((bf16[2,256,256]{2,1,0:T(8,128)(2,1)S(1)}, bf16[2,256,256]{2,1,0:T(8,128)(2,1)}, u32[]{:S(2)}, u32[]{:S(2)}) %collective-permute-start.10) | collective-permute-done | bytes 262176 | tf_op jit(solution)/shard_map/ppermute | solution.py:38
  101.9 1.7 %collective-permute-done.7.refs_0_ = bf16[2,256,256]{2,1,0:T(8,128)(2,1)} collective-permute-done((bf16[2,256,256]{2,1,0:T(8,128)(2,1)S(1)}, bf16[2,256,256]{2,1,0:T(8,128)(2,1)}, u32[]{:S(2)}, u32[]{:S(2)}) %collective-permute-start.7) | collective-permute-done | bytes 262176 | tf_op jit(solution)/shard_map/ppermute | solution.py:37
  103.6 3.1 %shard_map.128 = bf16[8,256,256]{2,1,0:T(8,128)(2,1)} custom-call(s32[8,2]{1,0:T(8,128)} %copy.39.table_ref, bf16[2,256,256]{2,1,0:T(8,128)(2,1)} %collective-permute-done.7.refs_0_, bf16[2,256,256]{2,1,0:T(8,128)(2,1)} %copy-done.9, bf16[2,256,256]{2,1,0:T(8,128)(2,1)} %copy-done.7, bf16[2,256,256]{2,1,0:T(8,128)(2,1)} %copy-done.3, ...), custom_call_target="tpu_custom_call" | custom-call | tf_op jit(solution)/shard_map/pallas_call | solution.py:70
  106.7 8.1 %collective-permute-start.11 = (bf16[8,256,256]{2,1,0:T(8,128)(2,1)}, bf16[8,256,256]{2,1,0:T(8,128)(2,1)S(1)}, u32[]{:S(2)}, u32[]{:S(2)}) collective-permute-start(bf16[8,256,256]{2,1,0:T(8,128)(2,1)} %shard_map.128), channel_id=1, source_target_pairs={{0,4},{4,0},{8,12},{12,8},{16,20},{20,16},{24,28},{28,24},{1,5},{5... | collective-permute-start | bytes 3145736 | tf_op jit(solution)/shard_map/ppermute | solution.py:45
  114.8 3.1 %fusion.2 = f32[1,1,2,256,256]{4,3,2,1,0:T(8,128)} fusion(f32[1,1,2,256,256]{4,3,2,1,0:T(8,128)} %param.13, f32[2,256,256]{2,1,0:T(8,128)S(1)} %convert_reduce_fusion, f32[2]{0:T(128)S(1)} %convert_element_type.35, pred[2]{0:T(512)(128)(4,1)S(1)} %dynamic-slice_reduce_fusion), kind=kOutput, calls=%fused_computation.5 | convolution fusion | flops 403308544 | bytes 1572874 | tf_op jit(solution)/shard_map/sji,sjk->sik/dot_general | solution.py:133
  117.9 2.7 %fusion.5 = f32[1,1,2,256,256]{4,3,2,1,0:T(8,128)} fusion(f32[1,1,2,256,256]{4,3,2,1,0:T(8,128)} %param.12, f32[2,256,256]{2,1,0:T(8,128)S(1)} %convert_reduce_fusion, f32[2]{0:T(128)S(1)} %convert_element_type.35, pred[2]{0:T(512)(128)(4,1)S(1)} %dynamic-slice_reduce_fusion), kind=kOutput, calls=%fused_computation.9 | convolution fusion | flops 403308544 | bytes 1572874 | tf_op jit(solution)/shard_map/sij,skj->sik/dot_general | solution.py:130
  (64 shorter events, 11.2 us)
Async XLA Ops:
  4.6 6.9 %copy-start.10 = (s32[9]{0:T(128)S(1)}, s32[9]{0:T(128)}, u32[]{:S(2)}) copy-start(s32[9]{0:T(128)} %param.11) | copy-start | bytes 112
  4.6 54.8 %all-to-all-start = ((bf16[8,2,256,256]{3,2,1,0:T(8,128)(2,1)}), bf16[8,2,256,256]{3,2,1,0:T(8,128)(2,1)}, u32[]{:S(2)}, u32[]{:S(2)}) async-start(bf16[8,2,256,256]{3,2,1,0:T(8,128)(2,1)} %bitcast.3), calls=%async_computation | async-start | bytes 4194304 | tf_op jit(solution)/shard_map/all_to_all | solution.py:114
  11.1 50.2 %copy-start.2 = (f32[1,1,2,256,256]{4,3,2,1,0:T(8,128)S(1)}, f32[1,1,2,256,256]{4,3,2,1,0:T(8,128)}, u32[]{:S(2)}) copy-start(f32[1,1,2,256,256]{4,3,2,1,0:T(8,128)} %param.16) | copy-start | bytes 1572868
  11.1 50.7 %copy-start.5 = (bf16[1,1,2,256,256]{4,3,2,1,0:T(8,128)(2,1)S(1)}, bf16[1,1,2,256,256]{4,3,2,1,0:T(8,128)(2,1)}, u32[]{:S(2)}) copy-start(bf16[1,1,2,256,256]{4,3,2,1,0:T(8,128)(2,1)} %param.15) | copy-start | bytes 786436
  12.0 64.2 %copy-start.4 = (f32[1,1,2,256,256]{4,3,2,1,0:T(8,128)S(1)}, f32[1,1,2,256,256]{4,3,2,1,0:T(8,128)}, u32[]{:S(2)}) copy-start(f32[1,1,2,256,256]{4,3,2,1,0:T(8,128)} %param.17) | copy-start | bytes 1572868
  61.3 37.7 %copy-start.11 = (s32[8,1]{0,1:T(1,128)S(1)}, s32[8,1]{0,1:T(1,128)}, u32[]{:S(2)}) copy-start(s32[8,1]{0,1:T(1,128)} %param.10) | copy-start | bytes 100
  63.5 1.8 %collective-permute-start = (f32[2,9]{1,0:T(2,128)S(1)}, f32[2,9]{1,0:T(2,128)S(1)}, u32[]{:S(2)}, u32[]{:S(2)}) collective-permute-start(f32[2,9]{1,0:T(2,128)S(1)} %pad_maximum_fusion), channel_id=1, source_target_pairs={{0,4},{4,0},{8,12},{12,8},{16,20},{20,16},{24,28},{28,24},{1,5},{5... | collective-permute-start | bytes 224 | tf_op jit(solution)/shard_map/ppermute | solution.py:20
  65.3 2.5 %collective-permute-start.1 = (f32[2,9]{1,0:T(2,128)S(1)}, f32[2,9]{1,0:T(2,128)S(1)}, u32[]{:S(2)}, u32[]{:S(2)}) collective-permute-start(f32[2,9]{1,0:T(2,128)S(1)} %fusion.29), channel_id=1, source_target_pairs={{0,8},{4,12},{8,0},{12,4},{16,24},{20,28},{24,16},{28,20},{1,9},{5... | collective-permute-start | bytes 224 | tf_op jit(solution)/shard_map/ppermute | solution.py:20
  67.8 3.4 %collective-permute-start.2 = (f32[2,9]{1,0:T(2,128)S(1)}, f32[2,9]{1,0:T(2,128)S(1)}, u32[]{:S(2)}, u32[]{:S(2)}) collective-permute-start(f32[2,9]{1,0:T(2,128)S(1)} %fusion.34), channel_id=1, source_target_pairs={{0,16},{4,20},{8,24},{12,28},{16,0},{20,4},{24,8},{28,12},{1,17},{... | collective-permute-start | bytes 224 | tf_op jit(solution)/shard_map/ppermute | solution.py:20
  71.2 2.4 %collective-permute-start.3 = (f32[2,9]{1,0:T(2,128)S(1)}, f32[2,9]{1,0:T(2,128)S(1)}, u32[]{:S(2)}, u32[]{:S(2)}) collective-permute-start(f32[2,9]{1,0:T(2,128)S(1)} %add.91), channel_id=1, source_target_pairs={{0,1},{1,0},{2,3},{3,2},{4,5},{5,4},{6,7},{7,6},{8,9},{9,8},{10,11... | collective-permute-start | bytes 224 | tf_op jit(solution)/shard_map/ppermute | solution.py:20
  73.6 2.4 %collective-permute-start.4 = (f32[2,9]{1,0:T(2,128)S(1)}, f32[2,9]{1,0:T(2,128)S(1)}, u32[]{:S(2)}, u32[]{:S(2)}) collective-permute-start(f32[2,9]{1,0:T(2,128)S(1)} %add.92), channel_id=1, source_target_pairs={{0,2},{1,3},{2,0},{3,1},{4,6},{5,7},{6,4},{7,5},{8,10},{9,11},{10,... | collective-permute-start | bytes 224 | tf_op jit(solution)/shard_map/ppermute | solution.py:20
  77.2 26.4 %copy-start.3 = (bf16[2,256,256]{2,1,0:T(8,128)(2,1)}, bf16[2,256,256]{2,1,0:T(8,128)(2,1)S(1)}, u32[]{:S(2)}) copy-start(bf16[2,256,256]{2,1,0:T(8,128)(2,1)S(1)} %get-tuple-element.7.refs_3_) | copy-start | bytes 786436
  77.2 7.1 %collective-permute-start.8 = (bf16[2,256,256]{2,1,0:T(8,128)(2,1)S(1)}, bf16[2,256,256]{2,1,0:T(8,128)(2,1)S(1)}, u32[]{:S(2)}, u32[]{:S(2)}) collective-permute-start(bf16[2,256,256]{2,1,0:T(8,128)(2,1)S(1)} %get-tuple-element.7.refs_3_), channel_id=1, source_target_pairs={{8,0},{12,4},{16,8},{20,12},{24,16},{28,20},{9,1},{13,5},{17,9},{2... | collective-permute-start | bytes 786440 | tf_op jit(solution)/shard_map/ppermute | solution.py:38
  78.5 7.3 %collective-permute-start.5 = (bf16[2,256,256]{2,1,0:T(8,128)(2,1)S(1)}, bf16[2,256,256]{2,1,0:T(8,128)(2,1)S(1)}, u32[]{:S(2)}, u32[]{:S(2)}) collective-permute-start(bf16[2,256,256]{2,1,0:T(8,128)(2,1)S(1)} %get-tuple-element.7.refs_3_), channel_id=1, source_target_pairs={{0,8},{4,12},{8,16},{12,20},{16,24},{20,28},{1,9},{5,13},{9,17},{1... | collective-permute-start | bytes 786440 | tf_op jit(solution)/shard_map/ppermute | solution.py:37
  84.3 19.2 %copy-start.6 = (bf16[2,256,256]{2,1,0:T(8,128)(2,1)}, bf16[2,256,256]{2,1,0:T(8,128)(2,1)S(1)}, u32[]{:S(2)}) copy-start(bf16[2,256,256]{2,1,0:T(8,128)(2,1)S(1)} %collective-permute-done.8.refs_4_) | copy-start | bytes 786436
  84.3 8.2 %collective-permute-start.9 = (bf16[2,256,256]{2,1,0:T(8,128)(2,1)S(1)}, bf16[2,256,256]{2,1,0:T(8,128)(2,1)S(1)}, u32[]{:S(2)}, u32[]{:S(2)}) collective-permute-start(bf16[2,256,256]{2,1,0:T(8,128)(2,1)S(1)} %collective-permute-done.8.refs_4_), channel_id=1, source_target_pairs={{8,0},{12,4},{16,8},{20,12},{24,16},{28,20},{9,1},{13,5},{17,9},{2... | collective-permute-start | bytes 786440 | tf_op jit(solution)/shard_map/ppermute | solution.py:38
  85.8 17.8 %copy-start.7 = (bf16[2,256,256]{2,1,0:T(8,128)(2,1)}, bf16[2,256,256]{2,1,0:T(8,128)(2,1)S(1)}, u32[]{:S(2)}) copy-start(bf16[2,256,256]{2,1,0:T(8,128)(2,1)S(1)} %collective-permute-done.5.refs_2_) | copy-start | bytes 786436
  85.8 8.5 %collective-permute-start.6 = (bf16[2,256,256]{2,1,0:T(8,128)(2,1)S(1)}, bf16[2,256,256]{2,1,0:T(8,128)(2,1)S(1)}, u32[]{:S(2)}, u32[]{:S(2)}) collective-permute-start(bf16[2,256,256]{2,1,0:T(8,128)(2,1)S(1)} %collective-permute-done.5.refs_2_), channel_id=1, source_target_pairs={{0,8},{4,12},{8,16},{12,20},{16,24},{20,28},{1,9},{5,13},{9,17},{1... | collective-permute-start | bytes 786440 | tf_op jit(solution)/shard_map/ppermute | solution.py:37
  92.5 11.1 %copy-start.8 = (bf16[2,256,256]{2,1,0:T(8,128)(2,1)}, bf16[2,256,256]{2,1,0:T(8,128)(2,1)S(1)}, u32[]{:S(2)}) copy-start(bf16[2,256,256]{2,1,0:T(8,128)(2,1)S(1)} %collective-permute-done.9.refs_5_) | copy-start | bytes 786436
  92.5 9.4 %collective-permute-start.10 = (bf16[2,256,256]{2,1,0:T(8,128)(2,1)S(1)}, bf16[2,256,256]{2,1,0:T(8,128)(2,1)}, u32[]{:S(2)}, u32[]{:S(2)}) collective-permute-start(bf16[2,256,256]{2,1,0:T(8,128)(2,1)S(1)} %collective-permute-done.9.refs_5_), channel_id=1, source_target_pairs={{8,0},{12,4},{16,8},{20,12},{24,16},{28,20},{9,1},{13,5},{17,9},{2... | collective-permute-start | bytes 786440 | tf_op jit(solution)/shard_map/ppermute | solution.py:38
  94.2 9.3 %copy-start.9 = (bf16[2,256,256]{2,1,0:T(8,128)(2,1)}, bf16[2,256,256]{2,1,0:T(8,128)(2,1)S(1)}, u32[]{:S(2)}) copy-start(bf16[2,256,256]{2,1,0:T(8,128)(2,1)S(1)} %collective-permute-done.6.refs_1_) | copy-start | bytes 786436
  94.2 9.3 %collective-permute-start.7 = (bf16[2,256,256]{2,1,0:T(8,128)(2,1)S(1)}, bf16[2,256,256]{2,1,0:T(8,128)(2,1)}, u32[]{:S(2)}, u32[]{:S(2)}) collective-permute-start(bf16[2,256,256]{2,1,0:T(8,128)(2,1)S(1)} %collective-permute-done.6.refs_1_), channel_id=1, source_target_pairs={{0,8},{4,12},{8,16},{12,20},{16,24},{20,28},{1,9},{5,13},{9,17},{1... | collective-permute-start | bytes 786440 | tf_op jit(solution)/shard_map/ppermute | solution.py:37
  106.7 14.9 %collective-permute-start.11 = (bf16[8,256,256]{2,1,0:T(8,128)(2,1)}, bf16[8,256,256]{2,1,0:T(8,128)(2,1)S(1)}, u32[]{:S(2)}, u32[]{:S(2)}) collective-permute-start(bf16[8,256,256]{2,1,0:T(8,128)(2,1)} %shard_map.128), channel_id=1, source_target_pairs={{0,4},{4,0},{8,12},{12,8},{16,20},{20,16},{24,28},{28,24},{1,5},{5... | collective-permute-start | bytes 3145736 | tf_op jit(solution)/shard_map/ppermute | solution.py:45
  114.8 6.7 %copy-start.1 = (bf16[8,256,256]{2,1,0:T(8,128)(2,1)S(1)}, bf16[8,256,256]{2,1,0:T(8,128)(2,1)}, u32[]{:S(2)}) copy-start(bf16[8,256,256]{2,1,0:T(8,128)(2,1)} %shard_map.128) | copy-start | bytes 3145732
  (1 other events, 2.0 us)

commit v11 on v8

--- a/solution.py
+++ b/solution.py
@@ -135,7 +135,7 @@
     vnew = BETA * moment + (1.0 - BETA) * owned_grad * owned_grad
     adam = owned_grad / (jnp.sqrt(vnew) + ADAM_EPS)
     adam_terms = jnp.sum(member * jnp.sum(adam * adam, axis=(1, 2))[:, None], axis=0)
-    highest = lax.Precision.HIGHEST
+    highest = lax.Precision.HIGH
     lnew = BETA * left + (1.0 - BETA) * jnp.einsum(
         "sij,skj->sik", owned_grad, owned_grad, precision=highest
     )

time: 117 us -> 117 us (level)
  transfers between devices with their start and end apart: 19 -> 19, of which waited for: 7 -> 7; matrix products, arithmetic and copies ran while one was open for 7% -> 6% of each run, Pallas kernels for 0% -> 0%
where the time goes in v11:
time: 117 us; the launch traced here: 116 us
  waiting for transfers between devices  58.3 us (50%)
  starting transfers between devices  35.3 us (30%)
  other arithmetic  7.11 us (6%)
  matrix products  6.59 us (6%)
  local copies, waits for them, and re-layouts  4.58 us (4%)
  Pallas kernels  3.15 us (3%)
    all_to_all x1, waiting for transfers between devices, local(): received = lax.all_to_all(by_owner, 'dp', 0, 0, tiled=True)  47.4 us
    ppermute x3, starting transfers between devices, gather_blocks(): from_left[step] = lax.ppermute(from_left[step - 1], 'dp', rightward)  10 us
    ppermute x5, waiting for transfers between devices, butterfly_sum(): x = x + lax.ppermute(x, axis, [(i, i ^ step) for i in range(size)])  8.91 us
    ppermute x1, starting transfers between devices, gather_blocks(): near_left[0] = lax.ppermute(mine, 'dp', partner)  7.05 us
    all_to_all x1, starting transfers between devices, local(): received = lax.all_to_all(by_owner, 'dp', 0, 0, tiled=True)  6.51 us
    ppermute x3, starting transfers between devices, gather_blocks(): near_right[step] = lax.ppermute(from_right[step], 'dp', partner)  4.18 us
    ppermute x3, starting transfers between devices, gather_blocks(): from_right[step] = lax.ppermute(from_right[step - 1], 'dp', leftward)  3.88 us
    ppermute x5, starting transfers between devices, butterfly_sum(): x = x + lax.ppermute(x, axis, [(i, i ^ step) for i in range(size)])  3.53 us
  transfers between devices with their start and end apart: 19, of which 7 were waited for; matrix products, arithmetic and copies ran while one was open for 6% of the time, Pallas kernels for 0%

profile of v11, /device:TPU:1, one launch (start us, length us, event | category | flops | bytes accessed | tf_op | source)
XLA Modules:
  0.0 116.0 jit_solution(17993783676229969284)
XLA Ops:
  2.6 2.0 %gather_fusion = bf16[16,256,256]{2,1,0:T(8,128)(2,1)} fusion(bf16[8,256,256]{2,1,0:T(8,128)(2,1)S(1)} %bitcast.52, s32[1024]{0:T(1024)S(1)} %pad_clamp_fusion), kind=kCustom, calls=%fused_computation | custom fusion | bytes 4194368 | tf_op jit(solution)/shard_map/jit(_take)/gather | solution.py:120
  4.6 6.5 %all-to-all-start = ((bf16[8,2,256,256]{3,2,1,0:T(8,128)(2,1)}), bf16[8,2,256,256]{3,2,1,0:T(8,128)(2,1)}, u32[]{:S(2)}, u32[]{:S(2)}) async-start(bf16[8,2,256,256]{3,2,1,0:T(8,128)(2,1)} %bitcast.3), calls=%async_computation | async-start | bytes 4194304 | tf_op jit(solution)/shard_map/all_to_all | solution.py:123
  12.0 47.4 %all-to-all-done = bf16[8,2,256,256]{3,2,1,0:T(8,128)(2,1)} async-done(((bf16[8,2,256,256]{3,2,1,0:T(8,128)(2,1)}), bf16[8,2,256,256]{3,2,1,0:T(8,128)(2,1)}, u32[]{:S(2)}, u32[]{:S(2)}) %all-to-all-start) | async-done | bytes 2097184 | tf_op jit(solution)/shard_map/all_to_all | solution.py:123
  59.4 1.9 %convert_reduce_fusion = f32[2,256,256]{2,1,0:T(8,128)S(1)} fusion(bf16[8,2,256,256]{3,2,1,0:T(8,128)(2,1)} %all-to-all-done), kind=kLoop, calls=%fused_computation.1 | loop fusion | flops 1966080 | bytes 2621440 | tf_op jit(solution)/shard_map/reduce_sum | solution.py:124
  61.8 1.6 %multiply_reduce_fusion = (f32[2]{0:T(128)S(1)}, f32[2,256,256]{2,1,0:T(8,128)S(1)}) fusion(bf16[1,1,2,256,256]{4,3,2,1,0:T(8,128)(2,1)S(1)} %copy-done.4, f32[2,256,256]{2,1,0:T(8,128)S(1)} %convert_reduce_fusion, bf16[1,1,2,256,256]{4,3,2,1,0:T(8,128)(2,1)} %param.14, f32[2]{0:T(128)S(1)} %convert_element_type.35), kind=kOutput, calls=%fused_computation.25 | convolution fusion | flops 134873088 | bytes 1572880 | tf_op jit(solution)/shard_map/sij,sjk->sik/dot_general | solution.py:149
  65.4 2.4 %collective-permute-done.1 = f32[2,9]{1,0:T(2,128)S(1)} collective-permute-done((f32[2,9]{1,0:T(2,128)S(1)}, f32[2,9]{1,0:T(2,128)S(1)}, u32[]{:S(2)}, u32[]{:S(2)}) %collective-permute-start.1) | collective-permute-done | bytes 104 | tf_op jit(solution)/shard_map/ppermute | solution.py:20
  67.9 3.3 %collective-permute-done.2 = f32[2,9]{1,0:T(2,128)S(1)} collective-permute-done((f32[2,9]{1,0:T(2,128)S(1)}, f32[2,9]{1,0:T(2,128)S(1)}, u32[]{:S(2)}, u32[]{:S(2)}) %collective-permute-start.2) | collective-permute-done | bytes 104 | tf_op jit(solution)/shard_map/ppermute | solution.py:20
  71.2 1.2 %collective-permute-start.3 = (f32[2,9]{1,0:T(2,128)S(1)}, f32[2,9]{1,0:T(2,128)S(1)}, u32[]{:S(2)}, u32[]{:S(2)}) collective-permute-start(f32[2,9]{1,0:T(2,128)S(1)} %add.92), channel_id=1, source_target_pairs={{0,1},{1,0},{2,3},{3,2},{4,5},{5,4},{6,7},{7,6},{8,9},{9,8},{10,11... | collective-permute-start | bytes 224 | tf_op jit(solution)/shard_map/ppermute | solution.py:20
  72.4 1.2 %collective-permute-done.3 = f32[2,9]{1,0:T(2,128)S(1)} collective-permute-done((f32[2,9]{1,0:T(2,128)S(1)}, f32[2,9]{1,0:T(2,128)S(1)}, u32[]{:S(2)}, u32[]{:S(2)}) %collective-permute-start.3) | collective-permute-done | bytes 104 | tf_op jit(solution)/shard_map/ppermute | solution.py:20
  73.6 1.2 %collective-permute-start.4 = (f32[2,9]{1,0:T(2,128)S(1)}, f32[2,9]{1,0:T(2,128)S(1)}, u32[]{:S(2)}, u32[]{:S(2)}) collective-permute-start(f32[2,9]{1,0:T(2,128)S(1)} %add.93), channel_id=1, source_target_pairs={{0,2},{1,3},{2,0},{3,1},{4,6},{5,7},{6,4},{7,5},{8,10},{9,11},{10,... | collective-permute-start | bytes 224 | tf_op jit(solution)/shard_map/ppermute | solution.py:20
  74.9 1.2 %collective-permute-done.4 = f32[2,9]{1,0:T(2,128)S(1)} collective-permute-done((f32[2,9]{1,0:T(2,128)S(1)}, f32[2,9]{1,0:T(2,128)S(1)}, u32[]{:S(2)}, u32[]{:S(2)}) %collective-permute-start.4) | collective-permute-done | bytes 104 | tf_op jit(solution)/shard_map/ppermute | solution.py:20
  77.2 1.9 %collective-permute-start.5 = (bf16[2,256,256]{2,1,0:T(8,128)(2,1)S(1)}, bf16[2,256,256]{2,1,0:T(8,128)(2,1)S(1)}, u32[]{:S(2)}, u32[]{:S(2)}) collective-permute-start(bf16[2,256,256]{2,1,0:T(8,128)(2,1)S(1)} %get-tuple-element.7.refs_3_), channel_id=1, source_target_pairs={{0,8},{4,12},{8,16},{12,20},{16,24},{20,28},{1,9},{5,13},{9,17},{1... | collective-permute-start | bytes 786440 | tf_op jit(solution)/shard_map/ppermute | solution.py:44
  79.1 1.3 %collective-permute-start.8 = (bf16[2,256,256]{2,1,0:T(8,128)(2,1)S(1)}, bf16[2,256,256]{2,1,0:T(8,128)(2,1)S(1)}, u32[]{:S(2)}, u32[]{:S(2)}) collective-permute-start(bf16[2,256,256]{2,1,0:T(8,128)(2,1)S(1)} %get-tuple-element.7.refs_3_), channel_id=1, source_target_pairs={{8,0},{12,4},{16,8},{20,12},{24,16},{28,20},{9,1},{13,5},{17,9},{2... | collective-permute-start | bytes 786440 | tf_op jit(solution)/shard_map/ppermute | solution.py:45
  80.5 2.0 %collective-permute-done.5.refs_2_ = bf16[2,256,256]{2,1,0:T(8,128)(2,1)S(1)} collective-permute-done((bf16[2,256,256]{2,1,0:T(8,128)(2,1)S(1)}, bf16[2,256,256]{2,1,0:T(8,128)(2,1)S(1)}, u32[]{:S(2)}, u32[]{:S(2)}) %collective-permute-start.5) | collective-permute-done | bytes 262176 | tf_op jit(solution)/shard_map/ppermute | solution.py:44
  82.4 3.8 %collective-permute-start.6 = (bf16[2,256,256]{2,1,0:T(8,128)(2,1)S(1)}, bf16[2,256,256]{2,1,0:T(8,128)(2,1)S(1)}, u32[]{:S(2)}, u32[]{:S(2)}) collective-permute-start(bf16[2,256,256]{2,1,0:T(8,128)(2,1)S(1)} %collective-permute-done.5.refs_2_), channel_id=1, source_target_pairs={{0,8},{4,12},{8,16},{12,20},{16,24},{20,28},{1,9},{5,13},{9,17},{1... | collective-permute-start | bytes 786440 | tf_op jit(solution)/shard_map/ppermute | solution.py:44
  86.3 1.3 %collective-permute-start.9 = (bf16[2,256,256]{2,1,0:T(8,128)(2,1)S(1)}, bf16[2,256,256]{2,1,0:T(8,128)(2,1)S(1)}, u32[]{:S(2)}, u32[]{:S(2)}) collective-permute-start(bf16[2,256,256]{2,1,0:T(8,128)(2,1)S(1)} %collective-permute-done.8.refs_4_), channel_id=1, source_target_pairs={{8,0},{12,4},{16,8},{20,12},{24,16},{28,20},{9,1},{13,5},{17,9},{2... | collective-permute-start | bytes 786440 | tf_op jit(solution)/shard_map/ppermute | solution.py:45
  88.3 7.1 %collective-permute-start.14 = (bf16[2,256,256]{2,1,0:T(8,128)(2,1)S(1)}, bf16[2,256,256]{2,1,0:T(8,128)(2,1)S(1)}, u32[]{:S(2)}, u32[]{:S(2)}) collective-permute-start(bf16[2,256,256]{2,1,0:T(8,128)(2,1)S(1)} %get-tuple-element.7.refs_3_), channel_id=1, source_target_pairs={{0,4},{4,0},{8,12},{12,8},{16,20},{20,16},{24,28},{28,24},{1,5},{5... | collective-permute-start | bytes 786440 | tf_op jit(solution)/shard_map/ppermute | solution.py:41
  95.3 4.3 %collective-permute-start.7 = (bf16[2,256,256]{2,1,0:T(8,128)(2,1)S(1)}, bf16[2,256,256]{2,1,0:T(8,128)(2,1)S(1)}, u32[]{:S(2)}, u32[]{:S(2)}) collective-permute-start(bf16[2,256,256]{2,1,0:T(8,128)(2,1)S(1)} %collective-permute-done.6.refs_1_), channel_id=1, source_target_pairs={{0,8},{4,12},{8,16},{12,20},{16,24},{20,28},{1,9},{5,13},{9,17},{1... | collective-permute-start | bytes 786440 | tf_op jit(solution)/shard_map/ppermute | solution.py:44
  99.6 1.3 %collective-permute-start.10 = (bf16[2,256,256]{2,1,0:T(8,128)(2,1)S(1)}, bf16[2,256,256]{2,1,0:T(8,128)(2,1)S(1)}, u32[]{:S(2)}, u32[]{:S(2)}) collective-permute-start(bf16[2,256,256]{2,1,0:T(8,128)(2,1)S(1)} %collective-permute-done.9.refs_5_), channel_id=1, source_target_pairs={{8,0},{12,4},{16,8},{20,12},{24,16},{28,20},{9,1},{13,5},{17,9},{2... | collective-permute-start | bytes 786440 | tf_op jit(solution)/shard_map/ppermute | solution.py:45
  100.9 2.6 %fusion.2 = f32[1,1,2,256,256]{4,3,2,1,0:T(8,128)} fusion(f32[1,1,2,256,256]{4,3,2,1,0:T(8,128)} %param.13, f32[2,256,256]{2,1,0:T(8,128)S(1)} %convert_reduce_fusion, f32[2]{0:T(128)S(1)} %convert_element_type.35, pred[2]{0:T(512)(128)(4,1)S(1)} %dynamic-slice_reduce_fusion), kind=kOutput, calls=%fused_computation.5 | convolution fusion | flops 201981952 | bytes 1572874 | tf_op jit(solution)/shard_map/sji,sjk->sik/dot_general | solution.py:142
  103.5 2.4 %fusion.5 = f32[1,1,2,256,256]{4,3,2,1,0:T(8,128)} fusion(f32[1,1,2,256,256]{4,3,2,1,0:T(8,128)} %param.12, f32[2,256,256]{2,1,0:T(8,128)S(1)} %convert_reduce_fusion, f32[2]{0:T(128)S(1)} %convert_element_type.35, pred[2]{0:T(512)(128)(4,1)S(1)} %dynamic-slice_reduce_fusion), kind=kOutput, calls=%fused_computation.9 | convolution fusion | flops 201981952 | bytes 1572874 | tf_op jit(solution)/shard_map/sij,skj->sik/dot_general | solution.py:139
  105.9 1.9 %collective-permute-start.15 = (bf16[2,256,256]{2,1,0:T(8,128)(2,1)S(1)}, bf16[2,256,256]{2,1,0:T(8,128)(2,1)S(1)}, u32[]{:S(2)}, u32[]{:S(2)}) collective-permute-start(bf16[2,256,256]{2,1,0:T(8,128)(2,1)S(1)} %collective-permute-done.8.refs_4_), channel_id=1, source_target_pairs={{0,4},{4,0},{8,12},{12,8},{16,20},{20,16},{24,28},{28,24},{1,5},{5... | collective-permute-start | bytes 786440 | tf_op jit(solution)/shard_map/ppermute | solution.py:47
  108.4 1.8 %collective-permute-start.17 = (bf16[2,256,256]{2,1,0:T(8,128)(2,1)S(1)}, bf16[2,256,256]{2,1,0:T(8,128)(2,1)}, u32[]{:S(2)}, u32[]{:S(2)}) collective-permute-start(bf16[2,256,256]{2,1,0:T(8,128)(2,1)S(1)} %collective-permute-done.10.refs_6_), channel_id=1, source_target_pairs={{0,4},{4,0},{8,12},{12,8},{16,20},{20,16},{24,28},{28,24},{1,5},{5... | collective-permute-start | bytes 786440 | tf_op jit(solution)/shard_map/ppermute | solution.py:47
  112.9 3.2 %shard_map.128 = bf16[8,256,256]{2,1,0:T(8,128)(2,1)} custom-call(s32[8,2]{1,0:T(8,128)} %copy.39.table_ref, bf16[2,256,256]{2,1,0:T(8,128)(2,1)} %copy-done.11, bf16[2,256,256]{2,1,0:T(8,128)(2,1)} %copy-done.7, bf16[2,256,256]{2,1,0:T(8,128)(2,1)} %copy-done.5, bf16[2,256,256]{2,1,0:T(8,128)(2,1)} %copy-done.2, bf16[2,256,256]{2,1,0:T(8,128)(2,1)} %copy-done.6, ...), custom_call_target="tpu_custom_call" | custom-call | tf_op jit(solution)/shard_map/pallas_call | solution.py:79
  (88 shorter events, 10.3 us)
Async XLA Ops:
  4.6 54.8 %all-to-all-start = ((bf16[8,2,256,256]{3,2,1,0:T(8,128)(2,1)}), bf16[8,2,256,256]{3,2,1,0:T(8,128)(2,1)}, u32[]{:S(2)}, u32[]{:S(2)}) async-start(bf16[8,2,256,256]{3,2,1,0:T(8,128)(2,1)} %bitcast.3), calls=%async_computation | async-start | bytes 4194304 | tf_op jit(solution)/shard_map/all_to_all | solution.py:123
  11.1 50.2 %copy-start.1 = (f32[1,1,2,256,256]{4,3,2,1,0:T(8,128)S(1)}, f32[1,1,2,256,256]{4,3,2,1,0:T(8,128)}, u32[]{:S(2)}) copy-start(f32[1,1,2,256,256]{4,3,2,1,0:T(8,128)} %param.16) | copy-start | bytes 1572868
  11.1 50.7 %copy-start.4 = (bf16[1,1,2,256,256]{4,3,2,1,0:T(8,128)(2,1)S(1)}, bf16[1,1,2,256,256]{4,3,2,1,0:T(8,128)(2,1)}, u32[]{:S(2)}) copy-start(bf16[1,1,2,256,256]{4,3,2,1,0:T(8,128)(2,1)} %param.15) | copy-start | bytes 786436
  12.0 64.2 %copy-start.3 = (f32[1,1,2,256,256]{4,3,2,1,0:T(8,128)S(1)}, f32[1,1,2,256,256]{4,3,2,1,0:T(8,128)}, u32[]{:S(2)}) copy-start(f32[1,1,2,256,256]{4,3,2,1,0:T(8,128)} %param.17) | copy-start | bytes 1572868
  63.5 1.8 %collective-permute-start = (f32[2,9]{1,0:T(2,128)S(1)}, f32[2,9]{1,0:T(2,128)S(1)}, u32[]{:S(2)}, u32[]{:S(2)}) collective-permute-start(f32[2,9]{1,0:T(2,128)S(1)} %pad_maximum_fusion), channel_id=1, source_target_pairs={{0,4},{4,0},{8,12},{12,8},{16,20},{20,16},{24,28},{28,24},{1,5},{5... | collective-permute-start | bytes 224 | tf_op jit(solution)/shard_map/ppermute | solution.py:20
  65.3 2.5 %collective-permute-start.1 = (f32[2,9]{1,0:T(2,128)S(1)}, f32[2,9]{1,0:T(2,128)S(1)}, u32[]{:S(2)}, u32[]{:S(2)}) collective-permute-start(f32[2,9]{1,0:T(2,128)S(1)} %fusion.30), channel_id=1, source_target_pairs={{0,8},{4,12},{8,0},{12,4},{16,24},{20,28},{24,16},{28,20},{1,9},{5... | collective-permute-start | bytes 224 | tf_op jit(solution)/shard_map/ppermute | solution.py:20
  67.8 3.4 %collective-permute-start.2 = (f32[2,9]{1,0:T(2,128)S(1)}, f32[2,9]{1,0:T(2,128)S(1)}, u32[]{:S(2)}, u32[]{:S(2)}) collective-permute-start(f32[2,9]{1,0:T(2,128)S(1)} %fusion.35), channel_id=1, source_target_pairs={{0,16},{4,20},{8,24},{12,28},{16,0},{20,4},{24,8},{28,12},{1,17},{... | collective-permute-start | bytes 224 | tf_op jit(solution)/shard_map/ppermute | solution.py:20
  71.2 2.4 %collective-permute-start.3 = (f32[2,9]{1,0:T(2,128)S(1)}, f32[2,9]{1,0:T(2,128)S(1)}, u32[]{:S(2)}, u32[]{:S(2)}) collective-permute-start(f32[2,9]{1,0:T(2,128)S(1)} %add.92), channel_id=1, source_target_pairs={{0,1},{1,0},{2,3},{3,2},{4,5},{5,4},{6,7},{7,6},{8,9},{9,8},{10,11... | collective-permute-start | bytes 224 | tf_op jit(solution)/shard_map/ppermute | solution.py:20
  73.6 2.4 %collective-permute-start.4 = (f32[2,9]{1,0:T(2,128)S(1)}, f32[2,9]{1,0:T(2,128)S(1)}, u32[]{:S(2)}, u32[]{:S(2)}) collective-permute-start(f32[2,9]{1,0:T(2,128)S(1)} %add.93), channel_id=1, source_target_pairs={{0,2},{1,3},{2,0},{3,1},{4,6},{5,7},{6,4},{7,5},{8,10},{9,11},{10,... | collective-permute-start | bytes 224 | tf_op jit(solution)/shard_map/ppermute | solution.py:20
  77.2 34.0 %copy-start.2 = (bf16[2,256,256]{2,1,0:T(8,128)(2,1)}, bf16[2,256,256]{2,1,0:T(8,128)(2,1)S(1)}, u32[]{:S(2)}) copy-start(bf16[2,256,256]{2,1,0:T(8,128)(2,1)S(1)} %get-tuple-element.7.refs_3_) | copy-start | bytes 786436
  77.2 5.2 %collective-permute-start.5 = (bf16[2,256,256]{2,1,0:T(8,128)(2,1)S(1)}, bf16[2,256,256]{2,1,0:T(8,128)(2,1)S(1)}, u32[]{:S(2)}, u32[]{:S(2)}) collective-permute-start(bf16[2,256,256]{2,1,0:T(8,128)(2,1)S(1)} %get-tuple-element.7.refs_3_), channel_id=1, source_target_pairs={{0,8},{4,12},{8,16},{12,20},{16,24},{20,28},{1,9},{5,13},{9,17},{1... | collective-permute-start | bytes 786440 | tf_op jit(solution)/shard_map/ppermute | solution.py:44
  79.1 7.1 %collective-permute-start.8 = (bf16[2,256,256]{2,1,0:T(8,128)(2,1)S(1)}, bf16[2,256,256]{2,1,0:T(8,128)(2,1)S(1)}, u32[]{:S(2)}, u32[]{:S(2)}) collective-permute-start(bf16[2,256,256]{2,1,0:T(8,128)(2,1)S(1)} %get-tuple-element.7.refs_3_), channel_id=1, source_target_pairs={{8,0},{12,4},{16,8},{20,12},{24,16},{28,20},{9,1},{13,5},{17,9},{2... | collective-permute-start | bytes 786440 | tf_op jit(solution)/shard_map/ppermute | solution.py:45
  82.4 28.8 %copy-start.5 = (bf16[2,256,256]{2,1,0:T(8,128)(2,1)}, bf16[2,256,256]{2,1,0:T(8,128)(2,1)S(1)}, u32[]{:S(2)}) copy-start(bf16[2,256,256]{2,1,0:T(8,128)(2,1)S(1)} %collective-permute-done.5.refs_2_) | copy-start | bytes 786436
  82.4 12.9 %collective-permute-start.6 = (bf16[2,256,256]{2,1,0:T(8,128)(2,1)S(1)}, bf16[2,256,256]{2,1,0:T(8,128)(2,1)S(1)}, u32[]{:S(2)}, u32[]{:S(2)}) collective-permute-start(bf16[2,256,256]{2,1,0:T(8,128)(2,1)S(1)} %collective-permute-done.5.refs_2_), channel_id=1, source_target_pairs={{0,8},{4,12},{8,16},{12,20},{16,24},{20,28},{1,9},{5,13},{9,17},{1... | collective-permute-start | bytes 786440 | tf_op jit(solution)/shard_map/ppermute | solution.py:44
  86.3 13.4 %collective-permute-start.9 = (bf16[2,256,256]{2,1,0:T(8,128)(2,1)S(1)}, bf16[2,256,256]{2,1,0:T(8,128)(2,1)S(1)}, u32[]{:S(2)}, u32[]{:S(2)}) collective-permute-start(bf16[2,256,256]{2,1,0:T(8,128)(2,1)S(1)} %collective-permute-done.8.refs_4_), channel_id=1, source_target_pairs={{8,0},{12,4},{16,8},{20,12},{24,16},{28,20},{9,1},{13,5},{17,9},{2... | collective-permute-start | bytes 786440 | tf_op jit(solution)/shard_map/ppermute | solution.py:45
  88.3 19.5 %collective-permute-start.14 = (bf16[2,256,256]{2,1,0:T(8,128)(2,1)S(1)}, bf16[2,256,256]{2,1,0:T(8,128)(2,1)S(1)}, u32[]{:S(2)}, u32[]{:S(2)}) collective-permute-start(bf16[2,256,256]{2,1,0:T(8,128)(2,1)S(1)} %get-tuple-element.7.refs_3_), channel_id=1, source_target_pairs={{0,4},{4,0},{8,12},{12,8},{16,20},{20,16},{24,28},{28,24},{1,5},{5... | collective-permute-start | bytes 786440 | tf_op jit(solution)/shard_map/ppermute | solution.py:41
  95.3 12.6 %collective-permute-start.13 = (bf16[2,256,256]{2,1,0:T(8,128)(2,1)S(1)}, bf16[2,256,256]{2,1,0:T(8,128)(2,1)S(1)}, u32[]{:S(2)}, u32[]{:S(2)}) collective-permute-start(bf16[2,256,256]{2,1,0:T(8,128)(2,1)S(1)} %collective-permute-done.5.refs_2_), channel_id=1, source_target_pairs={{0,4},{4,0},{8,12},{12,8},{16,20},{20,16},{24,28},{28,24},{1,5},{5... | collective-permute-start | bytes 786440 | tf_op jit(solution)/shard_map/ppermute | solution.py:46
  95.3 13.0 %collective-permute-start.7 = (bf16[2,256,256]{2,1,0:T(8,128)(2,1)S(1)}, bf16[2,256,256]{2,1,0:T(8,128)(2,1)S(1)}, u32[]{:S(2)}, u32[]{:S(2)}) collective-permute-start(bf16[2,256,256]{2,1,0:T(8,128)(2,1)S(1)} %collective-permute-done.6.refs_1_), channel_id=1, source_target_pairs={{0,8},{4,12},{8,16},{12,20},{16,24},{20,28},{1,9},{5,13},{9,17},{1... | collective-permute-start | bytes 786440 | tf_op jit(solution)/shard_map/ppermute | solution.py:44
  99.6 8.8 %collective-permute-start.10 = (bf16[2,256,256]{2,1,0:T(8,128)(2,1)S(1)}, bf16[2,256,256]{2,1,0:T(8,128)(2,1)S(1)}, u32[]{:S(2)}, u32[]{:S(2)}) collective-permute-start(bf16[2,256,256]{2,1,0:T(8,128)(2,1)S(1)} %collective-permute-done.9.refs_5_), channel_id=1, source_target_pairs={{8,0},{12,4},{16,8},{20,12},{24,16},{28,20},{9,1},{13,5},{17,9},{2... | collective-permute-start | bytes 786440 | tf_op jit(solution)/shard_map/ppermute | solution.py:45
  105.9 5.4 %collective-permute-start.15 = (bf16[2,256,256]{2,1,0:T(8,128)(2,1)S(1)}, bf16[2,256,256]{2,1,0:T(8,128)(2,1)S(1)}, u32[]{:S(2)}, u32[]{:S(2)}) collective-permute-start(bf16[2,256,256]{2,1,0:T(8,128)(2,1)S(1)} %collective-permute-done.8.refs_4_), channel_id=1, source_target_pairs={{0,4},{4,0},{8,12},{12,8},{16,20},{20,16},{24,28},{28,24},{1,5},{5... | collective-permute-start | bytes 786440 | tf_op jit(solution)/shard_map/ppermute | solution.py:47
  107.8 3.5 %collective-permute-start.12 = (bf16[2,256,256]{2,1,0:T(8,128)(2,1)S(1)}, bf16[2,256,256]{2,1,0:T(8,128)(2,1)S(1)}, u32[]{:S(2)}, u32[]{:S(2)}) collective-permute-start(bf16[2,256,256]{2,1,0:T(8,128)(2,1)S(1)} %collective-permute-done.6.refs_1_), channel_id=1, source_target_pairs={{0,4},{4,0},{8,12},{12,8},{16,20},{20,16},{24,28},{28,24},{1,5},{5... | collective-permute-start | bytes 786440 | tf_op jit(solution)/shard_map/ppermute | solution.py:46
  107.9 3.4 %collective-permute-start.16 = (bf16[2,256,256]{2,1,0:T(8,128)(2,1)S(1)}, bf16[2,256,256]{2,1,0:T(8,128)(2,1)S(1)}, u32[]{:S(2)}, u32[]{:S(2)}) collective-permute-start(bf16[2,256,256]{2,1,0:T(8,128)(2,1)S(1)} %collective-permute-done.9.refs_5_), channel_id=1, source_target_pairs={{0,4},{4,0},{8,12},{12,8},{16,20},{20,16},{24,28},{28,24},{1,5},{5... | collective-permute-start | bytes 786440 | tf_op jit(solution)/shard_map/ppermute | solution.py:47
  108.3 3.0 %collective-permute-start.11 = (bf16[2,256,256]{2,1,0:T(8,128)(2,1)S(1)}, bf16[2,256,256]{2,1,0:T(8,128)(2,1)S(1)}, u32[]{:S(2)}, u32[]{:S(2)}) collective-permute-start(bf16[2,256,256]{2,1,0:T(8,128)(2,1)S(1)} %collective-permute-done.7.refs_0_), channel_id=1, source_target_pairs={{0,4},{4,0},{8,12},{12,8},{16,20},{20,16},{24,28},{28,24},{1,5},{5... | collective-permute-start | bytes 786440 | tf_op jit(solution)/shard_map/ppermute | solution.py:46
  108.4 4.4 %collective-permute-start.17 = (bf16[2,256,256]{2,1,0:T(8,128)(2,1)S(1)}, bf16[2,256,256]{2,1,0:T(8,128)(2,1)}, u32[]{:S(2)}, u32[]{:S(2)}) collective-permute-start(bf16[2,256,256]{2,1,0:T(8,128)(2,1)S(1)} %collective-permute-done.10.refs_6_), channel_id=1, source_target_pairs={{0,4},{4,0},{8,12},{12,8},{16,20},{20,16},{24,28},{28,24},{1,5},{5... | collective-permute-start | bytes 786440 | tf_op jit(solution)/shard_map/ppermute | solution.py:47
  (14 other events, 103.5 us)

commit v12 on v8

--- a/solution.py
+++ b/solution.py
@@ -120,8 +120,8 @@
     by_owner = jnp.take(local_grads, slot_table.reshape(-1), axis=0, mode="clip").reshape(
         (replicas, slot_count) + local_grads.shape[1:]
     )
-    received = lax.all_to_all(by_owner, "dp", 0, 0, tiled=True)
-    owned_grad = jnp.sum(received.astype(jnp.float32), axis=0) * live_float
+    received = [lax.all_to_all(by_owner[:, slot], "dp", 0, 0, tiled=True) for slot in range(slot_count)]
+    owned_grad = jnp.stack([jnp.sum(part.astype(jnp.float32), axis=0) for part in received]) * live_float
     left = stats_left[0, 0]
     right = stats_right[0, 0]
     moment = second_moment[0, 0]

time: 117 us -> 127 us (1.085)
  blocking collectives: 0 us -> 32 us
  waiting for transfers between devices: 58.3 us -> 34.4 us
    all_to_all x0 -> x1, blocking collectives: none -> 32 us  [local(): lax.all_to_all(by_owner[:, slot], 'dp', 0, 0, tiled=True)]
    all_to_all x1, waiting for transfers between devices: 47.4 us -> 23.4 us  [local(): lax.all_to_all(by_owner[:, slot], 'dp', 0, 0, tiled=True)]
    ppermute x3, starting transfers between devices: 3.49 us -> 5.66 us  [gather_blocks(): near_right[step] = lax.ppermute(from_right[step], 'dp', partner)]
    all_to_all x1, starting transfers between devices: 6.51 us -> 4.63 us  [local(): lax.all_to_all(by_owner[:, slot], 'dp', 0, 0, tiled=True)]
    gather x1, local copies, waits for them, and re-layouts: 1.99 us -> 0.68 us  [local(): jnp.take(local_grads, slot_table.reshape(-1), axis=0, mode='clip')]
  transfers between devices with their start and end apart: 19 -> 19, of which waited for: 7 -> 7; matrix products, arithmetic and copies ran while one was open for 7% -> 8% of each run, Pallas kernels for 0% -> 0%
where the time goes in v12:
time: 127 us; the launch traced here: 126 us
  starting transfers between devices  35.6 us (28%)
  waiting for transfers between devices  34.4 us (27%)
  blocking collectives  32 us (25%)
  other arithmetic  7.77 us (6%)
  matrix products  7.28 us (6%)
  local copies, waits for them, and re-layouts  4.97 us (4%)
  Pallas kernels  3.13 us (2%)
    all_to_all x1, blocking collectives, local(): lax.all_to_all(by_owner[:, slot], 'dp', 0, 0, tiled=True)  32 us
    all_to_all x1, waiting for transfers between devices, local(): lax.all_to_all(by_owner[:, slot], 'dp', 0, 0, tiled=True)  23.4 us
    ppermute x3, starting transfers between devices, gather_blocks(): from_left[step] = lax.ppermute(from_left[step - 1], 'dp', rightward)  10.7 us
    ppermute x5, waiting for transfers between devices, butterfly_sum(): x = x + lax.ppermute(x, axis, [(i, i ^ step) for i in range(size)])  8.92 us
    ppermute x1, starting transfers between devices, gather_blocks(): near_left[0] = lax.ppermute(mine, 'dp', partner)  7.12 us
    ppermute x3, starting transfers between devices, gather_blocks(): near_right[step] = lax.ppermute(from_right[step], 'dp', partner)  5.66 us
    all_to_all x1, starting transfers between devices, local(): lax.all_to_all(by_owner[:, slot], 'dp', 0, 0, tiled=True)  4.63 us
    ppermute x3, starting transfers between devices, gather_blocks(): from_right[step] = lax.ppermute(from_right[step - 1], 'dp', leftward)  3.87 us
  transfers between devices with their start and end apart: 19, of which 7 were waited for; matrix products, arithmetic and copies ran while one was open for 8% of the time, Pallas kernels for 0%

profile of v12, /device:TPU:1, one launch (start us, length us, event | category | flops | bytes accessed | tf_op | source)
XLA Modules:
  0.0 126.0 jit_solution(3072073922810393847)
XLA Ops:
  4.4 32.0 %all_to_all.10 = bf16[8,256,256]{2,1,0:T(8,128)(2,1)} all-to-all(bf16[8,256,256]{2,1,0:T(8,128)(2,1)S(1)} %get-tuple-element.7), channel_id=1, replica_groups=mesh['dp'=8,'shard'=4] {'dp'}, dimensions={0} | all-to-all | bytes 2097152 | tf_op jit(solution)/shard_map/all_to_all | solution.py:123
  36.4 4.6 %all-to-all-start.1 = ((bf16[8,256,256]{2,1,0:T(8,128)(2,1)}), bf16[8,256,256]{2,1,0:T(8,128)(2,1)S(1)}, u32[]{:S(2)}, u32[]{:S(2)}) async-start(bf16[8,256,256]{2,1,0:T(8,128)(2,1)} %get-tuple-element.8), calls=%async_computation.1 | async-start | bytes 2097152 | tf_op jit(solution)/shard_map/all_to_all | solution.py:123
  41.9 1.4 %convert_reduce_fusion.1 = f32[256,256]{1,0:T(8,128)S(1)} fusion(bf16[8,256,256]{2,1,0:T(8,128)(2,1)} %all_to_all.10), kind=kLoop, calls=%fused_computation.2 | loop fusion | flops 983040 | bytes 1310720 | tf_op jit(solution)/shard_map/reduce_sum | solution.py:124
  43.3 23.4 %all-to-all-done.1 = bf16[8,256,256]{2,1,0:T(8,128)(2,1)S(1)} async-done(((bf16[8,256,256]{2,1,0:T(8,128)(2,1)}), bf16[8,256,256]{2,1,0:T(8,128)(2,1)S(1)}, u32[]{:S(2)}, u32[]{:S(2)}) %all-to-all-start.1) | async-done | bytes 1048608 | tf_op jit(solution)/shard_map/all_to_all | solution.py:123
  67.4 1.6 %multiply_reduce_fusion = (f32[2]{0:T(128)S(1)}, f32[2,256,256]{2,1,0:T(8,128)S(1)}) fusion(bf16[1,1,2,256,256]{4,3,2,1,0:T(8,128)(2,1)S(1)} %copy-done.3, bf16[1,1,2,256,256]{4,3,2,1,0:T(8,128)(2,1)} %param.14, f32[1,256,256]{2,1,0:T(8,128)S(1)} %bitcast.63, f32[1,256,256]{2,1,0:T(8,128)S(1)} %bitcast.58, f32[2]{0:T(128)S(1)} %convert_element_type.39), kind=kOutput, calls=%fused_computation.29 | convolution fusion | flops 135004160 | bytes 1572880 | tf_op jit(solution)/shard_map/sij,sjk->sik/dot_general | solution.py:149
  70.9 2.4 %collective-permute-done.1 = f32[2,9]{1,0:T(2,128)S(1)} collective-permute-done((f32[2,9]{1,0:T(2,128)S(1)}, f32[2,9]{1,0:T(2,128)S(1)}, u32[]{:S(2)}, u32[]{:S(2)}) %collective-permute-start.1) | collective-permute-done | bytes 104 | tf_op jit(solution)/shard_map/ppermute | solution.py:20
  73.4 3.3 %collective-permute-done.2 = f32[2,9]{1,0:T(2,128)S(1)} collective-permute-done((f32[2,9]{1,0:T(2,128)S(1)}, f32[2,9]{1,0:T(2,128)S(1)}, u32[]{:S(2)}, u32[]{:S(2)}) %collective-permute-start.2) | collective-permute-done | bytes 104 | tf_op jit(solution)/shard_map/ppermute | solution.py:20
  76.8 1.2 collective-permute-start.3
  78.0 1.2 collective-permute-done.3
  79.2 1.2 collective-permute-start.4
  81.8 2.0 %fusion.27 = (bf16[2,256,256]{2,1,0:T(8,128)(2,1)S(1)}, f32[1,1,2,256,256]{4,3,2,1,0:T(8,128)}) fusion(f32[2,256,256]{2,1,0:T(8,128)S(1)} %get-tuple-element.12, f32[2]{0:T(128)S(1)} %broadcast_multiply_fusion, f32[1,1,2,256,256]{4,3,2,1,0:T(8,128)} %param.17, pred[2]{0:T(512)(128)(4,1)S(1)} %dynamic-slice_reduce_fusion), kind=kLoop, calls=%fused_computation.67 | loop fusion | flops 524288 | bytes 1835018 | tf_op jit(solution)/shard_map/convert_element_type | solution.py:164
  83.8 1.9 %collective-permute-start.5 = (bf16[2,256,256]{2,1,0:T(8,128)(2,1)S(1)}, bf16[2,256,256]{2,1,0:T(8,128)(2,1)S(1)}, u32[]{:S(2)}, u32[]{:S(2)}) collective-permute-start(bf16[2,256,256]{2,1,0:T(8,128)(2,1)S(1)} %get-tuple-element.9.refs_3_), channel_id=1, source_target_pairs={{0,8},{4,12},{8,16},{12,20},{16,24},{20,28},{1,9},{5,13},{9,17},{1... | collective-permute-start | bytes 786440 | tf_op jit(solution)/shard_map/ppermute | solution.py:44
  85.7 1.3 %collective-permute-start.8 = (bf16[2,256,256]{2,1,0:T(8,128)(2,1)S(1)}, bf16[2,256,256]{2,1,0:T(8,128)(2,1)S(1)}, u32[]{:S(2)}, u32[]{:S(2)}) collective-permute-start(bf16[2,256,256]{2,1,0:T(8,128)(2,1)S(1)} %get-tuple-element.9.refs_3_), channel_id=1, source_target_pairs={{8,0},{12,4},{16,8},{20,12},{24,16},{28,20},{9,1},{13,5},{17,9},{2... | collective-permute-start | bytes 786440 | tf_op jit(solution)/shard_map/ppermute | solution.py:45
  87.0 2.0 %collective-permute-done.5.refs_2_ = bf16[2,256,256]{2,1,0:T(8,128)(2,1)S(1)} collective-permute-done((bf16[2,256,256]{2,1,0:T(8,128)(2,1)S(1)}, bf16[2,256,256]{2,1,0:T(8,128)(2,1)S(1)}, u32[]{:S(2)}, u32[]{:S(2)}) %collective-permute-start.5) | collective-permute-done | bytes 262176 | tf_op jit(solution)/shard_map/ppermute | solution.py:44
  89.0 3.8 %collective-permute-start.6 = (bf16[2,256,256]{2,1,0:T(8,128)(2,1)S(1)}, bf16[2,256,256]{2,1,0:T(8,128)(2,1)S(1)}, u32[]{:S(2)}, u32[]{:S(2)}) collective-permute-start(bf16[2,256,256]{2,1,0:T(8,128)(2,1)S(1)} %collective-permute-done.5.refs_2_), channel_id=1, source_target_pairs={{0,8},{4,12},{8,16},{12,20},{16,24},{20,28},{1,9},{5,13},{9,17},{1... | collective-permute-start | bytes 786440 | tf_op jit(solution)/shard_map/ppermute | solution.py:44
  92.8 1.3 %collective-permute-start.9 = (bf16[2,256,256]{2,1,0:T(8,128)(2,1)S(1)}, bf16[2,256,256]{2,1,0:T(8,128)(2,1)S(1)}, u32[]{:S(2)}, u32[]{:S(2)}) collective-permute-start(bf16[2,256,256]{2,1,0:T(8,128)(2,1)S(1)} %collective-permute-done.8.refs_4_), channel_id=1, source_target_pairs={{8,0},{12,4},{16,8},{20,12},{24,16},{28,20},{9,1},{13,5},{17,9},{2... | collective-permute-start | bytes 786440 | tf_op jit(solution)/shard_map/ppermute | solution.py:45
  94.2 7.1 %collective-permute-start.14 = (bf16[2,256,256]{2,1,0:T(8,128)(2,1)S(1)}, bf16[2,256,256]{2,1,0:T(8,128)(2,1)}, u32[]{:S(2)}, u32[]{:S(2)}) collective-permute-start(bf16[2,256,256]{2,1,0:T(8,128)(2,1)S(1)} %get-tuple-element.9.refs_3_), channel_id=1, source_target_pairs={{0,4},{4,0},{8,12},{12,8},{16,20},{20,16},{24,28},{28,24},{1,5},{5... | collective-permute-start | bytes 786440 | tf_op jit(solution)/shard_map/ppermute | solution.py:41
  101.4 5.0 %collective-permute-start.7 = (bf16[2,256,256]{2,1,0:T(8,128)(2,1)S(1)}, bf16[2,256,256]{2,1,0:T(8,128)(2,1)}, u32[]{:S(2)}, u32[]{:S(2)}) collective-permute-start(bf16[2,256,256]{2,1,0:T(8,128)(2,1)S(1)} %collective-permute-done.6.refs_1_), channel_id=1, source_target_pairs={{0,8},{4,12},{8,16},{12,20},{16,24},{20,28},{1,9},{5,13},{9,17},{1... | collective-permute-start | bytes 786440 | tf_op jit(solution)/shard_map/ppermute | solution.py:44
  106.4 1.3 %collective-permute-start.10 = (bf16[2,256,256]{2,1,0:T(8,128)(2,1)S(1)}, bf16[2,256,256]{2,1,0:T(8,128)(2,1)}, u32[]{:S(2)}, u32[]{:S(2)}) collective-permute-start(bf16[2,256,256]{2,1,0:T(8,128)(2,1)S(1)} %collective-permute-done.9.refs_5_), channel_id=1, source_target_pairs={{8,0},{12,4},{16,8},{20,12},{24,16},{28,20},{9,1},{13,5},{17,9},{2... | collective-permute-start | bytes 786440 | tf_op jit(solution)/shard_map/ppermute | solution.py:45
  108.3 3.0 %fusion.2 = f32[1,1,2,256,256]{4,3,2,1,0:T(8,128)} fusion(f32[1,1,2,256,256]{4,3,2,1,0:T(8,128)} %param.13, pred[2]{0:T(512)(128)(4,1)S(1)} %dynamic-slice_reduce_fusion, f32[1,256,256]{2,1,0:T(8,128)S(1)} %bitcast.64, f32[1,256,256]{2,1,0:T(8,128)S(1)} %bitcast.59, f32[2]{0:T(128)S(1)} %convert_element_type.39), kind=kOutput, calls=%fused_computation.6 | convolution fusion | flops 403439616 | bytes 1572874 | tf_op jit(solution)/shard_map/sji,sjk->sik/dot_general | solution.py:142
  111.3 2.2 %collective-permute-start.15 = (bf16[2,256,256]{2,1,0:T(8,128)(2,1)S(1)}, bf16[2,256,256]{2,1,0:T(8,128)(2,1)S(1)}, u32[]{:S(2)}, u32[]{:S(2)}) collective-permute-start(bf16[2,256,256]{2,1,0:T(8,128)(2,1)S(1)} %collective-permute-done.8.refs_4_), channel_id=1, source_target_pairs={{0,4},{4,0},{8,12},{12,8},{16,20},{20,16},{24,28},{28,24},{1,5},{5... | collective-permute-start | bytes 786440 | tf_op jit(solution)/shard_map/ppermute | solution.py:47
  114.1 3.0 %collective-permute-start.17 = (bf16[2,256,256]{2,1,0:T(8,128)(2,1)}, bf16[2,256,256]{2,1,0:T(8,128)(2,1)}, u32[]{:S(2)}, u32[]{:S(2)}) collective-permute-start(bf16[2,256,256]{2,1,0:T(8,128)(2,1)} %collective-permute-done.10.refs_6_), channel_id=1, source_target_pairs={{0,4},{4,0},{8,12},{12,8},{16,20},{20,16},{24,28},{28,24},{1,5},{5... | collective-permute-start | bytes 786440 | tf_op jit(solution)/shard_map/ppermute | solution.py:47
  117.1 2.7 %fusion.5 = f32[1,1,2,256,256]{4,3,2,1,0:T(8,128)} fusion(f32[1,1,2,256,256]{4,3,2,1,0:T(8,128)} %param.12, pred[2]{0:T(512)(128)(4,1)S(1)} %dynamic-slice_reduce_fusion, f32[1,256,256]{2,1,0:T(8,128)S(1)} %bitcast.65, f32[1,256,256]{2,1,0:T(8,128)S(1)} %bitcast.60, f32[2]{0:T(128)S(1)} %convert_element_type.39), kind=kOutput, calls=%fused_computation.10 | convolution fusion | flops 403439616 | bytes 1572874 | tf_op jit(solution)/shard_map/sij,skj->sik/dot_general | solution.py:139
  122.9 3.1 %shard_map.128 = bf16[8,256,256]{2,1,0:T(8,128)(2,1)} custom-call(s32[8,2]{1,0:T(8,128)} %copy.39.table_ref, bf16[2,256,256]{2,1,0:T(8,128)(2,1)} %collective-permute-done.7.refs_0_, bf16[2,256,256]{2,1,0:T(8,128)(2,1)} %copy-done.6, bf16[2,256,256]{2,1,0:T(8,128)(2,1)} %copy-done.4, bf16[2,256,256]{2,1,0:T(8,128)(2,1)} %copy-done.2, ...), custom_call_target="tpu_custom_call" | custom-call | tf_op jit(solution)/shard_map/pallas_call | solution.py:79
  (81 shorter events, 13.1 us)
Async XLA Ops:
  4.4 37.0 %copy-start.13 = (s32[9]{0:T(128)S(1)}, s32[9]{0:T(128)}, u32[]{:S(2)}) copy-start(s32[9]{0:T(128)} %param.11) | copy-start | bytes 112
  36.4 30.5 %copy-start.1 = (f32[1,1,2,256,256]{4,3,2,1,0:T(8,128)S(1)}, f32[1,1,2,256,256]{4,3,2,1,0:T(8,128)}, u32[]{:S(2)}) copy-start(f32[1,1,2,256,256]{4,3,2,1,0:T(8,128)} %param.16) | copy-start | bytes 1572868
  36.4 30.4 %all-to-all-start.1 = ((bf16[8,256,256]{2,1,0:T(8,128)(2,1)}), bf16[8,256,256]{2,1,0:T(8,128)(2,1)S(1)}, u32[]{:S(2)}, u32[]{:S(2)}) async-start(bf16[8,256,256]{2,1,0:T(8,128)(2,1)} %get-tuple-element.8), calls=%async_computation.1 | async-start | bytes 2097152 | tf_op jit(solution)/shard_map/all_to_all | solution.py:123
  69.1 1.8 %collective-permute-start = (f32[2,9]{1,0:T(2,128)S(1)}, f32[2,9]{1,0:T(2,128)S(1)}, u32[]{:S(2)}, u32[]{:S(2)}) collective-permute-start(f32[2,9]{1,0:T(2,128)S(1)} %pad_maximum_fusion), channel_id=1, source_target_pairs={{0,4},{4,0},{8,12},{12,8},{16,20},{20,16},{24,28},{28,24},{1,5},{5... | collective-permute-start | bytes 224 | tf_op jit(solution)/shard_map/ppermute | solution.py:20
  70.9 2.5 %collective-permute-start.1 = (f32[2,9]{1,0:T(2,128)S(1)}, f32[2,9]{1,0:T(2,128)S(1)}, u32[]{:S(2)}, u32[]{:S(2)}) collective-permute-start(f32[2,9]{1,0:T(2,128)S(1)} %fusion.26), channel_id=1, source_target_pairs={{0,8},{4,12},{8,0},{12,4},{16,24},{20,28},{24,16},{28,20},{1,9},{5... | collective-permute-start | bytes 224 | tf_op jit(solution)/shard_map/ppermute | solution.py:20
  73.4 3.4 %collective-permute-start.2 = (f32[2,9]{1,0:T(2,128)S(1)}, f32[2,9]{1,0:T(2,128)S(1)}, u32[]{:S(2)}, u32[]{:S(2)}) collective-permute-start(f32[2,9]{1,0:T(2,128)S(1)} %fusion.33), channel_id=1, source_target_pairs={{0,16},{4,20},{8,24},{12,28},{16,0},{20,4},{24,8},{28,12},{1,17},{... | collective-permute-start | bytes 224 | tf_op jit(solution)/shard_map/ppermute | solution.py:20
  76.8 2.4 %collective-permute-start.3 = (f32[2,9]{1,0:T(2,128)S(1)}, f32[2,9]{1,0:T(2,128)S(1)}, u32[]{:S(2)}, u32[]{:S(2)}) collective-permute-start(f32[2,9]{1,0:T(2,128)S(1)} %add.92), channel_id=1, source_target_pairs={{0,1},{1,0},{2,3},{3,2},{4,5},{5,4},{6,7},{7,6},{8,9},{9,8},{10,11... | collective-permute-start | bytes 224 | tf_op jit(solution)/shard_map/ppermute | solution.py:20
  79.2 2.4 %collective-permute-start.4 = (f32[2,9]{1,0:T(2,128)S(1)}, f32[2,9]{1,0:T(2,128)S(1)}, u32[]{:S(2)}, u32[]{:S(2)}) collective-permute-start(f32[2,9]{1,0:T(2,128)S(1)} %add.93), channel_id=1, source_target_pairs={{0,2},{1,3},{2,0},{3,1},{4,6},{5,7},{6,4},{7,5},{8,10},{9,11},{10,... | collective-permute-start | bytes 224 | tf_op jit(solution)/shard_map/ppermute | solution.py:20
  83.8 36.9 %copy-start.2 = (bf16[2,256,256]{2,1,0:T(8,128)(2,1)}, bf16[2,256,256]{2,1,0:T(8,128)(2,1)S(1)}, u32[]{:S(2)}) copy-start(bf16[2,256,256]{2,1,0:T(8,128)(2,1)S(1)} %get-tuple-element.9.refs_3_) | copy-start | bytes 786436
  83.8 5.2 %collective-permute-start.5 = (bf16[2,256,256]{2,1,0:T(8,128)(2,1)S(1)}, bf16[2,256,256]{2,1,0:T(8,128)(2,1)S(1)}, u32[]{:S(2)}, u32[]{:S(2)}) collective-permute-start(bf16[2,256,256]{2,1,0:T(8,128)(2,1)S(1)} %get-tuple-element.9.refs_3_), channel_id=1, source_target_pairs={{0,8},{4,12},{8,16},{12,20},{16,24},{20,28},{1,9},{5,13},{9,17},{1... | collective-permute-start | bytes 786440 | tf_op jit(solution)/shard_map/ppermute | solution.py:44
  85.7 7.1 %collective-permute-start.8 = (bf16[2,256,256]{2,1,0:T(8,128)(2,1)S(1)}, bf16[2,256,256]{2,1,0:T(8,128)(2,1)S(1)}, u32[]{:S(2)}, u32[]{:S(2)}) collective-permute-start(bf16[2,256,256]{2,1,0:T(8,128)(2,1)S(1)} %get-tuple-element.9.refs_3_), channel_id=1, source_target_pairs={{8,0},{12,4},{16,8},{20,12},{24,16},{28,20},{9,1},{13,5},{17,9},{2... | collective-permute-start | bytes 786440 | tf_op jit(solution)/shard_map/ppermute | solution.py:45
  89.0 31.7 %copy-start.4 = (bf16[2,256,256]{2,1,0:T(8,128)(2,1)}, bf16[2,256,256]{2,1,0:T(8,128)(2,1)S(1)}, u32[]{:S(2)}) copy-start(bf16[2,256,256]{2,1,0:T(8,128)(2,1)S(1)} %collective-permute-done.5.refs_2_) | copy-start | bytes 786436
  89.0 12.4 %collective-permute-start.6 = (bf16[2,256,256]{2,1,0:T(8,128)(2,1)S(1)}, bf16[2,256,256]{2,1,0:T(8,128)(2,1)S(1)}, u32[]{:S(2)}, u32[]{:S(2)}) collective-permute-start(bf16[2,256,256]{2,1,0:T(8,128)(2,1)S(1)} %collective-permute-done.5.refs_2_), channel_id=1, source_target_pairs={{0,8},{4,12},{8,16},{12,20},{16,24},{20,28},{1,9},{5,13},{9,17},{1... | collective-permute-start | bytes 786440 | tf_op jit(solution)/shard_map/ppermute | solution.py:44
  92.8 27.9 %copy-start.5 = (bf16[2,256,256]{2,1,0:T(8,128)(2,1)}, bf16[2,256,256]{2,1,0:T(8,128)(2,1)S(1)}, u32[]{:S(2)}) copy-start(bf16[2,256,256]{2,1,0:T(8,128)(2,1)S(1)} %collective-permute-done.8.refs_4_) | copy-start | bytes 786436
  92.8 13.5 %collective-permute-start.9 = (bf16[2,256,256]{2,1,0:T(8,128)(2,1)S(1)}, bf16[2,256,256]{2,1,0:T(8,128)(2,1)S(1)}, u32[]{:S(2)}, u32[]{:S(2)}) collective-permute-start(bf16[2,256,256]{2,1,0:T(8,128)(2,1)S(1)} %collective-permute-done.8.refs_4_), channel_id=1, source_target_pairs={{8,0},{12,4},{16,8},{20,12},{24,16},{28,20},{9,1},{13,5},{17,9},{2... | collective-permute-start | bytes 786440 | tf_op jit(solution)/shard_map/ppermute | solution.py:45
  94.2 19.3 %collective-permute-start.14 = (bf16[2,256,256]{2,1,0:T(8,128)(2,1)S(1)}, bf16[2,256,256]{2,1,0:T(8,128)(2,1)}, u32[]{:S(2)}, u32[]{:S(2)}) collective-permute-start(bf16[2,256,256]{2,1,0:T(8,128)(2,1)S(1)} %get-tuple-element.9.refs_3_), channel_id=1, source_target_pairs={{0,4},{4,0},{8,12},{12,8},{16,20},{20,16},{24,28},{28,24},{1,5},{5... | collective-permute-start | bytes 786440 | tf_op jit(solution)/shard_map/ppermute | solution.py:41
  101.3 12.2 %collective-permute-start.13 = (bf16[2,256,256]{2,1,0:T(8,128)(2,1)S(1)}, bf16[2,256,256]{2,1,0:T(8,128)(2,1)}, u32[]{:S(2)}, u32[]{:S(2)}) collective-permute-start(bf16[2,256,256]{2,1,0:T(8,128)(2,1)S(1)} %collective-permute-done.5.refs_2_), channel_id=1, source_target_pairs={{0,4},{4,0},{8,12},{12,8},{16,20},{20,16},{24,28},{28,24},{1,5},{5... | collective-permute-start | bytes 786440 | tf_op jit(solution)/shard_map/ppermute | solution.py:46
  101.4 12.6 %collective-permute-start.7 = (bf16[2,256,256]{2,1,0:T(8,128)(2,1)S(1)}, bf16[2,256,256]{2,1,0:T(8,128)(2,1)}, u32[]{:S(2)}, u32[]{:S(2)}) collective-permute-start(bf16[2,256,256]{2,1,0:T(8,128)(2,1)S(1)} %collective-permute-done.6.refs_1_), channel_id=1, source_target_pairs={{0,8},{4,12},{8,16},{12,20},{16,24},{20,28},{1,9},{5,13},{9,17},{1... | collective-permute-start | bytes 786440 | tf_op jit(solution)/shard_map/ppermute | solution.py:44
  106.4 7.8 %collective-permute-start.10 = (bf16[2,256,256]{2,1,0:T(8,128)(2,1)S(1)}, bf16[2,256,256]{2,1,0:T(8,128)(2,1)}, u32[]{:S(2)}, u32[]{:S(2)}) collective-permute-start(bf16[2,256,256]{2,1,0:T(8,128)(2,1)S(1)} %collective-permute-done.9.refs_5_), channel_id=1, source_target_pairs={{8,0},{12,4},{16,8},{20,12},{24,16},{28,20},{9,1},{13,5},{17,9},{2... | collective-permute-start | bytes 786440 | tf_op jit(solution)/shard_map/ppermute | solution.py:45
  111.3 9.4 %collective-permute-start.15 = (bf16[2,256,256]{2,1,0:T(8,128)(2,1)S(1)}, bf16[2,256,256]{2,1,0:T(8,128)(2,1)S(1)}, u32[]{:S(2)}, u32[]{:S(2)}) collective-permute-start(bf16[2,256,256]{2,1,0:T(8,128)(2,1)S(1)} %collective-permute-done.8.refs_4_), channel_id=1, source_target_pairs={{0,4},{4,0},{8,12},{12,8},{16,20},{20,16},{24,28},{28,24},{1,5},{5... | collective-permute-start | bytes 786440 | tf_op jit(solution)/shard_map/ppermute | solution.py:47
  113.5 7.2 %collective-permute-start.12 = (bf16[2,256,256]{2,1,0:T(8,128)(2,1)S(1)}, bf16[2,256,256]{2,1,0:T(8,128)(2,1)S(1)}, u32[]{:S(2)}, u32[]{:S(2)}) collective-permute-start(bf16[2,256,256]{2,1,0:T(8,128)(2,1)S(1)} %collective-permute-done.6.refs_1_), channel_id=1, source_target_pairs={{0,4},{4,0},{8,12},{12,8},{16,20},{20,16},{24,28},{28,24},{1,5},{5... | collective-permute-start | bytes 786440 | tf_op jit(solution)/shard_map/ppermute | solution.py:46
  113.5 7.2 %collective-permute-start.16 = (bf16[2,256,256]{2,1,0:T(8,128)(2,1)S(1)}, bf16[2,256,256]{2,1,0:T(8,128)(2,1)S(1)}, u32[]{:S(2)}, u32[]{:S(2)}) collective-permute-start(bf16[2,256,256]{2,1,0:T(8,128)(2,1)S(1)} %collective-permute-done.9.refs_5_), channel_id=1, source_target_pairs={{0,4},{4,0},{8,12},{12,8},{16,20},{20,16},{24,28},{28,24},{1,5},{5... | collective-permute-start | bytes 786440 | tf_op jit(solution)/shard_map/ppermute | solution.py:47
  114.1 7.4 %collective-permute-start.11 = (bf16[2,256,256]{2,1,0:T(8,128)(2,1)}, bf16[2,256,256]{2,1,0:T(8,128)(2,1)S(1)}, u32[]{:S(2)}, u32[]{:S(2)}) collective-permute-start(bf16[2,256,256]{2,1,0:T(8,128)(2,1)} %collective-permute-done.7.refs_0_), channel_id=1, source_target_pairs={{0,4},{4,0},{8,12},{12,8},{16,20},{20,16},{24,28},{28,24},{1,5},{5... | collective-permute-start | bytes 786440 | tf_op jit(solution)/shard_map/ppermute | solution.py:46
  114.1 8.8 %collective-permute-start.17 = (bf16[2,256,256]{2,1,0:T(8,128)(2,1)}, bf16[2,256,256]{2,1,0:T(8,128)(2,1)}, u32[]{:S(2)}, u32[]{:S(2)}) collective-permute-start(bf16[2,256,256]{2,1,0:T(8,128)(2,1)} %collective-permute-done.10.refs_6_), channel_id=1, source_target_pairs={{0,4},{4,0},{8,12},{12,8},{16,20},{20,16},{24,28},{28,24},{1,5},{5... | collective-permute-start | bytes 786440 | tf_op jit(solution)/shard_map/ppermute | solution.py:47
  (9 other events, 92.2 us)

commit v13 on v9

--- a/solution.py
+++ b/solution.py
@@ -29,14 +29,21 @@
         gathered = lax.all_gather(mine, "dp", axis=0, tiled=True)
         return jnp.take(gathered, owner_of * slot_count + slot_rank, axis=0)
     chips = size // 2
+    reach = chips // 2
+
+    def shifted(piece, offset):
+        pairs = [(i, i - 2 * offset) for i in range(size) if 0 <= i - 2 * offset < size]
+        return lax.ppermute(piece, "dp", pairs)
+
+    by_offset = {0: mine}
+    for distance in range(1, reach + 1):
+        for sign in (-1, 1):
+            by_offset[sign * distance] = shifted(mine, sign * distance)
+    for distance in range(reach + 1, chips):
+        for sign in (-1, 1):
+            by_offset[sign * distance] = shifted(by_offset[sign * (distance - reach)], sign * reach)
+    same_core = [by_offset[offset] for offset in range(1 - chips, chips)]
     partner = [(i, i ^ 1) for i in range(size)]
-    same_core = []
-    for offset in range(1 - chips, chips):
-        if offset == 0:
-            same_core.append(mine)
-            continue
-        pairs = [(i, i - 2 * offset) for i in range(size) if 0 <= i - 2 * offset < size]
-        same_core.append(lax.ppermute(mine, "dp", pairs))
     other_core = [lax.ppermute(piece, "dp", partner) for piece in same_core]
     pieces = same_core + other_core
     chip, core = replica // 2, replica % 2

time: 119 us -> 121 us (1.017)
  waiting for transfers between devices: 56.9 us -> 62.5 us
  starting transfers between devices: 38.5 us -> 35.1 us
    ppermute x7, starting transfers between devices: 18.2 us -> 10.1 us  [gather_blocks(): other_core = [lax.ppermute(piece, 'dp', partner) for piece in same_core]]
    ppermute x6, waiting for transfers between devices: 0.02 us -> 6.17 us  [shifted(): return lax.ppermute(piece, 'dp', pairs)]
    ppermute x6, starting transfers between devices: 10.3 us -> 14.9 us  [shifted(): return lax.ppermute(piece, 'dp', pairs)]
where the time goes in v13:
time: 121 us
  waiting for transfers between devices  62.5 us (52%)
  starting transfers between devices  35.1 us (29%)
  matrix products  7.28 us (6%)
  other arithmetic  7.11 us (6%)
  local copies, waits for them, and re-layouts  4.59 us (4%)
  Pallas kernels  3.13 us (3%)
    all_to_all x1, waiting for transfers between devices, local(): received = lax.all_to_all(by_owner, 'dp', 0, 0, tiled=True)  47.4 us
    ppermute x6, starting transfers between devices, shifted(): return lax.ppermute(piece, 'dp', pairs)  14.9 us
    ppermute x7, starting transfers between devices, gather_blocks(): other_core = [lax.ppermute(piece, 'dp', partner) for piece in same_core]  10.1 us
    ppermute x5, waiting for transfers between devices, butterfly_sum(): x = x + lax.ppermute(x, axis, [(i, i ^ step) for i in range(size)])  8.9 us
    all_to_all x1, starting transfers between devices, local(): received = lax.all_to_all(by_owner, 'dp', 0, 0, tiled=True)  6.51 us
    ppermute x6, waiting for transfers between devices, shifted(): return lax.ppermute(piece, 'dp', pairs)  6.17 us
    ppermute x5, starting transfers between devices, butterfly_sum(): x = x + lax.ppermute(x, axis, [(i, i ^ step) for i in range(size)])  3.53 us
    pallas_call x1, Pallas kernels, pick_blocks(): pl.pallas_call(pick_kernel, out_shape=jax.ShapeDtypeStruct((blocks,) + pi...  3.13 us
  transfers between devices with their start and end apart: 19, of which 7 were waited for; matrix products, arithmetic and copies ran while one was open for 7% of the time, Pallas kernels for 0%

profile of v13, /device:TPU:1, one launch (start us, length us, event | category | flops | bytes accessed | tf_op | source)
XLA Modules:
  0.0 120.6 jit_solution(2525006408782022606)
XLA Ops:
  2.6 2.0 %gather_fusion = bf16[16,256,256]{2,1,0:T(8,128)(2,1)} fusion(bf16[8,256,256]{2,1,0:T(8,128)(2,1)S(1)} %bitcast.52, s32[1024]{0:T(1024)S(1)} %pad_clamp_fusion), kind=kCustom, calls=%fused_computation | custom fusion | bytes 4194368 | tf_op jit(solution)/shard_map/jit(_take)/gather | solution.py:120
  4.6 6.5 %all-to-all-start = ((bf16[8,2,256,256]{3,2,1,0:T(8,128)(2,1)}), bf16[8,2,256,256]{3,2,1,0:T(8,128)(2,1)}, u32[]{:S(2)}, u32[]{:S(2)}) async-start(bf16[8,2,256,256]{3,2,1,0:T(8,128)(2,1)} %bitcast.3), calls=%async_computation | async-start | bytes 4194304 | tf_op jit(solution)/shard_map/all_to_all | solution.py:123
  12.0 47.4 %all-to-all-done = bf16[8,2,256,256]{3,2,1,0:T(8,128)(2,1)} async-done(((bf16[8,2,256,256]{3,2,1,0:T(8,128)(2,1)}), bf16[8,2,256,256]{3,2,1,0:T(8,128)(2,1)}, u32[]{:S(2)}, u32[]{:S(2)}) %all-to-all-start) | async-done | bytes 2097184 | tf_op jit(solution)/shard_map/all_to_all | solution.py:123
  59.4 1.9 %convert_reduce_fusion = f32[2,256,256]{2,1,0:T(8,128)S(1)} fusion(bf16[8,2,256,256]{3,2,1,0:T(8,128)(2,1)} %all-to-all-done), kind=kLoop, calls=%fused_computation.1 | loop fusion | flops 1966080 | bytes 2621440 | tf_op jit(solution)/shard_map/reduce_sum | solution.py:124
  61.8 1.6 %multiply_reduce_fusion = (f32[2]{0:T(128)S(1)}, f32[2,256,256]{2,1,0:T(8,128)S(1)}) fusion(bf16[1,1,2,256,256]{4,3,2,1,0:T(8,128)(2,1)S(1)} %copy-done.4, f32[2,256,256]{2,1,0:T(8,128)S(1)} %convert_reduce_fusion, bf16[1,1,2,256,256]{4,3,2,1,0:T(8,128)(2,1)} %param.14, f32[2]{0:T(128)S(1)} %convert_element_type.35), kind=kOutput, calls=%fused_computation.25 | convolution fusion | flops 134873088 | bytes 1572880 | tf_op jit(solution)/shard_map/sij,sjk->sik/dot_general | solution.py:149
  65.4 2.4 %collective-permute-done.1 = f32[2,9]{1,0:T(2,128)S(1)} collective-permute-done((f32[2,9]{1,0:T(2,128)S(1)}, f32[2,9]{1,0:T(2,128)S(1)}, u32[]{:S(2)}, u32[]{:S(2)}) %collective-permute-start.1) | collective-permute-done | bytes 104 | tf_op jit(solution)/shard_map/ppermute | solution.py:20
  67.9 3.3 %collective-permute-done.2 = f32[2,9]{1,0:T(2,128)S(1)} collective-permute-done((f32[2,9]{1,0:T(2,128)S(1)}, f32[2,9]{1,0:T(2,128)S(1)}, u32[]{:S(2)}, u32[]{:S(2)}) %collective-permute-start.2) | collective-permute-done | bytes 104 | tf_op jit(solution)/shard_map/ppermute | solution.py:20
  71.2 1.2 %collective-permute-start.3 = (f32[2,9]{1,0:T(2,128)S(1)}, f32[2,9]{1,0:T(2,128)S(1)}, u32[]{:S(2)}, u32[]{:S(2)}) collective-permute-start(f32[2,9]{1,0:T(2,128)S(1)} %add.92), channel_id=1, source_target_pairs={{0,1},{1,0},{2,3},{3,2},{4,5},{5,4},{6,7},{7,6},{8,9},{9,8},{10,11... | collective-permute-start | bytes 224 | tf_op jit(solution)/shard_map/ppermute | solution.py:20
  72.4 1.2 collective-permute-done.3
  73.6 1.2 %collective-permute-start.4 = (f32[2,9]{1,0:T(2,128)S(1)}, f32[2,9]{1,0:T(2,128)S(1)}, u32[]{:S(2)}, u32[]{:S(2)}) collective-permute-start(f32[2,9]{1,0:T(2,128)S(1)} %add.93), channel_id=1, source_target_pairs={{0,2},{1,3},{2,0},{3,1},{4,6},{5,7},{6,4},{7,5},{8,10},{9,11},{10,... | collective-permute-start | bytes 224 | tf_op jit(solution)/shard_map/ppermute | solution.py:20
  74.9 1.2 collective-permute-done.4
  77.2 1.9 %collective-permute-start.5 = (bf16[2,256,256]{2,1,0:T(8,128)(2,1)S(1)}, bf16[2,256,256]{2,1,0:T(8,128)(2,1)S(1)}, u32[]{:S(2)}, u32[]{:S(2)}) collective-permute-start(bf16[2,256,256]{2,1,0:T(8,128)(2,1)S(1)} %get-tuple-element.7.refs_3_), channel_id=1, source_target_pairs={{0,8},{4,12},{8,16},{12,20},{16,24},{20,28},{1,9},{5,13},{9,17},{1... | collective-permute-start | bytes 786440 | tf_op jit(solution)/shard_map/ppermute | solution.py:36
  79.1 1.3 %collective-permute-start.8 = (bf16[2,256,256]{2,1,0:T(8,128)(2,1)S(1)}, bf16[2,256,256]{2,1,0:T(8,128)(2,1)S(1)}, u32[]{:S(2)}, u32[]{:S(2)}) collective-permute-start(bf16[2,256,256]{2,1,0:T(8,128)(2,1)S(1)} %get-tuple-element.7.refs_3_), channel_id=1, source_target_pairs={{8,0},{12,4},{16,8},{20,12},{24,16},{28,20},{9,1},{13,5},{17,9},{2... | collective-permute-start | bytes 786440 | tf_op jit(solution)/shard_map/ppermute | solution.py:36
  80.4 4.0 %collective-permute-start.7 = (bf16[2,256,256]{2,1,0:T(8,128)(2,1)S(1)}, bf16[2,256,256]{2,1,0:T(8,128)(2,1)S(1)}, u32[]{:S(2)}, u32[]{:S(2)}) collective-permute-start(bf16[2,256,256]{2,1,0:T(8,128)(2,1)S(1)} %get-tuple-element.7.refs_3_), channel_id=1, source_target_pairs={{0,16},{4,20},{8,24},{12,28},{1,17},{5,21},{9,25},{13,29},{2,18},{... | collective-permute-start | bytes 786440 | tf_op jit(solution)/shard_map/ppermute | solution.py:36
  85.1 1.3 %collective-permute-start.9 = (bf16[2,256,256]{2,1,0:T(8,128)(2,1)S(1)}, bf16[2,256,256]{2,1,0:T(8,128)(2,1)S(1)}, u32[]{:S(2)}, u32[]{:S(2)}) collective-permute-start(bf16[2,256,256]{2,1,0:T(8,128)(2,1)S(1)} %get-tuple-element.7.refs_3_), channel_id=1, source_target_pairs={{16,0},{20,4},{24,8},{28,12},{17,1},{21,5},{25,9},{29,13},{18,2},{... | collective-permute-start | bytes 786440 | tf_op jit(solution)/shard_map/ppermute | solution.py:36
  86.4 5.5 %collective-permute-start.14 = (bf16[2,256,256]{2,1,0:T(8,128)(2,1)S(1)}, bf16[2,256,256]{2,1,0:T(8,128)(2,1)S(1)}, u32[]{:S(2)}, u32[]{:S(2)}) collective-permute-start(bf16[2,256,256]{2,1,0:T(8,128)(2,1)S(1)} %get-tuple-element.7.refs_3_), channel_id=1, source_target_pairs={{0,4},{4,0},{8,12},{12,8},{16,20},{20,16},{24,28},{28,24},{1,5},{5... | collective-permute-start | bytes 786440 | tf_op jit(solution)/shard_map/ppermute | solution.py:47
  92.0 5.2 %collective-permute-start.6 = (bf16[2,256,256]{2,1,0:T(8,128)(2,1)S(1)}, bf16[2,256,256]{2,1,0:T(8,128)(2,1)S(1)}, u32[]{:S(2)}, u32[]{:S(2)}) collective-permute-start(bf16[2,256,256]{2,1,0:T(8,128)(2,1)S(1)} %collective-permute-done.5.refs_2_), channel_id=1, source_target_pairs={{0,16},{4,20},{8,24},{12,28},{1,17},{5,21},{9,25},{13,29},{2,18},{... | collective-permute-start | bytes 786440 | tf_op jit(solution)/shard_map/ppermute | solution.py:36
  97.2 1.3 %collective-permute-start.10 = (bf16[2,256,256]{2,1,0:T(8,128)(2,1)S(1)}, bf16[2,256,256]{2,1,0:T(8,128)(2,1)S(1)}, u32[]{:S(2)}, u32[]{:S(2)}) collective-permute-start(bf16[2,256,256]{2,1,0:T(8,128)(2,1)S(1)} %collective-permute-done.8.refs_4_), channel_id=1, source_target_pairs={{16,0},{20,4},{24,8},{28,12},{17,1},{21,5},{25,9},{29,13},{18,2},{... | collective-permute-start | bytes 786440 | tf_op jit(solution)/shard_map/ppermute | solution.py:36
  98.5 2.5 %collective-permute-start.12 = (bf16[2,256,256]{2,1,0:T(8,128)(2,1)S(1)}, bf16[2,256,256]{2,1,0:T(8,128)(2,1)S(1)}, u32[]{:S(2)}, u32[]{:S(2)}) collective-permute-start(bf16[2,256,256]{2,1,0:T(8,128)(2,1)S(1)} %collective-permute-done.7.refs_1_), channel_id=1, source_target_pairs={{0,4},{4,0},{8,12},{12,8},{16,20},{20,16},{24,28},{28,24},{1,5},{5... | collective-permute-start | bytes 786440 | tf_op jit(solution)/shard_map/ppermute | solution.py:47
  101.0 3.0 %fusion.2 = f32[1,1,2,256,256]{4,3,2,1,0:T(8,128)} fusion(f32[1,1,2,256,256]{4,3,2,1,0:T(8,128)} %param.13, f32[2,256,256]{2,1,0:T(8,128)S(1)} %convert_reduce_fusion, f32[2]{0:T(128)S(1)} %convert_element_type.35, pred[2]{0:T(512)(128)(4,1)S(1)} %dynamic-slice_reduce_fusion), kind=kOutput, calls=%fused_computation.5 | convolution fusion | flops 403308544 | bytes 1572874 | tf_op jit(solution)/shard_map/sji,sjk->sik/dot_general | solution.py:142
  104.0 2.7 %fusion.5 = f32[1,1,2,256,256]{4,3,2,1,0:T(8,128)} fusion(f32[1,1,2,256,256]{4,3,2,1,0:T(8,128)} %param.12, f32[2,256,256]{2,1,0:T(8,128)S(1)} %convert_reduce_fusion, f32[2]{0:T(128)S(1)} %convert_element_type.35, pred[2]{0:T(512)(128)(4,1)S(1)} %dynamic-slice_reduce_fusion), kind=kOutput, calls=%fused_computation.9 | convolution fusion | flops 403308544 | bytes 1572874 | tf_op jit(solution)/shard_map/sij,skj->sik/dot_general | solution.py:139
  107.2 6.2 %collective-permute-done.10.refs_6_ = bf16[2,256,256]{2,1,0:T(8,128)(2,1)S(1)} collective-permute-done((bf16[2,256,256]{2,1,0:T(8,128)(2,1)S(1)}, bf16[2,256,256]{2,1,0:T(8,128)(2,1)S(1)}, u32[]{:S(2)}, u32[]{:S(2)}) %collective-permute-start.10) | collective-permute-done | bytes 262176 | tf_op jit(solution)/shard_map/ppermute | solution.py:36
  113.4 1.4 %collective-permute-start.11 = (bf16[2,256,256]{2,1,0:T(8,128)(2,1)S(1)}, bf16[2,256,256]{2,1,0:T(8,128)(2,1)S(1)}, u32[]{:S(2)}, u32[]{:S(2)}) collective-permute-start(bf16[2,256,256]{2,1,0:T(8,128)(2,1)S(1)} %collective-permute-done.6.refs_0_), channel_id=1, source_target_pairs={{0,4},{4,0},{8,12},{12,8},{16,20},{20,16},{24,28},{28,24},{1,5},{5... | collective-permute-start | bytes 786440 | tf_op jit(solution)/shard_map/ppermute | solution.py:47
  117.5 3.1 %shard_map.128 = bf16[8,256,256]{2,1,0:T(8,128)(2,1)} custom-call(s32[8,2]{1,0:T(8,128)} %copy.39.table_ref, bf16[2,256,256]{2,1,0:T(8,128)(2,1)} %copy-done.10, bf16[2,256,256]{2,1,0:T(8,128)(2,1)} %copy-done.7, bf16[2,256,256]{2,1,0:T(8,128)(2,1)} %copy-done.5, bf16[2,256,256]{2,1,0:T(8,128)(2,1)} %copy-done.2, bf16[2,256,256]{2,1,0:T(8,128)(2,1)} %copy-done.6, ...), custom_call_target="tpu_custom_call" | custom-call | tf_op jit(solution)/shard_map/pallas_call | solution.py:79
  (88 shorter events, 10.4 us)
Async XLA Ops:
  4.6 54.8 %all-to-all-start = ((bf16[8,2,256,256]{3,2,1,0:T(8,128)(2,1)}), bf16[8,2,256,256]{3,2,1,0:T(8,128)(2,1)}, u32[]{:S(2)}, u32[]{:S(2)}) async-start(bf16[8,2,256,256]{3,2,1,0:T(8,128)(2,1)} %bitcast.3), calls=%async_computation | async-start | bytes 4194304 | tf_op jit(solution)/shard_map/all_to_all | solution.py:123
  11.1 50.2 %copy-start.1 = (f32[1,1,2,256,256]{4,3,2,1,0:T(8,128)S(1)}, f32[1,1,2,256,256]{4,3,2,1,0:T(8,128)}, u32[]{:S(2)}) copy-start(f32[1,1,2,256,256]{4,3,2,1,0:T(8,128)} %param.16) | copy-start | bytes 1572868
  11.1 50.7 %copy-start.4 = (bf16[1,1,2,256,256]{4,3,2,1,0:T(8,128)(2,1)S(1)}, bf16[1,1,2,256,256]{4,3,2,1,0:T(8,128)(2,1)}, u32[]{:S(2)}) copy-start(bf16[1,1,2,256,256]{4,3,2,1,0:T(8,128)(2,1)} %param.15) | copy-start | bytes 786436
  12.0 64.2 %copy-start.3 = (f32[1,1,2,256,256]{4,3,2,1,0:T(8,128)S(1)}, f32[1,1,2,256,256]{4,3,2,1,0:T(8,128)}, u32[]{:S(2)}) copy-start(f32[1,1,2,256,256]{4,3,2,1,0:T(8,128)} %param.17) | copy-start | bytes 1572868
  63.5 1.8 %collective-permute-start = (f32[2,9]{1,0:T(2,128)S(1)}, f32[2,9]{1,0:T(2,128)S(1)}, u32[]{:S(2)}, u32[]{:S(2)}) collective-permute-start(f32[2,9]{1,0:T(2,128)S(1)} %pad_maximum_fusion), channel_id=1, source_target_pairs={{0,4},{4,0},{8,12},{12,8},{16,20},{20,16},{24,28},{28,24},{1,5},{5... | collective-permute-start | bytes 224 | tf_op jit(solution)/shard_map/ppermute | solution.py:20
  65.3 2.5 %collective-permute-start.1 = (f32[2,9]{1,0:T(2,128)S(1)}, f32[2,9]{1,0:T(2,128)S(1)}, u32[]{:S(2)}, u32[]{:S(2)}) collective-permute-start(f32[2,9]{1,0:T(2,128)S(1)} %fusion.30), channel_id=1, source_target_pairs={{0,8},{4,12},{8,0},{12,4},{16,24},{20,28},{24,16},{28,20},{1,9},{5... | collective-permute-start | bytes 224 | tf_op jit(solution)/shard_map/ppermute | solution.py:20
  67.8 3.4 %collective-permute-start.2 = (f32[2,9]{1,0:T(2,128)S(1)}, f32[2,9]{1,0:T(2,128)S(1)}, u32[]{:S(2)}, u32[]{:S(2)}) collective-permute-start(f32[2,9]{1,0:T(2,128)S(1)} %fusion.35), channel_id=1, source_target_pairs={{0,16},{4,20},{8,24},{12,28},{16,0},{20,4},{24,8},{28,12},{1,17},{... | collective-permute-start | bytes 224 | tf_op jit(solution)/shard_map/ppermute | solution.py:20
  71.2 2.4 %collective-permute-start.3 = (f32[2,9]{1,0:T(2,128)S(1)}, f32[2,9]{1,0:T(2,128)S(1)}, u32[]{:S(2)}, u32[]{:S(2)}) collective-permute-start(f32[2,9]{1,0:T(2,128)S(1)} %add.92), channel_id=1, source_target_pairs={{0,1},{1,0},{2,3},{3,2},{4,5},{5,4},{6,7},{7,6},{8,9},{9,8},{10,11... | collective-permute-start | bytes 224 | tf_op jit(solution)/shard_map/ppermute | solution.py:20
  73.6 2.4 %collective-permute-start.4 = (f32[2,9]{1,0:T(2,128)S(1)}, f32[2,9]{1,0:T(2,128)S(1)}, u32[]{:S(2)}, u32[]{:S(2)}) collective-permute-start(f32[2,9]{1,0:T(2,128)S(1)} %add.93), channel_id=1, source_target_pairs={{0,2},{1,3},{2,0},{3,1},{4,6},{5,7},{6,4},{7,5},{8,10},{9,11},{10,... | collective-permute-start | bytes 224 | tf_op jit(solution)/shard_map/ppermute | solution.py:20
  77.2 38.6 %copy-start.2 = (bf16[2,256,256]{2,1,0:T(8,128)(2,1)}, bf16[2,256,256]{2,1,0:T(8,128)(2,1)S(1)}, u32[]{:S(2)}) copy-start(bf16[2,256,256]{2,1,0:T(8,128)(2,1)S(1)} %get-tuple-element.7.refs_3_) | copy-start | bytes 786436
  77.2 14.8 %collective-permute-start.5 = (bf16[2,256,256]{2,1,0:T(8,128)(2,1)S(1)}, bf16[2,256,256]{2,1,0:T(8,128)(2,1)S(1)}, u32[]{:S(2)}, u32[]{:S(2)}) collective-permute-start(bf16[2,256,256]{2,1,0:T(8,128)(2,1)S(1)} %get-tuple-element.7.refs_3_), channel_id=1, source_target_pairs={{0,8},{4,12},{8,16},{12,20},{16,24},{20,28},{1,9},{5,13},{9,17},{1... | collective-permute-start | bytes 786440 | tf_op jit(solution)/shard_map/ppermute | solution.py:36
  79.1 18.1 %collective-permute-start.8 = (bf16[2,256,256]{2,1,0:T(8,128)(2,1)S(1)}, bf16[2,256,256]{2,1,0:T(8,128)(2,1)S(1)}, u32[]{:S(2)}, u32[]{:S(2)}) collective-permute-start(bf16[2,256,256]{2,1,0:T(8,128)(2,1)S(1)} %get-tuple-element.7.refs_3_), channel_id=1, source_target_pairs={{8,0},{12,4},{16,8},{20,12},{24,16},{28,20},{9,1},{13,5},{17,9},{2... | collective-permute-start | bytes 786440 | tf_op jit(solution)/shard_map/ppermute | solution.py:36
  80.4 18.1 %collective-permute-start.7 = (bf16[2,256,256]{2,1,0:T(8,128)(2,1)S(1)}, bf16[2,256,256]{2,1,0:T(8,128)(2,1)S(1)}, u32[]{:S(2)}, u32[]{:S(2)}) collective-permute-start(bf16[2,256,256]{2,1,0:T(8,128)(2,1)S(1)} %get-tuple-element.7.refs_3_), channel_id=1, source_target_pairs={{0,16},{4,20},{8,24},{12,28},{1,17},{5,21},{9,25},{13,29},{2,18},{... | collective-permute-start | bytes 786440 | tf_op jit(solution)/shard_map/ppermute | solution.py:36
  85.1 21.5 %collective-permute-start.9 = (bf16[2,256,256]{2,1,0:T(8,128)(2,1)S(1)}, bf16[2,256,256]{2,1,0:T(8,128)(2,1)S(1)}, u32[]{:S(2)}, u32[]{:S(2)}) collective-permute-start(bf16[2,256,256]{2,1,0:T(8,128)(2,1)S(1)} %get-tuple-element.7.refs_3_), channel_id=1, source_target_pairs={{16,0},{20,4},{24,8},{28,12},{17,1},{21,5},{25,9},{29,13},{18,2},{... | collective-permute-start | bytes 786440 | tf_op jit(solution)/shard_map/ppermute | solution.py:36
  86.4 20.2 %collective-permute-start.14 = (bf16[2,256,256]{2,1,0:T(8,128)(2,1)S(1)}, bf16[2,256,256]{2,1,0:T(8,128)(2,1)S(1)}, u32[]{:S(2)}, u32[]{:S(2)}) collective-permute-start(bf16[2,256,256]{2,1,0:T(8,128)(2,1)S(1)} %get-tuple-element.7.refs_3_), channel_id=1, source_target_pairs={{0,4},{4,0},{8,12},{12,8},{16,20},{20,16},{24,28},{28,24},{1,5},{5... | collective-permute-start | bytes 786440 | tf_op jit(solution)/shard_map/ppermute | solution.py:47
  92.0 23.9 %copy-start.5 = (bf16[2,256,256]{2,1,0:T(8,128)(2,1)}, bf16[2,256,256]{2,1,0:T(8,128)(2,1)S(1)}, u32[]{:S(2)}) copy-start(bf16[2,256,256]{2,1,0:T(8,128)(2,1)S(1)} %collective-permute-done.5.refs_2_) | copy-start | bytes 786436
  92.0 15.2 %collective-permute-start.6 = (bf16[2,256,256]{2,1,0:T(8,128)(2,1)S(1)}, bf16[2,256,256]{2,1,0:T(8,128)(2,1)S(1)}, u32[]{:S(2)}, u32[]{:S(2)}) collective-permute-start(bf16[2,256,256]{2,1,0:T(8,128)(2,1)S(1)} %collective-permute-done.5.refs_2_), channel_id=1, source_target_pairs={{0,16},{4,20},{8,24},{12,28},{1,17},{5,21},{9,25},{13,29},{2,18},{... | collective-permute-start | bytes 786440 | tf_op jit(solution)/shard_map/ppermute | solution.py:36
  97.2 16.2 %collective-permute-start.10 = (bf16[2,256,256]{2,1,0:T(8,128)(2,1)S(1)}, bf16[2,256,256]{2,1,0:T(8,128)(2,1)S(1)}, u32[]{:S(2)}, u32[]{:S(2)}) collective-permute-start(bf16[2,256,256]{2,1,0:T(8,128)(2,1)S(1)} %collective-permute-done.8.refs_4_), channel_id=1, source_target_pairs={{16,0},{20,4},{24,8},{28,12},{17,1},{21,5},{25,9},{29,13},{18,2},{... | collective-permute-start | bytes 786440 | tf_op jit(solution)/shard_map/ppermute | solution.py:36
  98.5 16.3 %collective-permute-start.12 = (bf16[2,256,256]{2,1,0:T(8,128)(2,1)S(1)}, bf16[2,256,256]{2,1,0:T(8,128)(2,1)S(1)}, u32[]{:S(2)}, u32[]{:S(2)}) collective-permute-start(bf16[2,256,256]{2,1,0:T(8,128)(2,1)S(1)} %collective-permute-done.7.refs_1_), channel_id=1, source_target_pairs={{0,4},{4,0},{8,12},{12,8},{16,20},{20,16},{24,28},{28,24},{1,5},{5... | collective-permute-start | bytes 786440 | tf_op jit(solution)/shard_map/ppermute | solution.py:47
  106.6 9.2 %collective-permute-start.13 = (bf16[2,256,256]{2,1,0:T(8,128)(2,1)S(1)}, bf16[2,256,256]{2,1,0:T(8,128)(2,1)S(1)}, u32[]{:S(2)}, u32[]{:S(2)}) collective-permute-start(bf16[2,256,256]{2,1,0:T(8,128)(2,1)S(1)} %collective-permute-done.5.refs_2_), channel_id=1, source_target_pairs={{0,4},{4,0},{8,12},{12,8},{16,20},{20,16},{24,28},{28,24},{1,5},{5... | collective-permute-start | bytes 786440 | tf_op jit(solution)/shard_map/ppermute | solution.py:47
  106.7 9.2 %collective-permute-start.15 = (bf16[2,256,256]{2,1,0:T(8,128)(2,1)S(1)}, bf16[2,256,256]{2,1,0:T(8,128)(2,1)S(1)}, u32[]{:S(2)}, u32[]{:S(2)}) collective-permute-start(bf16[2,256,256]{2,1,0:T(8,128)(2,1)S(1)} %collective-permute-done.8.refs_4_), channel_id=1, source_target_pairs={{0,4},{4,0},{8,12},{12,8},{16,20},{20,16},{24,28},{28,24},{1,5},{5... | collective-permute-start | bytes 786440 | tf_op jit(solution)/shard_map/ppermute | solution.py:47
  107.2 8.7 %collective-permute-start.16 = (bf16[2,256,256]{2,1,0:T(8,128)(2,1)S(1)}, bf16[2,256,256]{2,1,0:T(8,128)(2,1)S(1)}, u32[]{:S(2)}, u32[]{:S(2)}) collective-permute-start(bf16[2,256,256]{2,1,0:T(8,128)(2,1)S(1)} %collective-permute-done.9.refs_5_), channel_id=1, source_target_pairs={{0,4},{4,0},{8,12},{12,8},{16,20},{20,16},{24,28},{28,24},{1,5},{5... | collective-permute-start | bytes 786440 | tf_op jit(solution)/shard_map/ppermute | solution.py:47
  113.4 2.5 %collective-permute-start.11 = (bf16[2,256,256]{2,1,0:T(8,128)(2,1)S(1)}, bf16[2,256,256]{2,1,0:T(8,128)(2,1)S(1)}, u32[]{:S(2)}, u32[]{:S(2)}) collective-permute-start(bf16[2,256,256]{2,1,0:T(8,128)(2,1)S(1)} %collective-permute-done.6.refs_0_), channel_id=1, source_target_pairs={{0,4},{4,0},{8,12},{12,8},{16,20},{20,16},{24,28},{28,24},{1,5},{5... | collective-permute-start | bytes 786440 | tf_op jit(solution)/shard_map/ppermute | solution.py:47
  114.8 2.7 %collective-permute-start.17 = (bf16[2,256,256]{2,1,0:T(8,128)(2,1)S(1)}, bf16[2,256,256]{2,1,0:T(8,128)(2,1)}, u32[]{:S(2)}, u32[]{:S(2)}) collective-permute-start(bf16[2,256,256]{2,1,0:T(8,128)(2,1)S(1)} %collective-permute-done.10.refs_6_), channel_id=1, source_target_pairs={{0,4},{4,0},{8,12},{12,8},{16,20},{20,16},{24,28},{28,24},{1,5},{5... | collective-permute-start | bytes 786440 | tf_op jit(solution)/shard_map/ppermute | solution.py:47
  (14 other events, 103.5 us)

commit v14 on v8

--- a/solution.py
+++ b/solution.py
@@ -19,6 +19,24 @@
     while step < size:
         x = x + lax.ppermute(x, axis, [(i, i ^ step) for i in range(size)])
         step *= 2
+    return x
+
+
+def mesh_sum(x):
+    rows, cols = lax.axis_size("dp"), lax.axis_size("shard")
+    if rows & (rows - 1) or cols & (cols - 1):
+        return butterfly_sum(butterfly_sum(x, "dp"), "shard")
+    row_masks = [cols * (1 << k) for k in range(rows.bit_length() - 1)][::-1]
+    col_masks = [1 << k for k in range(cols.bit_length() - 1)]
+    size = rows * cols
+    for k in range(max(len(row_masks), len(col_masks))):
+        masks = row_masks[k:k + 1] + col_masks[k:k + 1]
+        if len(masks) == 2:
+            masks.append(masks[0] ^ masks[1])
+        total = x
+        for mask in masks:
+            total = total + lax.ppermute(x, ("dp", "shard"), [(i, i ^ mask) for i in range(size)])
+        x = total
     return x
 
 
@@ -150,7 +168,7 @@
         "sij,sjk->sik", inner, root_right[0, 0], preferred_element_type=jnp.float32
     )
     prec_terms = jnp.sum(member * jnp.sum(precond * precond, axis=(1, 2))[:, None], axis=0)
-    norms = butterfly_sum(butterfly_sum(jnp.stack([adam_terms, prec_terms]), "dp"), "shard")
+    norms = mesh_sum(jnp.stack([adam_terms, prec_terms]))
     norm_adam = norms[0]
     norm_prec = norms[1]
     scales = jnp.sqrt(norm_adam / (norm_prec + NORM_EPS))

time: 117 us -> 118 us (level)
  starting transfers between devices: 34.6 us -> 36 us
    ppermute x5 -> x7, starting transfers between devices: 3.53 us -> 10.4 us  [mesh_sum(): lax.ppermute(x, ('dp', 'shard'), [(i, i ^ mask) for i in range(size)])]
    ppermute x1, starting transfers between devices: 7.05 us -> 1.43 us  [gather_blocks(): near_left[0] = lax.ppermute(mine, 'dp', partner)]
    ppermute x3, waiting for transfers between devices: 1.96 us -> 4.97 us  [gather_blocks(): from_left[step] = lax.ppermute(from_left[step - 1], 'dp', rightward)]
    ppermute x5 -> x7, waiting for transfers between devices: 8.91 us -> 6.07 us  [mesh_sum(): lax.ppermute(x, ('dp', 'shard'), [(i, i ^ mask) for i in range(size)])]
  transfers between devices with their start and end apart: 19 -> 21, of which waited for: 7 -> 7; matrix products, arithmetic and copies ran while one was open for 7% -> 7% of each run, Pallas kernels for 0% -> 0%
where the time goes in v14:
time: 118 us
  waiting for transfers between devices  58.4 us (49%)
  starting transfers between devices  36 us (31%)
  matrix products  7.28 us (6%)
  other arithmetic  7.1 us (6%)
  local copies, waits for them, and re-layouts  4.56 us (4%)
  Pallas kernels  3.14 us (3%)
    all_to_all x1, waiting for transfers between devices, local(): received = lax.all_to_all(by_owner, 'dp', 0, 0, tiled=True)  47.4 us
    ppermute x7, starting transfers between devices, mesh_sum(): lax.ppermute(x, ('dp', 'shard'), [(i, i ^ mask) for i in range(size)])  10.4 us
    ppermute x3, starting transfers between devices, gather_blocks(): from_left[step] = lax.ppermute(from_left[step - 1], 'dp', rightward)  10.1 us
    all_to_all x1, starting transfers between devices, local(): received = lax.all_to_all(by_owner, 'dp', 0, 0, tiled=True)  6.51 us
    ppermute x7, waiting for transfers between devices, mesh_sum(): lax.ppermute(x, ('dp', 'shard'), [(i, i ^ mask) for i in range(size)])  6.07 us
    ppermute x3, waiting for transfers between devices, gather_blocks(): from_left[step] = lax.ppermute(from_left[step - 1], 'dp', rightward)  4.97 us
    ppermute x3, starting transfers between devices, gather_blocks(): from_right[step] = lax.ppermute(from_right[step - 1], 'dp', leftward)  3.88 us
    ppermute x3, starting transfers between devices, gather_blocks(): near_right[step] = lax.ppermute(from_right[step], 'dp', partner)  3.49 us
  transfers between devices with their start and end apart: 21, of which 7 were waited for; matrix products, arithmetic and copies ran while one was open for 7% of the time, Pallas kernels for 0%

profile of v14, /device:TPU:1, one launch (start us, length us, event | category | flops | bytes accessed | tf_op | source)
XLA Modules:
  0.0 117.5 jit_solution(12456263433868252686)
XLA Ops:
  2.6 2.0 %gather_fusion = bf16[16,256,256]{2,1,0:T(8,128)(2,1)} fusion(bf16[8,256,256]{2,1,0:T(8,128)(2,1)S(1)} %bitcast.52, s32[1024]{0:T(1024)S(1)} %pad_clamp_fusion), kind=kCustom, calls=%fused_computation | custom fusion | bytes 4194368 | tf_op jit(solution)/shard_map/jit(_take)/gather | solution.py:138
  4.6 6.5 %all-to-all-start = ((bf16[8,2,256,256]{3,2,1,0:T(8,128)(2,1)}), bf16[8,2,256,256]{3,2,1,0:T(8,128)(2,1)}, u32[]{:S(2)}, u32[]{:S(2)}) async-start(bf16[8,2,256,256]{3,2,1,0:T(8,128)(2,1)} %bitcast.3), calls=%async_computation | async-start | bytes 4194304 | tf_op jit(solution)/shard_map/all_to_all | solution.py:141
  12.0 47.4 %all-to-all-done = bf16[8,2,256,256]{3,2,1,0:T(8,128)(2,1)} async-done(((bf16[8,2,256,256]{3,2,1,0:T(8,128)(2,1)}), bf16[8,2,256,256]{3,2,1,0:T(8,128)(2,1)}, u32[]{:S(2)}, u32[]{:S(2)}) %all-to-all-start) | async-done | bytes 2097184 | tf_op jit(solution)/shard_map/all_to_all | solution.py:141
  59.4 1.9 %convert_reduce_fusion = f32[2,256,256]{2,1,0:T(8,128)S(1)} fusion(bf16[8,2,256,256]{3,2,1,0:T(8,128)(2,1)} %all-to-all-done), kind=kLoop, calls=%fused_computation.1 | loop fusion | flops 1966080 | bytes 2621440 | tf_op jit(solution)/shard_map/reduce_sum | solution.py:142
  61.8 1.6 %multiply_reduce_fusion = (f32[2]{0:T(128)S(1)}, f32[2,256,256]{2,1,0:T(8,128)S(1)}) fusion(bf16[1,1,2,256,256]{4,3,2,1,0:T(8,128)(2,1)S(1)} %copy-done.4, f32[2,256,256]{2,1,0:T(8,128)S(1)} %convert_reduce_fusion, bf16[1,1,2,256,256]{4,3,2,1,0:T(8,128)(2,1)} %param.14, f32[2]{0:T(128)S(1)} %convert_element_type.35), kind=kOutput, calls=%fused_computation.25 | convolution fusion | flops 134873088 | bytes 1572880 | tf_op jit(solution)/shard_map/sij,sjk->sik/dot_general | solution.py:167
  63.6 1.3 %collective-permute-start.1 = (f32[2,9]{1,0:T(2,128)S(1)}, f32[2,9]{1,0:T(2,128)S(1)}, u32[]{:S(2)}, u32[]{:S(2)}) collective-permute-start(f32[2,9]{1,0:T(2,128)S(1)} %pad_maximum_fusion), channel_id=1, source_target_pairs={{0,1},{1,0},{2,3},{3,2},{4,5},{5,4},{6,7},{7,6},{8,9},{9,8},{10,11... | collective-permute-start | bytes 224 | tf_op jit(solution)/shard_map/ppermute | solution.py:38
  64.9 2.3 %collective-permute-start.2 = (f32[2,9]{1,0:T(2,128)S(1)}, f32[2,9]{1,0:T(2,128)S(1)}, u32[]{:S(2)}, u32[]{:S(2)}) collective-permute-start(f32[2,9]{1,0:T(2,128)S(1)} %pad_maximum_fusion), channel_id=1, source_target_pairs={{0,17},{1,16},{2,19},{3,18},{4,21},{5,20},{6,23},{7,22},{8,25},{9,... | collective-permute-start | bytes 224 | tf_op jit(solution)/shard_map/ppermute | solution.py:38
  67.2 2.0 %collective-permute-done.2 = f32[2,9]{1,0:T(2,128)S(1)} collective-permute-done((f32[2,9]{1,0:T(2,128)S(1)}, f32[2,9]{1,0:T(2,128)S(1)}, u32[]{:S(2)}, u32[]{:S(2)}) %collective-permute-start.2) | collective-permute-done | bytes 104 | tf_op jit(solution)/shard_map/ppermute | solution.py:38
  69.1 1.7 %collective-permute-start.3 = (f32[2,9]{1,0:T(2,128)S(1)}, f32[2,9]{1,0:T(2,128)S(1)}, u32[]{:S(2)}, u32[]{:S(2)}) collective-permute-start(f32[2,9]{1,0:T(2,128)S(1)} %add_add_fusion.1), channel_id=1, source_target_pairs={{0,8},{1,9},{2,10},{3,11},{4,12},{5,13},{6,14},{7,15},{8,0},{9,1},... | collective-permute-start | bytes 224 | tf_op jit(solution)/shard_map/ppermute | solution.py:38
  70.8 1.2 %collective-permute-start.4 = (f32[2,9]{1,0:T(2,128)S(1)}, f32[2,9]{1,0:T(2,128)S(1)}, u32[]{:S(2)}, u32[]{:S(2)}) collective-permute-start(f32[2,9]{1,0:T(2,128)S(1)} %add_add_fusion.1), channel_id=1, source_target_pairs={{0,2},{1,3},{2,0},{3,1},{4,6},{5,7},{6,4},{7,5},{8,10},{9,11},{10,... | collective-permute-start | bytes 224 | tf_op jit(solution)/shard_map/ppermute | solution.py:38
  73.2 2.1 %collective-permute-done.5 = f32[2,9]{1,0:T(2,128)S(1)} collective-permute-done((f32[2,9]{1,0:T(2,128)S(1)}, f32[2,9]{1,0:T(2,128)S(1)}, u32[]{:S(2)}, u32[]{:S(2)}) %collective-permute-start.5) | collective-permute-done | bytes 104 | tf_op jit(solution)/shard_map/ppermute | solution.py:38
  75.4 3.9 %collective-permute-start.6 = (f32[2,9]{1,0:T(2,128)S(1)}, f32[2,9]{1,0:T(2,128)S(1)}, u32[]{:S(2)}, u32[]{:S(2)}) collective-permute-start(f32[2,9]{1,0:T(2,128)S(1)} %add_add_fusion), channel_id=1, source_target_pairs={{0,4},{1,5},{2,6},{3,7},{4,0},{5,1},{6,2},{7,3},{8,12},{9,13},{10,... | collective-permute-start | bytes 224 | tf_op jit(solution)/shard_map/ppermute | solution.py:38
  81.2 1.9 %collective-permute-start.7 = (bf16[2,256,256]{2,1,0:T(8,128)(2,1)S(1)}, bf16[2,256,256]{2,1,0:T(8,128)(2,1)S(1)}, u32[]{:S(2)}, u32[]{:S(2)}) collective-permute-start(bf16[2,256,256]{2,1,0:T(8,128)(2,1)S(1)} %get-tuple-element.7.refs_3_), channel_id=1, source_target_pairs={{0,8},{4,12},{8,16},{12,20},{16,24},{20,28},{1,9},{5,13},{9,17},{1... | collective-permute-start | bytes 786440 | tf_op jit(solution)/shard_map/ppermute | solution.py:62
  83.1 1.3 %collective-permute-start.10 = (bf16[2,256,256]{2,1,0:T(8,128)(2,1)S(1)}, bf16[2,256,256]{2,1,0:T(8,128)(2,1)S(1)}, u32[]{:S(2)}, u32[]{:S(2)}) collective-permute-start(bf16[2,256,256]{2,1,0:T(8,128)(2,1)S(1)} %get-tuple-element.7.refs_3_), channel_id=1, source_target_pairs={{8,0},{12,4},{16,8},{20,12},{24,16},{28,20},{9,1},{13,5},{17,9},{2... | collective-permute-start | bytes 786440 | tf_op jit(solution)/shard_map/ppermute | solution.py:63
  84.5 4.0 %collective-permute-done.7.refs_2_ = bf16[2,256,256]{2,1,0:T(8,128)(2,1)S(1)} collective-permute-done((bf16[2,256,256]{2,1,0:T(8,128)(2,1)S(1)}, bf16[2,256,256]{2,1,0:T(8,128)(2,1)S(1)}, u32[]{:S(2)}, u32[]{:S(2)}) %collective-permute-start.7) | collective-permute-done | bytes 262176 | tf_op jit(solution)/shard_map/ppermute | solution.py:62
  88.5 4.1 %collective-permute-start.8 = (bf16[2,256,256]{2,1,0:T(8,128)(2,1)S(1)}, bf16[2,256,256]{2,1,0:T(8,128)(2,1)S(1)}, u32[]{:S(2)}, u32[]{:S(2)}) collective-permute-start(bf16[2,256,256]{2,1,0:T(8,128)(2,1)S(1)} %collective-permute-done.7.refs_2_), channel_id=1, source_target_pairs={{0,8},{4,12},{8,16},{12,20},{16,24},{20,28},{1,9},{5,13},{9,17},{1... | collective-permute-start | bytes 786440 | tf_op jit(solution)/shard_map/ppermute | solution.py:62
  92.6 1.3 %collective-permute-start.11 = (bf16[2,256,256]{2,1,0:T(8,128)(2,1)S(1)}, bf16[2,256,256]{2,1,0:T(8,128)(2,1)S(1)}, u32[]{:S(2)}, u32[]{:S(2)}) collective-permute-start(bf16[2,256,256]{2,1,0:T(8,128)(2,1)S(1)} %collective-permute-done.10.refs_4_), channel_id=1, source_target_pairs={{8,0},{12,4},{16,8},{20,12},{24,16},{28,20},{9,1},{13,5},{17,9},{2... | collective-permute-start | bytes 786440 | tf_op jit(solution)/shard_map/ppermute | solution.py:63
  94.6 1.4 %collective-permute-start.16 = (bf16[2,256,256]{2,1,0:T(8,128)(2,1)S(1)}, bf16[2,256,256]{2,1,0:T(8,128)(2,1)S(1)}, u32[]{:S(2)}, u32[]{:S(2)}) collective-permute-start(bf16[2,256,256]{2,1,0:T(8,128)(2,1)S(1)} %get-tuple-element.7.refs_3_), channel_id=1, source_target_pairs={{0,4},{4,0},{8,12},{12,8},{16,20},{20,16},{24,28},{28,24},{1,5},{5... | collective-permute-start | bytes 786440 | tf_op jit(solution)/shard_map/ppermute | solution.py:59
  97.0 4.1 %collective-permute-start.9 = (bf16[2,256,256]{2,1,0:T(8,128)(2,1)S(1)}, bf16[2,256,256]{2,1,0:T(8,128)(2,1)S(1)}, u32[]{:S(2)}, u32[]{:S(2)}) collective-permute-start(bf16[2,256,256]{2,1,0:T(8,128)(2,1)S(1)} %collective-permute-done.8.refs_1_), channel_id=1, source_target_pairs={{0,8},{4,12},{8,16},{12,20},{16,24},{20,28},{1,9},{5,13},{9,17},{1... | collective-permute-start | bytes 786440 | tf_op jit(solution)/shard_map/ppermute | solution.py:62
  101.2 1.3 %collective-permute-start.12 = (bf16[2,256,256]{2,1,0:T(8,128)(2,1)S(1)}, bf16[2,256,256]{2,1,0:T(8,128)(2,1)S(1)}, u32[]{:S(2)}, u32[]{:S(2)}) collective-permute-start(bf16[2,256,256]{2,1,0:T(8,128)(2,1)S(1)} %collective-permute-done.11.refs_5_), channel_id=1, source_target_pairs={{8,0},{12,4},{16,8},{20,12},{24,16},{28,20},{9,1},{13,5},{17,9},{2... | collective-permute-start | bytes 786440 | tf_op jit(solution)/shard_map/ppermute | solution.py:63
  102.5 3.0 %fusion.2 = f32[1,1,2,256,256]{4,3,2,1,0:T(8,128)} fusion(f32[1,1,2,256,256]{4,3,2,1,0:T(8,128)} %param.13, f32[2,256,256]{2,1,0:T(8,128)S(1)} %convert_reduce_fusion, f32[2]{0:T(128)S(1)} %convert_element_type.35, pred[2]{0:T(512)(128)(4,1)S(1)} %dynamic-slice_reduce_fusion), kind=kOutput, calls=%fused_computation.5 | convolution fusion | flops 403308544 | bytes 1572874 | tf_op jit(solution)/shard_map/sji,sjk->sik/dot_general | solution.py:160
  105.4 2.7 %fusion.5 = f32[1,1,2,256,256]{4,3,2,1,0:T(8,128)} fusion(f32[1,1,2,256,256]{4,3,2,1,0:T(8,128)} %param.12, f32[2,256,256]{2,1,0:T(8,128)S(1)} %convert_reduce_fusion, f32[2]{0:T(128)S(1)} %convert_element_type.35, pred[2]{0:T(512)(128)(4,1)S(1)} %dynamic-slice_reduce_fusion), kind=kOutput, calls=%fused_computation.9 | convolution fusion | flops 403308544 | bytes 1572874 | tf_op jit(solution)/shard_map/sij,skj->sik/dot_general | solution.py:157
  108.1 2.3 %collective-permute-start.17 = (bf16[2,256,256]{2,1,0:T(8,128)(2,1)S(1)}, bf16[2,256,256]{2,1,0:T(8,128)(2,1)S(1)}, u32[]{:S(2)}, u32[]{:S(2)}) collective-permute-start(bf16[2,256,256]{2,1,0:T(8,128)(2,1)S(1)} %collective-permute-done.10.refs_4_), channel_id=1, source_target_pairs={{0,4},{4,0},{8,12},{12,8},{16,20},{20,16},{24,28},{28,24},{1,5},{5... | collective-permute-start | bytes 786440 | tf_op jit(solution)/shard_map/ppermute | solution.py:65
  114.4 3.1 %shard_map.128 = bf16[8,256,256]{2,1,0:T(8,128)(2,1)} custom-call(s32[8,2]{1,0:T(8,128)} %copy.39.table_ref, bf16[2,256,256]{2,1,0:T(8,128)(2,1)} %copy-done.11, bf16[2,256,256]{2,1,0:T(8,128)(2,1)} %copy-done.7, bf16[2,256,256]{2,1,0:T(8,128)(2,1)} %copy-done.5, bf16[2,256,256]{2,1,0:T(8,128)(2,1)} %copy-done.2, bf16[2,256,256]{2,1,0:T(8,128)(2,1)} %copy-done.6, ...), custom_call_target="tpu_custom_call" | custom-call | tf_op jit(solution)/shard_map/pallas_call | solution.py:97
  (90 shorter events, 12.1 us)
Async XLA Ops:
  4.6 54.8 %all-to-all-start = ((bf16[8,2,256,256]{3,2,1,0:T(8,128)(2,1)}), bf16[8,2,256,256]{3,2,1,0:T(8,128)(2,1)}, u32[]{:S(2)}, u32[]{:S(2)}) async-start(bf16[8,2,256,256]{3,2,1,0:T(8,128)(2,1)} %bitcast.3), calls=%async_computation | async-start | bytes 4194304 | tf_op jit(solution)/shard_map/all_to_all | solution.py:141
  11.1 50.2 %copy-start.1 = (f32[1,1,2,256,256]{4,3,2,1,0:T(8,128)S(1)}, f32[1,1,2,256,256]{4,3,2,1,0:T(8,128)}, u32[]{:S(2)}) copy-start(f32[1,1,2,256,256]{4,3,2,1,0:T(8,128)} %param.16) | copy-start | bytes 1572868
  11.1 50.7 %copy-start.4 = (bf16[1,1,2,256,256]{4,3,2,1,0:T(8,128)(2,1)S(1)}, bf16[1,1,2,256,256]{4,3,2,1,0:T(8,128)(2,1)}, u32[]{:S(2)}) copy-start(bf16[1,1,2,256,256]{4,3,2,1,0:T(8,128)(2,1)} %param.15) | copy-start | bytes 786436
  12.0 68.3 %copy-start.3 = (f32[1,1,2,256,256]{4,3,2,1,0:T(8,128)S(1)}, f32[1,1,2,256,256]{4,3,2,1,0:T(8,128)}, u32[]{:S(2)}) copy-start(f32[1,1,2,256,256]{4,3,2,1,0:T(8,128)} %param.17) | copy-start | bytes 1572868
  63.5 3.6 %collective-permute-start = (f32[2,9]{1,0:T(2,128)S(1)}, f32[2,9]{1,0:T(2,128)S(1)}, u32[]{:S(2)}, u32[]{:S(2)}) collective-permute-start(f32[2,9]{1,0:T(2,128)S(1)} %pad_maximum_fusion), channel_id=1, source_target_pairs={{0,16},{1,17},{2,18},{3,19},{4,20},{5,21},{6,22},{7,23},{8,24},{9,... | collective-permute-start | bytes 224 | tf_op jit(solution)/shard_map/ppermute | solution.py:38
  63.6 3.5 %collective-permute-start.1 = (f32[2,9]{1,0:T(2,128)S(1)}, f32[2,9]{1,0:T(2,128)S(1)}, u32[]{:S(2)}, u32[]{:S(2)}) collective-permute-start(f32[2,9]{1,0:T(2,128)S(1)} %pad_maximum_fusion), channel_id=1, source_target_pairs={{0,1},{1,0},{2,3},{3,2},{4,5},{5,4},{6,7},{7,6},{8,9},{9,8},{10,11... | collective-permute-start | bytes 224 | tf_op jit(solution)/shard_map/ppermute | solution.py:38
  64.9 4.2 %collective-permute-start.2 = (f32[2,9]{1,0:T(2,128)S(1)}, f32[2,9]{1,0:T(2,128)S(1)}, u32[]{:S(2)}, u32[]{:S(2)}) collective-permute-start(f32[2,9]{1,0:T(2,128)S(1)} %pad_maximum_fusion), channel_id=1, source_target_pairs={{0,17},{1,16},{2,19},{3,18},{4,21},{5,20},{6,23},{7,22},{8,25},{9,... | collective-permute-start | bytes 224 | tf_op jit(solution)/shard_map/ppermute | solution.py:38
  69.1 2.9 %collective-permute-start.3 = (f32[2,9]{1,0:T(2,128)S(1)}, f32[2,9]{1,0:T(2,128)S(1)}, u32[]{:S(2)}, u32[]{:S(2)}) collective-permute-start(f32[2,9]{1,0:T(2,128)S(1)} %add_add_fusion.1), channel_id=1, source_target_pairs={{0,8},{1,9},{2,10},{3,11},{4,12},{5,13},{6,14},{7,15},{8,0},{9,1},... | collective-permute-start | bytes 224 | tf_op jit(solution)/shard_map/ppermute | solution.py:38
  70.8 2.4 %collective-permute-start.4 = (f32[2,9]{1,0:T(2,128)S(1)}, f32[2,9]{1,0:T(2,128)S(1)}, u32[]{:S(2)}, u32[]{:S(2)}) collective-permute-start(f32[2,9]{1,0:T(2,128)S(1)} %add_add_fusion.1), channel_id=1, source_target_pairs={{0,2},{1,3},{2,0},{3,1},{4,6},{5,7},{6,4},{7,5},{8,10},{9,11},{10,... | collective-permute-start | bytes 224 | tf_op jit(solution)/shard_map/ppermute | solution.py:38
  72.0 3.3 %collective-permute-start.5 = (f32[2,9]{1,0:T(2,128)S(1)}, f32[2,9]{1,0:T(2,128)S(1)}, u32[]{:S(2)}, u32[]{:S(2)}) collective-permute-start(f32[2,9]{1,0:T(2,128)S(1)} %add_add_fusion.1), channel_id=1, source_target_pairs={{0,10},{1,11},{2,8},{3,9},{4,14},{5,15},{6,12},{7,13},{8,2},{9,3},... | collective-permute-start | bytes 224 | tf_op jit(solution)/shard_map/ppermute | solution.py:38
  75.4 4.7 %collective-permute-start.6 = (f32[2,9]{1,0:T(2,128)S(1)}, f32[2,9]{1,0:T(2,128)S(1)}, u32[]{:S(2)}, u32[]{:S(2)}) collective-permute-start(f32[2,9]{1,0:T(2,128)S(1)} %add_add_fusion), channel_id=1, source_target_pairs={{0,4},{1,5},{2,6},{3,7},{4,0},{5,1},{6,2},{7,3},{8,12},{9,13},{10,... | collective-permute-start | bytes 224 | tf_op jit(solution)/shard_map/ppermute | solution.py:38
  81.2 7.3 %collective-permute-start.7 = (bf16[2,256,256]{2,1,0:T(8,128)(2,1)S(1)}, bf16[2,256,256]{2,1,0:T(8,128)(2,1)S(1)}, u32[]{:S(2)}, u32[]{:S(2)}) collective-permute-start(bf16[2,256,256]{2,1,0:T(8,128)(2,1)S(1)} %get-tuple-element.7.refs_3_), channel_id=1, source_target_pairs={{0,8},{4,12},{8,16},{12,20},{16,24},{20,28},{1,9},{5,13},{9,17},{1... | collective-permute-start | bytes 786440 | tf_op jit(solution)/shard_map/ppermute | solution.py:62
  83.1 9.5 %collective-permute-start.10 = (bf16[2,256,256]{2,1,0:T(8,128)(2,1)S(1)}, bf16[2,256,256]{2,1,0:T(8,128)(2,1)S(1)}, u32[]{:S(2)}, u32[]{:S(2)}) collective-permute-start(bf16[2,256,256]{2,1,0:T(8,128)(2,1)S(1)} %get-tuple-element.7.refs_3_), channel_id=1, source_target_pairs={{8,0},{12,4},{16,8},{20,12},{24,16},{28,20},{9,1},{13,5},{17,9},{2... | collective-permute-start | bytes 786440 | tf_op jit(solution)/shard_map/ppermute | solution.py:63
  88.5 8.5 %collective-permute-start.8 = (bf16[2,256,256]{2,1,0:T(8,128)(2,1)S(1)}, bf16[2,256,256]{2,1,0:T(8,128)(2,1)S(1)}, u32[]{:S(2)}, u32[]{:S(2)}) collective-permute-start(bf16[2,256,256]{2,1,0:T(8,128)(2,1)S(1)} %collective-permute-done.7.refs_2_), channel_id=1, source_target_pairs={{0,8},{4,12},{8,16},{12,20},{16,24},{20,28},{1,9},{5,13},{9,17},{1... | collective-permute-start | bytes 786440 | tf_op jit(solution)/shard_map/ppermute | solution.py:62
  92.6 8.5 %collective-permute-start.11 = (bf16[2,256,256]{2,1,0:T(8,128)(2,1)S(1)}, bf16[2,256,256]{2,1,0:T(8,128)(2,1)S(1)}, u32[]{:S(2)}, u32[]{:S(2)}) collective-permute-start(bf16[2,256,256]{2,1,0:T(8,128)(2,1)S(1)} %collective-permute-done.10.refs_4_), channel_id=1, source_target_pairs={{8,0},{12,4},{16,8},{20,12},{24,16},{28,20},{9,1},{13,5},{17,9},{2... | collective-permute-start | bytes 786440 | tf_op jit(solution)/shard_map/ppermute | solution.py:63
  94.6 15.8 %collective-permute-start.16 = (bf16[2,256,256]{2,1,0:T(8,128)(2,1)S(1)}, bf16[2,256,256]{2,1,0:T(8,128)(2,1)S(1)}, u32[]{:S(2)}, u32[]{:S(2)}) collective-permute-start(bf16[2,256,256]{2,1,0:T(8,128)(2,1)S(1)} %get-tuple-element.7.refs_3_), channel_id=1, source_target_pairs={{0,4},{4,0},{8,12},{12,8},{16,20},{20,16},{24,28},{28,24},{1,5},{5... | collective-permute-start | bytes 786440 | tf_op jit(solution)/shard_map/ppermute | solution.py:59
  96.1 14.5 %collective-permute-start.15 = (bf16[2,256,256]{2,1,0:T(8,128)(2,1)S(1)}, bf16[2,256,256]{2,1,0:T(8,128)(2,1)S(1)}, u32[]{:S(2)}, u32[]{:S(2)}) collective-permute-start(bf16[2,256,256]{2,1,0:T(8,128)(2,1)S(1)} %collective-permute-done.7.refs_2_), channel_id=1, source_target_pairs={{0,4},{4,0},{8,12},{12,8},{16,20},{20,16},{24,28},{28,24},{1,5},{5... | collective-permute-start | bytes 786440 | tf_op jit(solution)/shard_map/ppermute | solution.py:64
  97.0 14.0 %collective-permute-start.9 = (bf16[2,256,256]{2,1,0:T(8,128)(2,1)S(1)}, bf16[2,256,256]{2,1,0:T(8,128)(2,1)S(1)}, u32[]{:S(2)}, u32[]{:S(2)}) collective-permute-start(bf16[2,256,256]{2,1,0:T(8,128)(2,1)S(1)} %collective-permute-done.8.refs_1_), channel_id=1, source_target_pairs={{0,8},{4,12},{8,16},{12,20},{16,24},{20,28},{1,9},{5,13},{9,17},{1... | collective-permute-start | bytes 786440 | tf_op jit(solution)/shard_map/ppermute | solution.py:62
  101.2 9.9 %collective-permute-start.12 = (bf16[2,256,256]{2,1,0:T(8,128)(2,1)S(1)}, bf16[2,256,256]{2,1,0:T(8,128)(2,1)S(1)}, u32[]{:S(2)}, u32[]{:S(2)}) collective-permute-start(bf16[2,256,256]{2,1,0:T(8,128)(2,1)S(1)} %collective-permute-done.11.refs_5_), channel_id=1, source_target_pairs={{8,0},{12,4},{16,8},{20,12},{24,16},{28,20},{9,1},{13,5},{17,9},{2... | collective-permute-start | bytes 786440 | tf_op jit(solution)/shard_map/ppermute | solution.py:63
  108.1 4.7 %collective-permute-start.17 = (bf16[2,256,256]{2,1,0:T(8,128)(2,1)S(1)}, bf16[2,256,256]{2,1,0:T(8,128)(2,1)S(1)}, u32[]{:S(2)}, u32[]{:S(2)}) collective-permute-start(bf16[2,256,256]{2,1,0:T(8,128)(2,1)S(1)} %collective-permute-done.10.refs_4_), channel_id=1, source_target_pairs={{0,4},{4,0},{8,12},{12,8},{16,20},{20,16},{24,28},{28,24},{1,5},{5... | collective-permute-start | bytes 786440 | tf_op jit(solution)/shard_map/ppermute | solution.py:65
  110.5 2.3 %collective-permute-start.14 = (bf16[2,256,256]{2,1,0:T(8,128)(2,1)S(1)}, bf16[2,256,256]{2,1,0:T(8,128)(2,1)S(1)}, u32[]{:S(2)}, u32[]{:S(2)}) collective-permute-start(bf16[2,256,256]{2,1,0:T(8,128)(2,1)S(1)} %collective-permute-done.8.refs_1_), channel_id=1, source_target_pairs={{0,4},{4,0},{8,12},{12,8},{16,20},{20,16},{24,28},{28,24},{1,5},{5... | collective-permute-start | bytes 786440 | tf_op jit(solution)/shard_map/ppermute | solution.py:64
  110.5 2.3 %collective-permute-start.18 = (bf16[2,256,256]{2,1,0:T(8,128)(2,1)S(1)}, bf16[2,256,256]{2,1,0:T(8,128)(2,1)S(1)}, u32[]{:S(2)}, u32[]{:S(2)}) collective-permute-start(bf16[2,256,256]{2,1,0:T(8,128)(2,1)S(1)} %collective-permute-done.11.refs_5_), channel_id=1, source_target_pairs={{0,4},{4,0},{8,12},{12,8},{16,20},{20,16},{24,28},{28,24},{1,5},{5... | collective-permute-start | bytes 786440 | tf_op jit(solution)/shard_map/ppermute | solution.py:65
  111.0 1.9 %collective-permute-start.13 = (bf16[2,256,256]{2,1,0:T(8,128)(2,1)S(1)}, bf16[2,256,256]{2,1,0:T(8,128)(2,1)S(1)}, u32[]{:S(2)}, u32[]{:S(2)}) collective-permute-start(bf16[2,256,256]{2,1,0:T(8,128)(2,1)S(1)} %collective-permute-done.9.refs_0_), channel_id=1, source_target_pairs={{0,4},{4,0},{8,12},{12,8},{16,20},{20,16},{24,28},{28,24},{1,5},{5... | collective-permute-start | bytes 786440 | tf_op jit(solution)/shard_map/ppermute | solution.py:64
  111.1 3.3 %collective-permute-start.19 = (bf16[2,256,256]{2,1,0:T(8,128)(2,1)S(1)}, bf16[2,256,256]{2,1,0:T(8,128)(2,1)}, u32[]{:S(2)}, u32[]{:S(2)}) collective-permute-start(bf16[2,256,256]{2,1,0:T(8,128)(2,1)S(1)} %collective-permute-done.12.refs_6_), channel_id=1, source_target_pairs={{0,4},{4,0},{8,12},{12,8},{16,20},{20,16},{24,28},{28,24},{1,5},{5... | collective-permute-start | bytes 786440 | tf_op jit(solution)/shard_map/ppermute | solution.py:65
  (16 other events, 156.1 us)

commit v15 on v8

--- a/solution.py
+++ b/solution.py
@@ -150,7 +150,9 @@
         "sij,sjk->sik", inner, root_right[0, 0], preferred_element_type=jnp.float32
     )
     prec_terms = jnp.sum(member * jnp.sum(precond * precond, axis=(1, 2))[:, None], axis=0)
-    norms = butterfly_sum(butterfly_sum(jnp.stack([adam_terms, prec_terms]), "dp"), "shard")
+    partial_norms = butterfly_sum(jnp.stack([adam_terms, prec_terms]), "dp")
+    partial_norms, lnew, rnew = lax.optimization_barrier((partial_norms, lnew, rnew))
+    norms = butterfly_sum(partial_norms, "shard")
     norm_adam = norms[0]
     norm_prec = norms[1]
     scales = jnp.sqrt(norm_adam / (norm_prec + NORM_EPS))

time: 117 us -> 117 us (level)
  starting transfers between devices: 34.6 us -> 39.4 us
  matrix products: 7.28 us -> 4.3 us
  waiting for transfers between devices: 58.3 us -> 56.3 us
    ppermute x3, starting transfers between devices: 0.16 us -> 4.48 us  [gather_blocks(): near_left[step] = lax.ppermute(from_left[step], 'dp', partner)]
    ppermute x3, starting transfers between devices: 10 us -> 12.8 us  [gather_blocks(): from_left[step] = lax.ppermute(from_left[step - 1], 'dp', rightward)]
    ppermute x3, starting transfers between devices: 3.49 us -> 0.82 us  [gather_blocks(): near_right[step] = lax.ppermute(from_right[step], 'dp', partner)]
    ppermute x5, waiting for transfers between devices: 8.91 us -> 6.93 us  [butterfly_sum(): x = x + lax.ppermute(x, axis, [(i, i ^ step) for i in range(size)])]
    dot_general x1, matrix products: 2.66 us -> 0.79 us  [local(): jnp.einsum('sij,skj->sik', owned_grad, owned_grad, precision=highest)]
    dot_general x1, matrix products: 2.99 us -> 1.17 us  [local(): jnp.einsum('sji,sjk->sik', owned_grad, owned_grad, precision=highest)]
    ppermute x3, waiting for transfers between devices: 0.01 us -> 1.81 us  [gather_blocks(): from_right[step] = lax.ppermute(from_right[step - 1], 'dp', leftward)]
    ppermute x3, waiting for transfers between devices: 1.96 us -> 0.19 us  [gather_blocks(): from_left[step] = lax.ppermute(from_left[step - 1], 'dp', rightward)]
  transfers between devices with their start and end apart: 19 -> 19, of which waited for: 7 -> 8; matrix products, arithmetic and copies ran while one was open for 7% -> 4% of each run, Pallas kernels for 0% -> 0%
where the time goes in v15:
time: 117 us
  waiting for transfers between devices  56.3 us (48%)
  starting transfers between devices  39.4 us (34%)
  other arithmetic  7.46 us (6%)
  local copies, waits for them, and re-layouts  5.2 us (4%)
  matrix products  4.3 us (4%)
  Pallas kernels  3.14 us (3%)
    all_to_all x1, waiting for transfers between devices, local(): received = lax.all_to_all(by_owner, 'dp', 0, 0, tiled=True)  47.4 us
    ppermute x3, starting transfers between devices, gather_blocks(): from_left[step] = lax.ppermute(from_left[step - 1], 'dp', rightward)  12.8 us
    ppermute x1, starting transfers between devices, gather_blocks(): near_left[0] = lax.ppermute(mine, 'dp', partner)  7.44 us
    ppermute x5, waiting for transfers between devices, butterfly_sum(): x = x + lax.ppermute(x, axis, [(i, i ^ step) for i in range(size)])  6.93 us
    all_to_all x1, starting transfers between devices, local(): received = lax.all_to_all(by_owner, 'dp', 0, 0, tiled=True)  6.51 us
    ppermute x3, starting transfers between devices, gather_blocks(): near_left[step] = lax.ppermute(from_left[step], 'dp', partner)  4.48 us
    ppermute x3, starting transfers between devices, gather_blocks(): from_right[step] = lax.ppermute(from_right[step - 1], 'dp', leftward)  3.84 us
    ppermute x5, starting transfers between devices, butterfly_sum(): x = x + lax.ppermute(x, axis, [(i, i ^ step) for i in range(size)])  3.51 us
  transfers between devices with their start and end apart: 19, of which 8 were waited for; matrix products, arithmetic and copies ran while one was open for 4% of the time, Pallas kernels for 0%

profile of v15, /device:TPU:1, one launch (start us, length us, event | category | flops | bytes accessed | tf_op | source)
XLA Modules:
  0.0 116.8 jit_solution(725232698115289193)
XLA Ops:
  2.6 2.0 %gather_fusion = bf16[16,256,256]{2,1,0:T(8,128)(2,1)} fusion(bf16[8,256,256]{2,1,0:T(8,128)(2,1)S(1)} %bitcast.56, s32[1024]{0:T(1024)S(1)} %pad_clamp_fusion), kind=kCustom, calls=%fused_computation | custom fusion | bytes 4194368 | tf_op jit(solution)/shard_map/jit(_take)/gather | solution.py:120
  4.6 6.5 %all-to-all-start = ((bf16[8,2,256,256]{3,2,1,0:T(8,128)(2,1)}), bf16[8,2,256,256]{3,2,1,0:T(8,128)(2,1)}, u32[]{:S(2)}, u32[]{:S(2)}) async-start(bf16[8,2,256,256]{3,2,1,0:T(8,128)(2,1)} %bitcast.4), calls=%async_computation | async-start | bytes 4194304 | tf_op jit(solution)/shard_map/all_to_all | solution.py:123
  12.0 47.4 %all-to-all-done = bf16[8,2,256,256]{3,2,1,0:T(8,128)(2,1)} async-done(((bf16[8,2,256,256]{3,2,1,0:T(8,128)(2,1)}), bf16[8,2,256,256]{3,2,1,0:T(8,128)(2,1)}, u32[]{:S(2)}, u32[]{:S(2)}) %all-to-all-start) | async-done | bytes 2097184 | tf_op jit(solution)/shard_map/all_to_all | solution.py:123
  59.4 1.9 %convert_reduce_fusion = f32[2,256,256]{2,1,0:T(8,128)S(1)} fusion(bf16[8,2,256,256]{3,2,1,0:T(8,128)(2,1)} %all-to-all-done), kind=kLoop, calls=%fused_computation.1 | loop fusion | flops 1966080 | bytes 2621440 | tf_op jit(solution)/shard_map/reduce_sum | solution.py:124
  61.8 2.3 %multiply_reduce_fusion = (f32[2]{0:T(128)S(1)}, f32[2,256,256]{2,1,0:T(8,128)}) fusion(bf16[1,1,2,256,256]{4,3,2,1,0:T(8,128)(2,1)S(1)} %copy-done.7, f32[2,256,256]{2,1,0:T(8,128)S(1)} %convert_reduce_fusion, bf16[1,1,2,256,256]{4,3,2,1,0:T(8,128)(2,1)} %param.14, f32[2]{0:T(128)S(1)} %convert_element_type.35), kind=kOutput, calls=%fused_computation.25 | convolution fusion | flops 134873088 | bytes 1572880 | tf_op jit(solution)/shard_map/sij,sjk->sik/dot_general | solution.py:149
  66.9 1.6 %collective-permute-done.1 = f32[2,9]{1,0:T(2,128)S(1)} collective-permute-done((f32[2,9]{1,0:T(2,128)S(1)}, f32[2,9]{1,0:T(2,128)S(1)}, u32[]{:S(2)}, u32[]{:S(2)}) %collective-permute-start.1) | collective-permute-done | bytes 104 | tf_op jit(solution)/shard_map/ppermute | solution.py:20
  68.6 1.2 fusion
  69.8 2.1 %collective-permute-done.2 = f32[2,9]{1,0:T(2,128)S(1)} collective-permute-done((f32[2,9]{1,0:T(2,128)S(1)}, f32[2,9]{1,0:T(2,128)S(1)}, u32[]{:S(2)}, u32[]{:S(2)}) %collective-permute-start.2) | collective-permute-done | bytes 104 | tf_op jit(solution)/shard_map/ppermute | solution.py:20
  71.9 1.2 %collective-permute-start.3 = (f32[2,9]{1,0:T(2,128)S(1)}, f32[2,9]{1,0:T(2,128)S(1)}, u32[]{:S(2)}, u32[]{:S(2)}) collective-permute-start(f32[2,9]{1,0:T(2,128)S(1)} %add.89), channel_id=1, source_target_pairs={{0,1},{1,0},{2,3},{3,2},{4,5},{5,4},{6,7},{7,6},{8,9},{9,8},{10,11... | collective-permute-start | bytes 224 | tf_op jit(solution)/shard_map/ppermute | solution.py:20
  73.1 1.2 %collective-permute-done.3 = f32[2,9]{1,0:T(2,128)S(1)} collective-permute-done((f32[2,9]{1,0:T(2,128)S(1)}, f32[2,9]{1,0:T(2,128)S(1)}, u32[]{:S(2)}, u32[]{:S(2)}) %collective-permute-start.3) | collective-permute-done | bytes 104 | tf_op jit(solution)/shard_map/ppermute | solution.py:20
  74.3 1.2 %collective-permute-start.4 = (f32[2,9]{1,0:T(2,128)S(1)}, f32[2,9]{1,0:T(2,128)S(1)}, u32[]{:S(2)}, u32[]{:S(2)}) collective-permute-start(f32[2,9]{1,0:T(2,128)S(1)} %add.93), channel_id=1, source_target_pairs={{0,2},{1,3},{2,0},{3,1},{4,6},{5,7},{6,4},{7,5},{8,10},{9,11},{10,... | collective-permute-start | bytes 224 | tf_op jit(solution)/shard_map/ppermute | solution.py:20
  75.6 1.2 %collective-permute-done.4 = f32[2,9]{1,0:T(2,128)S(1)} collective-permute-done((f32[2,9]{1,0:T(2,128)S(1)}, f32[2,9]{1,0:T(2,128)S(1)}, u32[]{:S(2)}, u32[]{:S(2)}) %collective-permute-start.4) | collective-permute-done | bytes 104 | tf_op jit(solution)/shard_map/ppermute | solution.py:20
  77.0 1.3 %fusion.29 = (bf16[2,256,256]{2,1,0:T(8,128)(2,1)S(1)}, f32[1,1,2,256,256]{4,3,2,1,0:T(8,128)}, f32[1,1,2,256,256]{4,3,2,1,0:T(8,128)}, f32[1,1,2,256,256]{4,3,2,1,0:T(8,128)}) fusion(f32[2,256,256]{2,1,0:T(8,128)S(1)} %copy-done.4, f32[2]{0:T(128)S(1)} %broadcast_multiply_fusion, f32[1,1,2,256,256]{4,3,2,1,0:T(8,128)S(1)} %copy-done.6, ...), kind=kLoop, calls=%fused_computation.68 | loop fusion | flops 786432 | bytes 4980746 | tf_op jit(solution)/shard_map/convert_element_type | solution.py:166
  78.3 1.3 %collective-permute-start.8 = (bf16[2,256,256]{2,1,0:T(8,128)(2,1)S(1)}, bf16[2,256,256]{2,1,0:T(8,128)(2,1)S(1)}, u32[]{:S(2)}, u32[]{:S(2)}) collective-permute-start(bf16[2,256,256]{2,1,0:T(8,128)(2,1)S(1)} %get-tuple-element.13.refs_3_), channel_id=1, source_target_pairs={{8,0},{12,4},{16,8},{20,12},{24,16},{28,20},{9,1},{13,5},{17,9},{2... | collective-permute-start | bytes 786440 | tf_op jit(solution)/shard_map/ppermute | solution.py:45
  79.6 4.0 %collective-permute-start.5 = (bf16[2,256,256]{2,1,0:T(8,128)(2,1)S(1)}, bf16[2,256,256]{2,1,0:T(8,128)(2,1)S(1)}, u32[]{:S(2)}, u32[]{:S(2)}) collective-permute-start(bf16[2,256,256]{2,1,0:T(8,128)(2,1)S(1)} %get-tuple-element.13.refs_3_), channel_id=1, source_target_pairs={{0,8},{4,12},{8,16},{12,20},{16,24},{20,28},{1,9},{5,13},{9,17},{1... | collective-permute-start | bytes 786440 | tf_op jit(solution)/shard_map/ppermute | solution.py:44
  83.6 1.8 %collective-permute-done.8.refs_4_ = bf16[2,256,256]{2,1,0:T(8,128)(2,1)S(1)} collective-permute-done((bf16[2,256,256]{2,1,0:T(8,128)(2,1)S(1)}, bf16[2,256,256]{2,1,0:T(8,128)(2,1)S(1)}, u32[]{:S(2)}, u32[]{:S(2)}) %collective-permute-start.8) | collective-permute-done | bytes 262176 | tf_op jit(solution)/shard_map/ppermute | solution.py:45
  85.4 1.3 %collective-permute-start.9 = (bf16[2,256,256]{2,1,0:T(8,128)(2,1)S(1)}, bf16[2,256,256]{2,1,0:T(8,128)(2,1)S(1)}, u32[]{:S(2)}, u32[]{:S(2)}) collective-permute-start(bf16[2,256,256]{2,1,0:T(8,128)(2,1)S(1)} %collective-permute-done.8.refs_4_), channel_id=1, source_target_pairs={{8,0},{12,4},{16,8},{20,12},{24,16},{28,20},{9,1},{13,5},{17,9},{2... | collective-permute-start | bytes 786440 | tf_op jit(solution)/shard_map/ppermute | solution.py:45
  86.9 4.1 %collective-permute-start.6 = (bf16[2,256,256]{2,1,0:T(8,128)(2,1)S(1)}, bf16[2,256,256]{2,1,0:T(8,128)(2,1)S(1)}, u32[]{:S(2)}, u32[]{:S(2)}) collective-permute-start(bf16[2,256,256]{2,1,0:T(8,128)(2,1)S(1)} %collective-permute-done.5.refs_2_), channel_id=1, source_target_pairs={{0,8},{4,12},{8,16},{12,20},{16,24},{20,28},{1,9},{5,13},{9,17},{1... | collective-permute-start | bytes 786440 | tf_op jit(solution)/shard_map/ppermute | solution.py:44
  91.0 7.4 %collective-permute-start.14 = (bf16[2,256,256]{2,1,0:T(8,128)(2,1)S(1)}, bf16[2,256,256]{2,1,0:T(8,128)(2,1)}, u32[]{:S(2)}, u32[]{:S(2)}) collective-permute-start(bf16[2,256,256]{2,1,0:T(8,128)(2,1)S(1)} %get-tuple-element.13.refs_3_), channel_id=1, source_target_pairs={{0,4},{4,0},{8,12},{12,8},{16,20},{20,16},{24,28},{28,24},{1,5},{5... | collective-permute-start | bytes 786440 | tf_op jit(solution)/shard_map/ppermute | solution.py:41
  98.5 1.3 %collective-permute-start.10 = (bf16[2,256,256]{2,1,0:T(8,128)(2,1)S(1)}, bf16[2,256,256]{2,1,0:T(8,128)(2,1)}, u32[]{:S(2)}, u32[]{:S(2)}) collective-permute-start(bf16[2,256,256]{2,1,0:T(8,128)(2,1)S(1)} %collective-permute-done.9.refs_5_), channel_id=1, source_target_pairs={{8,0},{12,4},{16,8},{20,12},{24,16},{28,20},{9,1},{13,5},{17,9},{2... | collective-permute-start | bytes 786440 | tf_op jit(solution)/shard_map/ppermute | solution.py:45
  99.8 4.7 %collective-permute-start.7 = (bf16[2,256,256]{2,1,0:T(8,128)(2,1)S(1)}, bf16[2,256,256]{2,1,0:T(8,128)(2,1)}, u32[]{:S(2)}, u32[]{:S(2)}) collective-permute-start(bf16[2,256,256]{2,1,0:T(8,128)(2,1)S(1)} %collective-permute-done.6.refs_1_), channel_id=1, source_target_pairs={{0,8},{4,12},{8,16},{12,20},{16,24},{20,28},{1,9},{5,13},{9,17},{1... | collective-permute-start | bytes 786440 | tf_op jit(solution)/shard_map/ppermute | solution.py:44
  105.2 2.8 %collective-permute-start.13 = (bf16[2,256,256]{2,1,0:T(8,128)(2,1)S(1)}, bf16[2,256,256]{2,1,0:T(8,128)(2,1)S(1)}, u32[]{:S(2)}, u32[]{:S(2)}) collective-permute-start(bf16[2,256,256]{2,1,0:T(8,128)(2,1)S(1)} %collective-permute-done.5.refs_2_), channel_id=1, source_target_pairs={{0,4},{4,0},{8,12},{12,8},{16,20},{20,16},{24,28},{28,24},{1,5},{5... | collective-permute-start | bytes 786440 | tf_op jit(solution)/shard_map/ppermute | solution.py:46
  109.2 1.2 %collective-permute-start.11 = (bf16[2,256,256]{2,1,0:T(8,128)(2,1)}, bf16[2,256,256]{2,1,0:T(8,128)(2,1)}, u32[]{:S(2)}, u32[]{:S(2)}) collective-permute-start(bf16[2,256,256]{2,1,0:T(8,128)(2,1)} %collective-permute-done.7.refs_0_), channel_id=1, source_target_pairs={{0,4},{4,0},{8,12},{12,8},{16,20},{20,16},{24,28},{28,24},{1,5},{5... | collective-permute-start | bytes 786440 | tf_op jit(solution)/shard_map/ppermute | solution.py:46
  113.6 3.1 %shard_map.128 = bf16[8,256,256]{2,1,0:T(8,128)(2,1)} custom-call(s32[8,2]{1,0:T(8,128)} %copy.39.table_ref, bf16[2,256,256]{2,1,0:T(8,128)(2,1)} %collective-permute-done.7.refs_0_, bf16[2,256,256]{2,1,0:T(8,128)(2,1)} %copy-done.11, bf16[2,256,256]{2,1,0:T(8,128)(2,1)} %copy-done.9, bf16[2,256,256]{2,1,0:T(8,128)(2,1)} %copy-done.5, ...), custom_call_target="tpu_custom_call" | custom-call | tf_op jit(solution)/shard_map/pallas_call | solution.py:79
  (86 shorter events, 11.7 us)
Async XLA Ops:
  4.6 54.8 %all-to-all-start = ((bf16[8,2,256,256]{3,2,1,0:T(8,128)(2,1)}), bf16[8,2,256,256]{3,2,1,0:T(8,128)(2,1)}, u32[]{:S(2)}, u32[]{:S(2)}) async-start(bf16[8,2,256,256]{3,2,1,0:T(8,128)(2,1)} %bitcast.4), calls=%async_computation | async-start | bytes 4194304 | tf_op jit(solution)/shard_map/all_to_all | solution.py:123
  11.1 50.2 %copy-start.1 = (f32[1,1,2,256,256]{4,3,2,1,0:T(8,128)S(1)}, f32[1,1,2,256,256]{4,3,2,1,0:T(8,128)}, u32[]{:S(2)}) copy-start(f32[1,1,2,256,256]{4,3,2,1,0:T(8,128)} %param.16) | copy-start | bytes 1572868
  11.1 50.7 %copy-start.7 = (bf16[1,1,2,256,256]{4,3,2,1,0:T(8,128)(2,1)S(1)}, bf16[1,1,2,256,256]{4,3,2,1,0:T(8,128)(2,1)}, u32[]{:S(2)}) copy-start(bf16[1,1,2,256,256]{4,3,2,1,0:T(8,128)(2,1)} %param.15) | copy-start | bytes 786436
  12.0 54.1 %copy-start.3 = (f32[1,1,2,256,256]{4,3,2,1,0:T(8,128)S(1)}, f32[1,1,2,256,256]{4,3,2,1,0:T(8,128)}, u32[]{:S(2)}) copy-start(f32[1,1,2,256,256]{4,3,2,1,0:T(8,128)} %param.12) | copy-start | bytes 1572868
  64.3 1.7 %collective-permute-start = (f32[2,9]{1,0:T(2,128)S(1)}, f32[2,9]{1,0:T(2,128)S(1)}, u32[]{:S(2)}, u32[]{:S(2)}) collective-permute-start(f32[2,9]{1,0:T(2,128)S(1)} %pad_maximum_fusion), channel_id=1, source_target_pairs={{0,4},{4,0},{8,12},{12,8},{16,20},{20,16},{24,28},{28,24},{1,5},{5... | collective-permute-start | bytes 224 | tf_op jit(solution)/shard_map/ppermute | solution.py:20
  66.0 2.5 %collective-permute-start.1 = (f32[2,9]{1,0:T(2,128)S(1)}, f32[2,9]{1,0:T(2,128)S(1)}, u32[]{:S(2)}, u32[]{:S(2)}) collective-permute-start(f32[2,9]{1,0:T(2,128)S(1)} %fusion.28), channel_id=1, source_target_pairs={{0,8},{4,12},{8,0},{12,4},{16,24},{20,28},{24,16},{28,20},{1,9},{5... | collective-permute-start | bytes 224 | tf_op jit(solution)/shard_map/ppermute | solution.py:20
  68.5 3.4 %collective-permute-start.2 = (f32[2,9]{1,0:T(2,128)S(1)}, f32[2,9]{1,0:T(2,128)S(1)}, u32[]{:S(2)}, u32[]{:S(2)}) collective-permute-start(f32[2,9]{1,0:T(2,128)S(1)} %fusion.33), channel_id=1, source_target_pairs={{0,16},{4,20},{8,24},{12,28},{16,0},{20,4},{24,8},{28,12},{1,17},{... | collective-permute-start | bytes 224 | tf_op jit(solution)/shard_map/ppermute | solution.py:20
  71.9 2.4 %collective-permute-start.3 = (f32[2,9]{1,0:T(2,128)S(1)}, f32[2,9]{1,0:T(2,128)S(1)}, u32[]{:S(2)}, u32[]{:S(2)}) collective-permute-start(f32[2,9]{1,0:T(2,128)S(1)} %add.89), channel_id=1, source_target_pairs={{0,1},{1,0},{2,3},{3,2},{4,5},{5,4},{6,7},{7,6},{8,9},{9,8},{10,11... | collective-permute-start | bytes 224 | tf_op jit(solution)/shard_map/ppermute | solution.py:20
  74.3 2.4 %collective-permute-start.4 = (f32[2,9]{1,0:T(2,128)S(1)}, f32[2,9]{1,0:T(2,128)S(1)}, u32[]{:S(2)}, u32[]{:S(2)}) collective-permute-start(f32[2,9]{1,0:T(2,128)S(1)} %add.93), channel_id=1, source_target_pairs={{0,2},{1,3},{2,0},{3,1},{4,6},{5,7},{6,4},{7,5},{8,10},{9,11},{10,... | collective-permute-start | bytes 224 | tf_op jit(solution)/shard_map/ppermute | solution.py:20
  78.3 35.3 %copy-start.5 = (bf16[2,256,256]{2,1,0:T(8,128)(2,1)}, bf16[2,256,256]{2,1,0:T(8,128)(2,1)S(1)}, u32[]{:S(2)}) copy-start(bf16[2,256,256]{2,1,0:T(8,128)(2,1)S(1)} %get-tuple-element.13.refs_3_) | copy-start | bytes 786436
  78.3 7.1 %collective-permute-start.8 = (bf16[2,256,256]{2,1,0:T(8,128)(2,1)S(1)}, bf16[2,256,256]{2,1,0:T(8,128)(2,1)S(1)}, u32[]{:S(2)}, u32[]{:S(2)}) collective-permute-start(bf16[2,256,256]{2,1,0:T(8,128)(2,1)S(1)} %get-tuple-element.13.refs_3_), channel_id=1, source_target_pairs={{8,0},{12,4},{16,8},{20,12},{24,16},{28,20},{9,1},{13,5},{17,9},{2... | collective-permute-start | bytes 786440 | tf_op jit(solution)/shard_map/ppermute | solution.py:45
  79.6 7.3 %collective-permute-start.5 = (bf16[2,256,256]{2,1,0:T(8,128)(2,1)S(1)}, bf16[2,256,256]{2,1,0:T(8,128)(2,1)S(1)}, u32[]{:S(2)}, u32[]{:S(2)}) collective-permute-start(bf16[2,256,256]{2,1,0:T(8,128)(2,1)S(1)} %get-tuple-element.13.refs_3_), channel_id=1, source_target_pairs={{0,8},{4,12},{8,16},{12,20},{16,24},{20,28},{1,9},{5,13},{9,17},{1... | collective-permute-start | bytes 786440 | tf_op jit(solution)/shard_map/ppermute | solution.py:44
  85.4 28.2 %copy-start.8 = (bf16[2,256,256]{2,1,0:T(8,128)(2,1)}, bf16[2,256,256]{2,1,0:T(8,128)(2,1)S(1)}, u32[]{:S(2)}) copy-start(bf16[2,256,256]{2,1,0:T(8,128)(2,1)S(1)} %collective-permute-done.8.refs_4_) | copy-start | bytes 786436
  85.4 13.1 %collective-permute-start.9 = (bf16[2,256,256]{2,1,0:T(8,128)(2,1)S(1)}, bf16[2,256,256]{2,1,0:T(8,128)(2,1)S(1)}, u32[]{:S(2)}, u32[]{:S(2)}) collective-permute-start(bf16[2,256,256]{2,1,0:T(8,128)(2,1)S(1)} %collective-permute-done.8.refs_4_), channel_id=1, source_target_pairs={{8,0},{12,4},{16,8},{20,12},{24,16},{28,20},{9,1},{13,5},{17,9},{2... | collective-permute-start | bytes 786440 | tf_op jit(solution)/shard_map/ppermute | solution.py:45
  86.9 13.0 %collective-permute-start.6 = (bf16[2,256,256]{2,1,0:T(8,128)(2,1)S(1)}, bf16[2,256,256]{2,1,0:T(8,128)(2,1)S(1)}, u32[]{:S(2)}, u32[]{:S(2)}) collective-permute-start(bf16[2,256,256]{2,1,0:T(8,128)(2,1)S(1)} %collective-permute-done.5.refs_2_), channel_id=1, source_target_pairs={{0,8},{4,12},{8,16},{12,20},{16,24},{20,28},{1,9},{5,13},{9,17},{1... | collective-permute-start | bytes 786440 | tf_op jit(solution)/shard_map/ppermute | solution.py:44
  91.0 17.0 %collective-permute-start.14 = (bf16[2,256,256]{2,1,0:T(8,128)(2,1)S(1)}, bf16[2,256,256]{2,1,0:T(8,128)(2,1)}, u32[]{:S(2)}, u32[]{:S(2)}) collective-permute-start(bf16[2,256,256]{2,1,0:T(8,128)(2,1)S(1)} %get-tuple-element.13.refs_3_), channel_id=1, source_target_pairs={{0,4},{4,0},{8,12},{12,8},{16,20},{20,16},{24,28},{28,24},{1,5},{5... | collective-permute-start | bytes 786440 | tf_op jit(solution)/shard_map/ppermute | solution.py:41
  98.4 9.6 %collective-permute-start.15 = (bf16[2,256,256]{2,1,0:T(8,128)(2,1)S(1)}, bf16[2,256,256]{2,1,0:T(8,128)(2,1)}, u32[]{:S(2)}, u32[]{:S(2)}) collective-permute-start(bf16[2,256,256]{2,1,0:T(8,128)(2,1)S(1)} %collective-permute-done.8.refs_4_), channel_id=1, source_target_pairs={{0,4},{4,0},{8,12},{12,8},{16,20},{20,16},{24,28},{28,24},{1,5},{5... | collective-permute-start | bytes 786440 | tf_op jit(solution)/shard_map/ppermute | solution.py:47
  98.5 10.0 %collective-permute-start.10 = (bf16[2,256,256]{2,1,0:T(8,128)(2,1)S(1)}, bf16[2,256,256]{2,1,0:T(8,128)(2,1)}, u32[]{:S(2)}, u32[]{:S(2)}) collective-permute-start(bf16[2,256,256]{2,1,0:T(8,128)(2,1)S(1)} %collective-permute-done.9.refs_5_), channel_id=1, source_target_pairs={{8,0},{12,4},{16,8},{20,12},{24,16},{28,20},{9,1},{13,5},{17,9},{2... | collective-permute-start | bytes 786440 | tf_op jit(solution)/shard_map/ppermute | solution.py:45
  99.8 9.4 %collective-permute-start.7 = (bf16[2,256,256]{2,1,0:T(8,128)(2,1)S(1)}, bf16[2,256,256]{2,1,0:T(8,128)(2,1)}, u32[]{:S(2)}, u32[]{:S(2)}) collective-permute-start(bf16[2,256,256]{2,1,0:T(8,128)(2,1)S(1)} %collective-permute-done.6.refs_1_), channel_id=1, source_target_pairs={{0,8},{4,12},{8,16},{12,20},{16,24},{20,28},{1,9},{5,13},{9,17},{1... | collective-permute-start | bytes 786440 | tf_op jit(solution)/shard_map/ppermute | solution.py:44
  105.2 6.2 %collective-permute-start.13 = (bf16[2,256,256]{2,1,0:T(8,128)(2,1)S(1)}, bf16[2,256,256]{2,1,0:T(8,128)(2,1)S(1)}, u32[]{:S(2)}, u32[]{:S(2)}) collective-permute-start(bf16[2,256,256]{2,1,0:T(8,128)(2,1)S(1)} %collective-permute-done.5.refs_2_), channel_id=1, source_target_pairs={{0,4},{4,0},{8,12},{12,8},{16,20},{20,16},{24,28},{28,24},{1,5},{5... | collective-permute-start | bytes 786440 | tf_op jit(solution)/shard_map/ppermute | solution.py:46
  108.0 3.4 %collective-permute-start.16 = (bf16[2,256,256]{2,1,0:T(8,128)(2,1)S(1)}, bf16[2,256,256]{2,1,0:T(8,128)(2,1)S(1)}, u32[]{:S(2)}, u32[]{:S(2)}) collective-permute-start(bf16[2,256,256]{2,1,0:T(8,128)(2,1)S(1)} %collective-permute-done.9.refs_5_), channel_id=1, source_target_pairs={{0,4},{4,0},{8,12},{12,8},{16,20},{20,16},{24,28},{28,24},{1,5},{5... | collective-permute-start | bytes 786440 | tf_op jit(solution)/shard_map/ppermute | solution.py:47
  108.0 3.5 %collective-permute-start.12 = (bf16[2,256,256]{2,1,0:T(8,128)(2,1)S(1)}, bf16[2,256,256]{2,1,0:T(8,128)(2,1)S(1)}, u32[]{:S(2)}, u32[]{:S(2)}) collective-permute-start(bf16[2,256,256]{2,1,0:T(8,128)(2,1)S(1)} %collective-permute-done.6.refs_1_), channel_id=1, source_target_pairs={{0,4},{4,0},{8,12},{12,8},{16,20},{20,16},{24,28},{28,24},{1,5},{5... | collective-permute-start | bytes 786440 | tf_op jit(solution)/shard_map/ppermute | solution.py:46
  108.5 3.6 %collective-permute-start.17 = (bf16[2,256,256]{2,1,0:T(8,128)(2,1)}, bf16[2,256,256]{2,1,0:T(8,128)(2,1)S(1)}, u32[]{:S(2)}, u32[]{:S(2)}) collective-permute-start(bf16[2,256,256]{2,1,0:T(8,128)(2,1)} %collective-permute-done.10.refs_6_), channel_id=1, source_target_pairs={{0,4},{4,0},{8,12},{12,8},{16,20},{20,16},{24,28},{28,24},{1,5},{5... | collective-permute-start | bytes 786440 | tf_op jit(solution)/shard_map/ppermute | solution.py:47
  109.2 4.3 %collective-permute-start.11 = (bf16[2,256,256]{2,1,0:T(8,128)(2,1)}, bf16[2,256,256]{2,1,0:T(8,128)(2,1)}, u32[]{:S(2)}, u32[]{:S(2)}) collective-permute-start(bf16[2,256,256]{2,1,0:T(8,128)(2,1)} %collective-permute-done.7.refs_0_), channel_id=1, source_target_pairs={{0,4},{4,0},{8,12},{12,8},{16,20},{20,16},{24,28},{28,24},{1,5},{5... | collective-permute-start | bytes 786440 | tf_op jit(solution)/shard_map/ppermute | solution.py:46
  (13 other events, 127.5 us)

commit v16 on v8

--- a/solution.py
+++ b/solution.py
@@ -36,15 +36,18 @@
     from_right = [None] * chips
     from_left[0] = mine
     from_right[0] = mine
-    near_left = [None] * chips
-    near_right = [None] * chips
-    near_left[0] = lax.ppermute(mine, "dp", partner)
-    near_right[0] = near_left[0]
     for step in range(1, chips):
         from_left[step] = lax.ppermute(from_left[step - 1], "dp", rightward)
         from_right[step] = lax.ppermute(from_right[step - 1], "dp", leftward)
-        near_left[step] = lax.ppermute(from_left[step], "dp", partner)
-        near_right[step] = lax.ppermute(from_right[step], "dp", partner)
+    near_left = [None] * chips
+    near_right = [None] * chips
+    for step in range(chips):
+        later = min(step + 1, chips - 1)
+        left, right, _, _ = lax.optimization_barrier(
+            (from_left[step], from_right[step], from_left[later], from_right[later])
+        )
+        near_left[step] = lax.ppermute(left, "dp", partner)
+        near_right[step] = lax.ppermute(right, "dp", partner) if step else near_left[0]
     pieces = from_left[::-1] + from_right[1:] + near_left[::-1] + near_right[1:]
     chip, core = replica // 2, replica % 2
     owner_chip, owner_core = owner_of // 2, owner_of % 2

time: 117 us -> 121 us (1.034)
  starting transfers between devices: 34.6 us -> 38.6 us
    ppermute x7, starting transfers between devices: 10.7 us -> 14.9 us  [the longest x4 13.7 us: gather_blocks(): near_left[step] = lax.ppermute(left, 'dp', partner)]
  transfers between devices with their start and end apart: 19 -> 19, of which waited for: 7 -> 8; matrix products, arithmetic and copies ran while one was open for 7% -> 7% of each run, Pallas kernels for 0% -> 0%
where the time goes in v16:
time: 121 us; the launch traced here: 120 us
  waiting for transfers between devices  58.8 us (49%)
  starting transfers between devices  38.6 us (32%)
  matrix products  7.28 us (6%)
  other arithmetic  7.11 us (6%)
  local copies, waits for them, and re-layouts  4.05 us (3%)
  Pallas kernels  3.15 us (3%)
    all_to_all x1, waiting for transfers between devices, local(): received = lax.all_to_all(by_owner, 'dp', 0, 0, tiled=True)  47.4 us
    ppermute x4, starting transfers between devices, gather_blocks(): near_left[step] = lax.ppermute(left, 'dp', partner)  13.7 us
    ppermute x3, starting transfers between devices, gather_blocks(): from_left[step] = lax.ppermute(from_left[step - 1], 'dp', rightward)  9.73 us
    ppermute x5, waiting for transfers between devices, butterfly_sum(): x = x + lax.ppermute(x, axis, [(i, i ^ step) for i in range(size)])  8.91 us
    all_to_all x1, starting transfers between devices, local(): received = lax.all_to_all(by_owner, 'dp', 0, 0, tiled=True)  6.51 us
    ppermute x3, starting transfers between devices, gather_blocks(): from_right[step] = lax.ppermute(from_right[step - 1], 'dp', leftward)  3.86 us
    ppermute x5, starting transfers between devices, butterfly_sum(): x = x + lax.ppermute(x, axis, [(i, i ^ step) for i in range(size)])  3.53 us
    pallas_call x1, Pallas kernels, pick_blocks(): pl.pallas_call(pick_kernel, out_shape=jax.ShapeDtypeStruct((blocks,) + pi...  3.15 us
  transfers between devices with their start and end apart: 19, of which 8 were waited for; matrix products, arithmetic and copies ran while one was open for 7% of the time, Pallas kernels for 0%

profile of v16, /device:TPU:1, one launch (start us, length us, event | category | flops | bytes accessed | tf_op | source)
XLA Modules:
  0.0 120.0 jit_solution(6650267508661509816)
XLA Ops:
  2.6 2.0 %gather_fusion = bf16[16,256,256]{2,1,0:T(8,128)(2,1)} fusion(bf16[8,256,256]{2,1,0:T(8,128)(2,1)S(1)} %bitcast.52, s32[1024]{0:T(1024)S(1)} %pad_clamp_fusion), kind=kCustom, calls=%fused_computation | custom fusion | bytes 4194368 | tf_op jit(solution)/shard_map/jit(_take)/gather | solution.py:123
  4.6 6.5 %all-to-all-start = ((bf16[8,2,256,256]{3,2,1,0:T(8,128)(2,1)}), bf16[8,2,256,256]{3,2,1,0:T(8,128)(2,1)}, u32[]{:S(2)}, u32[]{:S(2)}) async-start(bf16[8,2,256,256]{3,2,1,0:T(8,128)(2,1)} %bitcast.3), calls=%async_computation | async-start | bytes 4194304 | tf_op jit(solution)/shard_map/all_to_all | solution.py:126
  12.0 47.4 %all-to-all-done = bf16[8,2,256,256]{3,2,1,0:T(8,128)(2,1)} async-done(((bf16[8,2,256,256]{3,2,1,0:T(8,128)(2,1)}), bf16[8,2,256,256]{3,2,1,0:T(8,128)(2,1)}, u32[]{:S(2)}, u32[]{:S(2)}) %all-to-all-start) | async-done | bytes 2097184 | tf_op jit(solution)/shard_map/all_to_all | solution.py:126
  59.4 1.9 %convert_reduce_fusion = f32[2,256,256]{2,1,0:T(8,128)S(1)} fusion(bf16[8,2,256,256]{3,2,1,0:T(8,128)(2,1)} %all-to-all-done), kind=kLoop, calls=%fused_computation.1 | loop fusion | flops 1966080 | bytes 2621440 | tf_op jit(solution)/shard_map/reduce_sum | solution.py:127
  61.8 1.6 %multiply_reduce_fusion = (f32[2]{0:T(128)S(1)}, f32[2,256,256]{2,1,0:T(8,128)S(1)}) fusion(bf16[1,1,2,256,256]{4,3,2,1,0:T(8,128)(2,1)S(1)} %copy-done.4, f32[2,256,256]{2,1,0:T(8,128)S(1)} %convert_reduce_fusion, bf16[1,1,2,256,256]{4,3,2,1,0:T(8,128)(2,1)} %param.14, f32[2]{0:T(128)S(1)} %convert_element_type.35), kind=kOutput, calls=%fused_computation.25 | convolution fusion | flops 134873088 | bytes 1572880 | tf_op jit(solution)/shard_map/sij,sjk->sik/dot_general | solution.py:152
  65.4 2.4 %collective-permute-done.1 = f32[2,9]{1,0:T(2,128)S(1)} collective-permute-done((f32[2,9]{1,0:T(2,128)S(1)}, f32[2,9]{1,0:T(2,128)S(1)}, u32[]{:S(2)}, u32[]{:S(2)}) %collective-permute-start.1) | collective-permute-done | bytes 104 | tf_op jit(solution)/shard_map/ppermute | solution.py:20
  67.9 3.3 %collective-permute-done.2 = f32[2,9]{1,0:T(2,128)S(1)} collective-permute-done((f32[2,9]{1,0:T(2,128)S(1)}, f32[2,9]{1,0:T(2,128)S(1)}, u32[]{:S(2)}, u32[]{:S(2)}) %collective-permute-start.2) | collective-permute-done | bytes 104 | tf_op jit(solution)/shard_map/ppermute | solution.py:20
  71.2 1.2 %collective-permute-start.3 = (f32[2,9]{1,0:T(2,128)S(1)}, f32[2,9]{1,0:T(2,128)S(1)}, u32[]{:S(2)}, u32[]{:S(2)}) collective-permute-start(f32[2,9]{1,0:T(2,128)S(1)} %add.92), channel_id=1, source_target_pairs={{0,1},{1,0},{2,3},{3,2},{4,5},{5,4},{6,7},{7,6},{8,9},{9,8},{10,11... | collective-permute-start | bytes 224 | tf_op jit(solution)/shard_map/ppermute | solution.py:20
  72.4 1.2 %collective-permute-done.3 = f32[2,9]{1,0:T(2,128)S(1)} collective-permute-done((f32[2,9]{1,0:T(2,128)S(1)}, f32[2,9]{1,0:T(2,128)S(1)}, u32[]{:S(2)}, u32[]{:S(2)}) %collective-permute-start.3) | collective-permute-done | bytes 104 | tf_op jit(solution)/shard_map/ppermute | solution.py:20
  73.6 1.2 %collective-permute-start.4 = (f32[2,9]{1,0:T(2,128)S(1)}, f32[2,9]{1,0:T(2,128)S(1)}, u32[]{:S(2)}, u32[]{:S(2)}) collective-permute-start(f32[2,9]{1,0:T(2,128)S(1)} %add.93), channel_id=1, source_target_pairs={{0,2},{1,3},{2,0},{3,1},{4,6},{5,7},{6,4},{7,5},{8,10},{9,11},{10,... | collective-permute-start | bytes 224 | tf_op jit(solution)/shard_map/ppermute | solution.py:20
  74.9 1.2 collective-permute-done.4
  77.2 1.9 %collective-permute-start.5 = (bf16[2,256,256]{2,1,0:T(8,128)(2,1)S(1)}, bf16[2,256,256]{2,1,0:T(8,128)(2,1)S(1)}, u32[]{:S(2)}, u32[]{:S(2)}) collective-permute-start(bf16[2,256,256]{2,1,0:T(8,128)(2,1)S(1)} %get-tuple-element.15.refs_3_), channel_id=1, source_target_pairs={{0,8},{4,12},{8,16},{12,20},{16,24},{20,28},{1,9},{5,13},{9,17},{1... | collective-permute-start | bytes 786440 | tf_op jit(solution)/shard_map/ppermute | solution.py:40
  79.1 1.3 %collective-permute-start.8 = (bf16[2,256,256]{2,1,0:T(8,128)(2,1)S(1)}, bf16[2,256,256]{2,1,0:T(8,128)(2,1)S(1)}, u32[]{:S(2)}, u32[]{:S(2)}) collective-permute-start(bf16[2,256,256]{2,1,0:T(8,128)(2,1)S(1)} %get-tuple-element.15.refs_3_), channel_id=1, source_target_pairs={{8,0},{12,4},{16,8},{20,12},{24,16},{28,20},{9,1},{13,5},{17,9},{2... | collective-permute-start | bytes 786440 | tf_op jit(solution)/shard_map/ppermute | solution.py:41
  80.5 2.0 %collective-permute-done.5.refs_2_ = bf16[2,256,256]{2,1,0:T(8,128)(2,1)S(1)} collective-permute-done((bf16[2,256,256]{2,1,0:T(8,128)(2,1)S(1)}, bf16[2,256,256]{2,1,0:T(8,128)(2,1)S(1)}, u32[]{:S(2)}, u32[]{:S(2)}) %collective-permute-start.5) | collective-permute-done | bytes 262176 | tf_op jit(solution)/shard_map/ppermute | solution.py:40
  82.4 3.8 %collective-permute-start.6 = (bf16[2,256,256]{2,1,0:T(8,128)(2,1)S(1)}, bf16[2,256,256]{2,1,0:T(8,128)(2,1)S(1)}, u32[]{:S(2)}, u32[]{:S(2)}) collective-permute-start(bf16[2,256,256]{2,1,0:T(8,128)(2,1)S(1)} %collective-permute-done.5.refs_2_), channel_id=1, source_target_pairs={{0,8},{4,12},{8,16},{12,20},{16,24},{20,28},{1,9},{5,13},{9,17},{1... | collective-permute-start | bytes 786440 | tf_op jit(solution)/shard_map/ppermute | solution.py:40
  86.3 1.3 %collective-permute-start.9 = (bf16[2,256,256]{2,1,0:T(8,128)(2,1)S(1)}, bf16[2,256,256]{2,1,0:T(8,128)(2,1)S(1)}, u32[]{:S(2)}, u32[]{:S(2)}) collective-permute-start(bf16[2,256,256]{2,1,0:T(8,128)(2,1)S(1)} %collective-permute-done.8.refs_4_), channel_id=1, source_target_pairs={{8,0},{12,4},{16,8},{20,12},{24,16},{28,20},{9,1},{13,5},{17,9},{2... | collective-permute-start | bytes 786440 | tf_op jit(solution)/shard_map/ppermute | solution.py:41
  88.3 7.1 %collective-permute-start.14 = (bf16[2,256,256]{2,1,0:T(8,128)(2,1)S(1)}, bf16[2,256,256]{2,1,0:T(8,128)(2,1)S(1)}, u32[]{:S(2)}, u32[]{:S(2)}) collective-permute-start(bf16[2,256,256]{2,1,0:T(8,128)(2,1)S(1)} %get-tuple-element.15.refs_3_), channel_id=1, source_target_pairs={{0,4},{4,0},{8,12},{12,8},{16,20},{20,16},{24,28},{28,24},{1,5},{5... | collective-permute-start | bytes 786440 | tf_op jit(solution)/shard_map/ppermute | solution.py:49
  95.3 6.2 %collective-permute-start.13 = (bf16[2,256,256]{2,1,0:T(8,128)(2,1)S(1)}, bf16[2,256,256]{2,1,0:T(8,128)(2,1)S(1)}, u32[]{:S(2)}, u32[]{:S(2)}) collective-permute-start(bf16[2,256,256]{2,1,0:T(8,128)(2,1)S(1)} %collective-permute-done.5.refs_2_), channel_id=1, source_target_pairs={{0,4},{4,0},{8,12},{12,8},{16,20},{20,16},{24,28},{28,24},{1,5},{5... | collective-permute-start | bytes 786440 | tf_op jit(solution)/shard_map/ppermute | solution.py:49
  101.6 1.3 %collective-permute-start.10 = (bf16[2,256,256]{2,1,0:T(8,128)(2,1)S(1)}, bf16[2,256,256]{2,1,0:T(8,128)(2,1)S(1)}, u32[]{:S(2)}, u32[]{:S(2)}) collective-permute-start(bf16[2,256,256]{2,1,0:T(8,128)(2,1)S(1)} %collective-permute-done.9.refs_5_), channel_id=1, source_target_pairs={{8,0},{12,4},{16,8},{20,12},{24,16},{28,20},{9,1},{13,5},{17,9},{2... | collective-permute-start | bytes 786440 | tf_op jit(solution)/shard_map/ppermute | solution.py:41
  102.9 4.0 %collective-permute-start.7 = (bf16[2,256,256]{2,1,0:T(8,128)(2,1)S(1)}, bf16[2,256,256]{2,1,0:T(8,128)(2,1)S(1)}, u32[]{:S(2)}, u32[]{:S(2)}) collective-permute-start(bf16[2,256,256]{2,1,0:T(8,128)(2,1)S(1)} %collective-permute-done.6.refs_1_), channel_id=1, source_target_pairs={{0,8},{4,12},{8,16},{12,20},{16,24},{20,28},{1,9},{5,13},{9,17},{1... | collective-permute-start | bytes 786440 | tf_op jit(solution)/shard_map/ppermute | solution.py:40
  106.9 3.0 %fusion.2 = f32[1,1,2,256,256]{4,3,2,1,0:T(8,128)} fusion(f32[1,1,2,256,256]{4,3,2,1,0:T(8,128)} %param.13, f32[2,256,256]{2,1,0:T(8,128)S(1)} %convert_reduce_fusion, f32[2]{0:T(128)S(1)} %convert_element_type.35, pred[2]{0:T(512)(128)(4,1)S(1)} %dynamic-slice_reduce_fusion), kind=kOutput, calls=%fused_computation.5 | convolution fusion | flops 403308544 | bytes 1572874 | tf_op jit(solution)/shard_map/sji,sjk->sik/dot_general | solution.py:145
  109.9 2.7 %fusion.5 = f32[1,1,2,256,256]{4,3,2,1,0:T(8,128)} fusion(f32[1,1,2,256,256]{4,3,2,1,0:T(8,128)} %param.12, f32[2,256,256]{2,1,0:T(8,128)S(1)} %convert_reduce_fusion, f32[2]{0:T(128)S(1)} %convert_element_type.35, pred[2]{0:T(512)(128)(4,1)S(1)} %dynamic-slice_reduce_fusion), kind=kOutput, calls=%fused_computation.9 | convolution fusion | flops 403308544 | bytes 1572874 | tf_op jit(solution)/shard_map/sij,skj->sik/dot_general | solution.py:142
  114.2 1.0 fusion.8
  116.8 3.2 %shard_map.128 = bf16[8,256,256]{2,1,0:T(8,128)(2,1)} custom-call(s32[8,2]{1,0:T(8,128)} %copy.39.table_ref, bf16[2,256,256]{2,1,0:T(8,128)(2,1)} %copy-done.12, bf16[2,256,256]{2,1,0:T(8,128)(2,1)} %copy-done.7, bf16[2,256,256]{2,1,0:T(8,128)(2,1)} %copy-done.5, bf16[2,256,256]{2,1,0:T(8,128)(2,1)} %copy-done.2, bf16[2,256,256]{2,1,0:T(8,128)(2,1)} %copy-done.6, ...), custom_call_target="tpu_custom_call" | custom-call | tf_op jit(solution)/shard_map/pallas_call | solution.py:82
  (88 shorter events, 10.4 us)
Async XLA Ops:
  4.6 54.8 %all-to-all-start = ((bf16[8,2,256,256]{3,2,1,0:T(8,128)(2,1)}), bf16[8,2,256,256]{3,2,1,0:T(8,128)(2,1)}, u32[]{:S(2)}, u32[]{:S(2)}) async-start(bf16[8,2,256,256]{3,2,1,0:T(8,128)(2,1)} %bitcast.3), calls=%async_computation | async-start | bytes 4194304 | tf_op jit(solution)/shard_map/all_to_all | solution.py:126
  11.1 50.2 %copy-start.1 = (f32[1,1,2,256,256]{4,3,2,1,0:T(8,128)S(1)}, f32[1,1,2,256,256]{4,3,2,1,0:T(8,128)}, u32[]{:S(2)}) copy-start(f32[1,1,2,256,256]{4,3,2,1,0:T(8,128)} %param.16) | copy-start | bytes 1572868
  11.1 50.7 %copy-start.4 = (bf16[1,1,2,256,256]{4,3,2,1,0:T(8,128)(2,1)S(1)}, bf16[1,1,2,256,256]{4,3,2,1,0:T(8,128)(2,1)}, u32[]{:S(2)}) copy-start(bf16[1,1,2,256,256]{4,3,2,1,0:T(8,128)(2,1)} %param.15) | copy-start | bytes 786436
  12.0 64.2 %copy-start.3 = (f32[1,1,2,256,256]{4,3,2,1,0:T(8,128)S(1)}, f32[1,1,2,256,256]{4,3,2,1,0:T(8,128)}, u32[]{:S(2)}) copy-start(f32[1,1,2,256,256]{4,3,2,1,0:T(8,128)} %param.17) | copy-start | bytes 1572868
  63.5 1.8 %collective-permute-start = (f32[2,9]{1,0:T(2,128)S(1)}, f32[2,9]{1,0:T(2,128)S(1)}, u32[]{:S(2)}, u32[]{:S(2)}) collective-permute-start(f32[2,9]{1,0:T(2,128)S(1)} %pad_maximum_fusion), channel_id=1, source_target_pairs={{0,4},{4,0},{8,12},{12,8},{16,20},{20,16},{24,28},{28,24},{1,5},{5... | collective-permute-start | bytes 224 | tf_op jit(solution)/shard_map/ppermute | solution.py:20
  65.3 2.5 %collective-permute-start.1 = (f32[2,9]{1,0:T(2,128)S(1)}, f32[2,9]{1,0:T(2,128)S(1)}, u32[]{:S(2)}, u32[]{:S(2)}) collective-permute-start(f32[2,9]{1,0:T(2,128)S(1)} %fusion.30), channel_id=1, source_target_pairs={{0,8},{4,12},{8,0},{12,4},{16,24},{20,28},{24,16},{28,20},{1,9},{5... | collective-permute-start | bytes 224 | tf_op jit(solution)/shard_map/ppermute | solution.py:20
  67.8 3.4 %collective-permute-start.2 = (f32[2,9]{1,0:T(2,128)S(1)}, f32[2,9]{1,0:T(2,128)S(1)}, u32[]{:S(2)}, u32[]{:S(2)}) collective-permute-start(f32[2,9]{1,0:T(2,128)S(1)} %fusion.35), channel_id=1, source_target_pairs={{0,16},{4,20},{8,24},{12,28},{16,0},{20,4},{24,8},{28,12},{1,17},{... | collective-permute-start | bytes 224 | tf_op jit(solution)/shard_map/ppermute | solution.py:20
  71.2 2.4 %collective-permute-start.3 = (f32[2,9]{1,0:T(2,128)S(1)}, f32[2,9]{1,0:T(2,128)S(1)}, u32[]{:S(2)}, u32[]{:S(2)}) collective-permute-start(f32[2,9]{1,0:T(2,128)S(1)} %add.92), channel_id=1, source_target_pairs={{0,1},{1,0},{2,3},{3,2},{4,5},{5,4},{6,7},{7,6},{8,9},{9,8},{10,11... | collective-permute-start | bytes 224 | tf_op jit(solution)/shard_map/ppermute | solution.py:20
  73.6 2.4 %collective-permute-start.4 = (f32[2,9]{1,0:T(2,128)S(1)}, f32[2,9]{1,0:T(2,128)S(1)}, u32[]{:S(2)}, u32[]{:S(2)}) collective-permute-start(f32[2,9]{1,0:T(2,128)S(1)} %add.93), channel_id=1, source_target_pairs={{0,2},{1,3},{2,0},{3,1},{4,6},{5,7},{6,4},{7,5},{8,10},{9,11},{10,... | collective-permute-start | bytes 224 | tf_op jit(solution)/shard_map/ppermute | solution.py:20
  77.2 38.0 %copy-start.2 = (bf16[2,256,256]{2,1,0:T(8,128)(2,1)}, bf16[2,256,256]{2,1,0:T(8,128)(2,1)S(1)}, u32[]{:S(2)}) copy-start(bf16[2,256,256]{2,1,0:T(8,128)(2,1)S(1)} %get-tuple-element.15.refs_3_) | copy-start | bytes 786436
  77.2 5.2 %collective-permute-start.5 = (bf16[2,256,256]{2,1,0:T(8,128)(2,1)S(1)}, bf16[2,256,256]{2,1,0:T(8,128)(2,1)S(1)}, u32[]{:S(2)}, u32[]{:S(2)}) collective-permute-start(bf16[2,256,256]{2,1,0:T(8,128)(2,1)S(1)} %get-tuple-element.15.refs_3_), channel_id=1, source_target_pairs={{0,8},{4,12},{8,16},{12,20},{16,24},{20,28},{1,9},{5,13},{9,17},{1... | collective-permute-start | bytes 786440 | tf_op jit(solution)/shard_map/ppermute | solution.py:40
  79.1 7.1 %collective-permute-start.8 = (bf16[2,256,256]{2,1,0:T(8,128)(2,1)S(1)}, bf16[2,256,256]{2,1,0:T(8,128)(2,1)S(1)}, u32[]{:S(2)}, u32[]{:S(2)}) collective-permute-start(bf16[2,256,256]{2,1,0:T(8,128)(2,1)S(1)} %get-tuple-element.15.refs_3_), channel_id=1, source_target_pairs={{8,0},{12,4},{16,8},{20,12},{24,16},{28,20},{9,1},{13,5},{17,9},{2... | collective-permute-start | bytes 786440 | tf_op jit(solution)/shard_map/ppermute | solution.py:41
  82.4 32.8 %copy-start.5 = (bf16[2,256,256]{2,1,0:T(8,128)(2,1)}, bf16[2,256,256]{2,1,0:T(8,128)(2,1)S(1)}, u32[]{:S(2)}) copy-start(bf16[2,256,256]{2,1,0:T(8,128)(2,1)S(1)} %collective-permute-done.5.refs_2_) | copy-start | bytes 786436
  82.4 12.9 %collective-permute-start.6 = (bf16[2,256,256]{2,1,0:T(8,128)(2,1)S(1)}, bf16[2,256,256]{2,1,0:T(8,128)(2,1)S(1)}, u32[]{:S(2)}, u32[]{:S(2)}) collective-permute-start(bf16[2,256,256]{2,1,0:T(8,128)(2,1)S(1)} %collective-permute-done.5.refs_2_), channel_id=1, source_target_pairs={{0,8},{4,12},{8,16},{12,20},{16,24},{20,28},{1,9},{5,13},{9,17},{1... | collective-permute-start | bytes 786440 | tf_op jit(solution)/shard_map/ppermute | solution.py:40
  86.3 9.1 %collective-permute-start.9 = (bf16[2,256,256]{2,1,0:T(8,128)(2,1)S(1)}, bf16[2,256,256]{2,1,0:T(8,128)(2,1)S(1)}, u32[]{:S(2)}, u32[]{:S(2)}) collective-permute-start(bf16[2,256,256]{2,1,0:T(8,128)(2,1)S(1)} %collective-permute-done.8.refs_4_), channel_id=1, source_target_pairs={{8,0},{12,4},{16,8},{20,12},{24,16},{28,20},{9,1},{13,5},{17,9},{2... | collective-permute-start | bytes 786440 | tf_op jit(solution)/shard_map/ppermute | solution.py:41
  88.3 25.4 %collective-permute-start.14 = (bf16[2,256,256]{2,1,0:T(8,128)(2,1)S(1)}, bf16[2,256,256]{2,1,0:T(8,128)(2,1)S(1)}, u32[]{:S(2)}, u32[]{:S(2)}) collective-permute-start(bf16[2,256,256]{2,1,0:T(8,128)(2,1)S(1)} %get-tuple-element.15.refs_3_), channel_id=1, source_target_pairs={{0,4},{4,0},{8,12},{12,8},{16,20},{20,16},{24,28},{28,24},{1,5},{5... | collective-permute-start | bytes 786440 | tf_op jit(solution)/shard_map/ppermute | solution.py:49
  95.3 18.5 %collective-permute-start.13 = (bf16[2,256,256]{2,1,0:T(8,128)(2,1)S(1)}, bf16[2,256,256]{2,1,0:T(8,128)(2,1)S(1)}, u32[]{:S(2)}, u32[]{:S(2)}) collective-permute-start(bf16[2,256,256]{2,1,0:T(8,128)(2,1)S(1)} %collective-permute-done.5.refs_2_), channel_id=1, source_target_pairs={{0,4},{4,0},{8,12},{12,8},{16,20},{20,16},{24,28},{28,24},{1,5},{5... | collective-permute-start | bytes 786440 | tf_op jit(solution)/shard_map/ppermute | solution.py:49
  101.6 11.5 %collective-permute-start.10 = (bf16[2,256,256]{2,1,0:T(8,128)(2,1)S(1)}, bf16[2,256,256]{2,1,0:T(8,128)(2,1)S(1)}, u32[]{:S(2)}, u32[]{:S(2)}) collective-permute-start(bf16[2,256,256]{2,1,0:T(8,128)(2,1)S(1)} %collective-permute-done.9.refs_5_), channel_id=1, source_target_pairs={{8,0},{12,4},{16,8},{20,12},{24,16},{28,20},{9,1},{13,5},{17,9},{2... | collective-permute-start | bytes 786440 | tf_op jit(solution)/shard_map/ppermute | solution.py:41
  102.9 10.2 %collective-permute-start.7 = (bf16[2,256,256]{2,1,0:T(8,128)(2,1)S(1)}, bf16[2,256,256]{2,1,0:T(8,128)(2,1)S(1)}, u32[]{:S(2)}, u32[]{:S(2)}) collective-permute-start(bf16[2,256,256]{2,1,0:T(8,128)(2,1)S(1)} %collective-permute-done.6.refs_1_), channel_id=1, source_target_pairs={{0,8},{4,12},{8,16},{12,20},{16,24},{20,28},{1,9},{5,13},{9,17},{1... | collective-permute-start | bytes 786440 | tf_op jit(solution)/shard_map/ppermute | solution.py:40
  112.5 2.7 %collective-permute-start.15 = (bf16[2,256,256]{2,1,0:T(8,128)(2,1)S(1)}, bf16[2,256,256]{2,1,0:T(8,128)(2,1)S(1)}, u32[]{:S(2)}, u32[]{:S(2)}) collective-permute-start(bf16[2,256,256]{2,1,0:T(8,128)(2,1)S(1)} %collective-permute-done.8.refs_4_), channel_id=1, source_target_pairs={{0,4},{4,0},{8,12},{12,8},{16,20},{20,16},{24,28},{28,24},{1,5},{5... | collective-permute-start | bytes 786440 | tf_op jit(solution)/shard_map/ppermute | solution.py:50
  113.1 2.1 %collective-permute-start.12 = (bf16[2,256,256]{2,1,0:T(8,128)(2,1)S(1)}, bf16[2,256,256]{2,1,0:T(8,128)(2,1)S(1)}, u32[]{:S(2)}, u32[]{:S(2)}) collective-permute-start(bf16[2,256,256]{2,1,0:T(8,128)(2,1)S(1)} %collective-permute-done.6.refs_1_), channel_id=1, source_target_pairs={{0,4},{4,0},{8,12},{12,8},{16,20},{20,16},{24,28},{28,24},{1,5},{5... | collective-permute-start | bytes 786440 | tf_op jit(solution)/shard_map/ppermute | solution.py:49
  113.4 1.9 %collective-permute-start.16 = (bf16[2,256,256]{2,1,0:T(8,128)(2,1)S(1)}, bf16[2,256,256]{2,1,0:T(8,128)(2,1)S(1)}, u32[]{:S(2)}, u32[]{:S(2)}) collective-permute-start(bf16[2,256,256]{2,1,0:T(8,128)(2,1)S(1)} %collective-permute-done.9.refs_5_), channel_id=1, source_target_pairs={{0,4},{4,0},{8,12},{12,8},{16,20},{20,16},{24,28},{28,24},{1,5},{5... | collective-permute-start | bytes 786440 | tf_op jit(solution)/shard_map/ppermute | solution.py:50
  113.7 2.1 %collective-permute-start.11 = (bf16[2,256,256]{2,1,0:T(8,128)(2,1)S(1)}, bf16[2,256,256]{2,1,0:T(8,128)(2,1)S(1)}, u32[]{:S(2)}, u32[]{:S(2)}) collective-permute-start(bf16[2,256,256]{2,1,0:T(8,128)(2,1)S(1)} %collective-permute-done.7.refs_0_), channel_id=1, source_target_pairs={{0,4},{4,0},{8,12},{12,8},{16,20},{20,16},{24,28},{28,24},{1,5},{5... | collective-permute-start | bytes 786440 | tf_op jit(solution)/shard_map/ppermute | solution.py:49
  113.9 2.9 %collective-permute-start.17 = (bf16[2,256,256]{2,1,0:T(8,128)(2,1)S(1)}, bf16[2,256,256]{2,1,0:T(8,128)(2,1)}, u32[]{:S(2)}, u32[]{:S(2)}) collective-permute-start(bf16[2,256,256]{2,1,0:T(8,128)(2,1)S(1)} %collective-permute-done.10.refs_6_), channel_id=1, source_target_pairs={{0,4},{4,0},{8,12},{12,8},{16,20},{20,16},{24,28},{28,24},{1,5},{5... | collective-permute-start | bytes 786440 | tf_op jit(solution)/shard_map/ppermute | solution.py:50
  (14 other events, 115.8 us)

commit v17 on v10

--- a/solution.py
+++ b/solution.py
@@ -29,21 +29,23 @@
         gathered = lax.all_gather(mine, "dp", axis=0, tiled=True)
         return jnp.take(gathered, owner_of * slot_count + slot_rank, axis=0)
     chips = size // 2
-    rightward = [(i, i + 2) for i in range(size - 2)]
-    leftward = [(i + 2, i) for i in range(size - 2)]
-    from_left = [mine]
-    from_right = [mine]
+    partner = [(i, i ^ 1) for i in range(size)]
+    line = [(i, i + 2 - 4 * (i % 2)) for i in range(size) if 0 <= i + 2 - 4 * (i % 2) < size]
+    chain = [jnp.concatenate([mine, lax.ppermute(mine, "dp", partner)])]
     for step in range(1, chips):
-        from_left.append(lax.ppermute(from_left[-1], "dp", rightward))
-        from_right.append(lax.ppermute(from_right[-1], "dp", leftward))
-    pieces = from_left[::-1] + from_right[1:]
+        chain.append(lax.ppermute(chain[-1], "dp", line))
+    beside = [lax.ppermute(piece, "dp", partner) for piece in chain[1:]]
+    pieces = chain + beside
     chip, core = replica // 2, replica % 2
     owner_chip, owner_core = owner_of // 2, owner_of % 2
-    source = jnp.clip(owner_chip - chip + chips - 1, 0, len(pieces) - 1)
-    table = jnp.stack([source, jnp.clip(slot_rank, 0, slot_count - 1)], axis=1).astype(jnp.int32)
-    line_blocks = pick_blocks(table, pieces)
-    other_blocks = lax.ppermute(line_blocks, "dp", [(i, i ^ 1) for i in range(size)])
-    return jnp.where((owner_core == core)[:, None, None], line_blocks, other_blocks)
+    ahead = owner_chip - chip
+    own_line = (ahead == 0) | ((core == 0) & (ahead < 0)) | ((core == 1) & (ahead > 0))
+    step = jnp.abs(ahead)
+    source = jnp.clip(jnp.where(own_line, step, chips - 1 + step), 0, len(pieces) - 1)
+    sender = jnp.where(own_line, core, 1 - core)
+    place = jnp.where(owner_core == sender, 0, slot_count) + slot_rank
+    table = jnp.stack([source, jnp.clip(place, 0, 2 * slot_count - 1)], axis=1).astype(jnp.int32)
+    return pick_blocks(table, pieces)
 
 
 def pick_kernel(table_ref, *refs):

time: 123 us -> 126 us (1.024)
  waiting for transfers between devices: 65.1 us -> 79.2 us
  starting transfers between devices: 34.9 us -> 24.2 us
  local copies, waits for them, and re-layouts: 3.05 us -> 4.64 us
    ppermute x7, waiting for transfers between devices: 8.83 us -> 22.9 us  [the longest x3 21.8 us: gather_blocks(): chain.append(lax.ppermute(chain[-1], 'dp', line))]
    ppermute x7, starting transfers between devices: 24.9 us -> 14.2 us  [the longest x3 5.44 us: gather_blocks(): beside = [lax.ppermute(piece, 'dp', partner) for piece in chain[1:]]]
    unnamed x24 -> x20, local copies, waits for them, and re-layouts: 0.05 us -> 1.65 us
  transfers between devices with their start and end apart: 13 -> 13, of which waited for: 12 -> 10; matrix products, arithmetic and copies ran while one was open for 7% -> 6% of each run, Pallas kernels for 0% -> 0%
where the time goes in v17:
time: 126 us; the launch traced here: 125 us
  waiting for transfers between devices  79.2 us (63%)
  starting transfers between devices  24.2 us (19%)
  other arithmetic  7.18 us (6%)
  matrix products  6.25 us (5%)
  local copies, waits for them, and re-layouts  4.64 us (4%)
  Pallas kernels  3.1 us (2%)
    all_to_all x1, waiting for transfers between devices, local(): received = lax.all_to_all(by_owner, 'dp', 0, 0, tiled=True)  47.4 us
    ppermute x3, waiting for transfers between devices, gather_blocks(): chain.append(lax.ppermute(chain[-1], 'dp', line))  21.8 us
    ppermute x5, waiting for transfers between devices, butterfly_sum(): x = x + lax.ppermute(x, axis, [(i, i ^ step) for i in range(size)])  8.92 us
    all_to_all x1, starting transfers between devices, local(): received = lax.all_to_all(by_owner, 'dp', 0, 0, tiled=True)  6.51 us
    ppermute x3, starting transfers between devices, gather_blocks(): beside = [lax.ppermute(piece, 'dp', partner) for piece in chain[1:]]  5.44 us
    ppermute x1, starting transfers between devices, gather_blocks(): chain = [jnp.concatenate([mine, lax.ppermute(mine, 'dp', partner)])]  4.92 us
    ppermute x3, starting transfers between devices, gather_blocks(): chain.append(lax.ppermute(chain[-1], 'dp', line))  3.85 us
    ppermute x5, starting transfers between devices, butterfly_sum(): x = x + lax.ppermute(x, axis, [(i, i ^ step) for i in range(size)])  3.52 us
  transfers between devices with their start and end apart: 13, of which 10 were waited for; matrix products, arithmetic and copies ran while one was open for 6% of the time, Pallas kernels for 0%

profile of v17, /device:TPU:1, one launch (start us, length us, event | category | flops | bytes accessed | tf_op | source)
XLA Modules:
  0.0 125.5 jit_solution(16875725991762732963)
XLA Ops:
  2.6 2.0 %gather_fusion = bf16[16,256,256]{2,1,0:T(8,128)(2,1)} fusion(bf16[8,256,256]{2,1,0:T(8,128)(2,1)S(1)} %bitcast.54, s32[1024]{0:T(1024)S(1)} %pad_clamp_fusion), kind=kCustom, calls=%fused_computation | custom fusion | bytes 4194368 | tf_op jit(solution)/shard_map/jit(_take)/gather | solution.py:113
  4.6 6.5 %all-to-all-start = ((bf16[8,2,256,256]{3,2,1,0:T(8,128)(2,1)}), bf16[8,2,256,256]{3,2,1,0:T(8,128)(2,1)}, u32[]{:S(2)}, u32[]{:S(2)}) async-start(bf16[8,2,256,256]{3,2,1,0:T(8,128)(2,1)} %bitcast.3), calls=%async_computation | async-start | bytes 4194304 | tf_op jit(solution)/shard_map/all_to_all | solution.py:116
  12.0 47.4 %all-to-all-done = bf16[8,2,256,256]{3,2,1,0:T(8,128)(2,1)} async-done(((bf16[8,2,256,256]{3,2,1,0:T(8,128)(2,1)}), bf16[8,2,256,256]{3,2,1,0:T(8,128)(2,1)}, u32[]{:S(2)}, u32[]{:S(2)}) %all-to-all-start) | async-done | bytes 2097184 | tf_op jit(solution)/shard_map/all_to_all | solution.py:116
  59.4 1.9 %convert_reduce_fusion = f32[2,256,256]{2,1,0:T(8,128)S(1)} fusion(bf16[8,2,256,256]{3,2,1,0:T(8,128)(2,1)} %all-to-all-done), kind=kLoop, calls=%fused_computation.1 | loop fusion | flops 1966080 | bytes 2621440 | tf_op jit(solution)/shard_map/reduce_sum | solution.py:117
  61.8 1.6 %multiply_reduce_fusion = (f32[2]{0:T(128)S(1)}, f32[2,256,256]{2,1,0:T(8,128)S(1)}) fusion(bf16[1,1,2,256,256]{4,3,2,1,0:T(8,128)(2,1)S(1)} %copy-done.7, f32[2,256,256]{2,1,0:T(8,128)S(1)} %convert_reduce_fusion, bf16[1,1,2,256,256]{4,3,2,1,0:T(8,128)(2,1)} %param.14, f32[2]{0:T(128)S(1)} %convert_element_type.35), kind=kOutput, calls=%fused_computation.26 | convolution fusion | flops 134873088 | bytes 1572880 | tf_op jit(solution)/shard_map/sij,sjk->sik/dot_general | solution.py:142
  65.4 2.4 %collective-permute-done.1 = f32[2,9]{1,0:T(2,128)S(1)} collective-permute-done((f32[2,9]{1,0:T(2,128)S(1)}, f32[2,9]{1,0:T(2,128)S(1)}, u32[]{:S(2)}, u32[]{:S(2)}) %collective-permute-start.1) | collective-permute-done | bytes 104 | tf_op jit(solution)/shard_map/ppermute | solution.py:20
  67.9 3.3 %collective-permute-done.2 = f32[2,9]{1,0:T(2,128)S(1)} collective-permute-done((f32[2,9]{1,0:T(2,128)S(1)}, f32[2,9]{1,0:T(2,128)S(1)}, u32[]{:S(2)}, u32[]{:S(2)}) %collective-permute-start.2) | collective-permute-done | bytes 104 | tf_op jit(solution)/shard_map/ppermute | solution.py:20
  71.2 1.2 collective-permute-start.3
  72.4 1.2 collective-permute-done.3
  73.6 1.2 collective-permute-start.4
  74.8 1.2 collective-permute-done.4
  77.2 4.9 %collective-permute-start.5 = (bf16[2,256,256]{2,1,0:T(8,128)(2,1)S(1)}, bf16[2,256,256]{2,1,0:T(8,128)(2,1)S(1)}, u32[]{:S(2)}, u32[]{:S(2)}) collective-permute-start(bf16[2,256,256]{2,1,0:T(8,128)(2,1)S(1)} %get-tuple-element.9), channel_id=1, source_target_pairs={{0,4},{4,0},{8,12},{12,8},{16,20},{20,16},{24,28},{28,24},{1,5},{5... | collective-permute-start | bytes 786440 | tf_op jit(solution)/shard_map/ppermute | solution.py:34
  82.1 1.2 collective-permute-done.5
  83.3 1.3 %collective-permute-start.6 = (bf16[4,256,256]{2,1,0:T(8,128)(2,1)S(1)}, bf16[4,256,256]{2,1,0:T(8,128)(2,1)}, u32[]{:S(2)}, u32[]{:S(2)}) collective-permute-start(bf16[4,256,256]{2,1,0:T(8,128)(2,1)S(1)} %pad_maximum_fusion.refs_0_), channel_id=1, source_target_pairs={{0,8},{8,16},{12,4},{16,24},{20,12},{28,20},{1,9},{9,17},{13,5},{1... | collective-permute-start | bytes 1572872 | tf_op jit(solution)/shard_map/ppermute | solution.py:36
  84.6 8.7 %collective-permute-done.6.refs_1_ = bf16[4,256,256]{2,1,0:T(8,128)(2,1)} collective-permute-done((bf16[4,256,256]{2,1,0:T(8,128)(2,1)S(1)}, bf16[4,256,256]{2,1,0:T(8,128)(2,1)}, u32[]{:S(2)}, u32[]{:S(2)}) %collective-permute-start.6) | collective-permute-done | bytes 524320 | tf_op jit(solution)/shard_map/ppermute | solution.py:36
  93.4 1.3 %collective-permute-start.7 = (bf16[4,256,256]{2,1,0:T(8,128)(2,1)}, bf16[4,256,256]{2,1,0:T(8,128)(2,1)}, u32[]{:S(2)}, u32[]{:S(2)}) collective-permute-start(bf16[4,256,256]{2,1,0:T(8,128)(2,1)} %collective-permute-done.6.refs_1_), channel_id=1, source_target_pairs={{0,8},{8,16},{12,4},{16,24},{20,12},{28,20},{1,9},{9,17},{13,5},{1... | collective-permute-start | bytes 1572872 | tf_op jit(solution)/shard_map/ppermute | solution.py:36
  94.7 8.9 %collective-permute-done.7.refs_2_ = bf16[4,256,256]{2,1,0:T(8,128)(2,1)} collective-permute-done((bf16[4,256,256]{2,1,0:T(8,128)(2,1)}, bf16[4,256,256]{2,1,0:T(8,128)(2,1)}, u32[]{:S(2)}, u32[]{:S(2)}) %collective-permute-start.7) | collective-permute-done | bytes 524320 | tf_op jit(solution)/shard_map/ppermute | solution.py:36
  103.6 1.3 %collective-permute-start.8 = (bf16[4,256,256]{2,1,0:T(8,128)(2,1)}, bf16[4,256,256]{2,1,0:T(8,128)(2,1)}, u32[]{:S(2)}, u32[]{:S(2)}) collective-permute-start(bf16[4,256,256]{2,1,0:T(8,128)(2,1)} %collective-permute-done.7.refs_2_), channel_id=1, source_target_pairs={{0,8},{8,16},{12,4},{16,24},{20,12},{28,20},{1,9},{9,17},{13,5},{1... | collective-permute-start | bytes 1572872 | tf_op jit(solution)/shard_map/ppermute | solution.py:36
  105.6 4.1 %collective-permute-start.9 = (bf16[4,256,256]{2,1,0:T(8,128)(2,1)}, bf16[4,256,256]{2,1,0:T(8,128)(2,1)S(1)}, u32[]{:S(2)}, u32[]{:S(2)}) collective-permute-start(bf16[4,256,256]{2,1,0:T(8,128)(2,1)} %collective-permute-done.6.refs_1_), channel_id=1, source_target_pairs={{0,4},{4,0},{8,12},{12,8},{16,20},{20,16},{24,28},{28,24},{1,5},{5... | collective-permute-start | bytes 1572872 | tf_op jit(solution)/shard_map/ppermute | solution.py:37
  109.7 4.1 %collective-permute-done.8.refs_3_ = bf16[4,256,256]{2,1,0:T(8,128)(2,1)} collective-permute-done((bf16[4,256,256]{2,1,0:T(8,128)(2,1)}, bf16[4,256,256]{2,1,0:T(8,128)(2,1)}, u32[]{:S(2)}, u32[]{:S(2)}) %collective-permute-start.8) | collective-permute-done | bytes 524320 | tf_op jit(solution)/shard_map/ppermute | solution.py:36
  113.8 1.3 %collective-permute-start.11 = (bf16[4,256,256]{2,1,0:T(8,128)(2,1)}, bf16[4,256,256]{2,1,0:T(8,128)(2,1)}, u32[]{:S(2)}, u32[]{:S(2)}) collective-permute-start(bf16[4,256,256]{2,1,0:T(8,128)(2,1)} %collective-permute-done.8.refs_3_), channel_id=1, source_target_pairs={{0,4},{4,0},{8,12},{12,8},{16,20},{20,16},{24,28},{28,24},{1,5},{5... | collective-permute-start | bytes 1572872 | tf_op jit(solution)/shard_map/ppermute | solution.py:37
  115.2 3.0 %fusion.2 = f32[1,1,2,256,256]{4,3,2,1,0:T(8,128)} fusion(f32[1,1,2,256,256]{4,3,2,1,0:T(8,128)} %param.13, f32[2,256,256]{2,1,0:T(8,128)S(1)} %convert_reduce_fusion, f32[2]{0:T(128)S(1)} %convert_element_type.35, pred[2]{0:T(512)(128)(4,1)S(1)} %dynamic-slice_reduce_fusion), kind=kOutput, calls=%fused_computation.5 | convolution fusion | flops 403308544 | bytes 1572874 | tf_op jit(solution)/shard_map/sji,sjk->sik/dot_general | solution.py:135
  118.2 1.6 %fusion.5 = f32[1,1,2,256,256]{4,3,2,1,0:T(8,128)} fusion(f32[1,1,2,256,256]{4,3,2,1,0:T(8,128)S(1)} %copy-done.4, f32[2,256,256]{2,1,0:T(8,128)S(1)} %convert_reduce_fusion, f32[2]{0:T(128)S(1)} %convert_element_type.35, pred[2]{0:T(512)(128)(4,1)S(1)} %dynamic-slice_reduce_fusion), kind=kOutput, calls=%fused_computation.9 | convolution fusion | flops 403308544 | bytes 1572874 | tf_op jit(solution)/shard_map/sij,skj->sik/dot_general | solution.py:132
  122.4 3.1 %shard_map.128 = bf16[8,256,256]{2,1,0:T(8,128)(2,1)} custom-call(s32[8,2]{1,0:T(8,128)} %copy.39.table_ref, bf16[4,256,256]{2,1,0:T(8,128)(2,1)} %copy-done.2, bf16[4,256,256]{2,1,0:T(8,128)(2,1)} %collective-permute-done.6.refs_1_, bf16[4,256,256]{2,1,0:T(8,128)(2,1)} %collective-permute-done.7.refs_2_, ...), custom_call_target="tpu_custom_call" | custom-call | tf_op jit(solution)/shard_map/pallas_call | solution.py:72
  (59 shorter events, 9.8 us)
Async XLA Ops:
  0.6 2.0 %copy-start = (bf16[1,8,256,256]{3,2,1,0:T(8,128)(2,1)S(1)}, bf16[1,8,256,256]{3,2,1,0:T(8,128)(2,1)}, u32[]{:S(2)}) copy-start(bf16[1,8,256,256]{3,2,1,0:T(8,128)(2,1)} %param.9) | copy-start | bytes 3145732
  4.6 6.9 %copy-start.9 = (s32[9]{0:T(128)S(1)}, s32[9]{0:T(128)}, u32[]{:S(2)}) copy-start(s32[9]{0:T(128)} %param.11) | copy-start | bytes 112
  4.6 54.8 %all-to-all-start = ((bf16[8,2,256,256]{3,2,1,0:T(8,128)(2,1)}), bf16[8,2,256,256]{3,2,1,0:T(8,128)(2,1)}, u32[]{:S(2)}, u32[]{:S(2)}) async-start(bf16[8,2,256,256]{3,2,1,0:T(8,128)(2,1)} %bitcast.3), calls=%async_computation | async-start | bytes 4194304 | tf_op jit(solution)/shard_map/all_to_all | solution.py:116
  11.1 50.2 %copy-start.1 = (f32[1,1,2,256,256]{4,3,2,1,0:T(8,128)S(1)}, f32[1,1,2,256,256]{4,3,2,1,0:T(8,128)}, u32[]{:S(2)}) copy-start(f32[1,1,2,256,256]{4,3,2,1,0:T(8,128)} %param.16) | copy-start | bytes 1572868
  11.1 50.7 %copy-start.7 = (bf16[1,1,2,256,256]{4,3,2,1,0:T(8,128)(2,1)S(1)}, bf16[1,1,2,256,256]{4,3,2,1,0:T(8,128)(2,1)}, u32[]{:S(2)}) copy-start(bf16[1,1,2,256,256]{4,3,2,1,0:T(8,128)(2,1)} %param.15) | copy-start | bytes 786436
  12.0 64.2 %copy-start.3 = (f32[1,1,2,256,256]{4,3,2,1,0:T(8,128)S(1)}, f32[1,1,2,256,256]{4,3,2,1,0:T(8,128)}, u32[]{:S(2)}) copy-start(f32[1,1,2,256,256]{4,3,2,1,0:T(8,128)} %param.17) | copy-start | bytes 1572868
  61.8 43.1 %copy-start.8 = (s32[8,1]{0,1:T(1,128)S(1)}, s32[8,1]{0,1:T(1,128)}, u32[]{:S(2)}) copy-start(s32[8,1]{0,1:T(1,128)} %param.10) | copy-start | bytes 100
  63.5 1.8 %collective-permute-start = (f32[2,9]{1,0:T(2,128)S(1)}, f32[2,9]{1,0:T(2,128)S(1)}, u32[]{:S(2)}, u32[]{:S(2)}) collective-permute-start(f32[2,9]{1,0:T(2,128)S(1)} %pad_maximum_fusion.1), channel_id=1, source_target_pairs={{0,4},{4,0},{8,12},{12,8},{16,20},{20,16},{24,28},{28,24},{1,5},{5... | collective-permute-start | bytes 224 | tf_op jit(solution)/shard_map/ppermute | solution.py:20
  65.3 2.5 %collective-permute-start.1 = (f32[2,9]{1,0:T(2,128)S(1)}, f32[2,9]{1,0:T(2,128)S(1)}, u32[]{:S(2)}, u32[]{:S(2)}) collective-permute-start(f32[2,9]{1,0:T(2,128)S(1)} %fusion.31), channel_id=1, source_target_pairs={{0,8},{4,12},{8,0},{12,4},{16,24},{20,28},{24,16},{28,20},{1,9},{5... | collective-permute-start | bytes 224 | tf_op jit(solution)/shard_map/ppermute | solution.py:20
  67.8 3.4 %collective-permute-start.2 = (f32[2,9]{1,0:T(2,128)S(1)}, f32[2,9]{1,0:T(2,128)S(1)}, u32[]{:S(2)}, u32[]{:S(2)}) collective-permute-start(f32[2,9]{1,0:T(2,128)S(1)} %fusion.37), channel_id=1, source_target_pairs={{0,16},{4,20},{8,24},{12,28},{16,0},{20,4},{24,8},{28,12},{1,17},{... | collective-permute-start | bytes 224 | tf_op jit(solution)/shard_map/ppermute | solution.py:20
  71.2 2.4 %collective-permute-start.3 = (f32[2,9]{1,0:T(2,128)S(1)}, f32[2,9]{1,0:T(2,128)S(1)}, u32[]{:S(2)}, u32[]{:S(2)}) collective-permute-start(f32[2,9]{1,0:T(2,128)S(1)} %add.91), channel_id=1, source_target_pairs={{0,1},{1,0},{2,3},{3,2},{4,5},{5,4},{6,7},{7,6},{8,9},{9,8},{10,11... | collective-permute-start | bytes 224 | tf_op jit(solution)/shard_map/ppermute | solution.py:20
  73.6 2.4 %collective-permute-start.4 = (f32[2,9]{1,0:T(2,128)S(1)}, f32[2,9]{1,0:T(2,128)S(1)}, u32[]{:S(2)}, u32[]{:S(2)}) collective-permute-start(f32[2,9]{1,0:T(2,128)S(1)} %add.92), channel_id=1, source_target_pairs={{0,2},{1,3},{2,0},{3,1},{4,6},{5,7},{6,4},{7,5},{8,10},{9,11},{10,... | collective-permute-start | bytes 224 | tf_op jit(solution)/shard_map/ppermute | solution.py:20
  77.2 41.0 %copy-start.4 = (f32[1,1,2,256,256]{4,3,2,1,0:T(8,128)S(1)}, f32[1,1,2,256,256]{4,3,2,1,0:T(8,128)}, u32[]{:S(2)}) copy-start(f32[1,1,2,256,256]{4,3,2,1,0:T(8,128)} %param.12) | copy-start | bytes 1572868
  77.2 6.1 %collective-permute-start.5 = (bf16[2,256,256]{2,1,0:T(8,128)(2,1)S(1)}, bf16[2,256,256]{2,1,0:T(8,128)(2,1)S(1)}, u32[]{:S(2)}, u32[]{:S(2)}) collective-permute-start(bf16[2,256,256]{2,1,0:T(8,128)(2,1)S(1)} %get-tuple-element.9), channel_id=1, source_target_pairs={{0,4},{4,0},{8,12},{12,8},{16,20},{20,16},{24,28},{28,24},{1,5},{5... | collective-permute-start | bytes 786440 | tf_op jit(solution)/shard_map/ppermute | solution.py:34
  83.3 37.4 %copy-start.2 = (bf16[4,256,256]{2,1,0:T(8,128)(2,1)}, bf16[4,256,256]{2,1,0:T(8,128)(2,1)S(1)}, u32[]{:S(2)}) copy-start(bf16[4,256,256]{2,1,0:T(8,128)(2,1)S(1)} %pad_maximum_fusion.refs_0_) | copy-start | bytes 1572868
  83.3 10.0 %collective-permute-start.6 = (bf16[4,256,256]{2,1,0:T(8,128)(2,1)S(1)}, bf16[4,256,256]{2,1,0:T(8,128)(2,1)}, u32[]{:S(2)}, u32[]{:S(2)}) collective-permute-start(bf16[4,256,256]{2,1,0:T(8,128)(2,1)S(1)} %pad_maximum_fusion.refs_0_), channel_id=1, source_target_pairs={{0,8},{8,16},{12,4},{16,24},{20,12},{28,20},{1,9},{9,17},{13,5},{1... | collective-permute-start | bytes 1572872 | tf_op jit(solution)/shard_map/ppermute | solution.py:36
  93.4 10.2 %collective-permute-start.7 = (bf16[4,256,256]{2,1,0:T(8,128)(2,1)}, bf16[4,256,256]{2,1,0:T(8,128)(2,1)}, u32[]{:S(2)}, u32[]{:S(2)}) collective-permute-start(bf16[4,256,256]{2,1,0:T(8,128)(2,1)} %collective-permute-done.6.refs_1_), channel_id=1, source_target_pairs={{0,8},{8,16},{12,4},{16,24},{20,12},{28,20},{1,9},{9,17},{13,5},{1... | collective-permute-start | bytes 1572872 | tf_op jit(solution)/shard_map/ppermute | solution.py:36
  103.6 10.2 %collective-permute-start.8 = (bf16[4,256,256]{2,1,0:T(8,128)(2,1)}, bf16[4,256,256]{2,1,0:T(8,128)(2,1)}, u32[]{:S(2)}, u32[]{:S(2)}) collective-permute-start(bf16[4,256,256]{2,1,0:T(8,128)(2,1)} %collective-permute-done.7.refs_2_), channel_id=1, source_target_pairs={{0,8},{8,16},{12,4},{16,24},{20,12},{28,20},{1,9},{9,17},{13,5},{1... | collective-permute-start | bytes 1572872 | tf_op jit(solution)/shard_map/ppermute | solution.py:36
  105.6 15.1 %collective-permute-start.9 = (bf16[4,256,256]{2,1,0:T(8,128)(2,1)}, bf16[4,256,256]{2,1,0:T(8,128)(2,1)S(1)}, u32[]{:S(2)}, u32[]{:S(2)}) collective-permute-start(bf16[4,256,256]{2,1,0:T(8,128)(2,1)} %collective-permute-done.6.refs_1_), channel_id=1, source_target_pairs={{0,4},{4,0},{8,12},{12,8},{16,20},{20,16},{24,28},{28,24},{1,5},{5... | collective-permute-start | bytes 1572872 | tf_op jit(solution)/shard_map/ppermute | solution.py:37
  109.7 11.8 %collective-permute-start.10 = (bf16[4,256,256]{2,1,0:T(8,128)(2,1)}, bf16[4,256,256]{2,1,0:T(8,128)(2,1)S(1)}, u32[]{:S(2)}, u32[]{:S(2)}) collective-permute-start(bf16[4,256,256]{2,1,0:T(8,128)(2,1)} %collective-permute-done.7.refs_2_), channel_id=1, source_target_pairs={{0,4},{4,0},{8,12},{12,8},{16,20},{20,16},{24,28},{28,24},{1,5},{5... | collective-permute-start | bytes 1572872 | tf_op jit(solution)/shard_map/ppermute | solution.py:37
  113.8 8.5 %collective-permute-start.11 = (bf16[4,256,256]{2,1,0:T(8,128)(2,1)}, bf16[4,256,256]{2,1,0:T(8,128)(2,1)}, u32[]{:S(2)}, u32[]{:S(2)}) collective-permute-start(bf16[4,256,256]{2,1,0:T(8,128)(2,1)} %collective-permute-done.8.refs_3_), channel_id=1, source_target_pairs={{0,4},{4,0},{8,12},{12,8},{16,20},{20,16},{24,28},{28,24},{1,5},{5... | collective-permute-start | bytes 1572872 | tf_op jit(solution)/shard_map/ppermute | solution.py:37
  120.8 0.8 copy-start.5
  121.6 0.8 copy-start.6

commit v18 on v8

--- a/solution.py
+++ b/solution.py
@@ -28,6 +28,12 @@
     if size % 2 or size < 4:
         gathered = lax.all_gather(mine, "dp", axis=0, tiled=True)
         return jnp.take(gathered, owner_of * slot_count + slot_rank, axis=0)
+    if slot_count > 1:
+        parts = [gather_blocks(mine[slot:slot + 1], owner_of, jnp.zeros_like(slot_rank), replica) for slot in range(slot_count)]
+        picked = parts[0]
+        for slot in range(1, slot_count):
+            picked = jnp.where((slot_rank == slot)[:, None, None], parts[slot], picked)
+        return picked
     chips = size // 2
     rightward = [(i, i + 2) for i in range(size - 2)]
     leftward = [(i + 2, i) for i in range(size - 2)]

time: 117 us -> 139 us (1.19)
  starting transfers between devices: 34.6 us -> 52.8 us
  Pallas kernels: 3.15 us -> 6.33 us
  other arithmetic: 7.11 us -> 10.1 us
  matrix products: 7.28 us -> 5.2 us
    ppermute x3 -> x6, starting transfers between devices: 10 us -> 24.4 us  [gather_blocks(): from_left[step] = lax.ppermute(from_left[step - 1], 'dp', rightward)]
    ppermute x3 -> x6, starting transfers between devices: 3.88 us -> 7.71 us  [gather_blocks(): from_right[step] = lax.ppermute(from_right[step - 1], 'dp', leftward)]
    pallas_call x1 -> x2, Pallas kernels: 3.15 us -> 6.33 us  [pick_blocks(): pl.pallas_call(pick_kernel, out_shape=jax.ShapeDtypeStruct((blocks,) + pi...]
    select_n x0 -> x1, other arithmetic: none -> 2.37 us  [gather_blocks(): picked = jnp.where((slot_rank == slot)[:, None, None], parts[slot], picked)]
    ppermute x3 -> x6, starting transfers between devices: 0.16 us -> 2.28 us  [gather_blocks(): near_left[step] = lax.ppermute(from_left[step], 'dp', partner)]
    ppermute x3 -> x6, waiting for transfers between devices: 1.96 us -> 0.02 us  [gather_blocks(): from_left[step] = lax.ppermute(from_left[step - 1], 'dp', rightward)]
    ppermute x3 -> x6, waiting for transfers between devices: 0.01 us -> 1.9 us  [gather_blocks(): from_right[step] = lax.ppermute(from_right[step - 1], 'dp', leftward)]
    ppermute x1 -> x2, starting transfers between devices: 7.05 us -> 5.36 us  [gather_blocks(): near_left[0] = lax.ppermute(mine, 'dp', partner)]
  transfers between devices with their start and end apart: 19 -> 32, of which waited for: 7 -> 7; matrix products, arithmetic and copies ran while one was open for 7% -> 5% of each run, Pallas kernels for 0% -> 2%
where the time goes in v18:
time: 139 us; the launch traced here: 138 us
  waiting for transfers between devices  58.3 us (42%)
  starting transfers between devices  52.8 us (38%)
  other arithmetic  10.1 us (7%)
  Pallas kernels  6.33 us (5%)
  matrix products  5.2 us (4%)
  local copies, waits for them, and re-layouts  4.51 us (3%)
    all_to_all x1, waiting for transfers between devices, local(): received = lax.all_to_all(by_owner, 'dp', 0, 0, tiled=True)  47.4 us
    ppermute x6, starting transfers between devices, gather_blocks(): from_left[step] = lax.ppermute(from_left[step - 1], 'dp', rightward)  24.4 us
    ppermute x5, waiting for transfers between devices, butterfly_sum(): x = x + lax.ppermute(x, axis, [(i, i ^ step) for i in range(size)])  8.92 us
    ppermute x6, starting transfers between devices, gather_blocks(): from_right[step] = lax.ppermute(from_right[step - 1], 'dp', leftward)  7.71 us
    all_to_all x1, starting transfers between devices, local(): received = lax.all_to_all(by_owner, 'dp', 0, 0, tiled=True)  6.51 us
    pallas_call x2, Pallas kernels, pick_blocks(): pl.pallas_call(pick_kernel, out_shape=jax.ShapeDtypeStruct((blocks,) + pi...  6.33 us
    ppermute x2, starting transfers between devices, gather_blocks(): near_left[0] = lax.ppermute(mine, 'dp', partner)  5.36 us
    ppermute x5, starting transfers between devices, butterfly_sum(): x = x + lax.ppermute(x, axis, [(i, i ^ step) for i in range(size)])  3.52 us
  transfers between devices with their start and end apart: 32, of which 7 were waited for; matrix products, arithmetic and copies ran while one was open for 5% of the time, Pallas kernels for 2%

profile of v18, /device:TPU:1, one launch (start us, length us, event | category | flops | bytes accessed | tf_op | source)
XLA Modules:
  0.0 138.3 jit_solution(12585774856389148270)
XLA Ops:
  2.6 2.0 %gather_fusion = bf16[16,256,256]{2,1,0:T(8,128)(2,1)} fusion(bf16[8,256,256]{2,1,0:T(8,128)(2,1)S(1)} %bitcast.50, s32[1024]{0:T(1024)S(1)} %pad_clamp_fusion), kind=kCustom, calls=%fused_computation | custom fusion | bytes 4194368 | tf_op jit(solution)/shard_map/jit(_take)/gather | solution.py:126
  4.6 6.5 %all-to-all-start = ((bf16[8,2,256,256]{3,2,1,0:T(8,128)(2,1)}), bf16[8,2,256,256]{3,2,1,0:T(8,128)(2,1)}, u32[]{:S(2)}, u32[]{:S(2)}) async-start(bf16[8,2,256,256]{3,2,1,0:T(8,128)(2,1)} %bitcast.3), calls=%async_computation | async-start | bytes 4194304 | tf_op jit(solution)/shard_map/all_to_all | solution.py:129
  12.0 47.4 %all-to-all-done = bf16[8,2,256,256]{3,2,1,0:T(8,128)(2,1)} async-done(((bf16[8,2,256,256]{3,2,1,0:T(8,128)(2,1)}), bf16[8,2,256,256]{3,2,1,0:T(8,128)(2,1)}, u32[]{:S(2)}, u32[]{:S(2)}) %all-to-all-start) | async-done | bytes 2097184 | tf_op jit(solution)/shard_map/all_to_all | solution.py:129
  59.4 1.9 %convert_reduce_fusion = f32[2,256,256]{2,1,0:T(8,128)S(1)} fusion(bf16[8,2,256,256]{3,2,1,0:T(8,128)(2,1)} %all-to-all-done), kind=kLoop, calls=%fused_computation.1 | loop fusion | flops 1966080 | bytes 2621440 | tf_op jit(solution)/shard_map/reduce_sum | solution.py:130
  61.8 1.6 %multiply_reduce_fusion = (f32[2]{0:T(128)S(1)}, f32[2,256,256]{2,1,0:T(8,128)S(1)}) fusion(bf16[1,1,2,256,256]{4,3,2,1,0:T(8,128)(2,1)S(1)} %copy-done.8, f32[2,256,256]{2,1,0:T(8,128)S(1)} %convert_reduce_fusion, bf16[1,1,2,256,256]{4,3,2,1,0:T(8,128)(2,1)} %param.14, f32[2]{0:T(128)S(1)} %convert_element_type.35), kind=kOutput, calls=%fused_computation.26 | convolution fusion | flops 134873088 | bytes 1572880 | tf_op jit(solution)/shard_map/sij,sjk->sik/dot_general | solution.py:155
  65.4 2.4 %collective-permute-done.1 = f32[2,9]{1,0:T(2,128)S(1)} collective-permute-done((f32[2,9]{1,0:T(2,128)S(1)}, f32[2,9]{1,0:T(2,128)S(1)}, u32[]{:S(2)}, u32[]{:S(2)}) %collective-permute-start.1) | collective-permute-done | bytes 104 | tf_op jit(solution)/shard_map/ppermute | solution.py:20
  67.9 3.3 %collective-permute-done.2 = f32[2,9]{1,0:T(2,128)S(1)} collective-permute-done((f32[2,9]{1,0:T(2,128)S(1)}, f32[2,9]{1,0:T(2,128)S(1)}, u32[]{:S(2)}, u32[]{:S(2)}) %collective-permute-start.2) | collective-permute-done | bytes 104 | tf_op jit(solution)/shard_map/ppermute | solution.py:20
  77.3 2.0 %collective-permute-start.18 = (bf16[1,256,256]{2,1,0:T(8,128)(2,1)S(1)}, bf16[1,256,256]{2,1,0:T(8,128)(2,1)S(1)}, u32[]{:S(2)}, u32[]{:S(2)}) collective-permute-start(bf16[1,256,256]{2,1,0:T(8,128)(2,1)S(1)} %get-tuple-element.9.refs_3_), channel_id=1, source_target_pairs={{0,8},{4,12},{8,16},{12,20},{16,24},{20,28},{1,9},{5,13},{9,17},{1... | collective-permute-start | bytes 393224 | tf_op jit(solution)/shard_map/ppermute | solution.py:50
  80.7 5.0 %collective-permute-start.27 = (bf16[1,256,256]{2,1,0:T(8,128)(2,1)S(1)}, bf16[1,256,256]{2,1,0:T(8,128)(2,1)S(1)}, u32[]{:S(2)}, u32[]{:S(2)}) collective-permute-start(bf16[1,256,256]{2,1,0:T(8,128)(2,1)S(1)} %get-tuple-element.9.refs_3_), channel_id=1, source_target_pairs={{0,4},{4,0},{8,12},{12,8},{16,20},{20,16},{24,28},{28,24},{1,5},{5... | collective-permute-start | bytes 393224 | tf_op jit(solution)/shard_map/ppermute | solution.py:47
  85.7 4.3 %collective-permute-start.5 = (bf16[1,256,256]{2,1,0:T(8,128)(2,1)S(1)}, bf16[1,256,256]{2,1,0:T(8,128)(2,1)S(1)}, u32[]{:S(2)}, u32[]{:S(2)}) collective-permute-start(bf16[1,256,256]{2,1,0:T(8,128)(2,1)S(1)} %get-tuple-element.10.refs_3_), channel_id=1, source_target_pairs={{0,8},{4,12},{8,16},{12,20},{16,24},{20,28},{1,9},{5,13},{9,17},{1... | collective-permute-start | bytes 393224 | tf_op jit(solution)/shard_map/ppermute | solution.py:50
  90.0 1.3 collective-permute-start.8
  92.3 4.3 %collective-permute-start.19 = (bf16[1,256,256]{2,1,0:T(8,128)(2,1)S(1)}, bf16[1,256,256]{2,1,0:T(8,128)(2,1)S(1)}, u32[]{:S(2)}, u32[]{:S(2)}) collective-permute-start(bf16[1,256,256]{2,1,0:T(8,128)(2,1)S(1)} %collective-permute-done.18.refs_2_), channel_id=1, source_target_pairs={{0,8},{4,12},{8,16},{12,20},{16,24},{20,28},{1,9},{5,13},{9,17},{1... | collective-permute-start | bytes 393224 | tf_op jit(solution)/shard_map/ppermute | solution.py:50
  98.5 4.9 %collective-permute-start.6 = (bf16[1,256,256]{2,1,0:T(8,128)(2,1)S(1)}, bf16[1,256,256]{2,1,0:T(8,128)(2,1)}, u32[]{:S(2)}, u32[]{:S(2)}) collective-permute-start(bf16[1,256,256]{2,1,0:T(8,128)(2,1)S(1)} %collective-permute-done.5.refs_2_), channel_id=1, source_target_pairs={{0,8},{4,12},{8,16},{12,20},{16,24},{20,28},{1,9},{5,13},{9,17},{1... | collective-permute-start | bytes 393224 | tf_op jit(solution)/shard_map/ppermute | solution.py:50
  104.5 1.3 collective-permute-start.9
  105.8 4.0 %collective-permute-start.20 = (bf16[1,256,256]{2,1,0:T(8,128)(2,1)S(1)}, bf16[1,256,256]{2,1,0:T(8,128)(2,1)S(1)}, u32[]{:S(2)}, u32[]{:S(2)}) collective-permute-start(bf16[1,256,256]{2,1,0:T(8,128)(2,1)S(1)} %collective-permute-done.19.refs_1_), channel_id=1, source_target_pairs={{0,8},{4,12},{8,16},{12,20},{16,24},{20,28},{1,9},{5,13},{9,17},{1... | collective-permute-start | bytes 393224 | tf_op jit(solution)/shard_map/ppermute | solution.py:50
  110.7 1.3 collective-permute-start.23
  113.5 4.9 %collective-permute-start.7 = (bf16[1,256,256]{2,1,0:T(8,128)(2,1)}, bf16[1,256,256]{2,1,0:T(8,128)(2,1)}, u32[]{:S(2)}, u32[]{:S(2)}) collective-permute-start(bf16[1,256,256]{2,1,0:T(8,128)(2,1)} %collective-permute-done.6.refs_1_), channel_id=1, source_target_pairs={{0,8},{4,12},{8,16},{12,20},{16,24},{20,28},{1,9},{5,13},{9,17},{1... | collective-permute-start | bytes 393224 | tf_op jit(solution)/shard_map/ppermute | solution.py:50
  118.5 1.3 collective-permute-start.10
  121.0 1.9 %fusion.2 = f32[1,1,2,256,256]{4,3,2,1,0:T(8,128)} fusion(f32[1,1,2,256,256]{4,3,2,1,0:T(8,128)S(1)} %copy-done.6, f32[2,256,256]{2,1,0:T(8,128)S(1)} %convert_reduce_fusion, f32[2]{0:T(128)S(1)} %convert_element_type.35, pred[2]{0:T(512)(128)(4,1)S(1)} %dynamic-slice_reduce_fusion), kind=kOutput, calls=%fused_computation.5 | convolution fusion | flops 403308544 | bytes 1572874 | tf_op jit(solution)/shard_map/sji,sjk->sik/dot_general | solution.py:148
  123.5 1.9 %collective-permute-done.10.refs_6_ = bf16[1,256,256]{2,1,0:T(8,128)(2,1)} collective-permute-done((bf16[1,256,256]{2,1,0:T(8,128)(2,1)}, bf16[1,256,256]{2,1,0:T(8,128)(2,1)}, u32[]{:S(2)}, u32[]{:S(2)}) %collective-permute-start.10) | collective-permute-done | bytes 131104 | tf_op jit(solution)/shard_map/ppermute | solution.py:51
  127.2 1.6 %fusion.5 = f32[1,1,2,256,256]{4,3,2,1,0:T(8,128)} fusion(f32[1,1,2,256,256]{4,3,2,1,0:T(8,128)S(1)} %copy-done.7, f32[2,256,256]{2,1,0:T(8,128)S(1)} %convert_reduce_fusion, f32[2]{0:T(128)S(1)} %convert_element_type.35, pred[2]{0:T(512)(128)(4,1)S(1)} %dynamic-slice_reduce_fusion), kind=kOutput, calls=%fused_computation.9 | convolution fusion | flops 403308544 | bytes 1572874 | tf_op jit(solution)/shard_map/sij,skj->sik/dot_general | solution.py:145
  128.8 3.2 %shard_map.129 = bf16[8,256,256]{2,1,0:T(8,128)(2,1)} custom-call(s32[8,2]{1,0:T(8,128)} %stack.20.table_ref, bf16[1,256,256]{2,1,0:T(8,128)(2,1)} %copy-done.19, bf16[1,256,256]{2,1,0:T(8,128)(2,1)} %copy-done.14, bf16[1,256,256]{2,1,0:T(8,128)(2,1)} %copy-done.9, bf16[1,256,256]{2,1,0:T(8,128)(2,1)} %copy-done.5, bf16[1,256,256]{2,1,0:T(8,128)(2,1)} %copy-done.12, ...), custom_call_target="tpu_custom_call" | custom-call | tf_op jit(solution)/shard_map/pallas_call | solution.py:85
  132.8 3.1 %shard_map.128 = bf16[8,256,256]{2,1,0:T(8,128)(2,1)} custom-call(s32[8,2]{1,0:T(8,128)} %stack.20.table_ref, bf16[1,256,256]{2,1,0:T(8,128)(2,1)} %collective-permute-done.7.refs_0_, bf16[1,256,256]{2,1,0:T(8,128)(2,1)} %collective-permute-done.6.refs_1_, bf16[1,256,256]{2,1,0:T(8,128)(2,1)} %copy-done.10, bf16[1,256,256]{2,1,0:T(8,128)(2,1)} %copy-done.4, ...), custom_call_target="tpu_custom_call" | custom-call | tf_op jit(solution)/shard_map/pallas_call | solution.py:85
  136.0 2.4 %broadcast_select_fusion = bf16[8,256,256]{2,1,0:T(8,128)(2,1)} fusion(bf16[8,256,256]{2,1,0:T(8,128)(2,1)} %shard_map.128, bf16[8,256,256]{2,1,0:T(8,128)(2,1)S(1)} %copy-done.1, pred[8]{0:T(512)(128)(4,1)S(1)} %broadcast_compare_fusion), kind=kLoop, calls=%fused_computation.12 | loop fusion | flops 524288 | bytes 3145736 | tf_op jit(solution)/shard_map/jit(_where)/select_n | solution.py:35
  (143 shorter events, 23.4 us)
Async XLA Ops:
  4.6 54.8 %all-to-all-start = ((bf16[8,2,256,256]{3,2,1,0:T(8,128)(2,1)}), bf16[8,2,256,256]{3,2,1,0:T(8,128)(2,1)}, u32[]{:S(2)}, u32[]{:S(2)}) async-start(bf16[8,2,256,256]{3,2,1,0:T(8,128)(2,1)} %bitcast.3), calls=%async_computation | async-start | bytes 4194304 | tf_op jit(solution)/shard_map/all_to_all | solution.py:129
  77.3 14.0 %collective-permute-start.18 = (bf16[1,256,256]{2,1,0:T(8,128)(2,1)S(1)}, bf16[1,256,256]{2,1,0:T(8,128)(2,1)S(1)}, u32[]{:S(2)}, u32[]{:S(2)}) collective-permute-start(bf16[1,256,256]{2,1,0:T(8,128)(2,1)S(1)} %get-tuple-element.9.refs_3_), channel_id=1, source_target_pairs={{0,8},{4,12},{8,16},{12,20},{16,24},{20,28},{1,9},{5,13},{9,17},{1... | collective-permute-start | bytes 393224 | tf_op jit(solution)/shard_map/ppermute | solution.py:50
  79.4 12.9 %collective-permute-start.21 = (bf16[1,256,256]{2,1,0:T(8,128)(2,1)S(1)}, bf16[1,256,256]{2,1,0:T(8,128)(2,1)S(1)}, u32[]{:S(2)}, u32[]{:S(2)}) collective-permute-start(bf16[1,256,256]{2,1,0:T(8,128)(2,1)S(1)} %get-tuple-element.9.refs_3_), channel_id=1, source_target_pairs={{8,0},{12,4},{16,8},{20,12},{24,16},{28,20},{9,1},{13,5},{17,9},{2... | collective-permute-start | bytes 393224 | tf_op jit(solution)/shard_map/ppermute | solution.py:51
  80.7 15.8 %collective-permute-start.27 = (bf16[1,256,256]{2,1,0:T(8,128)(2,1)S(1)}, bf16[1,256,256]{2,1,0:T(8,128)(2,1)S(1)}, u32[]{:S(2)}, u32[]{:S(2)}) collective-permute-start(bf16[1,256,256]{2,1,0:T(8,128)(2,1)S(1)} %get-tuple-element.9.refs_3_), channel_id=1, source_target_pairs={{0,4},{4,0},{8,12},{12,8},{16,20},{20,16},{24,28},{28,24},{1,5},{5... | collective-permute-start | bytes 393224 | tf_op jit(solution)/shard_map/ppermute | solution.py:47
  85.7 11.2 %collective-permute-start.5 = (bf16[1,256,256]{2,1,0:T(8,128)(2,1)S(1)}, bf16[1,256,256]{2,1,0:T(8,128)(2,1)S(1)}, u32[]{:S(2)}, u32[]{:S(2)}) collective-permute-start(bf16[1,256,256]{2,1,0:T(8,128)(2,1)S(1)} %get-tuple-element.10.refs_3_), channel_id=1, source_target_pairs={{0,8},{4,12},{8,16},{12,20},{16,24},{20,28},{1,9},{5,13},{9,17},{1... | collective-permute-start | bytes 393224 | tf_op jit(solution)/shard_map/ppermute | solution.py:50
  90.0 8.3 %collective-permute-start.8 = (bf16[1,256,256]{2,1,0:T(8,128)(2,1)S(1)}, bf16[1,256,256]{2,1,0:T(8,128)(2,1)}, u32[]{:S(2)}, u32[]{:S(2)}) collective-permute-start(bf16[1,256,256]{2,1,0:T(8,128)(2,1)S(1)} %get-tuple-element.10.refs_3_), channel_id=1, source_target_pairs={{8,0},{12,4},{16,8},{20,12},{24,16},{28,20},{9,1},{13,5},{17,9},{2... | collective-permute-start | bytes 393224 | tf_op jit(solution)/shard_map/ppermute | solution.py:51
  91.3 7.2 %collective-permute-start.14 = (bf16[1,256,256]{2,1,0:T(8,128)(2,1)S(1)}, bf16[1,256,256]{2,1,0:T(8,128)(2,1)S(1)}, u32[]{:S(2)}, u32[]{:S(2)}) collective-permute-start(bf16[1,256,256]{2,1,0:T(8,128)(2,1)S(1)} %get-tuple-element.10.refs_3_), channel_id=1, source_target_pairs={{0,4},{4,0},{8,12},{12,8},{16,20},{20,16},{24,28},{28,24},{1,5},{5... | collective-permute-start | bytes 393224 | tf_op jit(solution)/shard_map/ppermute | solution.py:47
  92.3 11.8 %collective-permute-start.19 = (bf16[1,256,256]{2,1,0:T(8,128)(2,1)S(1)}, bf16[1,256,256]{2,1,0:T(8,128)(2,1)S(1)}, u32[]{:S(2)}, u32[]{:S(2)}) collective-permute-start(bf16[1,256,256]{2,1,0:T(8,128)(2,1)S(1)} %collective-permute-done.18.refs_2_), channel_id=1, source_target_pairs={{0,8},{4,12},{8,16},{12,20},{16,24},{20,28},{1,9},{5,13},{9,17},{1... | collective-permute-start | bytes 393224 | tf_op jit(solution)/shard_map/ppermute | solution.py:50
  96.6 9.2 %collective-permute-start.26 = (bf16[1,256,256]{2,1,0:T(8,128)(2,1)S(1)}, bf16[1,256,256]{2,1,0:T(8,128)(2,1)S(1)}, u32[]{:S(2)}, u32[]{:S(2)}) collective-permute-start(bf16[1,256,256]{2,1,0:T(8,128)(2,1)S(1)} %collective-permute-done.18.refs_2_), channel_id=1, source_target_pairs={{0,4},{4,0},{8,12},{12,8},{16,20},{20,16},{24,28},{28,24},{1,5},{5... | collective-permute-start | bytes 393224 | tf_op jit(solution)/shard_map/ppermute | solution.py:52
  96.9 7.5 %collective-permute-start.22 = (bf16[1,256,256]{2,1,0:T(8,128)(2,1)S(1)}, bf16[1,256,256]{2,1,0:T(8,128)(2,1)S(1)}, u32[]{:S(2)}, u32[]{:S(2)}) collective-permute-start(bf16[1,256,256]{2,1,0:T(8,128)(2,1)S(1)} %collective-permute-done.21.refs_4_), channel_id=1, source_target_pairs={{8,0},{12,4},{16,8},{20,12},{24,16},{28,20},{9,1},{13,5},{17,9},{2... | collective-permute-start | bytes 393224 | tf_op jit(solution)/shard_map/ppermute | solution.py:51
  98.2 11.6 %collective-permute-start.28 = (bf16[1,256,256]{2,1,0:T(8,128)(2,1)S(1)}, bf16[1,256,256]{2,1,0:T(8,128)(2,1)S(1)}, u32[]{:S(2)}, u32[]{:S(2)}) collective-permute-start(bf16[1,256,256]{2,1,0:T(8,128)(2,1)S(1)} %collective-permute-done.21.refs_4_), channel_id=1, source_target_pairs={{0,4},{4,0},{8,12},{12,8},{16,20},{20,16},{24,28},{28,24},{1,5},{5... | collective-permute-start | bytes 393224 | tf_op jit(solution)/shard_map/ppermute | solution.py:53
  98.5 12.2 %collective-permute-start.6 = (bf16[1,256,256]{2,1,0:T(8,128)(2,1)S(1)}, bf16[1,256,256]{2,1,0:T(8,128)(2,1)}, u32[]{:S(2)}, u32[]{:S(2)}) collective-permute-start(bf16[1,256,256]{2,1,0:T(8,128)(2,1)S(1)} %collective-permute-done.5.refs_2_), channel_id=1, source_target_pairs={{0,8},{4,12},{8,16},{12,20},{16,24},{20,28},{1,9},{5,13},{9,17},{1... | collective-permute-start | bytes 393224 | tf_op jit(solution)/shard_map/ppermute | solution.py:50
  104.1 9.4 %collective-permute-start.13 = (bf16[1,256,256]{2,1,0:T(8,128)(2,1)S(1)}, bf16[1,256,256]{2,1,0:T(8,128)(2,1)S(1)}, u32[]{:S(2)}, u32[]{:S(2)}) collective-permute-start(bf16[1,256,256]{2,1,0:T(8,128)(2,1)S(1)} %collective-permute-done.5.refs_2_), channel_id=1, source_target_pairs={{0,4},{4,0},{8,12},{12,8},{16,20},{20,16},{24,28},{28,24},{1,5},{5... | collective-permute-start | bytes 393224 | tf_op jit(solution)/shard_map/ppermute | solution.py:52
  104.5 8.5 %collective-permute-start.9 = (bf16[1,256,256]{2,1,0:T(8,128)(2,1)}, bf16[1,256,256]{2,1,0:T(8,128)(2,1)}, u32[]{:S(2)}, u32[]{:S(2)}) collective-permute-start(bf16[1,256,256]{2,1,0:T(8,128)(2,1)} %collective-permute-done.8.refs_4_), channel_id=1, source_target_pairs={{8,0},{12,4},{16,8},{20,12},{24,16},{28,20},{9,1},{13,5},{17,9},{2... | collective-permute-start | bytes 393224 | tf_op jit(solution)/shard_map/ppermute | solution.py:51
  105.8 12.7 %collective-permute-start.20 = (bf16[1,256,256]{2,1,0:T(8,128)(2,1)S(1)}, bf16[1,256,256]{2,1,0:T(8,128)(2,1)S(1)}, u32[]{:S(2)}, u32[]{:S(2)}) collective-permute-start(bf16[1,256,256]{2,1,0:T(8,128)(2,1)S(1)} %collective-permute-done.19.refs_1_), channel_id=1, source_target_pairs={{0,8},{4,12},{8,16},{12,20},{16,24},{20,28},{1,9},{5,13},{9,17},{1... | collective-permute-start | bytes 393224 | tf_op jit(solution)/shard_map/ppermute | solution.py:50
  109.8 10.3 %collective-permute-start.25 = (bf16[1,256,256]{2,1,0:T(8,128)(2,1)S(1)}, bf16[1,256,256]{2,1,0:T(8,128)(2,1)S(1)}, u32[]{:S(2)}, u32[]{:S(2)}) collective-permute-start(bf16[1,256,256]{2,1,0:T(8,128)(2,1)S(1)} %collective-permute-done.19.refs_1_), channel_id=1, source_target_pairs={{0,4},{4,0},{8,12},{12,8},{16,20},{20,16},{24,28},{28,24},{1,5},{5... | collective-permute-start | bytes 393224 | tf_op jit(solution)/shard_map/ppermute | solution.py:52
  110.7 9.0 %collective-permute-start.23 = (bf16[1,256,256]{2,1,0:T(8,128)(2,1)S(1)}, bf16[1,256,256]{2,1,0:T(8,128)(2,1)S(1)}, u32[]{:S(2)}, u32[]{:S(2)}) collective-permute-start(bf16[1,256,256]{2,1,0:T(8,128)(2,1)S(1)} %collective-permute-done.22.refs_5_), channel_id=1, source_target_pairs={{8,0},{12,4},{16,8},{20,12},{24,16},{28,20},{9,1},{13,5},{17,9},{2... | collective-permute-start | bytes 393224 | tf_op jit(solution)/shard_map/ppermute | solution.py:51
  113.0 9.9 %collective-permute-start.29 = (bf16[1,256,256]{2,1,0:T(8,128)(2,1)S(1)}, bf16[1,256,256]{2,1,0:T(8,128)(2,1)S(1)}, u32[]{:S(2)}, u32[]{:S(2)}) collective-permute-start(bf16[1,256,256]{2,1,0:T(8,128)(2,1)S(1)} %collective-permute-done.22.refs_5_), channel_id=1, source_target_pairs={{0,4},{4,0},{8,12},{12,8},{16,20},{20,16},{24,28},{28,24},{1,5},{5... | collective-permute-start | bytes 393224 | tf_op jit(solution)/shard_map/ppermute | solution.py:53
  113.5 9.8 %collective-permute-start.7 = (bf16[1,256,256]{2,1,0:T(8,128)(2,1)}, bf16[1,256,256]{2,1,0:T(8,128)(2,1)}, u32[]{:S(2)}, u32[]{:S(2)}) collective-permute-start(bf16[1,256,256]{2,1,0:T(8,128)(2,1)} %collective-permute-done.6.refs_1_), channel_id=1, source_target_pairs={{0,8},{4,12},{8,16},{12,20},{16,24},{20,28},{1,9},{5,13},{9,17},{1... | collective-permute-start | bytes 393224 | tf_op jit(solution)/shard_map/ppermute | solution.py:50
  118.5 7.0 %collective-permute-start.10 = (bf16[1,256,256]{2,1,0:T(8,128)(2,1)}, bf16[1,256,256]{2,1,0:T(8,128)(2,1)}, u32[]{:S(2)}, u32[]{:S(2)}) collective-permute-start(bf16[1,256,256]{2,1,0:T(8,128)(2,1)} %collective-permute-done.9.refs_5_), channel_id=1, source_target_pairs={{8,0},{12,4},{16,8},{20,12},{24,16},{28,20},{9,1},{13,5},{17,9},{2... | collective-permute-start | bytes 393224 | tf_op jit(solution)/shard_map/ppermute | solution.py:51
  119.8 6.8 %collective-permute-start.24 = (bf16[1,256,256]{2,1,0:T(8,128)(2,1)S(1)}, bf16[1,256,256]{2,1,0:T(8,128)(2,1)S(1)}, u32[]{:S(2)}, u32[]{:S(2)}) collective-permute-start(bf16[1,256,256]{2,1,0:T(8,128)(2,1)S(1)} %collective-permute-done.20.refs_0_), channel_id=1, source_target_pairs={{0,4},{4,0},{8,12},{12,8},{16,20},{20,16},{24,28},{28,24},{1,5},{5... | collective-permute-start | bytes 393224 | tf_op jit(solution)/shard_map/ppermute | solution.py:52
  123.0 9.0 %collective-permute-start.15 = (bf16[1,256,256]{2,1,0:T(8,128)(2,1)}, bf16[1,256,256]{2,1,0:T(8,128)(2,1)S(1)}, u32[]{:S(2)}, u32[]{:S(2)}) collective-permute-start(bf16[1,256,256]{2,1,0:T(8,128)(2,1)} %collective-permute-done.8.refs_4_), channel_id=1, source_target_pairs={{0,4},{4,0},{8,12},{12,8},{16,20},{20,16},{24,28},{28,24},{1,5},{5... | collective-permute-start | bytes 393224 | tf_op jit(solution)/shard_map/ppermute | solution.py:53
  123.3 8.7 %collective-permute-start.12 = (bf16[1,256,256]{2,1,0:T(8,128)(2,1)}, bf16[1,256,256]{2,1,0:T(8,128)(2,1)S(1)}, u32[]{:S(2)}, u32[]{:S(2)}) collective-permute-start(bf16[1,256,256]{2,1,0:T(8,128)(2,1)} %collective-permute-done.6.refs_1_), channel_id=1, source_target_pairs={{0,4},{4,0},{8,12},{12,8},{16,20},{20,16},{24,28},{28,24},{1,5},{5... | collective-permute-start | bytes 393224 | tf_op jit(solution)/shard_map/ppermute | solution.py:52
  125.4 6.6 %collective-permute-start.16 = (bf16[1,256,256]{2,1,0:T(8,128)(2,1)}, bf16[1,256,256]{2,1,0:T(8,128)(2,1)S(1)}, u32[]{:S(2)}, u32[]{:S(2)}) collective-permute-start(bf16[1,256,256]{2,1,0:T(8,128)(2,1)} %collective-permute-done.9.refs_5_), channel_id=1, source_target_pairs={{0,4},{4,0},{8,12},{12,8},{16,20},{20,16},{24,28},{28,24},{1,5},{5... | collective-permute-start | bytes 393224 | tf_op jit(solution)/shard_map/ppermute | solution.py:53
  (40 other events, 585.9 us)

commit v19 on v8

--- a/solution.py
+++ b/solution.py
@@ -36,22 +36,22 @@
     from_right = [None] * chips
     from_left[0] = mine
     from_right[0] = mine
-    near_left = [None] * chips
-    near_right = [None] * chips
-    near_left[0] = lax.ppermute(mine, "dp", partner)
-    near_right[0] = near_left[0]
+    beside = [lax.ppermute(mine, "dp", partner)]
     for step in range(1, chips):
         from_left[step] = lax.ppermute(from_left[step - 1], "dp", rightward)
         from_right[step] = lax.ppermute(from_right[step - 1], "dp", leftward)
-        near_left[step] = lax.ppermute(from_left[step], "dp", partner)
-        near_right[step] = lax.ppermute(from_right[step], "dp", partner)
-    pieces = from_left[::-1] + from_right[1:] + near_left[::-1] + near_right[1:]
+        both = jnp.concatenate([from_left[step], from_right[step]])
+        beside.append(lax.ppermute(both, "dp", partner))
+    pieces = from_left[::-1] + from_right[1:] + beside
     chip, core = replica // 2, replica % 2
     owner_chip, owner_core = owner_of // 2, owner_of % 2
-    offset = owner_chip - chip + chips - 1
-    which = jnp.where(owner_core == core, 0, 1)
-    source = jnp.clip(which * (2 * chips - 1) + offset, 0, len(pieces) - 1)
-    table = jnp.stack([source, jnp.clip(slot_rank, 0, slot_count - 1)], axis=1).astype(jnp.int32)
+    ahead = owner_chip - chip
+    rank = jnp.clip(slot_rank, 0, slot_count - 1)
+    same = owner_core == core
+    source = jnp.where(same, ahead + chips - 1, 2 * chips - 1 + jnp.abs(ahead))
+    place = jnp.where(same | (ahead <= 0), rank, slot_count + rank)
+    source = jnp.clip(source, 0, len(pieces) - 1)
+    table = jnp.stack([source, place], axis=1).astype(jnp.int32)
     return pick_blocks(table, pieces)
 
 

time: 117 us -> 123 us (1.051)
  starting transfers between devices: 34.6 us -> 38.6 us
  waiting for transfers between devices: 58.3 us -> 61.8 us
  matrix products: 7.28 us -> 5.2 us
    ppermute x3, waiting for transfers between devices: 0.01 us -> 4.34 us  [gather_blocks(): from_right[step] = lax.ppermute(from_right[step - 1], 'dp', leftward)]
    ppermute x3, starting transfers between devices: 10 us -> 12.9 us  [gather_blocks(): from_left[step] = lax.ppermute(from_left[step - 1], 'dp', rightward)]
    ppermute x3, waiting for transfers between devices: 1.96 us -> 0.65 us  [gather_blocks(): from_left[step] = lax.ppermute(from_left[step - 1], 'dp', rightward)]
    ppermute x7 -> x4, starting transfers between devices: 10.7 us -> 11.8 us  [the longest x3 11.8 us: gather_blocks(): beside.append(lax.ppermute(both, 'dp', partner))]
  transfers between devices with their start and end apart: 19 -> 16, of which waited for: 7 -> 11; matrix products, arithmetic and copies ran while one was open for 7% -> 6% of each run, Pallas kernels for 0% -> 0%
where the time goes in v19:
time: 123 us
  waiting for transfers between devices  61.8 us (50%)
  starting transfers between devices  38.6 us (31%)
  other arithmetic  8.29 us (7%)
  matrix products  5.2 us (4%)
  local copies, waits for them, and re-layouts  4.69 us (4%)
  Pallas kernels  3.12 us (3%)
    all_to_all x1, waiting for transfers between devices, local(): received = lax.all_to_all(by_owner, 'dp', 0, 0, tiled=True)  47.4 us
    ppermute x3, starting transfers between devices, gather_blocks(): from_left[step] = lax.ppermute(from_left[step - 1], 'dp', rightward)  12.9 us
    ppermute x3, starting transfers between devices, gather_blocks(): beside.append(lax.ppermute(both, 'dp', partner))  11.8 us
    ppermute x5, waiting for transfers between devices, butterfly_sum(): x = x + lax.ppermute(x, axis, [(i, i ^ step) for i in range(size)])  8.92 us
    all_to_all x1, starting transfers between devices, local(): received = lax.all_to_all(by_owner, 'dp', 0, 0, tiled=True)  6.51 us
    ppermute x3, waiting for transfers between devices, gather_blocks(): from_right[step] = lax.ppermute(from_right[step - 1], 'dp', leftward)  4.34 us
    ppermute x3, starting transfers between devices, gather_blocks(): from_right[step] = lax.ppermute(from_right[step - 1], 'dp', leftward)  3.84 us
    ppermute x5, starting transfers between devices, butterfly_sum(): x = x + lax.ppermute(x, axis, [(i, i ^ step) for i in range(size)])  3.52 us
  transfers between devices with their start and end apart: 16, of which 11 were waited for; matrix products, arithmetic and copies ran while one was open for 6% of the time, Pallas kernels for 0%

profile of v19, /device:TPU:1, one launch (start us, length us, event | category | flops | bytes accessed | tf_op | source)
XLA Modules:
  0.0 122.6 jit_solution(1003454644084004059)
XLA Ops:
  2.6 2.0 %gather_fusion = bf16[16,256,256]{2,1,0:T(8,128)(2,1)} fusion(bf16[8,256,256]{2,1,0:T(8,128)(2,1)S(1)} %bitcast.52, s32[1024]{0:T(1024)S(1)} %pad_clamp_fusion), kind=kCustom, calls=%fused_computation | custom fusion | bytes 4194368 | tf_op jit(solution)/shard_map/jit(_take)/gather | solution.py:120
  4.6 6.5 %all-to-all-start = ((bf16[8,2,256,256]{3,2,1,0:T(8,128)(2,1)}), bf16[8,2,256,256]{3,2,1,0:T(8,128)(2,1)}, u32[]{:S(2)}, u32[]{:S(2)}) async-start(bf16[8,2,256,256]{3,2,1,0:T(8,128)(2,1)} %bitcast.3), calls=%async_computation | async-start | bytes 4194304 | tf_op jit(solution)/shard_map/all_to_all | solution.py:123
  12.0 47.4 %all-to-all-done = bf16[8,2,256,256]{3,2,1,0:T(8,128)(2,1)} async-done(((bf16[8,2,256,256]{3,2,1,0:T(8,128)(2,1)}), bf16[8,2,256,256]{3,2,1,0:T(8,128)(2,1)}, u32[]{:S(2)}, u32[]{:S(2)}) %all-to-all-start) | async-done | bytes 2097184 | tf_op jit(solution)/shard_map/all_to_all | solution.py:123
  59.4 1.9 %convert_reduce_fusion = f32[2,256,256]{2,1,0:T(8,128)S(1)} fusion(bf16[8,2,256,256]{3,2,1,0:T(8,128)(2,1)} %all-to-all-done), kind=kLoop, calls=%fused_computation.1 | loop fusion | flops 1966080 | bytes 2621440 | tf_op jit(solution)/shard_map/reduce_sum | solution.py:124
  61.8 1.6 %multiply_reduce_fusion = (f32[2]{0:T(128)S(1)}, f32[2,256,256]{2,1,0:T(8,128)S(1)}) fusion(bf16[1,1,2,256,256]{4,3,2,1,0:T(8,128)(2,1)S(1)} %copy-done.12, f32[2,256,256]{2,1,0:T(8,128)S(1)} %convert_reduce_fusion, bf16[1,1,2,256,256]{4,3,2,1,0:T(8,128)(2,1)} %param.14, f32[2]{0:T(128)S(1)} %convert_element_type.35), kind=kOutput, calls=%fused_computation.28 | convolution fusion | flops 134873088 | bytes 1572880 | tf_op jit(solution)/shard_map/sij,sjk->sik/dot_general | solution.py:149
  65.4 2.4 %collective-permute-done.1 = f32[2,9]{1,0:T(2,128)S(1)} collective-permute-done((f32[2,9]{1,0:T(2,128)S(1)}, f32[2,9]{1,0:T(2,128)S(1)}, u32[]{:S(2)}, u32[]{:S(2)}) %collective-permute-start.1) | collective-permute-done | bytes 104 | tf_op jit(solution)/shard_map/ppermute | solution.py:20
  67.9 3.3 %collective-permute-done.2 = f32[2,9]{1,0:T(2,128)S(1)} collective-permute-done((f32[2,9]{1,0:T(2,128)S(1)}, f32[2,9]{1,0:T(2,128)S(1)}, u32[]{:S(2)}, u32[]{:S(2)}) %collective-permute-start.2) | collective-permute-done | bytes 104 | tf_op jit(solution)/shard_map/ppermute | solution.py:20
  71.2 1.2 collective-permute-start.3
  72.4 1.2 collective-permute-done.3
  73.6 1.2 %collective-permute-start.4 = (f32[2,9]{1,0:T(2,128)S(1)}, f32[2,9]{1,0:T(2,128)S(1)}, u32[]{:S(2)}, u32[]{:S(2)}) collective-permute-start(f32[2,9]{1,0:T(2,128)S(1)} %add.105), channel_id=1, source_target_pairs={{0,2},{1,3},{2,0},{3,1},{4,6},{5,7},{6,4},{7,5},{8,10},{9,11},{10,... | collective-permute-start | bytes 224 | tf_op jit(solution)/shard_map/ppermute | solution.py:20
  74.8 1.2 collective-permute-done.4
  77.2 1.3 %collective-permute-start.8 = (bf16[2,256,256]{2,1,0:T(8,128)(2,1)S(1)}, bf16[2,256,256]{2,1,0:T(8,128)(2,1)S(1)}, u32[]{:S(2)}, u32[]{:S(2)}) collective-permute-start(bf16[2,256,256]{2,1,0:T(8,128)(2,1)S(1)} %get-tuple-element.9.refs_3_), channel_id=1, source_target_pairs={{8,0},{12,4},{16,8},{20,12},{24,16},{28,20},{9,1},{13,5},{17,9},{2... | collective-permute-start | bytes 786440 | tf_op jit(solution)/shard_map/ppermute | solution.py:42
  78.5 4.0 %collective-permute-start.5 = (bf16[2,256,256]{2,1,0:T(8,128)(2,1)S(1)}, bf16[2,256,256]{2,1,0:T(8,128)(2,1)S(1)}, u32[]{:S(2)}, u32[]{:S(2)}) collective-permute-start(bf16[2,256,256]{2,1,0:T(8,128)(2,1)S(1)} %get-tuple-element.9.refs_3_), channel_id=1, source_target_pairs={{0,8},{4,12},{8,16},{12,20},{16,24},{20,28},{1,9},{5,13},{9,17},{1... | collective-permute-start | bytes 786440 | tf_op jit(solution)/shard_map/ppermute | solution.py:41
  82.5 1.8 %collective-permute-done.8.refs_4_ = bf16[2,256,256]{2,1,0:T(8,128)(2,1)S(1)} collective-permute-done((bf16[2,256,256]{2,1,0:T(8,128)(2,1)S(1)}, bf16[2,256,256]{2,1,0:T(8,128)(2,1)S(1)}, u32[]{:S(2)}, u32[]{:S(2)}) %collective-permute-start.8) | collective-permute-done | bytes 262176 | tf_op jit(solution)/shard_map/ppermute | solution.py:42
  84.3 1.3 %collective-permute-start.9 = (bf16[2,256,256]{2,1,0:T(8,128)(2,1)S(1)}, bf16[2,256,256]{2,1,0:T(8,128)(2,1)S(1)}, u32[]{:S(2)}, u32[]{:S(2)}) collective-permute-start(bf16[2,256,256]{2,1,0:T(8,128)(2,1)S(1)} %collective-permute-done.8.refs_4_), channel_id=1, source_target_pairs={{8,0},{12,4},{16,8},{20,12},{24,16},{28,20},{9,1},{13,5},{17,9},{2... | collective-permute-start | bytes 786440 | tf_op jit(solution)/shard_map/ppermute | solution.py:42
  85.8 4.1 %collective-permute-start.6 = (bf16[2,256,256]{2,1,0:T(8,128)(2,1)S(1)}, bf16[2,256,256]{2,1,0:T(8,128)(2,1)S(1)}, u32[]{:S(2)}, u32[]{:S(2)}) collective-permute-start(bf16[2,256,256]{2,1,0:T(8,128)(2,1)S(1)} %collective-permute-done.5.refs_2_), channel_id=1, source_target_pairs={{0,8},{4,12},{8,16},{12,20},{16,24},{20,28},{1,9},{5,13},{9,17},{1... | collective-permute-start | bytes 786440 | tf_op jit(solution)/shard_map/ppermute | solution.py:41
  89.9 2.5 %collective-permute-done.9.refs_5_ = bf16[2,256,256]{2,1,0:T(8,128)(2,1)S(1)} collective-permute-done((bf16[2,256,256]{2,1,0:T(8,128)(2,1)S(1)}, bf16[2,256,256]{2,1,0:T(8,128)(2,1)S(1)}, u32[]{:S(2)}, u32[]{:S(2)}) %collective-permute-start.9) | collective-permute-done | bytes 262176 | tf_op jit(solution)/shard_map/ppermute | solution.py:42
  92.5 1.3 %collective-permute-start.10 = (bf16[2,256,256]{2,1,0:T(8,128)(2,1)S(1)}, bf16[2,256,256]{2,1,0:T(8,128)(2,1)}, u32[]{:S(2)}, u32[]{:S(2)}) collective-permute-start(bf16[2,256,256]{2,1,0:T(8,128)(2,1)S(1)} %collective-permute-done.9.refs_5_), channel_id=1, source_target_pairs={{8,0},{12,4},{16,8},{20,12},{24,16},{28,20},{9,1},{13,5},{17,9},{2... | collective-permute-start | bytes 786440 | tf_op jit(solution)/shard_map/ppermute | solution.py:42
  94.2 4.8 %collective-permute-start.7 = (bf16[2,256,256]{2,1,0:T(8,128)(2,1)S(1)}, bf16[2,256,256]{2,1,0:T(8,128)(2,1)}, u32[]{:S(2)}, u32[]{:S(2)}) collective-permute-start(bf16[2,256,256]{2,1,0:T(8,128)(2,1)S(1)} %collective-permute-done.6.refs_1_), channel_id=1, source_target_pairs={{0,8},{4,12},{8,16},{12,20},{16,24},{20,28},{1,9},{5,13},{9,17},{1... | collective-permute-start | bytes 786440 | tf_op jit(solution)/shard_map/ppermute | solution.py:41
  99.8 9.4 %collective-permute-start.12 = (bf16[4,256,256]{2,1,0:T(8,128)(2,1)S(1)}, bf16[4,256,256]{2,1,0:T(8,128)(2,1)S(1)}, u32[]{:S(2)}, u32[]{:S(2)}) collective-permute-start(bf16[4,256,256]{2,1,0:T(8,128)(2,1)S(1)} %pad_maximum_fusion), channel_id=1, source_target_pairs={{0,4},{4,0},{8,12},{12,8},{16,20},{20,16},{24,28},{28,24},{1,5},{5... | collective-permute-start | bytes 1572872 | tf_op jit(solution)/shard_map/ppermute | solution.py:44
  110.5 2.3 %collective-permute-start.14 = (bf16[4,256,256]{2,1,0:T(8,128)(2,1)S(1)}, bf16[4,256,256]{2,1,0:T(8,128)(2,1)}, u32[]{:S(2)}, u32[]{:S(2)}) collective-permute-start(bf16[4,256,256]{2,1,0:T(8,128)(2,1)S(1)} %pad_maximum_fusion.2), channel_id=1, source_target_pairs={{0,4},{4,0},{8,12},{12,8},{16,20},{20,16},{24,28},{28,24},{1,5},{5... | collective-permute-start | bytes 1572872 | tf_op jit(solution)/shard_map/ppermute | solution.py:44
  112.7 1.9 %fusion.2 = f32[1,1,2,256,256]{4,3,2,1,0:T(8,128)} fusion(f32[1,1,2,256,256]{4,3,2,1,0:T(8,128)S(1)} %copy-done.8, f32[2,256,256]{2,1,0:T(8,128)S(1)} %convert_reduce_fusion, f32[2]{0:T(128)S(1)} %convert_element_type.35, pred[2]{0:T(512)(128)(4,1)S(1)} %dynamic-slice_reduce_fusion), kind=kOutput, calls=%fused_computation.5 | convolution fusion | flops 403308544 | bytes 1572874 | tf_op jit(solution)/shard_map/sji,sjk->sik/dot_general | solution.py:142
  114.7 1.6 %fusion.5 = f32[1,1,2,256,256]{4,3,2,1,0:T(8,128)} fusion(f32[1,1,2,256,256]{4,3,2,1,0:T(8,128)S(1)} %copy-done.9, f32[2,256,256]{2,1,0:T(8,128)S(1)} %convert_reduce_fusion, f32[2]{0:T(128)S(1)} %convert_element_type.35, pred[2]{0:T(512)(128)(4,1)S(1)} %dynamic-slice_reduce_fusion), kind=kOutput, calls=%fused_computation.9 | convolution fusion | flops 403308544 | bytes 1572874 | tf_op jit(solution)/shard_map/sij,skj->sik/dot_general | solution.py:139
  119.5 3.1 %shard_map.128 = bf16[8,256,256]{2,1,0:T(8,128)(2,1)} custom-call(s32[8,2]{1,0:T(8,128)} %copy.41.table_ref, bf16[2,256,256]{2,1,0:T(8,128)(2,1)} %collective-permute-done.7.refs_0_, bf16[2,256,256]{2,1,0:T(8,128)(2,1)} %copy-done.6, bf16[2,256,256]{2,1,0:T(8,128)(2,1)} %copy-done.4, bf16[2,256,256]{2,1,0:T(8,128)(2,1)} %copy-done.2, ...), custom_call_target="tpu_custom_call" | custom-call | tf_op jit(solution)/shard_map/pallas_call | solution.py:79
  (79 shorter events, 12.3 us)
Async XLA Ops:
  4.6 54.8 %all-to-all-start = ((bf16[8,2,256,256]{3,2,1,0:T(8,128)(2,1)}), bf16[8,2,256,256]{3,2,1,0:T(8,128)(2,1)}, u32[]{:S(2)}, u32[]{:S(2)}) async-start(bf16[8,2,256,256]{3,2,1,0:T(8,128)(2,1)} %bitcast.3), calls=%async_computation | async-start | bytes 4194304 | tf_op jit(solution)/shard_map/all_to_all | solution.py:123
  11.1 50.2 %copy-start.1 = (f32[1,1,2,256,256]{4,3,2,1,0:T(8,128)S(1)}, f32[1,1,2,256,256]{4,3,2,1,0:T(8,128)}, u32[]{:S(2)}) copy-start(f32[1,1,2,256,256]{4,3,2,1,0:T(8,128)} %param.16) | copy-start | bytes 1572868
  11.1 50.7 %copy-start.12 = (bf16[1,1,2,256,256]{4,3,2,1,0:T(8,128)(2,1)S(1)}, bf16[1,1,2,256,256]{4,3,2,1,0:T(8,128)(2,1)}, u32[]{:S(2)}) copy-start(bf16[1,1,2,256,256]{4,3,2,1,0:T(8,128)(2,1)} %param.15) | copy-start | bytes 786436
  12.0 64.2 %copy-start.7 = (f32[1,1,2,256,256]{4,3,2,1,0:T(8,128)S(1)}, f32[1,1,2,256,256]{4,3,2,1,0:T(8,128)}, u32[]{:S(2)}) copy-start(f32[1,1,2,256,256]{4,3,2,1,0:T(8,128)} %param.17) | copy-start | bytes 1572868
  61.3 28.6 %copy-start.14 = (s32[8,1]{0,1:T(1,128)S(1)}, s32[8,1]{0,1:T(1,128)}, u32[]{:S(2)}) copy-start(s32[8,1]{0,1:T(1,128)} %param.10) | copy-start | bytes 100
  63.5 1.8 %collective-permute-start = (f32[2,9]{1,0:T(2,128)S(1)}, f32[2,9]{1,0:T(2,128)S(1)}, u32[]{:S(2)}, u32[]{:S(2)}) collective-permute-start(f32[2,9]{1,0:T(2,128)S(1)} %pad_maximum_fusion.3), channel_id=1, source_target_pairs={{0,4},{4,0},{8,12},{12,8},{16,20},{20,16},{24,28},{28,24},{1,5},{5... | collective-permute-start | bytes 224 | tf_op jit(solution)/shard_map/ppermute | solution.py:20
  65.3 2.5 %collective-permute-start.1 = (f32[2,9]{1,0:T(2,128)S(1)}, f32[2,9]{1,0:T(2,128)S(1)}, u32[]{:S(2)}, u32[]{:S(2)}) collective-permute-start(f32[2,9]{1,0:T(2,128)S(1)} %fusion.29), channel_id=1, source_target_pairs={{0,8},{4,12},{8,0},{12,4},{16,24},{20,28},{24,16},{28,20},{1,9},{5... | collective-permute-start | bytes 224 | tf_op jit(solution)/shard_map/ppermute | solution.py:20
  67.8 3.4 %collective-permute-start.2 = (f32[2,9]{1,0:T(2,128)S(1)}, f32[2,9]{1,0:T(2,128)S(1)}, u32[]{:S(2)}, u32[]{:S(2)}) collective-permute-start(f32[2,9]{1,0:T(2,128)S(1)} %fusion.35), channel_id=1, source_target_pairs={{0,16},{4,20},{8,24},{12,28},{16,0},{20,4},{24,8},{28,12},{1,17},{... | collective-permute-start | bytes 224 | tf_op jit(solution)/shard_map/ppermute | solution.py:20
  71.2 2.4 %collective-permute-start.3 = (f32[2,9]{1,0:T(2,128)S(1)}, f32[2,9]{1,0:T(2,128)S(1)}, u32[]{:S(2)}, u32[]{:S(2)}) collective-permute-start(f32[2,9]{1,0:T(2,128)S(1)} %add.104), channel_id=1, source_target_pairs={{0,1},{1,0},{2,3},{3,2},{4,5},{5,4},{6,7},{7,6},{8,9},{9,8},{10,11... | collective-permute-start | bytes 224 | tf_op jit(solution)/shard_map/ppermute | solution.py:20
  73.6 2.4 %collective-permute-start.4 = (f32[2,9]{1,0:T(2,128)S(1)}, f32[2,9]{1,0:T(2,128)S(1)}, u32[]{:S(2)}, u32[]{:S(2)}) collective-permute-start(f32[2,9]{1,0:T(2,128)S(1)} %add.105), channel_id=1, source_target_pairs={{0,2},{1,3},{2,0},{3,1},{4,6},{5,7},{6,4},{7,5},{8,10},{9,11},{10,... | collective-permute-start | bytes 224 | tf_op jit(solution)/shard_map/ppermute | solution.py:20
  77.2 39.1 %copy-start.2 = (bf16[2,256,256]{2,1,0:T(8,128)(2,1)}, bf16[2,256,256]{2,1,0:T(8,128)(2,1)S(1)}, u32[]{:S(2)}) copy-start(bf16[2,256,256]{2,1,0:T(8,128)(2,1)S(1)} %get-tuple-element.9.refs_3_) | copy-start | bytes 786436
  77.2 7.1 %collective-permute-start.8 = (bf16[2,256,256]{2,1,0:T(8,128)(2,1)S(1)}, bf16[2,256,256]{2,1,0:T(8,128)(2,1)S(1)}, u32[]{:S(2)}, u32[]{:S(2)}) collective-permute-start(bf16[2,256,256]{2,1,0:T(8,128)(2,1)S(1)} %get-tuple-element.9.refs_3_), channel_id=1, source_target_pairs={{8,0},{12,4},{16,8},{20,12},{24,16},{28,20},{9,1},{13,5},{17,9},{2... | collective-permute-start | bytes 786440 | tf_op jit(solution)/shard_map/ppermute | solution.py:42
  78.5 7.3 %collective-permute-start.5 = (bf16[2,256,256]{2,1,0:T(8,128)(2,1)S(1)}, bf16[2,256,256]{2,1,0:T(8,128)(2,1)S(1)}, u32[]{:S(2)}, u32[]{:S(2)}) collective-permute-start(bf16[2,256,256]{2,1,0:T(8,128)(2,1)S(1)} %get-tuple-element.9.refs_3_), channel_id=1, source_target_pairs={{0,8},{4,12},{8,16},{12,20},{16,24},{20,28},{1,9},{5,13},{9,17},{1... | collective-permute-start | bytes 786440 | tf_op jit(solution)/shard_map/ppermute | solution.py:41
  84.3 30.4 %copy-start.3 = (bf16[2,256,256]{2,1,0:T(8,128)(2,1)}, bf16[2,256,256]{2,1,0:T(8,128)(2,1)S(1)}, u32[]{:S(2)}) copy-start(bf16[2,256,256]{2,1,0:T(8,128)(2,1)S(1)} %collective-permute-done.8.refs_4_) | copy-start | bytes 786436
  84.3 8.2 %collective-permute-start.9 = (bf16[2,256,256]{2,1,0:T(8,128)(2,1)S(1)}, bf16[2,256,256]{2,1,0:T(8,128)(2,1)S(1)}, u32[]{:S(2)}, u32[]{:S(2)}) collective-permute-start(bf16[2,256,256]{2,1,0:T(8,128)(2,1)S(1)} %collective-permute-done.8.refs_4_), channel_id=1, source_target_pairs={{8,0},{12,4},{16,8},{20,12},{24,16},{28,20},{9,1},{13,5},{17,9},{2... | collective-permute-start | bytes 786440 | tf_op jit(solution)/shard_map/ppermute | solution.py:42
  85.8 28.9 %copy-start.4 = (bf16[2,256,256]{2,1,0:T(8,128)(2,1)}, bf16[2,256,256]{2,1,0:T(8,128)(2,1)S(1)}, u32[]{:S(2)}) copy-start(bf16[2,256,256]{2,1,0:T(8,128)(2,1)S(1)} %collective-permute-done.5.refs_2_) | copy-start | bytes 786436
  85.8 8.5 %collective-permute-start.6 = (bf16[2,256,256]{2,1,0:T(8,128)(2,1)S(1)}, bf16[2,256,256]{2,1,0:T(8,128)(2,1)S(1)}, u32[]{:S(2)}, u32[]{:S(2)}) collective-permute-start(bf16[2,256,256]{2,1,0:T(8,128)(2,1)S(1)} %collective-permute-done.5.refs_2_), channel_id=1, source_target_pairs={{0,8},{4,12},{8,16},{12,20},{16,24},{20,28},{1,9},{5,13},{9,17},{1... | collective-permute-start | bytes 786440 | tf_op jit(solution)/shard_map/ppermute | solution.py:41
  92.5 22.2 %copy-start.5 = (bf16[2,256,256]{2,1,0:T(8,128)(2,1)}, bf16[2,256,256]{2,1,0:T(8,128)(2,1)S(1)}, u32[]{:S(2)}) copy-start(bf16[2,256,256]{2,1,0:T(8,128)(2,1)S(1)} %collective-permute-done.9.refs_5_) | copy-start | bytes 786436
  92.5 16.9 %collective-permute-start.10 = (bf16[2,256,256]{2,1,0:T(8,128)(2,1)S(1)}, bf16[2,256,256]{2,1,0:T(8,128)(2,1)}, u32[]{:S(2)}, u32[]{:S(2)}) collective-permute-start(bf16[2,256,256]{2,1,0:T(8,128)(2,1)S(1)} %collective-permute-done.9.refs_5_), channel_id=1, source_target_pairs={{8,0},{12,4},{16,8},{20,12},{24,16},{28,20},{9,1},{13,5},{17,9},{2... | collective-permute-start | bytes 786440 | tf_op jit(solution)/shard_map/ppermute | solution.py:42
  94.2 15.1 %collective-permute-start.7 = (bf16[2,256,256]{2,1,0:T(8,128)(2,1)S(1)}, bf16[2,256,256]{2,1,0:T(8,128)(2,1)}, u32[]{:S(2)}, u32[]{:S(2)}) collective-permute-start(bf16[2,256,256]{2,1,0:T(8,128)(2,1)S(1)} %collective-permute-done.6.refs_1_), channel_id=1, source_target_pairs={{0,8},{4,12},{8,16},{12,20},{16,24},{20,28},{1,9},{5,13},{9,17},{1... | collective-permute-start | bytes 786440 | tf_op jit(solution)/shard_map/ppermute | solution.py:41
  99.8 18.1 %collective-permute-start.12 = (bf16[4,256,256]{2,1,0:T(8,128)(2,1)S(1)}, bf16[4,256,256]{2,1,0:T(8,128)(2,1)S(1)}, u32[]{:S(2)}, u32[]{:S(2)}) collective-permute-start(bf16[4,256,256]{2,1,0:T(8,128)(2,1)S(1)} %pad_maximum_fusion), channel_id=1, source_target_pairs={{0,4},{4,0},{8,12},{12,8},{16,20},{20,16},{24,28},{28,24},{1,5},{5... | collective-permute-start | bytes 1572872 | tf_op jit(solution)/shard_map/ppermute | solution.py:44
  109.3 8.6 %collective-permute-start.13 = (bf16[4,256,256]{2,1,0:T(8,128)(2,1)S(1)}, bf16[4,256,256]{2,1,0:T(8,128)(2,1)S(1)}, u32[]{:S(2)}, u32[]{:S(2)}) collective-permute-start(bf16[4,256,256]{2,1,0:T(8,128)(2,1)S(1)} %pad_maximum_fusion.1), channel_id=1, source_target_pairs={{0,4},{4,0},{8,12},{12,8},{16,20},{20,16},{24,28},{28,24},{1,5},{5... | collective-permute-start | bytes 1572872 | tf_op jit(solution)/shard_map/ppermute | solution.py:44
  110.5 9.0 %collective-permute-start.14 = (bf16[4,256,256]{2,1,0:T(8,128)(2,1)S(1)}, bf16[4,256,256]{2,1,0:T(8,128)(2,1)}, u32[]{:S(2)}, u32[]{:S(2)}) collective-permute-start(bf16[4,256,256]{2,1,0:T(8,128)(2,1)S(1)} %pad_maximum_fusion.2), channel_id=1, source_target_pairs={{0,4},{4,0},{8,12},{12,8},{16,20},{20,16},{24,28},{28,24},{1,5},{5... | collective-permute-start | bytes 1572872 | tf_op jit(solution)/shard_map/ppermute | solution.py:44
  116.3 1.5 %collective-permute-start.11 = (bf16[2,256,256]{2,1,0:T(8,128)(2,1)S(1)}, bf16[2,256,256]{2,1,0:T(8,128)(2,1)S(1)}, u32[]{:S(2)}, u32[]{:S(2)}) collective-permute-start(bf16[2,256,256]{2,1,0:T(8,128)(2,1)S(1)} %get-tuple-element.9.refs_3_), channel_id=1, source_target_pairs={{0,4},{4,0},{8,12},{12,8},{16,20},{20,16},{24,28},{28,24},{1,5},{5... | collective-permute-start | bytes 786440 | tf_op jit(solution)/shard_map/ppermute | solution.py:39
  (8 other events, 60.5 us)

commit v20 on v8

--- a/solution.py
+++ b/solution.py
@@ -150,7 +150,7 @@
         "sij,sjk->sik", inner, root_right[0, 0], preferred_element_type=jnp.float32
     )
     prec_terms = jnp.sum(member * jnp.sum(precond * precond, axis=(1, 2))[:, None], axis=0)
-    norms = butterfly_sum(butterfly_sum(jnp.stack([adam_terms, prec_terms]), "dp"), "shard")
+    norms = butterfly_sum(butterfly_sum(jnp.stack([adam_terms, prec_terms]), "shard"), "dp")
     norm_adam = norms[0]
     norm_prec = norms[1]
     scales = jnp.sqrt(norm_adam / (norm_prec + NORM_EPS))

time: 117 us -> 116 us (level)
    ppermute x1, starting transfers between devices: 7.05 us -> 3.78 us  [gather_blocks(): near_left[0] = lax.ppermute(mine, 'dp', partner)]
    ppermute x5, starting transfers between devices: 3.53 us -> 5.81 us  [butterfly_sum(): x = x + lax.ppermute(x, axis, [(i, i ^ step) for i in range(size)])]
where the time goes in v20:
time: 116 us; the launch traced here: 115 us
  waiting for transfers between devices  58.3 us (50%)
  starting transfers between devices  33.6 us (29%)
  matrix products  7.28 us (6%)
  other arithmetic  7.11 us (6%)
  local copies, waits for them, and re-layouts  4.58 us (4%)
  Pallas kernels  3.15 us (3%)
    all_to_all x1, waiting for transfers between devices, local(): received = lax.all_to_all(by_owner, 'dp', 0, 0, tiled=True)  47.4 us
    ppermute x3, starting transfers between devices, gather_blocks(): from_left[step] = lax.ppermute(from_left[step - 1], 'dp', rightward)  10 us
    ppermute x5, waiting for transfers between devices, butterfly_sum(): x = x + lax.ppermute(x, axis, [(i, i ^ step) for i in range(size)])  8.94 us
    all_to_all x1, starting transfers between devices, local(): received = lax.all_to_all(by_owner, 'dp', 0, 0, tiled=True)  6.51 us
    ppermute x5, starting transfers between devices, butterfly_sum(): x = x + lax.ppermute(x, axis, [(i, i ^ step) for i in range(size)])  5.81 us
    ppermute x3, starting transfers between devices, gather_blocks(): from_right[step] = lax.ppermute(from_right[step - 1], 'dp', leftward)  3.88 us
    ppermute x1, starting transfers between devices, gather_blocks(): near_left[0] = lax.ppermute(mine, 'dp', partner)  3.78 us
    ppermute x3, starting transfers between devices, gather_blocks(): near_right[step] = lax.ppermute(from_right[step], 'dp', partner)  3.49 us
  transfers between devices with their start and end apart: 19, of which 7 were waited for; matrix products, arithmetic and copies ran while one was open for 7% of the time, Pallas kernels for 0%

profile of v20, /device:TPU:1, one launch (start us, length us, event | category | flops | bytes accessed | tf_op | source)
XLA Modules:
  0.0 115.0 jit_solution(7454368462978772533)
XLA Ops:
  2.6 2.0 %gather_fusion = bf16[16,256,256]{2,1,0:T(8,128)(2,1)} fusion(bf16[8,256,256]{2,1,0:T(8,128)(2,1)S(1)} %bitcast.52, s32[1024]{0:T(1024)S(1)} %pad_clamp_fusion), kind=kCustom, calls=%fused_computation | custom fusion | bytes 4194368 | tf_op jit(solution)/shard_map/jit(_take)/gather | solution.py:120
  4.6 6.5 %all-to-all-start = ((bf16[8,2,256,256]{3,2,1,0:T(8,128)(2,1)}), bf16[8,2,256,256]{3,2,1,0:T(8,128)(2,1)}, u32[]{:S(2)}, u32[]{:S(2)}) async-start(bf16[8,2,256,256]{3,2,1,0:T(8,128)(2,1)} %bitcast.3), calls=%async_computation | async-start | bytes 4194304 | tf_op jit(solution)/shard_map/all_to_all | solution.py:123
  12.0 47.4 %all-to-all-done = bf16[8,2,256,256]{3,2,1,0:T(8,128)(2,1)} async-done(((bf16[8,2,256,256]{3,2,1,0:T(8,128)(2,1)}), bf16[8,2,256,256]{3,2,1,0:T(8,128)(2,1)}, u32[]{:S(2)}, u32[]{:S(2)}) %all-to-all-start) | async-done | bytes 2097184 | tf_op jit(solution)/shard_map/all_to_all | solution.py:123
  59.4 1.9 %convert_reduce_fusion = f32[2,256,256]{2,1,0:T(8,128)S(1)} fusion(bf16[8,2,256,256]{3,2,1,0:T(8,128)(2,1)} %all-to-all-done), kind=kLoop, calls=%fused_computation.1 | loop fusion | flops 1966080 | bytes 2621440 | tf_op jit(solution)/shard_map/reduce_sum | solution.py:124
  61.8 1.6 %multiply_reduce_fusion = (f32[2]{0:T(128)S(1)}, f32[2,256,256]{2,1,0:T(8,128)S(1)}) fusion(bf16[1,1,2,256,256]{4,3,2,1,0:T(8,128)(2,1)S(1)} %copy-done.4, f32[2,256,256]{2,1,0:T(8,128)S(1)} %convert_reduce_fusion, bf16[1,1,2,256,256]{4,3,2,1,0:T(8,128)(2,1)} %param.14, f32[2]{0:T(128)S(1)} %convert_element_type.35), kind=kOutput, calls=%fused_computation.25 | convolution fusion | flops 134873088 | bytes 1572880 | tf_op jit(solution)/shard_map/sij,sjk->sik/dot_general | solution.py:149
  63.5 1.3 %collective-permute-start = (f32[2,9]{1,0:T(2,128)S(1)}, f32[2,9]{1,0:T(2,128)S(1)}, u32[]{:S(2)}, u32[]{:S(2)}) collective-permute-start(f32[2,9]{1,0:T(2,128)S(1)} %pad_maximum_fusion), channel_id=1, source_target_pairs={{0,1},{1,0},{2,3},{3,2},{4,5},{5,4},{6,7},{7,6},{8,9},{9,8},{10,11... | collective-permute-start | bytes 224 | tf_op jit(solution)/shard_map/ppermute | solution.py:20
  64.8 1.2 %collective-permute-done = f32[2,9]{1,0:T(2,128)S(1)} collective-permute-done((f32[2,9]{1,0:T(2,128)S(1)}, f32[2,9]{1,0:T(2,128)S(1)}, u32[]{:S(2)}, u32[]{:S(2)}) %collective-permute-start) | collective-permute-done | bytes 104 | tf_op jit(solution)/shard_map/ppermute | solution.py:20
  66.0 1.3 %collective-permute-start.1 = (f32[2,9]{1,0:T(2,128)S(1)}, f32[2,9]{1,0:T(2,128)S(1)}, u32[]{:S(2)}, u32[]{:S(2)}) collective-permute-start(f32[2,9]{1,0:T(2,128)S(1)} %fusion.30), channel_id=1, source_target_pairs={{0,2},{1,3},{2,0},{3,1},{4,6},{5,7},{6,4},{7,5},{8,10},{9,11},{10,... | collective-permute-start | bytes 224 | tf_op jit(solution)/shard_map/ppermute | solution.py:20
  67.3 1.2 %collective-permute-done.1 = f32[2,9]{1,0:T(2,128)S(1)} collective-permute-done((f32[2,9]{1,0:T(2,128)S(1)}, f32[2,9]{1,0:T(2,128)S(1)}, u32[]{:S(2)}, u32[]{:S(2)}) %collective-permute-start.1) | collective-permute-done | bytes 104 | tf_op jit(solution)/shard_map/ppermute | solution.py:20
  68.5 3.2 %collective-permute-start.2 = (f32[2,9]{1,0:T(2,128)S(1)}, f32[2,9]{1,0:T(2,128)S(1)}, u32[]{:S(2)}, u32[]{:S(2)}) collective-permute-start(f32[2,9]{1,0:T(2,128)S(1)} %fusion.35), channel_id=1, source_target_pairs={{0,4},{4,0},{8,12},{12,8},{16,20},{20,16},{24,28},{28,24},{1,5},{5... | collective-permute-start | bytes 224 | tf_op jit(solution)/shard_map/ppermute | solution.py:20
  72.6 2.4 %collective-permute-done.3 = f32[2,9]{1,0:T(2,128)S(1)} collective-permute-done((f32[2,9]{1,0:T(2,128)S(1)}, f32[2,9]{1,0:T(2,128)S(1)}, u32[]{:S(2)}, u32[]{:S(2)}) %collective-permute-start.3) | collective-permute-done | bytes 104 | tf_op jit(solution)/shard_map/ppermute | solution.py:20
  75.0 3.3 %collective-permute-done.4 = f32[2,9]{1,0:T(2,128)S(1)} collective-permute-done((f32[2,9]{1,0:T(2,128)S(1)}, f32[2,9]{1,0:T(2,128)S(1)}, u32[]{:S(2)}, u32[]{:S(2)}) %collective-permute-start.4) | collective-permute-done | bytes 104 | tf_op jit(solution)/shard_map/ppermute | solution.py:20
  79.5 1.9 %collective-permute-start.5 = (bf16[2,256,256]{2,1,0:T(8,128)(2,1)S(1)}, bf16[2,256,256]{2,1,0:T(8,128)(2,1)S(1)}, u32[]{:S(2)}, u32[]{:S(2)}) collective-permute-start(bf16[2,256,256]{2,1,0:T(8,128)(2,1)S(1)} %get-tuple-element.7.refs_3_), channel_id=1, source_target_pairs={{0,8},{4,12},{8,16},{12,20},{16,24},{20,28},{1,9},{5,13},{9,17},{1... | collective-permute-start | bytes 786440 | tf_op jit(solution)/shard_map/ppermute | solution.py:44
  81.4 1.3 %collective-permute-start.8 = (bf16[2,256,256]{2,1,0:T(8,128)(2,1)S(1)}, bf16[2,256,256]{2,1,0:T(8,128)(2,1)S(1)}, u32[]{:S(2)}, u32[]{:S(2)}) collective-permute-start(bf16[2,256,256]{2,1,0:T(8,128)(2,1)S(1)} %get-tuple-element.7.refs_3_), channel_id=1, source_target_pairs={{8,0},{12,4},{16,8},{20,12},{24,16},{28,20},{9,1},{13,5},{17,9},{2... | collective-permute-start | bytes 786440 | tf_op jit(solution)/shard_map/ppermute | solution.py:45
  82.8 2.0 %collective-permute-done.5.refs_2_ = bf16[2,256,256]{2,1,0:T(8,128)(2,1)S(1)} collective-permute-done((bf16[2,256,256]{2,1,0:T(8,128)(2,1)S(1)}, bf16[2,256,256]{2,1,0:T(8,128)(2,1)S(1)}, u32[]{:S(2)}, u32[]{:S(2)}) %collective-permute-start.5) | collective-permute-done | bytes 262176 | tf_op jit(solution)/shard_map/ppermute | solution.py:44
  84.7 3.8 %collective-permute-start.6 = (bf16[2,256,256]{2,1,0:T(8,128)(2,1)S(1)}, bf16[2,256,256]{2,1,0:T(8,128)(2,1)S(1)}, u32[]{:S(2)}, u32[]{:S(2)}) collective-permute-start(bf16[2,256,256]{2,1,0:T(8,128)(2,1)S(1)} %collective-permute-done.5.refs_2_), channel_id=1, source_target_pairs={{0,8},{4,12},{8,16},{12,20},{16,24},{20,28},{1,9},{5,13},{9,17},{1... | collective-permute-start | bytes 786440 | tf_op jit(solution)/shard_map/ppermute | solution.py:44
  88.6 1.3 %collective-permute-start.9 = (bf16[2,256,256]{2,1,0:T(8,128)(2,1)S(1)}, bf16[2,256,256]{2,1,0:T(8,128)(2,1)S(1)}, u32[]{:S(2)}, u32[]{:S(2)}) collective-permute-start(bf16[2,256,256]{2,1,0:T(8,128)(2,1)S(1)} %collective-permute-done.8.refs_4_), channel_id=1, source_target_pairs={{8,0},{12,4},{16,8},{20,12},{24,16},{28,20},{9,1},{13,5},{17,9},{2... | collective-permute-start | bytes 786440 | tf_op jit(solution)/shard_map/ppermute | solution.py:45
  90.6 3.8 %collective-permute-start.14 = (bf16[2,256,256]{2,1,0:T(8,128)(2,1)S(1)}, bf16[2,256,256]{2,1,0:T(8,128)(2,1)S(1)}, u32[]{:S(2)}, u32[]{:S(2)}) collective-permute-start(bf16[2,256,256]{2,1,0:T(8,128)(2,1)S(1)} %get-tuple-element.7.refs_3_), channel_id=1, source_target_pairs={{0,4},{4,0},{8,12},{12,8},{16,20},{20,16},{24,28},{28,24},{1,5},{5... | collective-permute-start | bytes 786440 | tf_op jit(solution)/shard_map/ppermute | solution.py:41
  94.4 4.3 %collective-permute-start.7 = (bf16[2,256,256]{2,1,0:T(8,128)(2,1)S(1)}, bf16[2,256,256]{2,1,0:T(8,128)(2,1)S(1)}, u32[]{:S(2)}, u32[]{:S(2)}) collective-permute-start(bf16[2,256,256]{2,1,0:T(8,128)(2,1)S(1)} %collective-permute-done.6.refs_1_), channel_id=1, source_target_pairs={{0,8},{4,12},{8,16},{12,20},{16,24},{20,28},{1,9},{5,13},{9,17},{1... | collective-permute-start | bytes 786440 | tf_op jit(solution)/shard_map/ppermute | solution.py:44
  98.7 1.3 %collective-permute-start.10 = (bf16[2,256,256]{2,1,0:T(8,128)(2,1)S(1)}, bf16[2,256,256]{2,1,0:T(8,128)(2,1)S(1)}, u32[]{:S(2)}, u32[]{:S(2)}) collective-permute-start(bf16[2,256,256]{2,1,0:T(8,128)(2,1)S(1)} %collective-permute-done.9.refs_5_), channel_id=1, source_target_pairs={{8,0},{12,4},{16,8},{20,12},{24,16},{28,20},{9,1},{13,5},{17,9},{2... | collective-permute-start | bytes 786440 | tf_op jit(solution)/shard_map/ppermute | solution.py:45
  100.0 3.0 %fusion.2 = f32[1,1,2,256,256]{4,3,2,1,0:T(8,128)} fusion(f32[1,1,2,256,256]{4,3,2,1,0:T(8,128)} %param.13, f32[2,256,256]{2,1,0:T(8,128)S(1)} %convert_reduce_fusion, f32[2]{0:T(128)S(1)} %convert_element_type.35, pred[2]{0:T(512)(128)(4,1)S(1)} %dynamic-slice_reduce_fusion), kind=kOutput, calls=%fused_computation.5 | convolution fusion | flops 403308544 | bytes 1572874 | tf_op jit(solution)/shard_map/sji,sjk->sik/dot_general | solution.py:142
  103.0 2.7 %fusion.5 = f32[1,1,2,256,256]{4,3,2,1,0:T(8,128)} fusion(f32[1,1,2,256,256]{4,3,2,1,0:T(8,128)} %param.12, f32[2,256,256]{2,1,0:T(8,128)S(1)} %convert_reduce_fusion, f32[2]{0:T(128)S(1)} %convert_element_type.35, pred[2]{0:T(512)(128)(4,1)S(1)} %dynamic-slice_reduce_fusion), kind=kOutput, calls=%fused_computation.9 | convolution fusion | flops 403308544 | bytes 1572874 | tf_op jit(solution)/shard_map/sij,skj->sik/dot_general | solution.py:139
  105.6 1.9 %collective-permute-start.15 = (bf16[2,256,256]{2,1,0:T(8,128)(2,1)S(1)}, bf16[2,256,256]{2,1,0:T(8,128)(2,1)S(1)}, u32[]{:S(2)}, u32[]{:S(2)}) collective-permute-start(bf16[2,256,256]{2,1,0:T(8,128)(2,1)S(1)} %collective-permute-done.8.refs_4_), channel_id=1, source_target_pairs={{0,4},{4,0},{8,12},{12,8},{16,20},{20,16},{24,28},{28,24},{1,5},{5... | collective-permute-start | bytes 786440 | tf_op jit(solution)/shard_map/ppermute | solution.py:47
  111.9 3.2 %shard_map.128 = bf16[8,256,256]{2,1,0:T(8,128)(2,1)} custom-call(s32[8,2]{1,0:T(8,128)} %copy.39.table_ref, bf16[2,256,256]{2,1,0:T(8,128)(2,1)} %copy-done.11, bf16[2,256,256]{2,1,0:T(8,128)(2,1)} %copy-done.7, bf16[2,256,256]{2,1,0:T(8,128)(2,1)} %copy-done.5, bf16[2,256,256]{2,1,0:T(8,128)(2,1)} %copy-done.2, bf16[2,256,256]{2,1,0:T(8,128)(2,1)} %copy-done.6, ...), custom_call_target="tpu_custom_call" | custom-call | tf_op jit(solution)/shard_map/pallas_call | solution.py:79
  (88 shorter events, 10.4 us)
Async XLA Ops:
  4.6 54.8 %all-to-all-start = ((bf16[8,2,256,256]{3,2,1,0:T(8,128)(2,1)}), bf16[8,2,256,256]{3,2,1,0:T(8,128)(2,1)}, u32[]{:S(2)}, u32[]{:S(2)}) async-start(bf16[8,2,256,256]{3,2,1,0:T(8,128)(2,1)} %bitcast.3), calls=%async_computation | async-start | bytes 4194304 | tf_op jit(solution)/shard_map/all_to_all | solution.py:123
  11.1 50.2 %copy-start.1 = (f32[1,1,2,256,256]{4,3,2,1,0:T(8,128)S(1)}, f32[1,1,2,256,256]{4,3,2,1,0:T(8,128)}, u32[]{:S(2)}) copy-start(f32[1,1,2,256,256]{4,3,2,1,0:T(8,128)} %param.16) | copy-start | bytes 1572868
  11.1 50.7 %copy-start.4 = (bf16[1,1,2,256,256]{4,3,2,1,0:T(8,128)(2,1)S(1)}, bf16[1,1,2,256,256]{4,3,2,1,0:T(8,128)(2,1)}, u32[]{:S(2)}) copy-start(bf16[1,1,2,256,256]{4,3,2,1,0:T(8,128)(2,1)} %param.15) | copy-start | bytes 786436
  12.0 66.5 %copy-start.3 = (f32[1,1,2,256,256]{4,3,2,1,0:T(8,128)S(1)}, f32[1,1,2,256,256]{4,3,2,1,0:T(8,128)}, u32[]{:S(2)}) copy-start(f32[1,1,2,256,256]{4,3,2,1,0:T(8,128)} %param.17) | copy-start | bytes 1572868
  61.3 28.5 %copy-start.17 = (s32[8,1]{0,1:T(1,128)S(1)}, s32[8,1]{0,1:T(1,128)}, u32[]{:S(2)}) copy-start(s32[8,1]{0,1:T(1,128)} %param.10) | copy-start | bytes 100
  63.5 2.5 %collective-permute-start = (f32[2,9]{1,0:T(2,128)S(1)}, f32[2,9]{1,0:T(2,128)S(1)}, u32[]{:S(2)}, u32[]{:S(2)}) collective-permute-start(f32[2,9]{1,0:T(2,128)S(1)} %pad_maximum_fusion), channel_id=1, source_target_pairs={{0,1},{1,0},{2,3},{3,2},{4,5},{5,4},{6,7},{7,6},{8,9},{9,8},{10,11... | collective-permute-start | bytes 224 | tf_op jit(solution)/shard_map/ppermute | solution.py:20
  66.0 2.5 %collective-permute-start.1 = (f32[2,9]{1,0:T(2,128)S(1)}, f32[2,9]{1,0:T(2,128)S(1)}, u32[]{:S(2)}, u32[]{:S(2)}) collective-permute-start(f32[2,9]{1,0:T(2,128)S(1)} %fusion.30), channel_id=1, source_target_pairs={{0,2},{1,3},{2,0},{3,1},{4,6},{5,7},{6,4},{7,5},{8,10},{9,11},{10,... | collective-permute-start | bytes 224 | tf_op jit(solution)/shard_map/ppermute | solution.py:20
  68.5 4.1 %collective-permute-start.2 = (f32[2,9]{1,0:T(2,128)S(1)}, f32[2,9]{1,0:T(2,128)S(1)}, u32[]{:S(2)}, u32[]{:S(2)}) collective-permute-start(f32[2,9]{1,0:T(2,128)S(1)} %fusion.35), channel_id=1, source_target_pairs={{0,4},{4,0},{8,12},{12,8},{16,20},{20,16},{24,28},{28,24},{1,5},{5... | collective-permute-start | bytes 224 | tf_op jit(solution)/shard_map/ppermute | solution.py:20
  72.6 2.4 %collective-permute-start.3 = (f32[2,9]{1,0:T(2,128)S(1)}, f32[2,9]{1,0:T(2,128)S(1)}, u32[]{:S(2)}, u32[]{:S(2)}) collective-permute-start(f32[2,9]{1,0:T(2,128)S(1)} %add.92), channel_id=1, source_target_pairs={{0,8},{4,12},{8,0},{12,4},{16,24},{20,28},{24,16},{28,20},{1,9},{5... | collective-permute-start | bytes 224 | tf_op jit(solution)/shard_map/ppermute | solution.py:20
  75.0 3.3 %collective-permute-start.4 = (f32[2,9]{1,0:T(2,128)S(1)}, f32[2,9]{1,0:T(2,128)S(1)}, u32[]{:S(2)}, u32[]{:S(2)}) collective-permute-start(f32[2,9]{1,0:T(2,128)S(1)} %add.93), channel_id=1, source_target_pairs={{0,16},{4,20},{8,24},{12,28},{16,0},{20,4},{24,8},{28,12},{1,17},{... | collective-permute-start | bytes 224 | tf_op jit(solution)/shard_map/ppermute | solution.py:20
  79.5 30.8 %copy-start.2 = (bf16[2,256,256]{2,1,0:T(8,128)(2,1)}, bf16[2,256,256]{2,1,0:T(8,128)(2,1)S(1)}, u32[]{:S(2)}) copy-start(bf16[2,256,256]{2,1,0:T(8,128)(2,1)S(1)} %get-tuple-element.7.refs_3_) | copy-start | bytes 786436
  79.5 5.2 %collective-permute-start.5 = (bf16[2,256,256]{2,1,0:T(8,128)(2,1)S(1)}, bf16[2,256,256]{2,1,0:T(8,128)(2,1)S(1)}, u32[]{:S(2)}, u32[]{:S(2)}) collective-permute-start(bf16[2,256,256]{2,1,0:T(8,128)(2,1)S(1)} %get-tuple-element.7.refs_3_), channel_id=1, source_target_pairs={{0,8},{4,12},{8,16},{12,20},{16,24},{20,28},{1,9},{5,13},{9,17},{1... | collective-permute-start | bytes 786440 | tf_op jit(solution)/shard_map/ppermute | solution.py:44
  81.4 7.1 %collective-permute-start.8 = (bf16[2,256,256]{2,1,0:T(8,128)(2,1)S(1)}, bf16[2,256,256]{2,1,0:T(8,128)(2,1)S(1)}, u32[]{:S(2)}, u32[]{:S(2)}) collective-permute-start(bf16[2,256,256]{2,1,0:T(8,128)(2,1)S(1)} %get-tuple-element.7.refs_3_), channel_id=1, source_target_pairs={{8,0},{12,4},{16,8},{20,12},{24,16},{28,20},{9,1},{13,5},{17,9},{2... | collective-permute-start | bytes 786440 | tf_op jit(solution)/shard_map/ppermute | solution.py:45
  84.7 9.6 %collective-permute-start.6 = (bf16[2,256,256]{2,1,0:T(8,128)(2,1)S(1)}, bf16[2,256,256]{2,1,0:T(8,128)(2,1)S(1)}, u32[]{:S(2)}, u32[]{:S(2)}) collective-permute-start(bf16[2,256,256]{2,1,0:T(8,128)(2,1)S(1)} %collective-permute-done.5.refs_2_), channel_id=1, source_target_pairs={{0,8},{4,12},{8,16},{12,20},{16,24},{20,28},{1,9},{5,13},{9,17},{1... | collective-permute-start | bytes 786440 | tf_op jit(solution)/shard_map/ppermute | solution.py:44
  88.6 10.1 %collective-permute-start.9 = (bf16[2,256,256]{2,1,0:T(8,128)(2,1)S(1)}, bf16[2,256,256]{2,1,0:T(8,128)(2,1)S(1)}, u32[]{:S(2)}, u32[]{:S(2)}) collective-permute-start(bf16[2,256,256]{2,1,0:T(8,128)(2,1)S(1)} %collective-permute-done.8.refs_4_), channel_id=1, source_target_pairs={{8,0},{12,4},{16,8},{20,12},{24,16},{28,20},{9,1},{13,5},{17,9},{2... | collective-permute-start | bytes 786440 | tf_op jit(solution)/shard_map/ppermute | solution.py:45
  90.6 17.0 %collective-permute-start.14 = (bf16[2,256,256]{2,1,0:T(8,128)(2,1)S(1)}, bf16[2,256,256]{2,1,0:T(8,128)(2,1)S(1)}, u32[]{:S(2)}, u32[]{:S(2)}) collective-permute-start(bf16[2,256,256]{2,1,0:T(8,128)(2,1)S(1)} %get-tuple-element.7.refs_3_), channel_id=1, source_target_pairs={{0,4},{4,0},{8,12},{12,8},{16,20},{20,16},{24,28},{28,24},{1,5},{5... | collective-permute-start | bytes 786440 | tf_op jit(solution)/shard_map/ppermute | solution.py:41
  94.3 13.3 %collective-permute-start.13 = (bf16[2,256,256]{2,1,0:T(8,128)(2,1)S(1)}, bf16[2,256,256]{2,1,0:T(8,128)(2,1)S(1)}, u32[]{:S(2)}, u32[]{:S(2)}) collective-permute-start(bf16[2,256,256]{2,1,0:T(8,128)(2,1)S(1)} %collective-permute-done.5.refs_2_), channel_id=1, source_target_pairs={{0,4},{4,0},{8,12},{12,8},{16,20},{20,16},{24,28},{28,24},{1,5},{5... | collective-permute-start | bytes 786440 | tf_op jit(solution)/shard_map/ppermute | solution.py:46
  94.4 13.7 %collective-permute-start.7 = (bf16[2,256,256]{2,1,0:T(8,128)(2,1)S(1)}, bf16[2,256,256]{2,1,0:T(8,128)(2,1)S(1)}, u32[]{:S(2)}, u32[]{:S(2)}) collective-permute-start(bf16[2,256,256]{2,1,0:T(8,128)(2,1)S(1)} %collective-permute-done.6.refs_1_), channel_id=1, source_target_pairs={{0,8},{4,12},{8,16},{12,20},{16,24},{20,28},{1,9},{5,13},{9,17},{1... | collective-permute-start | bytes 786440 | tf_op jit(solution)/shard_map/ppermute | solution.py:44
  98.7 9.5 %collective-permute-start.10 = (bf16[2,256,256]{2,1,0:T(8,128)(2,1)S(1)}, bf16[2,256,256]{2,1,0:T(8,128)(2,1)S(1)}, u32[]{:S(2)}, u32[]{:S(2)}) collective-permute-start(bf16[2,256,256]{2,1,0:T(8,128)(2,1)S(1)} %collective-permute-done.9.refs_5_), channel_id=1, source_target_pairs={{8,0},{12,4},{16,8},{20,12},{24,16},{28,20},{9,1},{13,5},{17,9},{2... | collective-permute-start | bytes 786440 | tf_op jit(solution)/shard_map/ppermute | solution.py:45
  105.6 4.7 %collective-permute-start.15 = (bf16[2,256,256]{2,1,0:T(8,128)(2,1)S(1)}, bf16[2,256,256]{2,1,0:T(8,128)(2,1)S(1)}, u32[]{:S(2)}, u32[]{:S(2)}) collective-permute-start(bf16[2,256,256]{2,1,0:T(8,128)(2,1)S(1)} %collective-permute-done.8.refs_4_), channel_id=1, source_target_pairs={{0,4},{4,0},{8,12},{12,8},{16,20},{20,16},{24,28},{28,24},{1,5},{5... | collective-permute-start | bytes 786440 | tf_op jit(solution)/shard_map/ppermute | solution.py:47
  107.5 2.8 %collective-permute-start.12 = (bf16[2,256,256]{2,1,0:T(8,128)(2,1)S(1)}, bf16[2,256,256]{2,1,0:T(8,128)(2,1)S(1)}, u32[]{:S(2)}, u32[]{:S(2)}) collective-permute-start(bf16[2,256,256]{2,1,0:T(8,128)(2,1)S(1)} %collective-permute-done.6.refs_1_), channel_id=1, source_target_pairs={{0,4},{4,0},{8,12},{12,8},{16,20},{20,16},{24,28},{28,24},{1,5},{5... | collective-permute-start | bytes 786440 | tf_op jit(solution)/shard_map/ppermute | solution.py:46
  107.6 2.7 %collective-permute-start.16 = (bf16[2,256,256]{2,1,0:T(8,128)(2,1)S(1)}, bf16[2,256,256]{2,1,0:T(8,128)(2,1)S(1)}, u32[]{:S(2)}, u32[]{:S(2)}) collective-permute-start(bf16[2,256,256]{2,1,0:T(8,128)(2,1)S(1)} %collective-permute-done.9.refs_5_), channel_id=1, source_target_pairs={{0,4},{4,0},{8,12},{12,8},{16,20},{20,16},{24,28},{28,24},{1,5},{5... | collective-permute-start | bytes 786440 | tf_op jit(solution)/shard_map/ppermute | solution.py:47
  108.1 2.3 %collective-permute-start.11 = (bf16[2,256,256]{2,1,0:T(8,128)(2,1)S(1)}, bf16[2,256,256]{2,1,0:T(8,128)(2,1)S(1)}, u32[]{:S(2)}, u32[]{:S(2)}) collective-permute-start(bf16[2,256,256]{2,1,0:T(8,128)(2,1)S(1)} %collective-permute-done.7.refs_0_), channel_id=1, source_target_pairs={{0,4},{4,0},{8,12},{12,8},{16,20},{20,16},{24,28},{28,24},{1,5},{5... | collective-permute-start | bytes 786440 | tf_op jit(solution)/shard_map/ppermute | solution.py:46
  108.2 3.7 %collective-permute-start.17 = (bf16[2,256,256]{2,1,0:T(8,128)(2,1)S(1)}, bf16[2,256,256]{2,1,0:T(8,128)(2,1)}, u32[]{:S(2)}, u32[]{:S(2)}) collective-permute-start(bf16[2,256,256]{2,1,0:T(8,128)(2,1)S(1)} %collective-permute-done.10.refs_6_), channel_id=1, source_target_pairs={{0,4},{4,0},{8,12},{12,8},{16,20},{20,16},{24,28},{28,24},{1,5},{5... | collective-permute-start | bytes 786440 | tf_op jit(solution)/shard_map/ppermute | solution.py:47
  (14 other events, 96.7 us)

commit v21 on v20

--- a/solution.py
+++ b/solution.py
@@ -15,10 +15,10 @@
     size = lax.axis_size(axis)
     if size & (size - 1):
         return lax.psum(x, axis)
-    step = 1
-    while step < size:
+    step = size // 2
+    while step:
         x = x + lax.ppermute(x, axis, [(i, i ^ step) for i in range(size)])
-        step *= 2
+        step //= 2
     return x
 
 

time: 116 us -> 118 us (1.017)
  waiting for transfers between devices: 58.3 us -> 61.3 us
    ppermute x3, waiting for transfers between devices: 1.96 us -> 4.96 us  [gather_blocks(): from_left[step] = lax.ppermute(from_left[step - 1], 'dp', rightward)]
    ppermute x1, starting transfers between devices: 3.78 us -> 1.43 us  [gather_blocks(): near_left[0] = lax.ppermute(mine, 'dp', partner)]
    ppermute x5, starting transfers between devices: 5.81 us -> 8.12 us  [butterfly_sum(): x = x + lax.ppermute(x, axis, [(i, i ^ step) for i in range(size)])]
  transfers between devices with their start and end apart: 19 -> 19, of which waited for: 7 -> 8; matrix products, arithmetic and copies ran while one was open for 7% -> 7% of each run, Pallas kernels for 0% -> 0%
where the time goes in v21:
time: 118 us
  waiting for transfers between devices  61.3 us (52%)
  starting transfers between devices  33.4 us (28%)
  matrix products  7.28 us (6%)
  other arithmetic  7.11 us (6%)
  local copies, waits for them, and re-layouts  4.58 us (4%)
  Pallas kernels  3.12 us (3%)
    all_to_all x1, waiting for transfers between devices, local(): received = lax.all_to_all(by_owner, 'dp', 0, 0, tiled=True)  47.4 us
    ppermute x3, starting transfers between devices, gather_blocks(): from_left[step] = lax.ppermute(from_left[step - 1], 'dp', rightward)  9.85 us
    ppermute x5, waiting for transfers between devices, butterfly_sum(): x = x + lax.ppermute(x, axis, [(i, i ^ step) for i in range(size)])  8.93 us
    ppermute x5, starting transfers between devices, butterfly_sum(): x = x + lax.ppermute(x, axis, [(i, i ^ step) for i in range(size)])  8.12 us
    all_to_all x1, starting transfers between devices, local(): received = lax.all_to_all(by_owner, 'dp', 0, 0, tiled=True)  6.51 us
    ppermute x3, waiting for transfers between devices, gather_blocks(): from_left[step] = lax.ppermute(from_left[step - 1], 'dp', rightward)  4.96 us
    ppermute x3, starting transfers between devices, gather_blocks(): from_right[step] = lax.ppermute(from_right[step - 1], 'dp', leftward)  3.88 us
    ppermute x3, starting transfers between devices, gather_blocks(): near_right[step] = lax.ppermute(from_right[step], 'dp', partner)  3.49 us
  transfers between devices with their start and end apart: 19, of which 8 were waited for; matrix products, arithmetic and copies ran while one was open for 7% of the time, Pallas kernels for 0%

profile of v21, /device:TPU:1, one launch (start us, length us, event | category | flops | bytes accessed | tf_op | source)
XLA Modules:
  0.0 117.8 jit_solution(9830918718747300737)
XLA Ops:
  2.6 2.0 %gather_fusion = bf16[16,256,256]{2,1,0:T(8,128)(2,1)} fusion(bf16[8,256,256]{2,1,0:T(8,128)(2,1)S(1)} %bitcast.52, s32[1024]{0:T(1024)S(1)} %pad_clamp_fusion), kind=kCustom, calls=%fused_computation | custom fusion | bytes 4194368 | tf_op jit(solution)/shard_map/jit(_take)/gather | solution.py:120
  4.6 6.5 %all-to-all-start = ((bf16[8,2,256,256]{3,2,1,0:T(8,128)(2,1)}), bf16[8,2,256,256]{3,2,1,0:T(8,128)(2,1)}, u32[]{:S(2)}, u32[]{:S(2)}) async-start(bf16[8,2,256,256]{3,2,1,0:T(8,128)(2,1)} %bitcast.3), calls=%async_computation | async-start | bytes 4194304 | tf_op jit(solution)/shard_map/all_to_all | solution.py:123
  12.0 47.4 %all-to-all-done = bf16[8,2,256,256]{3,2,1,0:T(8,128)(2,1)} async-done(((bf16[8,2,256,256]{3,2,1,0:T(8,128)(2,1)}), bf16[8,2,256,256]{3,2,1,0:T(8,128)(2,1)}, u32[]{:S(2)}, u32[]{:S(2)}) %all-to-all-start) | async-done | bytes 2097184 | tf_op jit(solution)/shard_map/all_to_all | solution.py:123
  59.4 1.9 %convert_reduce_fusion = f32[2,256,256]{2,1,0:T(8,128)S(1)} fusion(bf16[8,2,256,256]{3,2,1,0:T(8,128)(2,1)} %all-to-all-done), kind=kLoop, calls=%fused_computation.1 | loop fusion | flops 1966080 | bytes 2621440 | tf_op jit(solution)/shard_map/reduce_sum | solution.py:124
  61.8 1.6 %multiply_reduce_fusion = (f32[2]{0:T(128)S(1)}, f32[2,256,256]{2,1,0:T(8,128)S(1)}) fusion(bf16[1,1,2,256,256]{4,3,2,1,0:T(8,128)(2,1)S(1)} %copy-done.4, f32[2,256,256]{2,1,0:T(8,128)S(1)} %convert_reduce_fusion, bf16[1,1,2,256,256]{4,3,2,1,0:T(8,128)(2,1)} %param.14, f32[2]{0:T(128)S(1)} %convert_element_type.35), kind=kOutput, calls=%fused_computation.25 | convolution fusion | flops 134873088 | bytes 1572880 | tf_op jit(solution)/shard_map/sij,sjk->sik/dot_general | solution.py:149
  63.5 1.3 %collective-permute-start = (f32[2,9]{1,0:T(2,128)S(1)}, f32[2,9]{1,0:T(2,128)S(1)}, u32[]{:S(2)}, u32[]{:S(2)}) collective-permute-start(f32[2,9]{1,0:T(2,128)S(1)} %pad_maximum_fusion), channel_id=1, source_target_pairs={{0,2},{1,3},{2,0},{3,1},{4,6},{5,7},{6,4},{7,5},{8,10},{9,11},{10,... | collective-permute-start | bytes 224 | tf_op jit(solution)/shard_map/ppermute | solution.py:20
  64.8 1.2 %collective-permute-done = f32[2,9]{1,0:T(2,128)S(1)} collective-permute-done((f32[2,9]{1,0:T(2,128)S(1)}, f32[2,9]{1,0:T(2,128)S(1)}, u32[]{:S(2)}, u32[]{:S(2)}) %collective-permute-start) | collective-permute-done | bytes 104 | tf_op jit(solution)/shard_map/ppermute | solution.py:20
  66.0 1.3 %collective-permute-start.1 = (f32[2,9]{1,0:T(2,128)S(1)}, f32[2,9]{1,0:T(2,128)S(1)}, u32[]{:S(2)}, u32[]{:S(2)}) collective-permute-start(f32[2,9]{1,0:T(2,128)S(1)} %fusion.30), channel_id=1, source_target_pairs={{0,1},{1,0},{2,3},{3,2},{4,5},{5,4},{6,7},{7,6},{8,9},{9,8},{10,11... | collective-permute-start | bytes 224 | tf_op jit(solution)/shard_map/ppermute | solution.py:20
  67.3 1.2 %collective-permute-done.1 = f32[2,9]{1,0:T(2,128)S(1)} collective-permute-done((f32[2,9]{1,0:T(2,128)S(1)}, f32[2,9]{1,0:T(2,128)S(1)}, u32[]{:S(2)}, u32[]{:S(2)}) %collective-permute-start.1) | collective-permute-done | bytes 104 | tf_op jit(solution)/shard_map/ppermute | solution.py:20
  68.6 3.3 %collective-permute-done.2 = f32[2,9]{1,0:T(2,128)S(1)} collective-permute-done((f32[2,9]{1,0:T(2,128)S(1)}, f32[2,9]{1,0:T(2,128)S(1)}, u32[]{:S(2)}, u32[]{:S(2)}) %collective-permute-start.2) | collective-permute-done | bytes 104 | tf_op jit(solution)/shard_map/ppermute | solution.py:20
  71.9 2.4 %collective-permute-done.3 = f32[2,9]{1,0:T(2,128)S(1)} collective-permute-done((f32[2,9]{1,0:T(2,128)S(1)}, f32[2,9]{1,0:T(2,128)S(1)}, u32[]{:S(2)}, u32[]{:S(2)}) %collective-permute-start.3) | collective-permute-done | bytes 104 | tf_op jit(solution)/shard_map/ppermute | solution.py:20
  74.4 5.5 %collective-permute-start.4 = (f32[2,9]{1,0:T(2,128)S(1)}, f32[2,9]{1,0:T(2,128)S(1)}, u32[]{:S(2)}, u32[]{:S(2)}) collective-permute-start(f32[2,9]{1,0:T(2,128)S(1)} %add.93), channel_id=1, source_target_pairs={{0,4},{4,0},{8,12},{12,8},{16,20},{20,16},{24,28},{28,24},{1,5},{5... | collective-permute-start | bytes 224 | tf_op jit(solution)/shard_map/ppermute | solution.py:20
  81.8 1.6 %collective-permute-start.5 = (bf16[2,256,256]{2,1,0:T(8,128)(2,1)S(1)}, bf16[2,256,256]{2,1,0:T(8,128)(2,1)S(1)}, u32[]{:S(2)}, u32[]{:S(2)}) collective-permute-start(bf16[2,256,256]{2,1,0:T(8,128)(2,1)S(1)} %get-tuple-element.7.refs_3_), channel_id=1, source_target_pairs={{0,8},{4,12},{8,16},{12,20},{16,24},{20,28},{1,9},{5,13},{9,17},{1... | collective-permute-start | bytes 786440 | tf_op jit(solution)/shard_map/ppermute | solution.py:44
  83.4 1.3 %collective-permute-start.8 = (bf16[2,256,256]{2,1,0:T(8,128)(2,1)S(1)}, bf16[2,256,256]{2,1,0:T(8,128)(2,1)S(1)}, u32[]{:S(2)}, u32[]{:S(2)}) collective-permute-start(bf16[2,256,256]{2,1,0:T(8,128)(2,1)S(1)} %get-tuple-element.7.refs_3_), channel_id=1, source_target_pairs={{8,0},{12,4},{16,8},{20,12},{24,16},{28,20},{9,1},{13,5},{17,9},{2... | collective-permute-start | bytes 786440 | tf_op jit(solution)/shard_map/ppermute | solution.py:45
  84.8 4.0 %collective-permute-done.5.refs_2_ = bf16[2,256,256]{2,1,0:T(8,128)(2,1)S(1)} collective-permute-done((bf16[2,256,256]{2,1,0:T(8,128)(2,1)S(1)}, bf16[2,256,256]{2,1,0:T(8,128)(2,1)S(1)}, u32[]{:S(2)}, u32[]{:S(2)}) %collective-permute-start.5) | collective-permute-done | bytes 262176 | tf_op jit(solution)/shard_map/ppermute | solution.py:44
  88.8 4.1 %collective-permute-start.6 = (bf16[2,256,256]{2,1,0:T(8,128)(2,1)S(1)}, bf16[2,256,256]{2,1,0:T(8,128)(2,1)S(1)}, u32[]{:S(2)}, u32[]{:S(2)}) collective-permute-start(bf16[2,256,256]{2,1,0:T(8,128)(2,1)S(1)} %collective-permute-done.5.refs_2_), channel_id=1, source_target_pairs={{0,8},{4,12},{8,16},{12,20},{16,24},{20,28},{1,9},{5,13},{9,17},{1... | collective-permute-start | bytes 786440 | tf_op jit(solution)/shard_map/ppermute | solution.py:44
  92.9 1.3 %collective-permute-start.9 = (bf16[2,256,256]{2,1,0:T(8,128)(2,1)S(1)}, bf16[2,256,256]{2,1,0:T(8,128)(2,1)S(1)}, u32[]{:S(2)}, u32[]{:S(2)}) collective-permute-start(bf16[2,256,256]{2,1,0:T(8,128)(2,1)S(1)} %collective-permute-done.8.refs_4_), channel_id=1, source_target_pairs={{8,0},{12,4},{16,8},{20,12},{24,16},{28,20},{9,1},{13,5},{17,9},{2... | collective-permute-start | bytes 786440 | tf_op jit(solution)/shard_map/ppermute | solution.py:45
  94.9 1.4 %collective-permute-start.14 = (bf16[2,256,256]{2,1,0:T(8,128)(2,1)S(1)}, bf16[2,256,256]{2,1,0:T(8,128)(2,1)S(1)}, u32[]{:S(2)}, u32[]{:S(2)}) collective-permute-start(bf16[2,256,256]{2,1,0:T(8,128)(2,1)S(1)} %get-tuple-element.7.refs_3_), channel_id=1, source_target_pairs={{0,4},{4,0},{8,12},{12,8},{16,20},{20,16},{24,28},{28,24},{1,5},{5... | collective-permute-start | bytes 786440 | tf_op jit(solution)/shard_map/ppermute | solution.py:41
  97.3 4.1 %collective-permute-start.7 = (bf16[2,256,256]{2,1,0:T(8,128)(2,1)S(1)}, bf16[2,256,256]{2,1,0:T(8,128)(2,1)S(1)}, u32[]{:S(2)}, u32[]{:S(2)}) collective-permute-start(bf16[2,256,256]{2,1,0:T(8,128)(2,1)S(1)} %collective-permute-done.6.refs_1_), channel_id=1, source_target_pairs={{0,8},{4,12},{8,16},{12,20},{16,24},{20,28},{1,9},{5,13},{9,17},{1... | collective-permute-start | bytes 786440 | tf_op jit(solution)/shard_map/ppermute | solution.py:44
  101.5 1.3 %collective-permute-start.10 = (bf16[2,256,256]{2,1,0:T(8,128)(2,1)S(1)}, bf16[2,256,256]{2,1,0:T(8,128)(2,1)S(1)}, u32[]{:S(2)}, u32[]{:S(2)}) collective-permute-start(bf16[2,256,256]{2,1,0:T(8,128)(2,1)S(1)} %collective-permute-done.9.refs_5_), channel_id=1, source_target_pairs={{8,0},{12,4},{16,8},{20,12},{24,16},{28,20},{9,1},{13,5},{17,9},{2... | collective-permute-start | bytes 786440 | tf_op jit(solution)/shard_map/ppermute | solution.py:45
  102.8 3.0 %fusion.2 = f32[1,1,2,256,256]{4,3,2,1,0:T(8,128)} fusion(f32[1,1,2,256,256]{4,3,2,1,0:T(8,128)} %param.13, f32[2,256,256]{2,1,0:T(8,128)S(1)} %convert_reduce_fusion, f32[2]{0:T(128)S(1)} %convert_element_type.35, pred[2]{0:T(512)(128)(4,1)S(1)} %dynamic-slice_reduce_fusion), kind=kOutput, calls=%fused_computation.5 | convolution fusion | flops 403308544 | bytes 1572874 | tf_op jit(solution)/shard_map/sji,sjk->sik/dot_general | solution.py:142
  105.8 2.7 %fusion.5 = f32[1,1,2,256,256]{4,3,2,1,0:T(8,128)} fusion(f32[1,1,2,256,256]{4,3,2,1,0:T(8,128)} %param.12, f32[2,256,256]{2,1,0:T(8,128)S(1)} %convert_reduce_fusion, f32[2]{0:T(128)S(1)} %convert_element_type.35, pred[2]{0:T(512)(128)(4,1)S(1)} %dynamic-slice_reduce_fusion), kind=kOutput, calls=%fused_computation.9 | convolution fusion | flops 403308544 | bytes 1572874 | tf_op jit(solution)/shard_map/sij,skj->sik/dot_general | solution.py:139
  108.4 2.3 %collective-permute-start.15 = (bf16[2,256,256]{2,1,0:T(8,128)(2,1)S(1)}, bf16[2,256,256]{2,1,0:T(8,128)(2,1)S(1)}, u32[]{:S(2)}, u32[]{:S(2)}) collective-permute-start(bf16[2,256,256]{2,1,0:T(8,128)(2,1)S(1)} %collective-permute-done.8.refs_4_), channel_id=1, source_target_pairs={{0,4},{4,0},{8,12},{12,8},{16,20},{20,16},{24,28},{28,24},{1,5},{5... | collective-permute-start | bytes 786440 | tf_op jit(solution)/shard_map/ppermute | solution.py:47
  114.7 3.1 %shard_map.128 = bf16[8,256,256]{2,1,0:T(8,128)(2,1)} custom-call(s32[8,2]{1,0:T(8,128)} %copy.39.table_ref, bf16[2,256,256]{2,1,0:T(8,128)(2,1)} %copy-done.11, bf16[2,256,256]{2,1,0:T(8,128)(2,1)} %copy-done.7, bf16[2,256,256]{2,1,0:T(8,128)(2,1)} %copy-done.5, bf16[2,256,256]{2,1,0:T(8,128)(2,1)} %copy-done.2, bf16[2,256,256]{2,1,0:T(8,128)(2,1)} %copy-done.6, ...), custom_call_target="tpu_custom_call" | custom-call | tf_op jit(solution)/shard_map/pallas_call | solution.py:79
  (88 shorter events, 11.0 us)
Async XLA Ops:
  4.6 54.8 %all-to-all-start = ((bf16[8,2,256,256]{3,2,1,0:T(8,128)(2,1)}), bf16[8,2,256,256]{3,2,1,0:T(8,128)(2,1)}, u32[]{:S(2)}, u32[]{:S(2)}) async-start(bf16[8,2,256,256]{3,2,1,0:T(8,128)(2,1)} %bitcast.3), calls=%async_computation | async-start | bytes 4194304 | tf_op jit(solution)/shard_map/all_to_all | solution.py:123
  11.1 50.2 %copy-start.1 = (f32[1,1,2,256,256]{4,3,2,1,0:T(8,128)S(1)}, f32[1,1,2,256,256]{4,3,2,1,0:T(8,128)}, u32[]{:S(2)}) copy-start(f32[1,1,2,256,256]{4,3,2,1,0:T(8,128)} %param.16) | copy-start | bytes 1572868
  11.1 50.7 %copy-start.4 = (bf16[1,1,2,256,256]{4,3,2,1,0:T(8,128)(2,1)S(1)}, bf16[1,1,2,256,256]{4,3,2,1,0:T(8,128)(2,1)}, u32[]{:S(2)}) copy-start(bf16[1,1,2,256,256]{4,3,2,1,0:T(8,128)(2,1)} %param.15) | copy-start | bytes 786436
  12.0 68.8 %copy-start.3 = (f32[1,1,2,256,256]{4,3,2,1,0:T(8,128)S(1)}, f32[1,1,2,256,256]{4,3,2,1,0:T(8,128)}, u32[]{:S(2)}) copy-start(f32[1,1,2,256,256]{4,3,2,1,0:T(8,128)} %param.17) | copy-start | bytes 1572868
  61.3 32.9 %copy-start.17 = (s32[8,1]{0,1:T(1,128)S(1)}, s32[8,1]{0,1:T(1,128)}, u32[]{:S(2)}) copy-start(s32[8,1]{0,1:T(1,128)} %param.10) | copy-start | bytes 100
  63.5 2.5 %collective-permute-start = (f32[2,9]{1,0:T(2,128)S(1)}, f32[2,9]{1,0:T(2,128)S(1)}, u32[]{:S(2)}, u32[]{:S(2)}) collective-permute-start(f32[2,9]{1,0:T(2,128)S(1)} %pad_maximum_fusion), channel_id=1, source_target_pairs={{0,2},{1,3},{2,0},{3,1},{4,6},{5,7},{6,4},{7,5},{8,10},{9,11},{10,... | collective-permute-start | bytes 224 | tf_op jit(solution)/shard_map/ppermute | solution.py:20
  66.0 2.5 %collective-permute-start.1 = (f32[2,9]{1,0:T(2,128)S(1)}, f32[2,9]{1,0:T(2,128)S(1)}, u32[]{:S(2)}, u32[]{:S(2)}) collective-permute-start(f32[2,9]{1,0:T(2,128)S(1)} %fusion.30), channel_id=1, source_target_pairs={{0,1},{1,0},{2,3},{3,2},{4,5},{5,4},{6,7},{7,6},{8,9},{9,8},{10,11... | collective-permute-start | bytes 224 | tf_op jit(solution)/shard_map/ppermute | solution.py:20
  68.5 3.4 %collective-permute-start.2 = (f32[2,9]{1,0:T(2,128)S(1)}, f32[2,9]{1,0:T(2,128)S(1)}, u32[]{:S(2)}, u32[]{:S(2)}) collective-permute-start(f32[2,9]{1,0:T(2,128)S(1)} %fusion.35), channel_id=1, source_target_pairs={{0,16},{4,20},{8,24},{12,28},{16,0},{20,4},{24,8},{28,12},{1,17},{... | collective-permute-start | bytes 224 | tf_op jit(solution)/shard_map/ppermute | solution.py:20
  71.9 2.4 %collective-permute-start.3 = (f32[2,9]{1,0:T(2,128)S(1)}, f32[2,9]{1,0:T(2,128)S(1)}, u32[]{:S(2)}, u32[]{:S(2)}) collective-permute-start(f32[2,9]{1,0:T(2,128)S(1)} %add.92), channel_id=1, source_target_pairs={{0,8},{4,12},{8,0},{12,4},{16,24},{20,28},{24,16},{28,20},{1,9},{5... | collective-permute-start | bytes 224 | tf_op jit(solution)/shard_map/ppermute | solution.py:20
  74.4 6.3 %collective-permute-start.4 = (f32[2,9]{1,0:T(2,128)S(1)}, f32[2,9]{1,0:T(2,128)S(1)}, u32[]{:S(2)}, u32[]{:S(2)}) collective-permute-start(f32[2,9]{1,0:T(2,128)S(1)} %add.93), channel_id=1, source_target_pairs={{0,4},{4,0},{8,12},{12,8},{16,20},{20,16},{24,28},{28,24},{1,5},{5... | collective-permute-start | bytes 224 | tf_op jit(solution)/shard_map/ppermute | solution.py:20
  81.8 31.2 %copy-start.2 = (bf16[2,256,256]{2,1,0:T(8,128)(2,1)}, bf16[2,256,256]{2,1,0:T(8,128)(2,1)S(1)}, u32[]{:S(2)}) copy-start(bf16[2,256,256]{2,1,0:T(8,128)(2,1)S(1)} %get-tuple-element.7.refs_3_) | copy-start | bytes 786436
  81.8 7.0 %collective-permute-start.5 = (bf16[2,256,256]{2,1,0:T(8,128)(2,1)S(1)}, bf16[2,256,256]{2,1,0:T(8,128)(2,1)S(1)}, u32[]{:S(2)}, u32[]{:S(2)}) collective-permute-start(bf16[2,256,256]{2,1,0:T(8,128)(2,1)S(1)} %get-tuple-element.7.refs_3_), channel_id=1, source_target_pairs={{0,8},{4,12},{8,16},{12,20},{16,24},{20,28},{1,9},{5,13},{9,17},{1... | collective-permute-start | bytes 786440 | tf_op jit(solution)/shard_map/ppermute | solution.py:44
  83.4 9.5 %collective-permute-start.8 = (bf16[2,256,256]{2,1,0:T(8,128)(2,1)S(1)}, bf16[2,256,256]{2,1,0:T(8,128)(2,1)S(1)}, u32[]{:S(2)}, u32[]{:S(2)}) collective-permute-start(bf16[2,256,256]{2,1,0:T(8,128)(2,1)S(1)} %get-tuple-element.7.refs_3_), channel_id=1, source_target_pairs={{8,0},{12,4},{16,8},{20,12},{24,16},{28,20},{9,1},{13,5},{17,9},{2... | collective-permute-start | bytes 786440 | tf_op jit(solution)/shard_map/ppermute | solution.py:45
  88.8 8.5 %collective-permute-start.6 = (bf16[2,256,256]{2,1,0:T(8,128)(2,1)S(1)}, bf16[2,256,256]{2,1,0:T(8,128)(2,1)S(1)}, u32[]{:S(2)}, u32[]{:S(2)}) collective-permute-start(bf16[2,256,256]{2,1,0:T(8,128)(2,1)S(1)} %collective-permute-done.5.refs_2_), channel_id=1, source_target_pairs={{0,8},{4,12},{8,16},{12,20},{16,24},{20,28},{1,9},{5,13},{9,17},{1... | collective-permute-start | bytes 786440 | tf_op jit(solution)/shard_map/ppermute | solution.py:44
  92.9 8.5 %collective-permute-start.9 = (bf16[2,256,256]{2,1,0:T(8,128)(2,1)S(1)}, bf16[2,256,256]{2,1,0:T(8,128)(2,1)S(1)}, u32[]{:S(2)}, u32[]{:S(2)}) collective-permute-start(bf16[2,256,256]{2,1,0:T(8,128)(2,1)S(1)} %collective-permute-done.8.refs_4_), channel_id=1, source_target_pairs={{8,0},{12,4},{16,8},{20,12},{24,16},{28,20},{9,1},{13,5},{17,9},{2... | collective-permute-start | bytes 786440 | tf_op jit(solution)/shard_map/ppermute | solution.py:45
  94.9 15.8 %collective-permute-start.14 = (bf16[2,256,256]{2,1,0:T(8,128)(2,1)S(1)}, bf16[2,256,256]{2,1,0:T(8,128)(2,1)S(1)}, u32[]{:S(2)}, u32[]{:S(2)}) collective-permute-start(bf16[2,256,256]{2,1,0:T(8,128)(2,1)S(1)} %get-tuple-element.7.refs_3_), channel_id=1, source_target_pairs={{0,4},{4,0},{8,12},{12,8},{16,20},{20,16},{24,28},{28,24},{1,5},{5... | collective-permute-start | bytes 786440 | tf_op jit(solution)/shard_map/ppermute | solution.py:41
  96.4 14.5 %collective-permute-start.13 = (bf16[2,256,256]{2,1,0:T(8,128)(2,1)S(1)}, bf16[2,256,256]{2,1,0:T(8,128)(2,1)S(1)}, u32[]{:S(2)}, u32[]{:S(2)}) collective-permute-start(bf16[2,256,256]{2,1,0:T(8,128)(2,1)S(1)} %collective-permute-done.5.refs_2_), channel_id=1, source_target_pairs={{0,4},{4,0},{8,12},{12,8},{16,20},{20,16},{24,28},{28,24},{1,5},{5... | collective-permute-start | bytes 786440 | tf_op jit(solution)/shard_map/ppermute | solution.py:46
  97.3 14.0 %collective-permute-start.7 = (bf16[2,256,256]{2,1,0:T(8,128)(2,1)S(1)}, bf16[2,256,256]{2,1,0:T(8,128)(2,1)S(1)}, u32[]{:S(2)}, u32[]{:S(2)}) collective-permute-start(bf16[2,256,256]{2,1,0:T(8,128)(2,1)S(1)} %collective-permute-done.6.refs_1_), channel_id=1, source_target_pairs={{0,8},{4,12},{8,16},{12,20},{16,24},{20,28},{1,9},{5,13},{9,17},{1... | collective-permute-start | bytes 786440 | tf_op jit(solution)/shard_map/ppermute | solution.py:44
  101.5 9.9 %collective-permute-start.10 = (bf16[2,256,256]{2,1,0:T(8,128)(2,1)S(1)}, bf16[2,256,256]{2,1,0:T(8,128)(2,1)S(1)}, u32[]{:S(2)}, u32[]{:S(2)}) collective-permute-start(bf16[2,256,256]{2,1,0:T(8,128)(2,1)S(1)} %collective-permute-done.9.refs_5_), channel_id=1, source_target_pairs={{8,0},{12,4},{16,8},{20,12},{24,16},{28,20},{9,1},{13,5},{17,9},{2... | collective-permute-start | bytes 786440 | tf_op jit(solution)/shard_map/ppermute | solution.py:45
  108.4 4.7 %collective-permute-start.15 = (bf16[2,256,256]{2,1,0:T(8,128)(2,1)S(1)}, bf16[2,256,256]{2,1,0:T(8,128)(2,1)S(1)}, u32[]{:S(2)}, u32[]{:S(2)}) collective-permute-start(bf16[2,256,256]{2,1,0:T(8,128)(2,1)S(1)} %collective-permute-done.8.refs_4_), channel_id=1, source_target_pairs={{0,4},{4,0},{8,12},{12,8},{16,20},{20,16},{24,28},{28,24},{1,5},{5... | collective-permute-start | bytes 786440 | tf_op jit(solution)/shard_map/ppermute | solution.py:47
  110.8 2.3 %collective-permute-start.12 = (bf16[2,256,256]{2,1,0:T(8,128)(2,1)S(1)}, bf16[2,256,256]{2,1,0:T(8,128)(2,1)S(1)}, u32[]{:S(2)}, u32[]{:S(2)}) collective-permute-start(bf16[2,256,256]{2,1,0:T(8,128)(2,1)S(1)} %collective-permute-done.6.refs_1_), channel_id=1, source_target_pairs={{0,4},{4,0},{8,12},{12,8},{16,20},{20,16},{24,28},{28,24},{1,5},{5... | collective-permute-start | bytes 786440 | tf_op jit(solution)/shard_map/ppermute | solution.py:46
  110.8 2.3 %collective-permute-start.16 = (bf16[2,256,256]{2,1,0:T(8,128)(2,1)S(1)}, bf16[2,256,256]{2,1,0:T(8,128)(2,1)S(1)}, u32[]{:S(2)}, u32[]{:S(2)}) collective-permute-start(bf16[2,256,256]{2,1,0:T(8,128)(2,1)S(1)} %collective-permute-done.9.refs_5_), channel_id=1, source_target_pairs={{0,4},{4,0},{8,12},{12,8},{16,20},{20,16},{24,28},{28,24},{1,5},{5... | collective-permute-start | bytes 786440 | tf_op jit(solution)/shard_map/ppermute | solution.py:47
  111.3 1.9 %collective-permute-start.11 = (bf16[2,256,256]{2,1,0:T(8,128)(2,1)S(1)}, bf16[2,256,256]{2,1,0:T(8,128)(2,1)S(1)}, u32[]{:S(2)}, u32[]{:S(2)}) collective-permute-start(bf16[2,256,256]{2,1,0:T(8,128)(2,1)S(1)} %collective-permute-done.7.refs_0_), channel_id=1, source_target_pairs={{0,4},{4,0},{8,12},{12,8},{16,20},{20,16},{24,28},{28,24},{1,5},{5... | collective-permute-start | bytes 786440 | tf_op jit(solution)/shard_map/ppermute | solution.py:46
  111.4 3.3 %collective-permute-start.17 = (bf16[2,256,256]{2,1,0:T(8,128)(2,1)S(1)}, bf16[2,256,256]{2,1,0:T(8,128)(2,1)}, u32[]{:S(2)}, u32[]{:S(2)}) collective-permute-start(bf16[2,256,256]{2,1,0:T(8,128)(2,1)S(1)} %collective-permute-done.10.refs_6_), channel_id=1, source_target_pairs={{0,4},{4,0},{8,12},{12,8},{16,20},{20,16},{24,28},{28,24},{1,5},{5... | collective-permute-start | bytes 786440 | tf_op jit(solution)/shard_map/ppermute | solution.py:47
  (14 other events, 92.0 us)

commit v22 on v20

--- a/solution.py
+++ b/solution.py
@@ -114,6 +114,13 @@
         axis=2,
     )
     slot_live = jnp.any(matches, axis=2)
+    if slot_count == 2:
+        owned = owner_of[None, :] == jnp.arange(replicas, dtype=jnp.int32)[:, None]
+        count = jnp.sum(owned.astype(jnp.int32), axis=1)
+        first = jnp.min(jnp.where(owned, block_ids[None, :], column_blocks), axis=1)
+        last = jnp.max(jnp.where(owned, block_ids[None, :], -1), axis=1)
+        slot_live = jnp.stack([count >= 1, count >= 2], axis=1)
+        slot_table = jnp.where(slot_live, jnp.stack([first, last], axis=1), 0)
     my_table = lax.dynamic_index_in_dim(slot_table, replica, 0, keepdims=False)
     my_live = lax.dynamic_index_in_dim(slot_live, replica, 0, keepdims=False)
     live_float = my_live.astype(jnp.float32)[:, None, None]

time: 116 us -> 115 us (level)
  no operation moved by 1% of the time
where the time goes in v22:
time: 115 us; the launch traced here: 114 us
  waiting for transfers between devices  58.5 us (51%)
  starting transfers between devices  33.6 us (29%)
  matrix products  7.28 us (6%)
  other arithmetic  6.21 us (5%)
  local copies, waits for them, and re-layouts  4.64 us (4%)
  Pallas kernels  3.15 us (3%)
    all_to_all x1, waiting for transfers between devices, local(): received = lax.all_to_all(by_owner, 'dp', 0, 0, tiled=True)  47.5 us
    ppermute x3, starting transfers between devices, gather_blocks(): from_left[step] = lax.ppermute(from_left[step - 1], 'dp', rightward)  10 us
    ppermute x5, waiting for transfers between devices, butterfly_sum(): x = x + lax.ppermute(x, axis, [(i, i ^ step) for i in range(size)])  8.93 us
    all_to_all x1, starting transfers between devices, local(): received = lax.all_to_all(by_owner, 'dp', 0, 0, tiled=True)  6.51 us
    ppermute x5, starting transfers between devices, butterfly_sum(): x = x + lax.ppermute(x, axis, [(i, i ^ step) for i in range(size)])  5.83 us
    ppermute x3, starting transfers between devices, gather_blocks(): from_right[step] = lax.ppermute(from_right[step - 1], 'dp', leftward)  3.88 us
    ppermute x1, starting transfers between devices, gather_blocks(): near_left[0] = lax.ppermute(mine, 'dp', partner)  3.78 us
    ppermute x3, starting transfers between devices, gather_blocks(): near_right[step] = lax.ppermute(from_right[step], 'dp', partner)  3.49 us
  transfers between devices with their start and end apart: 19, of which 7 were waited for; matrix products, arithmetic and copies ran while one was open for 7% of the time, Pallas kernels for 0%

profile of v22, /device:TPU:1, one launch (start us, length us, event | category | flops | bytes accessed | tf_op | source)
XLA Modules:
  0.0 114.3 jit_solution(9876343601930155097)
XLA Ops:
  1.9 2.0 %gather_fusion = bf16[16,256,256]{2,1,0:T(8,128)(2,1)} fusion(bf16[8,256,256]{2,1,0:T(8,128)(2,1)S(1)} %bitcast.58, s32[1024]{0:T(1024)S(1)} %pad_clamp_fusion), kind=kCustom, calls=%fused_computation | custom fusion | bytes 4194368 | tf_op jit(solution)/shard_map/jit(_take)/gather | solution.py:127
  3.9 6.5 %all-to-all-start = ((bf16[8,2,256,256]{3,2,1,0:T(8,128)(2,1)}), bf16[8,2,256,256]{3,2,1,0:T(8,128)(2,1)}, u32[]{:S(2)}, u32[]{:S(2)}) async-start(bf16[8,2,256,256]{3,2,1,0:T(8,128)(2,1)} %bitcast.7), calls=%async_computation | async-start | bytes 4194304 | tf_op jit(solution)/shard_map/all_to_all | solution.py:130
  11.2 47.5 %all-to-all-done = bf16[8,2,256,256]{3,2,1,0:T(8,128)(2,1)} async-done(((bf16[8,2,256,256]{3,2,1,0:T(8,128)(2,1)}), bf16[8,2,256,256]{3,2,1,0:T(8,128)(2,1)}, u32[]{:S(2)}, u32[]{:S(2)}) %all-to-all-start) | async-done | bytes 2097184 | tf_op jit(solution)/shard_map/all_to_all | solution.py:130
  58.7 1.9 %convert_reduce_fusion = f32[2,256,256]{2,1,0:T(8,128)S(1)} fusion(bf16[8,2,256,256]{3,2,1,0:T(8,128)(2,1)} %all-to-all-done), kind=kLoop, calls=%fused_computation.1 | loop fusion | flops 1966080 | bytes 2621440 | tf_op jit(solution)/shard_map/reduce_sum | solution.py:131
  61.1 1.6 %multiply_reduce_fusion = (f32[2]{0:T(128)S(1)}, f32[2,256,256]{2,1,0:T(8,128)S(1)}) fusion(bf16[1,1,2,256,256]{4,3,2,1,0:T(8,128)(2,1)S(1)} %copy-done.4, f32[2,256,256]{2,1,0:T(8,128)S(1)} %convert_reduce_fusion, bf16[1,1,2,256,256]{4,3,2,1,0:T(8,128)(2,1)} %param.14, f32[2]{0:T(128)S(1)} %convert_element_type.37), kind=kOutput, calls=%fused_computation.25 | convolution fusion | flops 134873088 | bytes 1572880 | tf_op jit(solution)/shard_map/sij,sjk->sik/dot_general | solution.py:156
  62.8 1.3 %collective-permute-start = (f32[2,9]{1,0:T(2,128)S(1)}, f32[2,9]{1,0:T(2,128)S(1)}, u32[]{:S(2)}, u32[]{:S(2)}) collective-permute-start(f32[2,9]{1,0:T(2,128)S(1)} %pad_maximum_fusion), channel_id=1, source_target_pairs={{0,1},{1,0},{2,3},{3,2},{4,5},{5,4},{6,7},{7,6},{8,9},{9,8},{10,11... | collective-permute-start | bytes 224 | tf_op jit(solution)/shard_map/ppermute | solution.py:20
  64.1 1.2 %collective-permute-done = f32[2,9]{1,0:T(2,128)S(1)} collective-permute-done((f32[2,9]{1,0:T(2,128)S(1)}, f32[2,9]{1,0:T(2,128)S(1)}, u32[]{:S(2)}, u32[]{:S(2)}) %collective-permute-start) | collective-permute-done | bytes 104 | tf_op jit(solution)/shard_map/ppermute | solution.py:20
  65.3 1.3 %collective-permute-start.1 = (f32[2,9]{1,0:T(2,128)S(1)}, f32[2,9]{1,0:T(2,128)S(1)}, u32[]{:S(2)}, u32[]{:S(2)}) collective-permute-start(f32[2,9]{1,0:T(2,128)S(1)} %fusion.29), channel_id=1, source_target_pairs={{0,2},{1,3},{2,0},{3,1},{4,6},{5,7},{6,4},{7,5},{8,10},{9,11},{10,... | collective-permute-start | bytes 224 | tf_op jit(solution)/shard_map/ppermute | solution.py:20
  66.6 1.2 %collective-permute-done.1 = f32[2,9]{1,0:T(2,128)S(1)} collective-permute-done((f32[2,9]{1,0:T(2,128)S(1)}, f32[2,9]{1,0:T(2,128)S(1)}, u32[]{:S(2)}, u32[]{:S(2)}) %collective-permute-start.1) | collective-permute-done | bytes 104 | tf_op jit(solution)/shard_map/ppermute | solution.py:20
  67.8 3.2 %collective-permute-start.2 = (f32[2,9]{1,0:T(2,128)S(1)}, f32[2,9]{1,0:T(2,128)S(1)}, u32[]{:S(2)}, u32[]{:S(2)}) collective-permute-start(f32[2,9]{1,0:T(2,128)S(1)} %fusion.34), channel_id=1, source_target_pairs={{0,4},{4,0},{8,12},{12,8},{16,20},{20,16},{24,28},{28,24},{1,5},{5... | collective-permute-start | bytes 224 | tf_op jit(solution)/shard_map/ppermute | solution.py:20
  71.9 2.4 %collective-permute-done.3 = f32[2,9]{1,0:T(2,128)S(1)} collective-permute-done((f32[2,9]{1,0:T(2,128)S(1)}, f32[2,9]{1,0:T(2,128)S(1)}, u32[]{:S(2)}, u32[]{:S(2)}) %collective-permute-start.3) | collective-permute-done | bytes 104 | tf_op jit(solution)/shard_map/ppermute | solution.py:20
  74.3 3.3 %collective-permute-done.4 = f32[2,9]{1,0:T(2,128)S(1)} collective-permute-done((f32[2,9]{1,0:T(2,128)S(1)}, f32[2,9]{1,0:T(2,128)S(1)}, u32[]{:S(2)}, u32[]{:S(2)}) %collective-permute-start.4) | collective-permute-done | bytes 104 | tf_op jit(solution)/shard_map/ppermute | solution.py:20
  78.8 1.9 %collective-permute-start.5 = (bf16[2,256,256]{2,1,0:T(8,128)(2,1)S(1)}, bf16[2,256,256]{2,1,0:T(8,128)(2,1)S(1)}, u32[]{:S(2)}, u32[]{:S(2)}) collective-permute-start(bf16[2,256,256]{2,1,0:T(8,128)(2,1)S(1)} %get-tuple-element.13.refs_3_), channel_id=1, source_target_pairs={{0,8},{4,12},{8,16},{12,20},{16,24},{20,28},{1,9},{5,13},{9,17},{1... | collective-permute-start | bytes 786440 | tf_op jit(solution)/shard_map/ppermute | solution.py:44
  80.7 1.3 %collective-permute-start.8 = (bf16[2,256,256]{2,1,0:T(8,128)(2,1)S(1)}, bf16[2,256,256]{2,1,0:T(8,128)(2,1)S(1)}, u32[]{:S(2)}, u32[]{:S(2)}) collective-permute-start(bf16[2,256,256]{2,1,0:T(8,128)(2,1)S(1)} %get-tuple-element.13.refs_3_), channel_id=1, source_target_pairs={{8,0},{12,4},{16,8},{20,12},{24,16},{28,20},{9,1},{13,5},{17,9},{2... | collective-permute-start | bytes 786440 | tf_op jit(solution)/shard_map/ppermute | solution.py:45
  82.1 2.0 %collective-permute-done.5.refs_2_ = bf16[2,256,256]{2,1,0:T(8,128)(2,1)S(1)} collective-permute-done((bf16[2,256,256]{2,1,0:T(8,128)(2,1)S(1)}, bf16[2,256,256]{2,1,0:T(8,128)(2,1)S(1)}, u32[]{:S(2)}, u32[]{:S(2)}) %collective-permute-start.5) | collective-permute-done | bytes 262176 | tf_op jit(solution)/shard_map/ppermute | solution.py:44
  84.0 3.8 %collective-permute-start.6 = (bf16[2,256,256]{2,1,0:T(8,128)(2,1)S(1)}, bf16[2,256,256]{2,1,0:T(8,128)(2,1)S(1)}, u32[]{:S(2)}, u32[]{:S(2)}) collective-permute-start(bf16[2,256,256]{2,1,0:T(8,128)(2,1)S(1)} %collective-permute-done.5.refs_2_), channel_id=1, source_target_pairs={{0,8},{4,12},{8,16},{12,20},{16,24},{20,28},{1,9},{5,13},{9,17},{1... | collective-permute-start | bytes 786440 | tf_op jit(solution)/shard_map/ppermute | solution.py:44
  87.9 1.3 %collective-permute-start.9 = (bf16[2,256,256]{2,1,0:T(8,128)(2,1)S(1)}, bf16[2,256,256]{2,1,0:T(8,128)(2,1)S(1)}, u32[]{:S(2)}, u32[]{:S(2)}) collective-permute-start(bf16[2,256,256]{2,1,0:T(8,128)(2,1)S(1)} %collective-permute-done.8.refs_4_), channel_id=1, source_target_pairs={{8,0},{12,4},{16,8},{20,12},{24,16},{28,20},{9,1},{13,5},{17,9},{2... | collective-permute-start | bytes 786440 | tf_op jit(solution)/shard_map/ppermute | solution.py:45
  89.9 3.8 %collective-permute-start.14 = (bf16[2,256,256]{2,1,0:T(8,128)(2,1)S(1)}, bf16[2,256,256]{2,1,0:T(8,128)(2,1)S(1)}, u32[]{:S(2)}, u32[]{:S(2)}) collective-permute-start(bf16[2,256,256]{2,1,0:T(8,128)(2,1)S(1)} %get-tuple-element.13.refs_3_), channel_id=1, source_target_pairs={{0,4},{4,0},{8,12},{12,8},{16,20},{20,16},{24,28},{28,24},{1,5},{5... | collective-permute-start | bytes 786440 | tf_op jit(solution)/shard_map/ppermute | solution.py:41
  93.7 4.3 %collective-permute-start.7 = (bf16[2,256,256]{2,1,0:T(8,128)(2,1)S(1)}, bf16[2,256,256]{2,1,0:T(8,128)(2,1)S(1)}, u32[]{:S(2)}, u32[]{:S(2)}) collective-permute-start(bf16[2,256,256]{2,1,0:T(8,128)(2,1)S(1)} %collective-permute-done.6.refs_1_), channel_id=1, source_target_pairs={{0,8},{4,12},{8,16},{12,20},{16,24},{20,28},{1,9},{5,13},{9,17},{1... | collective-permute-start | bytes 786440 | tf_op jit(solution)/shard_map/ppermute | solution.py:44
  98.0 1.3 %collective-permute-start.10 = (bf16[2,256,256]{2,1,0:T(8,128)(2,1)S(1)}, bf16[2,256,256]{2,1,0:T(8,128)(2,1)S(1)}, u32[]{:S(2)}, u32[]{:S(2)}) collective-permute-start(bf16[2,256,256]{2,1,0:T(8,128)(2,1)S(1)} %collective-permute-done.9.refs_5_), channel_id=1, source_target_pairs={{8,0},{12,4},{16,8},{20,12},{24,16},{28,20},{9,1},{13,5},{17,9},{2... | collective-permute-start | bytes 786440 | tf_op jit(solution)/shard_map/ppermute | solution.py:45
  99.3 3.0 %fusion.2 = f32[1,1,2,256,256]{4,3,2,1,0:T(8,128)} fusion(f32[1,1,2,256,256]{4,3,2,1,0:T(8,128)} %param.13, f32[2,256,256]{2,1,0:T(8,128)S(1)} %convert_reduce_fusion, f32[2]{0:T(128)S(1)} %convert_element_type.37, pred[2]{0:T(512)(128)(4,1)S(1)} %dynamic-slice_reduce_fusion), kind=kOutput, calls=%fused_computation.5 | convolution fusion | flops 403308544 | bytes 1572874 | tf_op jit(solution)/shard_map/sji,sjk->sik/dot_general | solution.py:149
  102.3 2.7 %fusion.5 = f32[1,1,2,256,256]{4,3,2,1,0:T(8,128)} fusion(f32[1,1,2,256,256]{4,3,2,1,0:T(8,128)} %param.12, f32[2,256,256]{2,1,0:T(8,128)S(1)} %convert_reduce_fusion, f32[2]{0:T(128)S(1)} %convert_element_type.37, pred[2]{0:T(512)(128)(4,1)S(1)} %dynamic-slice_reduce_fusion), kind=kOutput, calls=%fused_computation.9 | convolution fusion | flops 403308544 | bytes 1572874 | tf_op jit(solution)/shard_map/sij,skj->sik/dot_general | solution.py:146
  104.9 1.9 %collective-permute-start.15 = (bf16[2,256,256]{2,1,0:T(8,128)(2,1)S(1)}, bf16[2,256,256]{2,1,0:T(8,128)(2,1)S(1)}, u32[]{:S(2)}, u32[]{:S(2)}) collective-permute-start(bf16[2,256,256]{2,1,0:T(8,128)(2,1)S(1)} %collective-permute-done.8.refs_4_), channel_id=1, source_target_pairs={{0,4},{4,0},{8,12},{12,8},{16,20},{20,16},{24,28},{28,24},{1,5},{5... | collective-permute-start | bytes 786440 | tf_op jit(solution)/shard_map/ppermute | solution.py:47
  111.2 3.1 %shard_map.128 = bf16[8,256,256]{2,1,0:T(8,128)(2,1)} custom-call(s32[8,2]{1,0:T(8,128)} %copy.37.table_ref, bf16[2,256,256]{2,1,0:T(8,128)(2,1)} %copy-done.11, bf16[2,256,256]{2,1,0:T(8,128)(2,1)} %copy-done.7, bf16[2,256,256]{2,1,0:T(8,128)(2,1)} %copy-done.5, bf16[2,256,256]{2,1,0:T(8,128)(2,1)} %copy-done.2, bf16[2,256,256]{2,1,0:T(8,128)(2,1)} %copy-done.6, ...), custom_call_target="tpu_custom_call" | custom-call | tf_op jit(solution)/shard_map/pallas_call | solution.py:79
  (86 shorter events, 9.5 us)
Async XLA Ops:
  3.9 54.8 %all-to-all-start = ((bf16[8,2,256,256]{3,2,1,0:T(8,128)(2,1)}), bf16[8,2,256,256]{3,2,1,0:T(8,128)(2,1)}, u32[]{:S(2)}, u32[]{:S(2)}) async-start(bf16[8,2,256,256]{3,2,1,0:T(8,128)(2,1)} %bitcast.7), calls=%async_computation | async-start | bytes 4194304 | tf_op jit(solution)/shard_map/all_to_all | solution.py:130
  10.4 50.2 %copy-start.1 = (f32[1,1,2,256,256]{4,3,2,1,0:T(8,128)S(1)}, f32[1,1,2,256,256]{4,3,2,1,0:T(8,128)}, u32[]{:S(2)}) copy-start(f32[1,1,2,256,256]{4,3,2,1,0:T(8,128)} %param.16) | copy-start | bytes 1572868
  10.4 50.7 %copy-start.4 = (bf16[1,1,2,256,256]{4,3,2,1,0:T(8,128)(2,1)S(1)}, bf16[1,1,2,256,256]{4,3,2,1,0:T(8,128)(2,1)}, u32[]{:S(2)}) copy-start(bf16[1,1,2,256,256]{4,3,2,1,0:T(8,128)(2,1)} %param.15) | copy-start | bytes 786436
  11.2 66.7 %copy-start.3 = (f32[1,1,2,256,256]{4,3,2,1,0:T(8,128)S(1)}, f32[1,1,2,256,256]{4,3,2,1,0:T(8,128)}, u32[]{:S(2)}) copy-start(f32[1,1,2,256,256]{4,3,2,1,0:T(8,128)} %param.17) | copy-start | bytes 1572868
  60.6 28.5 %copy-start.17 = (s32[8,1]{0,1:T(1,128)S(1)}, s32[8,1]{0,1:T(1,128)}, u32[]{:S(2)}) copy-start(s32[8,1]{0,1:T(1,128)} %param.10) | copy-start | bytes 100
  62.8 2.5 %collective-permute-start = (f32[2,9]{1,0:T(2,128)S(1)}, f32[2,9]{1,0:T(2,128)S(1)}, u32[]{:S(2)}, u32[]{:S(2)}) collective-permute-start(f32[2,9]{1,0:T(2,128)S(1)} %pad_maximum_fusion), channel_id=1, source_target_pairs={{0,1},{1,0},{2,3},{3,2},{4,5},{5,4},{6,7},{7,6},{8,9},{9,8},{10,11... | collective-permute-start | bytes 224 | tf_op jit(solution)/shard_map/ppermute | solution.py:20
  65.3 2.5 %collective-permute-start.1 = (f32[2,9]{1,0:T(2,128)S(1)}, f32[2,9]{1,0:T(2,128)S(1)}, u32[]{:S(2)}, u32[]{:S(2)}) collective-permute-start(f32[2,9]{1,0:T(2,128)S(1)} %fusion.29), channel_id=1, source_target_pairs={{0,2},{1,3},{2,0},{3,1},{4,6},{5,7},{6,4},{7,5},{8,10},{9,11},{10,... | collective-permute-start | bytes 224 | tf_op jit(solution)/shard_map/ppermute | solution.py:20
  67.8 4.1 %collective-permute-start.2 = (f32[2,9]{1,0:T(2,128)S(1)}, f32[2,9]{1,0:T(2,128)S(1)}, u32[]{:S(2)}, u32[]{:S(2)}) collective-permute-start(f32[2,9]{1,0:T(2,128)S(1)} %fusion.34), channel_id=1, source_target_pairs={{0,4},{4,0},{8,12},{12,8},{16,20},{20,16},{24,28},{28,24},{1,5},{5... | collective-permute-start | bytes 224 | tf_op jit(solution)/shard_map/ppermute | solution.py:20
  71.9 2.4 %collective-permute-start.3 = (f32[2,9]{1,0:T(2,128)S(1)}, f32[2,9]{1,0:T(2,128)S(1)}, u32[]{:S(2)}, u32[]{:S(2)}) collective-permute-start(f32[2,9]{1,0:T(2,128)S(1)} %add.92), channel_id=1, source_target_pairs={{0,8},{4,12},{8,0},{12,4},{16,24},{20,28},{24,16},{28,20},{1,9},{5... | collective-permute-start | bytes 224 | tf_op jit(solution)/shard_map/ppermute | solution.py:20
  74.3 3.3 %collective-permute-start.4 = (f32[2,9]{1,0:T(2,128)S(1)}, f32[2,9]{1,0:T(2,128)S(1)}, u32[]{:S(2)}, u32[]{:S(2)}) collective-permute-start(f32[2,9]{1,0:T(2,128)S(1)} %add.93), channel_id=1, source_target_pairs={{0,16},{4,20},{8,24},{12,28},{16,0},{20,4},{24,8},{28,12},{1,17},{... | collective-permute-start | bytes 224 | tf_op jit(solution)/shard_map/ppermute | solution.py:20
  78.8 30.8 %copy-start.2 = (bf16[2,256,256]{2,1,0:T(8,128)(2,1)}, bf16[2,256,256]{2,1,0:T(8,128)(2,1)S(1)}, u32[]{:S(2)}) copy-start(bf16[2,256,256]{2,1,0:T(8,128)(2,1)S(1)} %get-tuple-element.13.refs_3_) | copy-start | bytes 786436
  78.8 5.2 %collective-permute-start.5 = (bf16[2,256,256]{2,1,0:T(8,128)(2,1)S(1)}, bf16[2,256,256]{2,1,0:T(8,128)(2,1)S(1)}, u32[]{:S(2)}, u32[]{:S(2)}) collective-permute-start(bf16[2,256,256]{2,1,0:T(8,128)(2,1)S(1)} %get-tuple-element.13.refs_3_), channel_id=1, source_target_pairs={{0,8},{4,12},{8,16},{12,20},{16,24},{20,28},{1,9},{5,13},{9,17},{1... | collective-permute-start | bytes 786440 | tf_op jit(solution)/shard_map/ppermute | solution.py:44
  80.7 7.1 %collective-permute-start.8 = (bf16[2,256,256]{2,1,0:T(8,128)(2,1)S(1)}, bf16[2,256,256]{2,1,0:T(8,128)(2,1)S(1)}, u32[]{:S(2)}, u32[]{:S(2)}) collective-permute-start(bf16[2,256,256]{2,1,0:T(8,128)(2,1)S(1)} %get-tuple-element.13.refs_3_), channel_id=1, source_target_pairs={{8,0},{12,4},{16,8},{20,12},{24,16},{28,20},{9,1},{13,5},{17,9},{2... | collective-permute-start | bytes 786440 | tf_op jit(solution)/shard_map/ppermute | solution.py:45
  84.0 9.6 %collective-permute-start.6 = (bf16[2,256,256]{2,1,0:T(8,128)(2,1)S(1)}, bf16[2,256,256]{2,1,0:T(8,128)(2,1)S(1)}, u32[]{:S(2)}, u32[]{:S(2)}) collective-permute-start(bf16[2,256,256]{2,1,0:T(8,128)(2,1)S(1)} %collective-permute-done.5.refs_2_), channel_id=1, source_target_pairs={{0,8},{4,12},{8,16},{12,20},{16,24},{20,28},{1,9},{5,13},{9,17},{1... | collective-permute-start | bytes 786440 | tf_op jit(solution)/shard_map/ppermute | solution.py:44
  87.9 10.1 %collective-permute-start.9 = (bf16[2,256,256]{2,1,0:T(8,128)(2,1)S(1)}, bf16[2,256,256]{2,1,0:T(8,128)(2,1)S(1)}, u32[]{:S(2)}, u32[]{:S(2)}) collective-permute-start(bf16[2,256,256]{2,1,0:T(8,128)(2,1)S(1)} %collective-permute-done.8.refs_4_), channel_id=1, source_target_pairs={{8,0},{12,4},{16,8},{20,12},{24,16},{28,20},{9,1},{13,5},{17,9},{2... | collective-permute-start | bytes 786440 | tf_op jit(solution)/shard_map/ppermute | solution.py:45
  89.9 17.0 %collective-permute-start.14 = (bf16[2,256,256]{2,1,0:T(8,128)(2,1)S(1)}, bf16[2,256,256]{2,1,0:T(8,128)(2,1)S(1)}, u32[]{:S(2)}, u32[]{:S(2)}) collective-permute-start(bf16[2,256,256]{2,1,0:T(8,128)(2,1)S(1)} %get-tuple-element.13.refs_3_), channel_id=1, source_target_pairs={{0,4},{4,0},{8,12},{12,8},{16,20},{20,16},{24,28},{28,24},{1,5},{5... | collective-permute-start | bytes 786440 | tf_op jit(solution)/shard_map/ppermute | solution.py:41
  93.7 13.3 %collective-permute-start.13 = (bf16[2,256,256]{2,1,0:T(8,128)(2,1)S(1)}, bf16[2,256,256]{2,1,0:T(8,128)(2,1)S(1)}, u32[]{:S(2)}, u32[]{:S(2)}) collective-permute-start(bf16[2,256,256]{2,1,0:T(8,128)(2,1)S(1)} %collective-permute-done.5.refs_2_), channel_id=1, source_target_pairs={{0,4},{4,0},{8,12},{12,8},{16,20},{20,16},{24,28},{28,24},{1,5},{5... | collective-permute-start | bytes 786440 | tf_op jit(solution)/shard_map/ppermute | solution.py:46
  93.7 13.7 %collective-permute-start.7 = (bf16[2,256,256]{2,1,0:T(8,128)(2,1)S(1)}, bf16[2,256,256]{2,1,0:T(8,128)(2,1)S(1)}, u32[]{:S(2)}, u32[]{:S(2)}) collective-permute-start(bf16[2,256,256]{2,1,0:T(8,128)(2,1)S(1)} %collective-permute-done.6.refs_1_), channel_id=1, source_target_pairs={{0,8},{4,12},{8,16},{12,20},{16,24},{20,28},{1,9},{5,13},{9,17},{1... | collective-permute-start | bytes 786440 | tf_op jit(solution)/shard_map/ppermute | solution.py:44
  98.0 9.5 %collective-permute-start.10 = (bf16[2,256,256]{2,1,0:T(8,128)(2,1)S(1)}, bf16[2,256,256]{2,1,0:T(8,128)(2,1)S(1)}, u32[]{:S(2)}, u32[]{:S(2)}) collective-permute-start(bf16[2,256,256]{2,1,0:T(8,128)(2,1)S(1)} %collective-permute-done.9.refs_5_), channel_id=1, source_target_pairs={{8,0},{12,4},{16,8},{20,12},{24,16},{28,20},{9,1},{13,5},{17,9},{2... | collective-permute-start | bytes 786440 | tf_op jit(solution)/shard_map/ppermute | solution.py:45
  104.9 4.7 %collective-permute-start.15 = (bf16[2,256,256]{2,1,0:T(8,128)(2,1)S(1)}, bf16[2,256,256]{2,1,0:T(8,128)(2,1)S(1)}, u32[]{:S(2)}, u32[]{:S(2)}) collective-permute-start(bf16[2,256,256]{2,1,0:T(8,128)(2,1)S(1)} %collective-permute-done.8.refs_4_), channel_id=1, source_target_pairs={{0,4},{4,0},{8,12},{12,8},{16,20},{20,16},{24,28},{28,24},{1,5},{5... | collective-permute-start | bytes 786440 | tf_op jit(solution)/shard_map/ppermute | solution.py:47
  106.8 2.8 %collective-permute-start.12 = (bf16[2,256,256]{2,1,0:T(8,128)(2,1)S(1)}, bf16[2,256,256]{2,1,0:T(8,128)(2,1)S(1)}, u32[]{:S(2)}, u32[]{:S(2)}) collective-permute-start(bf16[2,256,256]{2,1,0:T(8,128)(2,1)S(1)} %collective-permute-done.6.refs_1_), channel_id=1, source_target_pairs={{0,4},{4,0},{8,12},{12,8},{16,20},{20,16},{24,28},{28,24},{1,5},{5... | collective-permute-start | bytes 786440 | tf_op jit(solution)/shard_map/ppermute | solution.py:46
  106.9 2.7 %collective-permute-start.16 = (bf16[2,256,256]{2,1,0:T(8,128)(2,1)S(1)}, bf16[2,256,256]{2,1,0:T(8,128)(2,1)S(1)}, u32[]{:S(2)}, u32[]{:S(2)}) collective-permute-start(bf16[2,256,256]{2,1,0:T(8,128)(2,1)S(1)} %collective-permute-done.9.refs_5_), channel_id=1, source_target_pairs={{0,4},{4,0},{8,12},{12,8},{16,20},{20,16},{24,28},{28,24},{1,5},{5... | collective-permute-start | bytes 786440 | tf_op jit(solution)/shard_map/ppermute | solution.py:47
  107.4 2.3 %collective-permute-start.11 = (bf16[2,256,256]{2,1,0:T(8,128)(2,1)S(1)}, bf16[2,256,256]{2,1,0:T(8,128)(2,1)S(1)}, u32[]{:S(2)}, u32[]{:S(2)}) collective-permute-start(bf16[2,256,256]{2,1,0:T(8,128)(2,1)S(1)} %collective-permute-done.7.refs_0_), channel_id=1, source_target_pairs={{0,4},{4,0},{8,12},{12,8},{16,20},{20,16},{24,28},{28,24},{1,5},{5... | collective-permute-start | bytes 786440 | tf_op jit(solution)/shard_map/ppermute | solution.py:46
  107.5 3.7 %collective-permute-start.17 = (bf16[2,256,256]{2,1,0:T(8,128)(2,1)S(1)}, bf16[2,256,256]{2,1,0:T(8,128)(2,1)}, u32[]{:S(2)}, u32[]{:S(2)}) collective-permute-start(bf16[2,256,256]{2,1,0:T(8,128)(2,1)S(1)} %collective-permute-done.10.refs_6_), channel_id=1, source_target_pairs={{0,4},{4,0},{8,12},{12,8},{16,20},{20,16},{24,28},{28,24},{1,5},{5... | collective-permute-start | bytes 786440 | tf_op jit(solution)/shard_map/ppermute | solution.py:47
  (14 other events, 95.9 us)

commit v23 on v22

--- a/solution.py
+++ b/solution.py
@@ -168,7 +168,7 @@
     out_right = jnp.where(live_mask, rnew, right)
     out_moment = jnp.where(live_mask, vnew, moment)
     out_master = jnp.where(live_mask, wnew, weights)
-    regathered = gather_blocks(out_master.astype(jnp.bfloat16), owner_of, slot_rank, replica)
+    regathered = gather_blocks(wnew.astype(jnp.bfloat16), owner_of, slot_rank, replica)
     return (
         out_left[None, None],
         out_right[None, None],

time: 115 us -> 115 us (level)
  no operation moved by 1% of the time
where the time goes in v23:
time: 115 us; the launch traced here: 114 us
  waiting for transfers between devices  58.5 us (51%)
  starting transfers between devices  33.6 us (29%)
  matrix products  7.28 us (6%)
  other arithmetic  6.21 us (5%)
  local copies, waits for them, and re-layouts  4.64 us (4%)
  Pallas kernels  3.13 us (3%)
    all_to_all x1, waiting for transfers between devices, local(): received = lax.all_to_all(by_owner, 'dp', 0, 0, tiled=True)  47.5 us
    ppermute x3, starting transfers between devices, gather_blocks(): from_left[step] = lax.ppermute(from_left[step - 1], 'dp', rightward)  10 us
    ppermute x5, waiting for transfers between devices, butterfly_sum(): x = x + lax.ppermute(x, axis, [(i, i ^ step) for i in range(size)])  8.93 us
    all_to_all x1, starting transfers between devices, local(): received = lax.all_to_all(by_owner, 'dp', 0, 0, tiled=True)  6.51 us
    ppermute x5, starting transfers between devices, butterfly_sum(): x = x + lax.ppermute(x, axis, [(i, i ^ step) for i in range(size)])  5.83 us
    ppermute x3, starting transfers between devices, gather_blocks(): from_right[step] = lax.ppermute(from_right[step - 1], 'dp', leftward)  3.88 us
    ppermute x1, starting transfers between devices, gather_blocks(): near_left[0] = lax.ppermute(mine, 'dp', partner)  3.78 us
    ppermute x3, starting transfers between devices, gather_blocks(): near_right[step] = lax.ppermute(from_right[step], 'dp', partner)  3.49 us
  transfers between devices with their start and end apart: 19, of which 7 were waited for; matrix products, arithmetic and copies ran while one was open for 7% of the time, Pallas kernels for 0%

profile of v23, /device:TPU:1, one launch (start us, length us, event | category | flops | bytes accessed | tf_op | source)
XLA Modules:
  0.0 114.3 jit_solution(11115745036903109686)
XLA Ops:
  1.9 2.0 %gather_fusion = bf16[16,256,256]{2,1,0:T(8,128)(2,1)} fusion(bf16[8,256,256]{2,1,0:T(8,128)(2,1)S(1)} %bitcast.61, s32[1024]{0:T(1024)S(1)} %pad_clamp_fusion), kind=kCustom, calls=%fused_computation | custom fusion | bytes 4194368 | tf_op jit(solution)/shard_map/jit(_take)/gather | solution.py:127
  3.9 6.5 %all-to-all-start = ((bf16[8,2,256,256]{3,2,1,0:T(8,128)(2,1)}), bf16[8,2,256,256]{3,2,1,0:T(8,128)(2,1)}, u32[]{:S(2)}, u32[]{:S(2)}) async-start(bf16[8,2,256,256]{3,2,1,0:T(8,128)(2,1)} %bitcast.7), calls=%async_computation | async-start | bytes 4194304 | tf_op jit(solution)/shard_map/all_to_all | solution.py:130
  11.2 47.5 %all-to-all-done = bf16[8,2,256,256]{3,2,1,0:T(8,128)(2,1)} async-done(((bf16[8,2,256,256]{3,2,1,0:T(8,128)(2,1)}), bf16[8,2,256,256]{3,2,1,0:T(8,128)(2,1)}, u32[]{:S(2)}, u32[]{:S(2)}) %all-to-all-start) | async-done | bytes 2097184 | tf_op jit(solution)/shard_map/all_to_all | solution.py:130
  58.7 1.9 %convert_reduce_fusion = f32[2,256,256]{2,1,0:T(8,128)S(1)} fusion(bf16[8,2,256,256]{3,2,1,0:T(8,128)(2,1)} %all-to-all-done), kind=kLoop, calls=%fused_computation.1 | loop fusion | flops 1966080 | bytes 2621440 | tf_op jit(solution)/shard_map/reduce_sum | solution.py:131
  61.1 1.6 %multiply_reduce_fusion = (f32[2]{0:T(128)S(1)}, f32[2,256,256]{2,1,0:T(8,128)S(1)}) fusion(bf16[1,1,2,256,256]{4,3,2,1,0:T(8,128)(2,1)S(1)} %copy-done.4, f32[2,256,256]{2,1,0:T(8,128)S(1)} %convert_reduce_fusion, bf16[1,1,2,256,256]{4,3,2,1,0:T(8,128)(2,1)} %param.14, f32[2]{0:T(128)S(1)} %convert_element_type.37), kind=kOutput, calls=%fused_computation.27 | convolution fusion | flops 134873088 | bytes 1572880 | tf_op jit(solution)/shard_map/sij,sjk->sik/dot_general | solution.py:156
  62.8 1.3 %collective-permute-start = (f32[2,9]{1,0:T(2,128)S(1)}, f32[2,9]{1,0:T(2,128)S(1)}, u32[]{:S(2)}, u32[]{:S(2)}) collective-permute-start(f32[2,9]{1,0:T(2,128)S(1)} %pad_maximum_fusion), channel_id=1, source_target_pairs={{0,1},{1,0},{2,3},{3,2},{4,5},{5,4},{6,7},{7,6},{8,9},{9,8},{10,11... | collective-permute-start | bytes 224 | tf_op jit(solution)/shard_map/ppermute | solution.py:20
  64.1 1.2 %collective-permute-done = f32[2,9]{1,0:T(2,128)S(1)} collective-permute-done((f32[2,9]{1,0:T(2,128)S(1)}, f32[2,9]{1,0:T(2,128)S(1)}, u32[]{:S(2)}, u32[]{:S(2)}) %collective-permute-start) | collective-permute-done | bytes 104 | tf_op jit(solution)/shard_map/ppermute | solution.py:20
  65.3 1.3 %collective-permute-start.1 = (f32[2,9]{1,0:T(2,128)S(1)}, f32[2,9]{1,0:T(2,128)S(1)}, u32[]{:S(2)}, u32[]{:S(2)}) collective-permute-start(f32[2,9]{1,0:T(2,128)S(1)} %fusion.31), channel_id=1, source_target_pairs={{0,2},{1,3},{2,0},{3,1},{4,6},{5,7},{6,4},{7,5},{8,10},{9,11},{10,... | collective-permute-start | bytes 224 | tf_op jit(solution)/shard_map/ppermute | solution.py:20
  66.6 1.2 %collective-permute-done.1 = f32[2,9]{1,0:T(2,128)S(1)} collective-permute-done((f32[2,9]{1,0:T(2,128)S(1)}, f32[2,9]{1,0:T(2,128)S(1)}, u32[]{:S(2)}, u32[]{:S(2)}) %collective-permute-start.1) | collective-permute-done | bytes 104 | tf_op jit(solution)/shard_map/ppermute | solution.py:20
  67.8 3.2 %collective-permute-start.2 = (f32[2,9]{1,0:T(2,128)S(1)}, f32[2,9]{1,0:T(2,128)S(1)}, u32[]{:S(2)}, u32[]{:S(2)}) collective-permute-start(f32[2,9]{1,0:T(2,128)S(1)} %fusion.34), channel_id=1, source_target_pairs={{0,4},{4,0},{8,12},{12,8},{16,20},{20,16},{24,28},{28,24},{1,5},{5... | collective-permute-start | bytes 224 | tf_op jit(solution)/shard_map/ppermute | solution.py:20
  71.9 2.4 %collective-permute-done.3 = f32[2,9]{1,0:T(2,128)S(1)} collective-permute-done((f32[2,9]{1,0:T(2,128)S(1)}, f32[2,9]{1,0:T(2,128)S(1)}, u32[]{:S(2)}, u32[]{:S(2)}) %collective-permute-start.3) | collective-permute-done | bytes 104 | tf_op jit(solution)/shard_map/ppermute | solution.py:20
  74.3 3.3 %collective-permute-done.4 = f32[2,9]{1,0:T(2,128)S(1)} collective-permute-done((f32[2,9]{1,0:T(2,128)S(1)}, f32[2,9]{1,0:T(2,128)S(1)}, u32[]{:S(2)}, u32[]{:S(2)}) %collective-permute-start.4) | collective-permute-done | bytes 104 | tf_op jit(solution)/shard_map/ppermute | solution.py:20
  78.8 1.9 %collective-permute-start.5 = (bf16[2,256,256]{2,1,0:T(8,128)(2,1)S(1)}, bf16[2,256,256]{2,1,0:T(8,128)(2,1)S(1)}, u32[]{:S(2)}, u32[]{:S(2)}) collective-permute-start(bf16[2,256,256]{2,1,0:T(8,128)(2,1)S(1)} %get-tuple-element.13.refs_3_), channel_id=1, source_target_pairs={{0,8},{4,12},{8,16},{12,20},{16,24},{20,28},{1,9},{5,13},{9,17},{1... | collective-permute-start | bytes 786440 | tf_op jit(solution)/shard_map/ppermute | solution.py:44
  80.7 1.3 %collective-permute-start.8 = (bf16[2,256,256]{2,1,0:T(8,128)(2,1)S(1)}, bf16[2,256,256]{2,1,0:T(8,128)(2,1)S(1)}, u32[]{:S(2)}, u32[]{:S(2)}) collective-permute-start(bf16[2,256,256]{2,1,0:T(8,128)(2,1)S(1)} %get-tuple-element.13.refs_3_), channel_id=1, source_target_pairs={{8,0},{12,4},{16,8},{20,12},{24,16},{28,20},{9,1},{13,5},{17,9},{2... | collective-permute-start | bytes 786440 | tf_op jit(solution)/shard_map/ppermute | solution.py:45
  82.1 2.0 %collective-permute-done.5.refs_2_ = bf16[2,256,256]{2,1,0:T(8,128)(2,1)S(1)} collective-permute-done((bf16[2,256,256]{2,1,0:T(8,128)(2,1)S(1)}, bf16[2,256,256]{2,1,0:T(8,128)(2,1)S(1)}, u32[]{:S(2)}, u32[]{:S(2)}) %collective-permute-start.5) | collective-permute-done | bytes 262176 | tf_op jit(solution)/shard_map/ppermute | solution.py:44
  84.0 3.8 %collective-permute-start.6 = (bf16[2,256,256]{2,1,0:T(8,128)(2,1)S(1)}, bf16[2,256,256]{2,1,0:T(8,128)(2,1)S(1)}, u32[]{:S(2)}, u32[]{:S(2)}) collective-permute-start(bf16[2,256,256]{2,1,0:T(8,128)(2,1)S(1)} %collective-permute-done.5.refs_2_), channel_id=1, source_target_pairs={{0,8},{4,12},{8,16},{12,20},{16,24},{20,28},{1,9},{5,13},{9,17},{1... | collective-permute-start | bytes 786440 | tf_op jit(solution)/shard_map/ppermute | solution.py:44
  87.9 1.3 %collective-permute-start.9 = (bf16[2,256,256]{2,1,0:T(8,128)(2,1)S(1)}, bf16[2,256,256]{2,1,0:T(8,128)(2,1)S(1)}, u32[]{:S(2)}, u32[]{:S(2)}) collective-permute-start(bf16[2,256,256]{2,1,0:T(8,128)(2,1)S(1)} %collective-permute-done.8.refs_4_), channel_id=1, source_target_pairs={{8,0},{12,4},{16,8},{20,12},{24,16},{28,20},{9,1},{13,5},{17,9},{2... | collective-permute-start | bytes 786440 | tf_op jit(solution)/shard_map/ppermute | solution.py:45
  89.9 3.8 %collective-permute-start.14 = (bf16[2,256,256]{2,1,0:T(8,128)(2,1)S(1)}, bf16[2,256,256]{2,1,0:T(8,128)(2,1)S(1)}, u32[]{:S(2)}, u32[]{:S(2)}) collective-permute-start(bf16[2,256,256]{2,1,0:T(8,128)(2,1)S(1)} %get-tuple-element.13.refs_3_), channel_id=1, source_target_pairs={{0,4},{4,0},{8,12},{12,8},{16,20},{20,16},{24,28},{28,24},{1,5},{5... | collective-permute-start | bytes 786440 | tf_op jit(solution)/shard_map/ppermute | solution.py:41
  93.7 4.3 %collective-permute-start.7 = (bf16[2,256,256]{2,1,0:T(8,128)(2,1)S(1)}, bf16[2,256,256]{2,1,0:T(8,128)(2,1)S(1)}, u32[]{:S(2)}, u32[]{:S(2)}) collective-permute-start(bf16[2,256,256]{2,1,0:T(8,128)(2,1)S(1)} %collective-permute-done.6.refs_1_), channel_id=1, source_target_pairs={{0,8},{4,12},{8,16},{12,20},{16,24},{20,28},{1,9},{5,13},{9,17},{1... | collective-permute-start | bytes 786440 | tf_op jit(solution)/shard_map/ppermute | solution.py:44
  98.0 1.3 %collective-permute-start.10 = (bf16[2,256,256]{2,1,0:T(8,128)(2,1)S(1)}, bf16[2,256,256]{2,1,0:T(8,128)(2,1)S(1)}, u32[]{:S(2)}, u32[]{:S(2)}) collective-permute-start(bf16[2,256,256]{2,1,0:T(8,128)(2,1)S(1)} %collective-permute-done.9.refs_5_), channel_id=1, source_target_pairs={{8,0},{12,4},{16,8},{20,12},{24,16},{28,20},{9,1},{13,5},{17,9},{2... | collective-permute-start | bytes 786440 | tf_op jit(solution)/shard_map/ppermute | solution.py:45
  99.3 3.0 %fusion.2 = f32[1,1,2,256,256]{4,3,2,1,0:T(8,128)} fusion(f32[1,1,2,256,256]{4,3,2,1,0:T(8,128)} %param.13, f32[2,256,256]{2,1,0:T(8,128)S(1)} %convert_reduce_fusion, f32[2]{0:T(128)S(1)} %convert_element_type.37, pred[2]{0:T(512)(128)(4,1)S(1)} %dynamic-slice_reduce_fusion), kind=kOutput, calls=%fused_computation.5 | convolution fusion | flops 403308544 | bytes 1572874 | tf_op jit(solution)/shard_map/sji,sjk->sik/dot_general | solution.py:149
  102.3 2.7 %fusion.5 = f32[1,1,2,256,256]{4,3,2,1,0:T(8,128)} fusion(f32[1,1,2,256,256]{4,3,2,1,0:T(8,128)} %param.12, f32[2,256,256]{2,1,0:T(8,128)S(1)} %convert_reduce_fusion, f32[2]{0:T(128)S(1)} %convert_element_type.37, pred[2]{0:T(512)(128)(4,1)S(1)} %dynamic-slice_reduce_fusion), kind=kOutput, calls=%fused_computation.9 | convolution fusion | flops 403308544 | bytes 1572874 | tf_op jit(solution)/shard_map/sij,skj->sik/dot_general | solution.py:146
  104.9 1.9 %collective-permute-start.15 = (bf16[2,256,256]{2,1,0:T(8,128)(2,1)S(1)}, bf16[2,256,256]{2,1,0:T(8,128)(2,1)S(1)}, u32[]{:S(2)}, u32[]{:S(2)}) collective-permute-start(bf16[2,256,256]{2,1,0:T(8,128)(2,1)S(1)} %collective-permute-done.8.refs_4_), channel_id=1, source_target_pairs={{0,4},{4,0},{8,12},{12,8},{16,20},{20,16},{24,28},{28,24},{1,5},{5... | collective-permute-start | bytes 786440 | tf_op jit(solution)/shard_map/ppermute | solution.py:47
  111.2 3.1 %shard_map.128 = bf16[8,256,256]{2,1,0:T(8,128)(2,1)} custom-call(s32[8,2]{1,0:T(8,128)} %copy.37.table_ref, bf16[2,256,256]{2,1,0:T(8,128)(2,1)} %copy-done.11, bf16[2,256,256]{2,1,0:T(8,128)(2,1)} %copy-done.7, bf16[2,256,256]{2,1,0:T(8,128)(2,1)} %copy-done.5, bf16[2,256,256]{2,1,0:T(8,128)(2,1)} %copy-done.2, bf16[2,256,256]{2,1,0:T(8,128)(2,1)} %copy-done.6, ...), custom_call_target="tpu_custom_call" | custom-call | tf_op jit(solution)/shard_map/pallas_call | solution.py:79
  (86 shorter events, 9.5 us)
Async XLA Ops:
  3.9 54.8 %all-to-all-start = ((bf16[8,2,256,256]{3,2,1,0:T(8,128)(2,1)}), bf16[8,2,256,256]{3,2,1,0:T(8,128)(2,1)}, u32[]{:S(2)}, u32[]{:S(2)}) async-start(bf16[8,2,256,256]{3,2,1,0:T(8,128)(2,1)} %bitcast.7), calls=%async_computation | async-start | bytes 4194304 | tf_op jit(solution)/shard_map/all_to_all | solution.py:130
  10.4 50.2 %copy-start.1 = (f32[1,1,2,256,256]{4,3,2,1,0:T(8,128)S(1)}, f32[1,1,2,256,256]{4,3,2,1,0:T(8,128)}, u32[]{:S(2)}) copy-start(f32[1,1,2,256,256]{4,3,2,1,0:T(8,128)} %param.16) | copy-start | bytes 1572868
  10.4 50.7 %copy-start.4 = (bf16[1,1,2,256,256]{4,3,2,1,0:T(8,128)(2,1)S(1)}, bf16[1,1,2,256,256]{4,3,2,1,0:T(8,128)(2,1)}, u32[]{:S(2)}) copy-start(bf16[1,1,2,256,256]{4,3,2,1,0:T(8,128)(2,1)} %param.15) | copy-start | bytes 786436
  11.2 66.7 %copy-start.3 = (f32[1,1,2,256,256]{4,3,2,1,0:T(8,128)S(1)}, f32[1,1,2,256,256]{4,3,2,1,0:T(8,128)}, u32[]{:S(2)}) copy-start(f32[1,1,2,256,256]{4,3,2,1,0:T(8,128)} %param.17) | copy-start | bytes 1572868
  60.6 28.5 %copy-start.17 = (s32[8,1]{0,1:T(1,128)S(1)}, s32[8,1]{0,1:T(1,128)}, u32[]{:S(2)}) copy-start(s32[8,1]{0,1:T(1,128)} %param.10) | copy-start | bytes 100
  62.8 2.5 %collective-permute-start = (f32[2,9]{1,0:T(2,128)S(1)}, f32[2,9]{1,0:T(2,128)S(1)}, u32[]{:S(2)}, u32[]{:S(2)}) collective-permute-start(f32[2,9]{1,0:T(2,128)S(1)} %pad_maximum_fusion), channel_id=1, source_target_pairs={{0,1},{1,0},{2,3},{3,2},{4,5},{5,4},{6,7},{7,6},{8,9},{9,8},{10,11... | collective-permute-start | bytes 224 | tf_op jit(solution)/shard_map/ppermute | solution.py:20
  65.3 2.5 %collective-permute-start.1 = (f32[2,9]{1,0:T(2,128)S(1)}, f32[2,9]{1,0:T(2,128)S(1)}, u32[]{:S(2)}, u32[]{:S(2)}) collective-permute-start(f32[2,9]{1,0:T(2,128)S(1)} %fusion.31), channel_id=1, source_target_pairs={{0,2},{1,3},{2,0},{3,1},{4,6},{5,7},{6,4},{7,5},{8,10},{9,11},{10,... | collective-permute-start | bytes 224 | tf_op jit(solution)/shard_map/ppermute | solution.py:20
  67.8 4.1 %collective-permute-start.2 = (f32[2,9]{1,0:T(2,128)S(1)}, f32[2,9]{1,0:T(2,128)S(1)}, u32[]{:S(2)}, u32[]{:S(2)}) collective-permute-start(f32[2,9]{1,0:T(2,128)S(1)} %fusion.34), channel_id=1, source_target_pairs={{0,4},{4,0},{8,12},{12,8},{16,20},{20,16},{24,28},{28,24},{1,5},{5... | collective-permute-start | bytes 224 | tf_op jit(solution)/shard_map/ppermute | solution.py:20
  71.9 2.4 %collective-permute-start.3 = (f32[2,9]{1,0:T(2,128)S(1)}, f32[2,9]{1,0:T(2,128)S(1)}, u32[]{:S(2)}, u32[]{:S(2)}) collective-permute-start(f32[2,9]{1,0:T(2,128)S(1)} %add.92), channel_id=1, source_target_pairs={{0,8},{4,12},{8,0},{12,4},{16,24},{20,28},{24,16},{28,20},{1,9},{5... | collective-permute-start | bytes 224 | tf_op jit(solution)/shard_map/ppermute | solution.py:20
  74.3 3.3 %collective-permute-start.4 = (f32[2,9]{1,0:T(2,128)S(1)}, f32[2,9]{1,0:T(2,128)S(1)}, u32[]{:S(2)}, u32[]{:S(2)}) collective-permute-start(f32[2,9]{1,0:T(2,128)S(1)} %add.93), channel_id=1, source_target_pairs={{0,16},{4,20},{8,24},{12,28},{16,0},{20,4},{24,8},{28,12},{1,17},{... | collective-permute-start | bytes 224 | tf_op jit(solution)/shard_map/ppermute | solution.py:20
  78.8 30.8 %copy-start.2 = (bf16[2,256,256]{2,1,0:T(8,128)(2,1)}, bf16[2,256,256]{2,1,0:T(8,128)(2,1)S(1)}, u32[]{:S(2)}) copy-start(bf16[2,256,256]{2,1,0:T(8,128)(2,1)S(1)} %get-tuple-element.13.refs_3_) | copy-start | bytes 786436
  78.8 5.2 %collective-permute-start.5 = (bf16[2,256,256]{2,1,0:T(8,128)(2,1)S(1)}, bf16[2,256,256]{2,1,0:T(8,128)(2,1)S(1)}, u32[]{:S(2)}, u32[]{:S(2)}) collective-permute-start(bf16[2,256,256]{2,1,0:T(8,128)(2,1)S(1)} %get-tuple-element.13.refs_3_), channel_id=1, source_target_pairs={{0,8},{4,12},{8,16},{12,20},{16,24},{20,28},{1,9},{5,13},{9,17},{1... | collective-permute-start | bytes 786440 | tf_op jit(solution)/shard_map/ppermute | solution.py:44
  80.7 7.1 %collective-permute-start.8 = (bf16[2,256,256]{2,1,0:T(8,128)(2,1)S(1)}, bf16[2,256,256]{2,1,0:T(8,128)(2,1)S(1)}, u32[]{:S(2)}, u32[]{:S(2)}) collective-permute-start(bf16[2,256,256]{2,1,0:T(8,128)(2,1)S(1)} %get-tuple-element.13.refs_3_), channel_id=1, source_target_pairs={{8,0},{12,4},{16,8},{20,12},{24,16},{28,20},{9,1},{13,5},{17,9},{2... | collective-permute-start | bytes 786440 | tf_op jit(solution)/shard_map/ppermute | solution.py:45
  84.0 9.6 %collective-permute-start.6 = (bf16[2,256,256]{2,1,0:T(8,128)(2,1)S(1)}, bf16[2,256,256]{2,1,0:T(8,128)(2,1)S(1)}, u32[]{:S(2)}, u32[]{:S(2)}) collective-permute-start(bf16[2,256,256]{2,1,0:T(8,128)(2,1)S(1)} %collective-permute-done.5.refs_2_), channel_id=1, source_target_pairs={{0,8},{4,12},{8,16},{12,20},{16,24},{20,28},{1,9},{5,13},{9,17},{1... | collective-permute-start | bytes 786440 | tf_op jit(solution)/shard_map/ppermute | solution.py:44
  87.9 10.1 %collective-permute-start.9 = (bf16[2,256,256]{2,1,0:T(8,128)(2,1)S(1)}, bf16[2,256,256]{2,1,0:T(8,128)(2,1)S(1)}, u32[]{:S(2)}, u32[]{:S(2)}) collective-permute-start(bf16[2,256,256]{2,1,0:T(8,128)(2,1)S(1)} %collective-permute-done.8.refs_4_), channel_id=1, source_target_pairs={{8,0},{12,4},{16,8},{20,12},{24,16},{28,20},{9,1},{13,5},{17,9},{2... | collective-permute-start | bytes 786440 | tf_op jit(solution)/shard_map/ppermute | solution.py:45
  89.9 17.0 %collective-permute-start.14 = (bf16[2,256,256]{2,1,0:T(8,128)(2,1)S(1)}, bf16[2,256,256]{2,1,0:T(8,128)(2,1)S(1)}, u32[]{:S(2)}, u32[]{:S(2)}) collective-permute-start(bf16[2,256,256]{2,1,0:T(8,128)(2,1)S(1)} %get-tuple-element.13.refs_3_), channel_id=1, source_target_pairs={{0,4},{4,0},{8,12},{12,8},{16,20},{20,16},{24,28},{28,24},{1,5},{5... | collective-permute-start | bytes 786440 | tf_op jit(solution)/shard_map/ppermute | solution.py:41
  93.6 13.3 %collective-permute-start.13 = (bf16[2,256,256]{2,1,0:T(8,128)(2,1)S(1)}, bf16[2,256,256]{2,1,0:T(8,128)(2,1)S(1)}, u32[]{:S(2)}, u32[]{:S(2)}) collective-permute-start(bf16[2,256,256]{2,1,0:T(8,128)(2,1)S(1)} %collective-permute-done.5.refs_2_), channel_id=1, source_target_pairs={{0,4},{4,0},{8,12},{12,8},{16,20},{20,16},{24,28},{28,24},{1,5},{5... | collective-permute-start | bytes 786440 | tf_op jit(solution)/shard_map/ppermute | solution.py:46
  93.7 13.7 %collective-permute-start.7 = (bf16[2,256,256]{2,1,0:T(8,128)(2,1)S(1)}, bf16[2,256,256]{2,1,0:T(8,128)(2,1)S(1)}, u32[]{:S(2)}, u32[]{:S(2)}) collective-permute-start(bf16[2,256,256]{2,1,0:T(8,128)(2,1)S(1)} %collective-permute-done.6.refs_1_), channel_id=1, source_target_pairs={{0,8},{4,12},{8,16},{12,20},{16,24},{20,28},{1,9},{5,13},{9,17},{1... | collective-permute-start | bytes 786440 | tf_op jit(solution)/shard_map/ppermute | solution.py:44
  98.0 9.5 %collective-permute-start.10 = (bf16[2,256,256]{2,1,0:T(8,128)(2,1)S(1)}, bf16[2,256,256]{2,1,0:T(8,128)(2,1)S(1)}, u32[]{:S(2)}, u32[]{:S(2)}) collective-permute-start(bf16[2,256,256]{2,1,0:T(8,128)(2,1)S(1)} %collective-permute-done.9.refs_5_), channel_id=1, source_target_pairs={{8,0},{12,4},{16,8},{20,12},{24,16},{28,20},{9,1},{13,5},{17,9},{2... | collective-permute-start | bytes 786440 | tf_op jit(solution)/shard_map/ppermute | solution.py:45
  104.9 4.7 %collective-permute-start.15 = (bf16[2,256,256]{2,1,0:T(8,128)(2,1)S(1)}, bf16[2,256,256]{2,1,0:T(8,128)(2,1)S(1)}, u32[]{:S(2)}, u32[]{:S(2)}) collective-permute-start(bf16[2,256,256]{2,1,0:T(8,128)(2,1)S(1)} %collective-permute-done.8.refs_4_), channel_id=1, source_target_pairs={{0,4},{4,0},{8,12},{12,8},{16,20},{20,16},{24,28},{28,24},{1,5},{5... | collective-permute-start | bytes 786440 | tf_op jit(solution)/shard_map/ppermute | solution.py:47
  106.8 2.8 %collective-permute-start.12 = (bf16[2,256,256]{2,1,0:T(8,128)(2,1)S(1)}, bf16[2,256,256]{2,1,0:T(8,128)(2,1)S(1)}, u32[]{:S(2)}, u32[]{:S(2)}) collective-permute-start(bf16[2,256,256]{2,1,0:T(8,128)(2,1)S(1)} %collective-permute-done.6.refs_1_), channel_id=1, source_target_pairs={{0,4},{4,0},{8,12},{12,8},{16,20},{20,16},{24,28},{28,24},{1,5},{5... | collective-permute-start | bytes 786440 | tf_op jit(solution)/shard_map/ppermute | solution.py:46
  106.9 2.7 %collective-permute-start.16 = (bf16[2,256,256]{2,1,0:T(8,128)(2,1)S(1)}, bf16[2,256,256]{2,1,0:T(8,128)(2,1)S(1)}, u32[]{:S(2)}, u32[]{:S(2)}) collective-permute-start(bf16[2,256,256]{2,1,0:T(8,128)(2,1)S(1)} %collective-permute-done.9.refs_5_), channel_id=1, source_target_pairs={{0,4},{4,0},{8,12},{12,8},{16,20},{20,16},{24,28},{28,24},{1,5},{5... | collective-permute-start | bytes 786440 | tf_op jit(solution)/shard_map/ppermute | solution.py:47
  107.4 2.3 %collective-permute-start.11 = (bf16[2,256,256]{2,1,0:T(8,128)(2,1)S(1)}, bf16[2,256,256]{2,1,0:T(8,128)(2,1)S(1)}, u32[]{:S(2)}, u32[]{:S(2)}) collective-permute-start(bf16[2,256,256]{2,1,0:T(8,128)(2,1)S(1)} %collective-permute-done.7.refs_0_), channel_id=1, source_target_pairs={{0,4},{4,0},{8,12},{12,8},{16,20},{20,16},{24,28},{28,24},{1,5},{5... | collective-permute-start | bytes 786440 | tf_op jit(solution)/shard_map/ppermute | solution.py:46
  107.5 3.7 %collective-permute-start.17 = (bf16[2,256,256]{2,1,0:T(8,128)(2,1)S(1)}, bf16[2,256,256]{2,1,0:T(8,128)(2,1)}, u32[]{:S(2)}, u32[]{:S(2)}) collective-permute-start(bf16[2,256,256]{2,1,0:T(8,128)(2,1)S(1)} %collective-permute-done.10.refs_6_), channel_id=1, source_target_pairs={{0,4},{4,0},{8,12},{12,8},{16,20},{20,16},{24,28},{28,24},{1,5},{5... | collective-permute-start | bytes 786440 | tf_op jit(solution)/shard_map/ppermute | solution.py:47
  (14 other events, 95.9 us)
